TPU v7x, 128 devices: a whole 4x4x4 slice. The times are simulated.
128 devices in a mesh: tm: 32 (over x, z, core), feat: 4 (over y).
Axes of the slice: x: 4, y: 4, z: 4, core: 2. Of those that a mesh axis runs over, the one named last changes fastest.
Arguments:
- activations: bfloat16 [81920, 2048], P(('tm', 'feat')), may hold values from -19 to 19
- targets: bfloat16 [81920, 128], P(('tm', 'feat')), may hold values from -8 to 8
- span_of: int32 [81920], P(('tm', 'feat')), may hold values from 0 to 31, as said below
Outputs:
- predictions: bfloat16 [81920, 128], P(('tm', 'feat'))
- surprise: float32 [81920], P(('tm', 'feat'))
Inputs may be any that keep to these rules, and one draw needn't show every extreme that they name: `span_of`: in each aligned block of 640 rows (the rows of one device) every span from 0 to 31 appears exactly 20 times.
All inputs are finite; a program needn't handle non-finite values.
Results may differ from a plain program's by a relative error of at most 0.0049.
Values may be sent and summed in bfloat16 or wider, within the bound.
No kernel may reach another device: no remote copies, remote signals or barrier semaphores. Data moves between devices by JAX's collectives and lax.ppermute only.
A program may use at most 320 MiB of HBM per device.

v0:
```python
import jax
import jax.numpy as jnp
from jax import lax
from jax.sharding import PartitionSpec as P

ITERS = 3


RIDGE = 0.1
TINY = 1e-06


def carried_in(shard, axis, combine, identity):
    length, position = (lax.axis_size(axis), lax.axis_index(axis))
    everything = jax.tree.map(lambda part: lax.all_gather(part, axis), shard)
    start = jax.tree.map(
        lambda part, zero: jnp.broadcast_to(jnp.asarray(zero, part.dtype), part.shape),
        shard,
        identity,
    )

    def hop(k, before):
        reached = k < position
        new = combine(before, jax.tree.map(lambda part: part[k], everything))
        return jax.tree.map(lambda a, b: jnp.where(reached, a, b), new, before)

    return lax.fori_loop(0, length, hop, start)


def body(activations, targets, span_of):
    spans = lax.axis_size("tm")
    feat_count = lax.axis_size("feat")
    tok_dev, width = activations.shape
    n_targets = targets.shape[1]
    block_rows = width // feat_count
    share = tok_dev // spans
    contract = (((0,), (0,)), ((), ()))
    highest = lax.Precision.HIGHEST
    order = jnp.argsort(span_of, stable=True)
    sorted_x = jnp.take(activations, order, axis=0).reshape(spans, share, width)
    sorted_y = jnp.take(targets, order, axis=0).reshape(spans, share, n_targets)
    moved_x, moved_y = (
        lax.all_to_all(sorted_x, "tm", split_axis=0, concat_axis=0, tiled=True),
        lax.all_to_all(sorted_y, "tm", split_axis=0, concat_axis=0, tiled=True),
    )
    local_x = moved_x.reshape(tok_dev, width)
    local_y = moved_y.reshape(tok_dev, n_targets)
    col_start = lax.axis_index("feat") * block_rows
    rows_x = lax.all_gather(local_x, "feat", axis=0, tiled=True)
    rows_y = lax.all_gather(local_y, "feat", axis=0, tiled=True)
    own = lax.dynamic_slice_in_dim(rows_x, col_start, block_rows, 1)
    gram_part = lax.dot_general(own, rows_x, contract, preferred_element_type=jnp.float32)
    cross_part = lax.dot_general(own, rows_y, contract, preferred_element_type=jnp.float32)

    def combine(earlier, later):
        return (earlier[0] + later[0], earlier[1] + later[1])

    identity = (jnp.zeros_like(gram_part), jnp.zeros_like(cross_part))
    gram_prefix, cross_prefix = carried_in((gram_part, cross_part), "tm", combine, identity)
    seen = (lax.axis_index("tm") * (tok_dev * feat_count)).astype(jnp.float32)
    scale = 1.0 / jnp.maximum(seen, 1.0)
    rhs = scale * cross_prefix

    def column_dot(left, right):
        return lax.psum(jnp.sum(left * right, axis=0), "feat")

    residual = rhs
    direction = rhs
    norm_now = column_dot(residual, residual)
    solution = None
    for step in range(ITERS):
        product = jnp.dot(
            gram_prefix,
            lax.all_gather(direction, "feat", axis=0, tiled=True),
            precision=highest,
            preferred_element_type=jnp.float32,
        )
        product, carried = (product, direction)
        image = scale * product + RIDGE * direction
        alpha = norm_now / (column_dot(direction, image) + TINY)
        update = alpha * carried
        solution = update if solution is None else solution + update
        if step + 1 < ITERS:
            residual = residual - alpha * image
            norm_next = column_dot(residual, residual)
            direction = residual + norm_next / (norm_now + TINY) * direction
            norm_now = norm_next
    weights = lax.all_gather(solution.astype(jnp.bfloat16), "feat", axis=0, tiled=True)
    predicted = jnp.dot(local_x, weights, preferred_element_type=jnp.float32).astype(jnp.bfloat16)
    returned = lax.all_to_all(
        predicted.reshape(spans, share, n_targets), "tm", split_axis=0, concat_axis=0, tiled=True
    )
    in_order = returned.reshape(tok_dev, n_targets)
    predictions = jnp.zeros_like(in_order).at[order].set(in_order)
    error = targets.astype(jnp.float32) - predictions.astype(jnp.float32)
    surprise = jnp.mean(error * error, axis=1)
    return (predictions, surprise)


def solution(mesh):
    return jax.shard_map(
        body,
        mesh=mesh,
        in_specs=(P(("tm", "feat"), None), P(("tm", "feat"), None), P(("tm", "feat"))),
        out_specs=(P(("tm", "feat"), None), P(("tm", "feat"))),
        check_vma=False,
    )
```

profile of v0, /device:TPU:1, one launch (start us, length us, event | category | flops | bytes accessed | tf_op | source)
XLA Modules:
  0.0 1049.8 jit_solution(8673995626986290233)
XLA Ops:
  24.1 48.7 %all_to_all.15 = bf16[32,20,2048]{2,1,0:T(8,128)(2,1)} all-to-all(bf16[32,20,2048]{2,1,0:T(8,128)(2,1)S(1)} %broadcast_select_fusion), channel_id=1, replica_groups=mesh['tm'=32,'feat'=4] {'tm'}, dimensions={0} | all-to-all | bytes 5242880 | tf_op jit(solution)/shard_map/all_to_all | solution.py:43
  85.0 8.2 all-to-all-done.1
  93.9 16.8 %all_gather.33 = bf16[2560,128]{1,0:T(8,128)(2,1)S(1)} all-gather(bf16[640,128]{1,0:T(8,128)(2,1)} %reshape.40), channel_id=1, replica_groups=mesh['tm'=32,'feat'=4] {'feat'}, dimensions={0}, use_global_device_ids=true | all-gather | bytes 819200 | tf_op jit(solution)/shard_map/all_gather | solution.py:50
  110.7 71.1 %all-gather.9.cloned.1.call-done = bf16[2560,2048]{1,0:T(8,128)(2,1)} async-done(((bf16[640,2048]{1,0:T(8,128)(2,1)}), bf16[2560,2048]{1,0:T(8,128)(2,1)}) %all-gather.9.cloned.1.call-update) | async-done | bytes 10485776 | tf_op jit(solution)/shard_map/all_gather | solution.py:49
  185.2 10.5 fusion.2
  195.8 43.9 %all-gather.19.cloned.1.call-done = f32[16384,128]{1,0:T(8,128)} async-done(((f32[512,128]{1,0:T(8,128)}), f32[16384,128]{1,0:T(8,128)}) %all-gather.19.cloned.1.call-update) | async-done | bytes 8388624 | tf_op jit(solution)/shard_map/all_gather | solution.py:15
  239.7 377.4 %all-gather.17.cloned.1.call-done = f32[16384,2048]{1,0:T(8,128)} async-done(((f32[512,2048]{1,0:T(8,128)}), f32[16384,2048]{1,0:T(8,128)}) %all-gather.17.cloned.1.call-update) | async-done | bytes 134217744 | tf_op jit(solution)/shard_map/all_gather | solution.py:15
  617.2 248.0 %while.16 = (s32[]{:T(128)}, f32[512,2048]{1,0:T(8,128)}, f32[512,128]{1,0:T(8,128)S(1)}, s32[]{:T(128)}, f32[32,512,2048]{2,1,0:T(8,128)}, /*index=5*/f32[32,512,128]{2,1,0:T(8,128)}, s32[]{:T(128)}, s32[]{:T(128)}) while((s32[]{:T(128)}, f32[512,2048]{1,0:T(8,128)}, f32[512,128]{1,0:T(8,128)S(1)}, s32[]{:T(128)}, ...), condition=%wide.region_2.3_spmd.clone, body=%wide.region_1.2_spmd.clone.sunk | while | flops 3342340 | bytes 13369459 | solution.py:27
  623.7 6.7 add_select_fusion.4
  631.5 6.7 add_select_fusion.4
  639.2 6.7 add_select_fusion.4
  647.0 6.7 add_select_fusion.4
  654.8 6.7 add_select_fusion.4
  662.6 6.7 add_select_fusion.4
  670.4 6.7 add_select_fusion.4
  678.2 6.7 add_select_fusion.4
  686.0 6.7 add_select_fusion.4
  693.8 6.7 add_select_fusion.4
  701.6 6.7 add_select_fusion.4
  709.4 6.7 add_select_fusion.4
  717.1 6.7 add_select_fusion.4
  724.9 6.7 add_select_fusion.4
  732.7 6.7 add_select_fusion.4
  740.5 6.7 add_select_fusion.4
  748.3 6.7 add_select_fusion.4
  756.1 6.7 add_select_fusion.4
  763.9 6.7 add_select_fusion.4
  771.7 6.7 add_select_fusion.4
  779.5 6.7 add_select_fusion.4
  787.3 6.7 add_select_fusion.4
  795.0 6.7 add_select_fusion.4
  802.8 6.7 add_select_fusion.4
  810.6 6.7 add_select_fusion.4
  818.4 6.7 add_select_fusion.4
  826.2 6.7 add_select_fusion.4
  834.0 6.7 add_select_fusion.4
  841.8 6.7 add_select_fusion.4
  849.6 6.7 add_select_fusion.4
  857.4 6.7 add_select_fusion.4
  866.0 20.6 %all-gather.11.cloned.1.call-done = f32[2048,128]{1,0:T(8,128)} async-done(((f32[512,128]{1,0:T(8,128)}), f32[2048,128]{1,0:T(8,128)}) %all-gather.11.cloned.1.call-update) | async-done | bytes 1048592 | tf_op jit(solution)/shard_map/all_gather | solution.py:74
  893.2 7.8 all-reduce
  908.9 27.8 %all-gather.13.cloned.1.call-done = f32[2048,128]{1,0:T(8,128)} async-done(((f32[512,128]{1,0:T(8,128)}), f32[2048,128]{1,0:T(8,128)}) %all-gather.13.cloned.1.call-update) | async-done | bytes 1048592 | tf_op jit(solution)/shard_map/all_gather | solution.py:74
  936.7 6.6 multiply_reduce_fusion.2
  943.4 7.7 psum.45
  960.0 27.8 %all-gather.15.cloned.1.call-done = f32[2048,128]{1,0:T(8,128)} async-done(((f32[512,128]{1,0:T(8,128)}), f32[2048,128]{1,0:T(8,128)}) %all-gather.15.cloned.1.call-update) | async-done | bytes 1048592 | tf_op jit(solution)/shard_map/all_gather | solution.py:74
  993.7 7.7 psum.47
  1002.5 10.6 %all_gather.39 = bf16[2048,128]{1,0:T(8,128)(2,1)S(1)} all-gather(bf16[512,128]{1,0:T(8,128)(2,1)S(1)} %add_convert_fusion), channel_id=1, replica_groups=mesh['tm'=32,'feat'=4] {'feat'}, dimensions={0}, use_global_device_ids=true | all-gather | bytes 655360 | tf_op jit(solution)/shard_map/all_gather | solution.py:88
  1015.7 22.1 %all_to_all.16 = bf16[32,20,128]{2,1,0:T(8,128)(2,1)S(1)} all-to-all(bf16[32,20,128]{2,1,0:T(8,128)(2,1)S(1)} %reshape.41), channel_id=1, replica_groups=mesh['tm'=32,'feat'=4] {'tm'}, dimensions={0} | all-to-all | bytes 327680 | tf_op jit(solution)/shard_map/all_to_all | solution.py:90
  (94 shorter events, 110.2 us)
Async XLA Ops:
  7.2 5.3 copy-start
  7.2 174.6 %all-gather.9.cloned.1.call-start = ((), (), s32[]{:S(2)}) async-start(), calls=%async_computation.3 | async-start | bytes 13107200 | tf_op jit(solution)/shard_map/all_gather | solution.py:49
  72.8 5.3 copy-start.1
  81.0 12.2 %all-to-all-start.1 = ((bf16[32,20,128]{2,1,0:T(8,128)(2,1)}), bf16[32,20,128]{2,1,0:T(8,128)(2,1)S(1)}, u32[]{:S(2)}, u32[]{:S(2)}) async-start(bf16[32,20,128]{2,1,0:T(8,128)(2,1)} %broadcast_select_fusion.1), calls=%async_computation.1 | async-start | bytes 393216 | tf_op jit(solution)/shard_map/all_to_all | solution.py:44
  84.9 154.8 %all-gather.19.cloned.1.call-start = ((), (), s32[]{:S(2)}) async-start(), calls=%async_computation.8 | async-start | bytes 8650752 | tf_op jit(solution)/shard_map/all_gather | solution.py:15
  185.2 432.0 %all-gather.17.cloned.1.call-start = ((), (), s32[]{:S(2)}) async-start(), calls=%async_computation.7 | async-start | bytes 138412032 | tf_op jit(solution)/shard_map/all_gather | solution.py:15
  195.7 690.9 %all-gather.11.cloned.1.call-start = ((), (), s32[]{:S(2)}) async-start(), calls=%async_computation.4 | async-start | bytes 1310720 | tf_op jit(solution)/shard_map/all_gather | solution.py:74
  865.9 70.8 %all-gather.13.cloned.1.call-start = ((), (), s32[]{:S(2)}) async-start(), calls=%async_computation.5 | async-start | bytes 1310720 | tf_op jit(solution)/shard_map/all_gather | solution.py:74
  902.1 6.0 copy-start.3
  908.9 49.3 %copy-start.2 = (f32[512,128]{1,0:T(8,128)S(1)}, f32[512,128]{1,0:T(8,128)}, u32[]{:S(2)}) copy-start(f32[512,128]{1,0:T(8,128)} %multiply_add_fusion.1) | copy-start | bytes 786436
  908.9 78.9 %all-gather.15.cloned.1.call-start = ((), (), s32[]{:S(2)}) async-start(), calls=%async_computation.6 | async-start | bytes 1310720 | tf_op jit(solution)/shard_map/all_gather | solution.py:74
  1042.2 0.8 copy-start.4
Sparse Core Ops, SparseCore 0:
  78.2 103.5 all-gather.8
  185.3 54.3 all-gather.18
  242.0 375.1 all-gather.16
  866.0 20.4 all-gather.10
  909.0 27.6 all-gather.12
  960.1 27.6 all-gather.14
where the time goes:
time: 1050 us
  waiting for transfers between devices  577 us (55%)
  other arithmetic  263 us (25%)
  blocking collectives  133 us (13%)
  matrix products  35.6 us (3%)
  local copies, waits for them, and re-layouts  21.7 us (2%)
  between operations  14.3 us (1%)
    all_gather x2, waiting for transfers between devices, carried_in(): everything = jax.tree.map(lambda part: lax.all_gather(part, axis), shard)  421 us
    select_n x64, other arithmetic, hop(): return jax.tree.map(lambda a, b: jnp.where(reached, a, b), new, before)  247 us
    all_gather x3, waiting for transfers between devices, body(): lax.all_gather(direction, 'feat', axis=0, tiled=True)  76.2 us
    all_gather x1, waiting for transfers between devices, body(): rows_x = lax.all_gather(local_x, 'feat', axis=0, tiled=True)  71.1 us
    all_to_all x1, blocking collectives, body(): lax.all_to_all(sorted_x, 'tm', split_axis=0, concat_axis=0, tiled=True)  48.7 us
    psum x5, blocking collectives, column_dot(): return lax.psum(jnp.sum(left * right, axis=0), 'feat')  35.2 us
    all_to_all x1, blocking collectives, body(): lax.all_to_all(predicted.reshape(spans, share, n_targets), 'tm', split_ax...  22.1 us
  transfers between devices with their start and end apart: 7, of which 7 were waited for; matrix products, arithmetic and copies ran while one was open for 1% of the time, Pallas kernels for 0%

commit v1 on v0

v1 whole, which is shorter than its diff:
```python
import jax
import jax.numpy as jnp
from jax import lax
from jax.sharding import Mesh, PartitionSpec as P

ITERS = 3


RIDGE = 0.1
TINY = 1e-06

TM = ("x", "z", "c")
SWAP = [(0, 1), (1, 0)]


def masked_sum(stack, position):
    keep = jnp.arange(stack.shape[0]) < position
    return jnp.sum(jnp.where(keep.reshape((-1,) + (1,) * (stack.ndim - 1)), stack, 0.0), axis=0)


def exclusive_prefix(block):
    ci = lax.axis_index("c")
    zi = lax.axis_index("z")
    xi = lax.axis_index("x")
    rows = block.shape[0]
    half = rows // 2
    partner = lax.ppermute(block, "c", SWAP)
    chip = block + partner
    below = jnp.where(ci == 1, partner, 0.0)
    mine = lax.dynamic_slice_in_dim(chip, ci * half, half, 0)
    along_z = lax.all_gather(mine, "z")
    before_z = masked_sum(along_z, zi)
    total_z = jnp.sum(along_z, axis=0)
    along_x = lax.all_gather(total_z, "x")
    before_x = masked_sum(along_x, xi)
    mine_prefix = before_x + before_z
    other_prefix = lax.ppermute(mine_prefix, "c", SWAP)
    joined = jnp.zeros((rows,) + block.shape[1:], block.dtype)
    joined = lax.dynamic_update_slice_in_dim(joined, mine_prefix, ci * half, 0)
    joined = lax.dynamic_update_slice_in_dim(joined, other_prefix, (1 - ci) * half, 0)
    return joined + below


def body(activations, targets, span_of):
    spans = lax.axis_size(TM)
    feat_count = lax.axis_size("feat")
    tok_dev, width = activations.shape
    n_targets = targets.shape[1]
    block_rows = width // feat_count
    share = tok_dev // spans
    contract = (((0,), (0,)), ((), ()))
    highest = lax.Precision.HIGHEST
    order = jnp.argsort(span_of, stable=True)
    sorted_x = jnp.take(activations, order, axis=0).reshape(spans, share, width)
    sorted_y = jnp.take(targets, order, axis=0).reshape(spans, share, n_targets)
    moved_x, moved_y = (
        lax.all_to_all(sorted_x, TM, split_axis=0, concat_axis=0, tiled=True),
        lax.all_to_all(sorted_y, TM, split_axis=0, concat_axis=0, tiled=True),
    )
    local_x = moved_x.reshape(tok_dev, width)
    local_y = moved_y.reshape(tok_dev, n_targets)
    col_start = lax.axis_index("feat") * block_rows
    rows_x = lax.all_gather(local_x, "feat", axis=0, tiled=True)
    rows_y = lax.all_gather(local_y, "feat", axis=0, tiled=True)
    own = lax.dynamic_slice_in_dim(rows_x, col_start, block_rows, 1)
    gram_part = lax.dot_general(own, rows_x, contract, preferred_element_type=jnp.float32)
    cross_part = lax.dot_general(own, rows_y, contract, preferred_element_type=jnp.float32)

    gram_prefix = exclusive_prefix(gram_part)
    cross_prefix = exclusive_prefix(cross_part)
    span = (lax.axis_index("x") * lax.axis_size("z") + lax.axis_index("z")) * lax.axis_size("c") + lax.axis_index("c")
    seen = (span * (tok_dev * feat_count)).astype(jnp.float32)
    scale = 1.0 / jnp.maximum(seen, 1.0)
    rhs = scale * cross_prefix

    def column_dot(left, right):
        return lax.psum(jnp.sum(left * right, axis=0), "feat")

    residual = rhs
    direction = rhs
    norm_now = column_dot(residual, residual)
    solution = None
    for step in range(ITERS):
        product = jnp.dot(
            gram_prefix,
            lax.all_gather(direction, "feat", axis=0, tiled=True),
            precision=highest,
            preferred_element_type=jnp.float32,
        )
        image = scale * product + RIDGE * direction
        alpha = norm_now / (column_dot(direction, image) + TINY)
        update = alpha * direction
        solution = update if solution is None else solution + update
        if step + 1 < ITERS:
            residual = residual - alpha * image
            norm_next = column_dot(residual, residual)
            direction = residual + norm_next / (norm_now + TINY) * direction
            norm_now = norm_next
    weights = lax.all_gather(solution.astype(jnp.bfloat16), "feat", axis=0, tiled=True)
    predicted = jnp.dot(local_x, weights, preferred_element_type=jnp.float32).astype(jnp.bfloat16)
    returned = lax.all_to_all(
        predicted.reshape(spans, share, n_targets), TM, split_axis=0, concat_axis=0, tiled=True
    )
    in_order = returned.reshape(tok_dev, n_targets)
    predictions = jnp.zeros_like(in_order).at[order].set(in_order)
    error = targets.astype(jnp.float32) - predictions.astype(jnp.float32)
    surprise = jnp.mean(error * error, axis=1)
    return (predictions, surprise)


def solution(mesh):
    tm = mesh.shape["tm"]
    feat = mesh.shape["feat"]
    fine = Mesh(mesh.devices.reshape(tm // 8, 4, 2, feat), TM + ("feat",))
    rows = TM + ("feat",)
    return jax.shard_map(
        body,
        mesh=fine,
        in_specs=(P(rows, None), P(rows, None), P(rows)),
        out_specs=(P(rows, None), P(rows)),
        check_vma=False,
    )
```

time: 1050 us -> 594 us (0.57)
  waiting for transfers between devices: 577 us -> 316 us
  other arithmetic: 263 us -> 37.2 us
  blocking collectives: 133 us -> 150 us
  starting transfers between devices: 4.17 us -> 16.6 us
    all_gather x2, waiting for transfers between devices: 421 us -> 133 us  [the longest x1 83.9 us: exclusive_prefix(): along_z = lax.all_gather(mine, 'z')]
    select_n x64 -> x0, other arithmetic: 247 us -> none  [hop(): return jax.tree.map(lambda a, b: jnp.where(reached, a, b), new, before)]
    all_gather x1, waiting for transfers between devices: 71.1 us -> 98.4 us  [body(): rows_x = lax.all_gather(local_x, 'feat', axis=0, tiled=True)]
    all_gather x0 -> x2, blocking collectives: none -> 21.6 us  [the longest x1 11.2 us: exclusive_prefix(): along_z = lax.all_gather(mine, 'z')]
    reduce_sum x0 -> x4, other arithmetic: none -> 11.4 us  [masked_sum(): jnp.sum(jnp.where(keep.reshape((-1,) + (1,) * (stack.ndim - 1)), stack, 0...]
    add x0 -> x3, other arithmetic: none -> 10.6 us  [the longest x1 6.63 us: exclusive_prefix(): return joined + below]
  transfers between devices with their start and end apart: 7 -> 11, of which waited for: 7 -> 9; matrix products, arithmetic and copies ran while one was open for 1% -> 4% of each run, Pallas kernels for 0% -> 0%
where the time goes in v1:
time: 594 us; the launch traced here: 593 us
  waiting for transfers between devices  316 us (53%)
  blocking collectives  150 us (25%)
  other arithmetic  37.2 us (6%)
  matrix products  33.2 us (6%)
  local copies, waits for them, and re-layouts  25.1 us (4%)
  starting transfers between devices  16.6 us (3%)
  between operations  14.4 us (2%)
    all_gather x1, waiting for transfers between devices, body(): rows_x = lax.all_gather(local_x, 'feat', axis=0, tiled=True)  98.4 us
    all_gather x1, waiting for transfers between devices, exclusive_prefix(): along_z = lax.all_gather(mine, 'z')  83.9 us
    all_gather x3, waiting for transfers between devices, body(): lax.all_gather(direction, 'feat', axis=0, tiled=True)  68.6 us
    all_gather x1, waiting for transfers between devices, exclusive_prefix(): along_x = lax.all_gather(total_z, 'x')  48.8 us
    all_to_all x1, blocking collectives, body(): lax.all_to_all(sorted_x, TM, split_axis=0, concat_axis=0, tiled=True)  48.7 us
    psum x5, blocking collectives, column_dot(): return lax.psum(jnp.sum(left * right, axis=0), 'feat')  35.1 us
    all_to_all x1, blocking collectives, body(): lax.all_to_all(predicted.reshape(spans, share, n_targets), TM, split_axis...  22.2 us
    dot_general x3, matrix products, body(): jnp.dot(gram_prefix, lax.all_gather(direction, 'feat', axis=0, tiled=True...  17.6 us
  transfers between devices with their start and end apart: 11, of which 9 were waited for; matrix products, arithmetic and copies ran while one was open for 4% of the time, Pallas kernels for 0%

profile of v1, /device:TPU:1, one launch (start us, length us, event | category | flops | bytes accessed | tf_op | source)
XLA Modules:
  0.0 592.7 jit_solution(11710074773149398378)
XLA Ops:
  7.2 5.2 sort.17
  12.5 4.1 gather_fusion
  16.6 5.2 gather.13
  21.9 2.2 broadcast_select_fusion
  24.1 48.7 %all_to_all.15 = bf16[32,20,2048]{2,1,0:T(8,128)(2,1)} all-to-all(bf16[32,20,2048]{2,1,0:T(8,128)(2,1)S(1)} %broadcast_select_fusion), channel_id=1, replica_groups=mesh['x'=4,'z'=4,'c'=2,'feat'=4] {'x','z','c'}, dimensions={0} | all-to-all | bytes 5242880 | tf_op jit(solution)/shard_map/all_to_all | solution.py:57
  72.8 5.2 reshape.51
  78.1 98.4 %all-gather.11.cloned.1.call-done = bf16[2560,2048]{1,0:T(8,128)(2,1)} async-done(((bf16[640,2048]{1,0:T(8,128)(2,1)}), bf16[2560,2048]{1,0:T(8,128)(2,1)}) %all-gather.11.cloned.1.call-update) | async-done | bytes 10485776 | tf_op jit(solution)/shard_map/all_gather | solution.py:63
  176.5 10.4 %fusion = f32[512,2048]{1,0:T(8,128)} fusion(bf16[2560,2048]{1,0:T(8,128)(2,1)} %all-gather.11.cloned.1.call-done, s32[]{:T(128)S(6)} %select_n.63), kind=kOutput, calls=%fused_computation.7 | convolution fusion | flops 5368709120 | bytes 17301508 | tf_op jit(solution)/shard_map/dot_general | solution.py:66
  186.9 0.8 collective-permute-start.2
  187.8 7.1 %collective-permute-done.2 = f32[512,2048]{1,0:T(8,128)} collective-permute-done((f32[512,2048]{1,0:T(8,128)}, f32[512,2048]{1,0:T(8,128)}, u32[]{:S(2)}, u32[]{:S(2)}) %collective-permute-start.2) | collective-permute-done | bytes 4194336 | tf_op jit(solution)/shard_map/ppermute | solution.py:27
  194.9 3.9 dynamic-slice_add_fusion
  198.9 83.9 %all-gather.19.cloned.1.call-done = f32[1024,2048]{1,0:T(8,128)} async-done(((f32[256,2048]{1,0:T(8,128)}), f32[1024,2048]{1,0:T(8,128)}) %all-gather.19.cloned.1.call-update) | async-done | bytes 8388624 | tf_op jit(solution)/shard_map/all_gather | solution.py:31
  282.8 6.5 %select_reduce_fusion = (f32[256,2048]{1,0:T(8,128)S(1)}, f32[256,2048]{1,0:T(8,128)}) fusion(f32[4,256,2048]{2,1,0:T(8,128)} %bitcast.14, pred[4]{0:T(512)(128)(4,1)S(1)} %iota_compare_fusion), kind=kLoop, calls=%fused_computation.3 | loop fusion | flops 5242880 | bytes 12582916 | tf_op jit(solution)/shard_map/reduce_sum | solution.py:18
  289.4 2.0 gather_fusion.1
  291.4 0.9 broadcast_select_fusion.1
  292.3 7.4 %all-to-all-start.1 = ((bf16[32,20,128]{2,1,0:T(8,128)(2,1)}), bf16[32,20,128]{2,1,0:T(8,128)(2,1)S(1)}, u32[]{:S(2)}, u32[]{:S(2)}) async-start(bf16[32,20,128]{2,1,0:T(8,128)(2,1)} %broadcast_select_fusion.1), calls=%async_computation.1 | async-start | bytes 393216 | tf_op jit(solution)/shard_map/all_to_all | solution.py:58
  299.7 8.2 %all-to-all-done.1 = bf16[32,20,128]{2,1,0:T(8,128)(2,1)S(1)} async-done(((bf16[32,20,128]{2,1,0:T(8,128)(2,1)}), bf16[32,20,128]{2,1,0:T(8,128)(2,1)S(1)}, u32[]{:S(2)}, u32[]{:S(2)}) %all-to-all-start.1) | async-done | bytes 163872 | tf_op jit(solution)/shard_map/all_to_all | solution.py:58
  308.0 11.8 %all_gather.43 = bf16[2560,128]{1,0:T(8,128)(2,1)S(1)} all-gather(bf16[640,128]{1,0:T(8,128)(2,1)S(1)} %reshape.52), channel_id=1, replica_groups=mesh['x'=4,'z'=4,'c'=2,'feat'=4] {'feat'}, dimensions={0}, use_global_device_ids=true | all-gather | bytes 819200 | tf_op jit(solution)/shard_map/all_gather | solution.py:64
  319.8 2.6 fusion.2
  322.4 2.1 collective-permute-start
  324.5 48.8 %all-gather.21.cloned.1.call-done = f32[1024,2048]{1,0:T(8,128)} async-done(((f32[256,2048]{1,0:T(8,128)}), f32[1024,2048]{1,0:T(8,128)}) %all-gather.21.cloned.1.call-update) | async-done | bytes 8388624 | tf_op jit(solution)/shard_map/all_gather | solution.py:34
  373.4 4.7 select_reduce_fusion.1
  378.1 2.5 broadcast_in_dim.92
  380.6 2.5 constant_dynamic-update-slice_fusion.1
  383.1 0.8 collective-permute-start.3
  383.9 11.2 %all-gather = f32[1024,128]{1,0:T(8,128)S(1)} all-gather(f32[256,128]{1,0:T(8,128)S(1)} %dynamic-slice_add_fusion.1), channel_id=2, replica_groups=mesh['x'=4,'z'=4,'c'=2,'feat'=4] {'z'}, dimensions={0}, use_global_device_ids=true | all-gather | bytes 655360 | tf_op jit(solution)/shard_map/all_gather | solution.py:31
  395.2 10.4 %all-gather.1 = f32[1024,128]{1,0:T(8,128)S(1)} all-gather(f32[256,128]{1,0:T(8,128)S(1)} %get-tuple-element.7), channel_id=3, replica_groups=mesh['x'=4,'z'=4,'c'=2,'feat'=4] {'x'}, dimensions={0}, use_global_device_ids=true | all-gather | bytes 655360 | tf_op jit(solution)/shard_map/all_gather | solution.py:34
  405.7 5.3 collective-permute-start.1
  411.1 0.9 collective-permute-done.1
  412.9 1.6 constant_dynamic-update-slice_fusion
  414.4 6.6 %select_add_fusion = f32[512,2048]{1,0:T(8,128)} fusion(f32[512,2048]{1,0:T(8,128)} %constant_dynamic-update-slice_fusion, f32[512,2048]{1,0:T(8,128)} %collective-permute-done.2, pred[]{:T(512)S(6)} %eq.4), kind=kLoop, calls=%fused_computation.5 | loop fusion | flops 2097152 | bytes 12582913 | tf_op jit(solution)/shard_map/add | solution.py:41
  421.1 13.0 %all-gather.13.cloned.1.call-done = f32[2048,128]{1,0:T(8,128)} async-done(((f32[512,128]{1,0:T(8,128)}), f32[2048,128]{1,0:T(8,128)}) %all-gather.13.cloned.1.call-update) | async-done | bytes 1048592 | tf_op jit(solution)/shard_map/all_gather | solution.py:86
  434.1 5.5 multiply_reduce_fusion.4
  439.6 7.7 %all-reduce = (f32[128]{0:T(128)S(1)}, f32[128]{0:T(128)S(1)}) all-reduce(f32[128]{0:T(128)S(1)} %get-tuple-element.9, f32[128]{0:T(128)S(1)} %get-tuple-element.8), channel_id=1, replica_groups=mesh['x'=4,'z'=4,'c'=2,'feat'=4] {'feat'}, use_global_device_ids=true, to_apply=%region_5.6 | all-reduce | flops 256 | bytes 2048 | tf_op jit(solution)/shard_map/psum | solution.py:77
  447.4 6.0 %psum.44 = f32[128]{0:T(128)S(1)} all-reduce(f32[128]{0:T(128)S(1)} %get-tuple-element.12), channel_id=1, replica_groups=mesh['x'=4,'z'=4,'c'=2,'feat'=4] {'feat'}, use_global_device_ids=true, to_apply=%region_12.13 | all-reduce | flops 128 | bytes 1024 | tf_op jit(solution)/shard_map/psum | solution.py:77
  454.2 27.8 %all-gather.15.cloned.1.call-done = f32[2048,128]{1,0:T(8,128)} async-done(((f32[512,128]{1,0:T(8,128)}), f32[2048,128]{1,0:T(8,128)}) %all-gather.15.cloned.1.call-update) | async-done | bytes 1048592 | tf_op jit(solution)/shard_map/all_gather | solution.py:86
  482.0 5.9 %multiply_reduce_fusion.2 = (f32[128]{0:T(128)S(1)}, f32[512,128]{1,0:T(8,128)S(1)}) fusion(f32[512,128]{1,0:T(8,128)} %multiply_add_fusion.1, f32[512,2048]{1,0:T(8,128)} %select_add_fusion, f32[2048,128]{1,0:T(8,128)} %all-gather.15.cloned.1.call-done, f32[]{:T(128)S(6)} %div.24), kind=kOutput, calls=%fused_computation.28 | convolution fusion | flops 1610940288 | bytes 5767684 | tf_op jit(solution)/shard_map/dot_general | solution.py:84
  488.0 7.7 %psum.45 = f32[128]{0:T(128)S(1)} all-reduce(f32[128]{0:T(128)S(1)} %get-tuple-element.19), channel_id=1, replica_groups=mesh['x'=4,'z'=4,'c'=2,'feat'=4] {'feat'}, use_global_device_ids=true, to_apply=%region_14.15 | all-reduce | flops 128 | bytes 1024 | tf_op jit(solution)/shard_map/psum | solution.py:77
  495.8 6.0 %psum.46 = f32[128]{0:T(128)S(1)} all-reduce(f32[128]{0:T(128)S(1)} %multiply_reduce_fusion.1), channel_id=1, replica_groups=mesh['x'=4,'z'=4,'c'=2,'feat'=4] {'feat'}, use_global_device_ids=true, to_apply=%region_16.17 | all-reduce | flops 128 | bytes 1024 | tf_op jit(solution)/shard_map/psum | solution.py:77
  501.8 0.8 multiply_add_fusion
  502.6 27.8 %all-gather.17.cloned.1.call-done = f32[2048,128]{1,0:T(8,128)} async-done(((f32[512,128]{1,0:T(8,128)}), f32[2048,128]{1,0:T(8,128)}) %all-gather.17.cloned.1.call-update) | async-done | bytes 1048592 | tf_op jit(solution)/shard_map/all_gather | solution.py:86
  530.4 6.1 %fusion.8 = f32[128]{0:T(128)S(1)} fusion(f32[512,128]{1,0:T(8,128)} %multiply_add_fusion, f32[512,2048]{1,0:T(8,128)} %select_add_fusion, f32[2048,128]{1,0:T(8,128)} %all-gather.17.cloned.1.call-done, f32[]{:T(128)S(6)} %div.24), kind=kOutput, calls=%fused_computation.20 | convolution fusion | flops 1610940288 | bytes 5505540 | tf_op jit(solution)/shard_map/dot_general | solution.py:84
  536.5 7.7 %psum.47 = f32[128]{0:T(128)S(1)} all-reduce(f32[128]{0:T(128)S(1)} %fusion.8), channel_id=1, replica_groups=mesh['x'=4,'z'=4,'c'=2,'feat'=4] {'feat'}, use_global_device_ids=true, to_apply=%region_18.19 | all-reduce | flops 128 | bytes 1024 | tf_op jit(solution)/shard_map/psum | solution.py:77
  544.2 1.0 add_convert_fusion
  545.2 10.8 %all_gather.55 = bf16[2048,128]{1,0:T(8,128)(2,1)S(1)} all-gather(bf16[512,128]{1,0:T(8,128)(2,1)S(1)} %add_convert_fusion), channel_id=1, replica_groups=mesh['x'=4,'z'=4,'c'=2,'feat'=4] {'feat'}, dimensions={0}, use_global_device_ids=true | all-gather | bytes 655360 | tf_op jit(solution)/shard_map/all_gather | solution.py:99
  556.0 2.6 convolution_convert_fusion
  558.6 22.2 %all_to_all.16 = bf16[32,20,128]{2,1,0:T(8,128)(2,1)S(1)} all-to-all(bf16[32,20,128]{2,1,0:T(8,128)(2,1)S(1)} %reshape.53), channel_id=1, replica_groups=mesh['x'=4,'z'=4,'c'=2,'feat'=4] {'x','z','c'}, dimensions={0} | all-to-all | bytes 327680 | tf_op jit(solution)/shard_map/all_to_all | solution.py:101
  580.8 4.3 scatter_custom_fusion
  (54 shorter events, 3.4 us)
Async XLA Ops:
  7.2 5.3 copy-start
  7.2 169.3 %all-gather.11.cloned.1.call-start = ((), (), s32[]{:S(2)}) async-start(), calls=%async_computation.3 | async-start | bytes 13107200 | tf_op jit(solution)/shard_map/all_gather | solution.py:63
  78.0 204.8 %all-gather.19.cloned.1.call-start = ((), (), s32[]{:S(2)}) async-start(), calls=%async_computation.7 | async-start | bytes 10485760 | tf_op jit(solution)/shard_map/all_gather | solution.py:31
  186.9 8.0 %collective-permute-start.2 = (f32[512,2048]{1,0:T(8,128)}, f32[512,2048]{1,0:T(8,128)}, u32[]{:S(2)}, u32[]{:S(2)}) collective-permute-start(f32[512,2048]{1,0:T(8,128)} %fusion), channel_id=1, source_target_pairs={{0,4},{4,0},{1,5},{5,1},{2,6},{6,2},{3,7},{7,3},{8,12},{12,8},{9,1... | collective-permute-start | bytes 12582920 | tf_op jit(solution)/shard_map/ppermute | solution.py:27
  198.9 174.5 %all-gather.21.cloned.1.call-start = ((), (), s32[]{:S(2)}) async-start(), calls=%async_computation.8 | async-start | bytes 10485760 | tf_op jit(solution)/shard_map/all_gather | solution.py:34
  282.8 6.6 %copy-start.2 = (bf16[640,128]{1,0:T(8,128)(2,1)S(1)}, bf16[640,128]{1,0:T(8,128)(2,1)}, u32[]{:S(2)}) copy-start(bf16[640,128]{1,0:T(8,128)(2,1)} %param.4) | copy-start | bytes 491524
  292.3 15.7 %all-to-all-start.1 = ((bf16[32,20,128]{2,1,0:T(8,128)(2,1)}), bf16[32,20,128]{2,1,0:T(8,128)(2,1)S(1)}, u32[]{:S(2)}, u32[]{:S(2)}) async-start(bf16[32,20,128]{2,1,0:T(8,128)(2,1)} %broadcast_select_fusion.1), calls=%async_computation.1 | async-start | bytes 393216 | tf_op jit(solution)/shard_map/all_to_all | solution.py:58
  299.7 134.4 %all-gather.13.cloned.1.call-start = ((), (), s32[]{:S(2)}) async-start(), calls=%async_computation.4 | async-start | bytes 1310720 | tf_op jit(solution)/shard_map/all_gather | solution.py:86
  322.4 61.4 %collective-permute-start = (f32[512,128]{1,0:T(8,128)S(1)}, f32[512,128]{1,0:T(8,128)S(1)}, u32[]{:S(2)}, u32[]{:S(2)}) collective-permute-start(f32[512,128]{1,0:T(8,128)S(1)} %fusion.2), channel_id=1, source_target_pairs={{0,4},{4,0},{1,5},{5,1},{2,6},{6,2},{3,7},{7,3},{8,12},{12,8},{9,1... | collective-permute-start | bytes 786440 | tf_op jit(solution)/shard_map/ppermute | solution.py:27
  383.1 29.8 %collective-permute-start.3 = (f32[256,2048]{1,0:T(8,128)}, f32[256,2048]{1,0:T(8,128)S(1)}, u32[]{:S(2)}, u32[]{:S(2)}) collective-permute-start(f32[256,2048]{1,0:T(8,128)} %get-tuple-element.15), channel_id=1, source_target_pairs={{0,4},{4,0},{1,5},{5,1},{2,6},{6,2},{3,7},{7,3},{8,12},{12,8},{9,1... | collective-permute-start | bytes 6291464 | tf_op jit(solution)/shard_map/ppermute | solution.py:37
  405.7 6.3 %collective-permute-start.1 = (f32[256,128]{1,0:T(8,128)S(1)}, f32[256,128]{1,0:T(8,128)S(1)}, u32[]{:S(2)}, u32[]{:S(2)}) collective-permute-start(f32[256,128]{1,0:T(8,128)S(1)} %get-tuple-element.17), channel_id=1, source_target_pairs={{0,4},{4,0},{1,5},{5,1},{2,6},{6,2},{3,7},{7,3},{8,12},{12,8},{9,1... | collective-permute-start | bytes 393224 | tf_op jit(solution)/shard_map/ppermute | solution.py:37
  412.8 69.2 %all-gather.15.cloned.1.call-start = ((), (), s32[]{:S(2)}) async-start(), calls=%async_computation.5 | async-start | bytes 1310720 | tf_op jit(solution)/shard_map/all_gather | solution.py:86
  414.4 19.7 %copy-start.3 = (f32[512,128]{1,0:T(8,128)S(1)}, f32[512,128]{1,0:T(8,128)}, u32[]{:S(2)}) copy-start(f32[512,128]{1,0:T(8,128)} %add_multiply_fusion) | copy-start | bytes 786436
  454.2 47.6 %copy-start.4 = (f32[512,128]{1,0:T(8,128)S(1)}, f32[512,128]{1,0:T(8,128)}, u32[]{:S(2)}) copy-start(f32[512,128]{1,0:T(8,128)} %multiply_add_fusion.1) | copy-start | bytes 786436
  454.2 76.2 %all-gather.17.cloned.1.call-start = ((), (), s32[]{:S(2)}) async-start(), calls=%async_computation.6 | async-start | bytes 1310720 | tf_op jit(solution)/shard_map/all_gather | solution.py:86
  530.4 55.5 %copy-start.1 = (bf16[640,2048]{1,0:T(8,128)(2,1)S(1)}, bf16[640,2048]{1,0:T(8,128)(2,1)}, u32[]{:S(2)}) copy-start(bf16[640,2048]{1,0:T(8,128)(2,1)} %param.3) | copy-start | bytes 7864324
  585.1 0.8 copy-start.5
Sparse Core Ops, SparseCore 0:
  78.1 98.3 all-gather.10
  199.0 83.7 all-gather.18
  289.5 83.8 all-gather.20
  412.9 21.1 all-gather.12
  454.3 27.6 all-gather.14
  502.7 27.6 all-gather.16

commit v2 on v1

--- a/solution.py
+++ b/solution.py
@@ -65,38 +65,31 @@
     own = lax.dynamic_slice_in_dim(rows_x, col_start, block_rows, 1)
     gram_part = lax.dot_general(own, rows_x, contract, preferred_element_type=jnp.float32)
     cross_part = lax.dot_general(own, rows_y, contract, preferred_element_type=jnp.float32)
-
-    gram_prefix = exclusive_prefix(gram_part)
-    cross_prefix = exclusive_prefix(cross_part)
+    moments = exclusive_prefix(jnp.concatenate([gram_part, cross_part], axis=1))
+    gram_prefix = moments[:, :width]
+    cross_prefix = lax.all_gather(moments[:, width:], "feat", axis=0, tiled=True)
     span = (lax.axis_index("x") * lax.axis_size("z") + lax.axis_index("z")) * lax.axis_size("c") + lax.axis_index("c")
     seen = (span * (tok_dev * feat_count)).astype(jnp.float32)
     scale = 1.0 / jnp.maximum(seen, 1.0)
     rhs = scale * cross_prefix
 
-    def column_dot(left, right):
-        return lax.psum(jnp.sum(left * right, axis=0), "feat")
-
     residual = rhs
     direction = rhs
-    norm_now = column_dot(residual, residual)
+    norm_now = jnp.sum(residual * residual, axis=0)
     solution = None
     for step in range(ITERS):
-        product = jnp.dot(
-            gram_prefix,
-            lax.all_gather(direction, "feat", axis=0, tiled=True),
-            precision=highest,
-            preferred_element_type=jnp.float32,
-        )
-        image = scale * product + RIDGE * direction
-        alpha = norm_now / (column_dot(direction, image) + TINY)
+        product = jnp.dot(gram_prefix, direction, precision=highest, preferred_element_type=jnp.float32)
+        own_dir = lax.dynamic_slice_in_dim(direction, col_start, block_rows, 0)
+        image = lax.all_gather(scale * product + RIDGE * own_dir, "feat", axis=0, tiled=True)
+        alpha = norm_now / (jnp.sum(direction * image, axis=0) + TINY)
         update = alpha * direction
         solution = update if solution is None else solution + update
         if step + 1 < ITERS:
             residual = residual - alpha * image
-            norm_next = column_dot(residual, residual)
+            norm_next = jnp.sum(residual * residual, axis=0)
             direction = residual + norm_next / (norm_now + TINY) * direction
             norm_now = norm_next
-    weights = lax.all_gather(solution.astype(jnp.bfloat16), "feat", axis=0, tiled=True)
+    weights = solution.astype(jnp.bfloat16)
     predicted = jnp.dot(local_x, weights, preferred_element_type=jnp.float32).astype(jnp.bfloat16)
     returned = lax.all_to_all(
         predicted.reshape(spans, share, n_targets), TM, split_axis=0, concat_axis=0, tiled=True

time: 594 us -> 577 us (0.971)
  blocking collectives: 150 us -> 83.2 us
  waiting for transfers between devices: 316 us -> 365 us
  starting transfers between devices: 16.6 us -> 6.11 us
    all_gather x1, waiting for transfers between devices: 48.8 us -> 88.4 us  [exclusive_prefix(): along_x = lax.all_gather(total_z, 'x')]
    psum x5 -> x0, blocking collectives: 35.1 us -> none  [column_dot(): return lax.psum(jnp.sum(left * right, axis=0), 'feat')]
    all_gather x3 -> x0, blocking collectives: 32.4 us -> none  [the longest x1 11.2 us: exclusive_prefix(): along_z = lax.all_gather(mine, 'z')]
    all_gather x3 -> x4, waiting for transfers between devices: 68.6 us -> 96 us  [the longest x3 73.5 us: body(): lax.all_gather(scale * product + RIDGE * own_dir, 'feat', axis=0, tiled=T...]
    all_gather x1, waiting for transfers between devices: 98.4 us -> 72 us  [body(): rows_x = lax.all_gather(local_x, 'feat', axis=0, tiled=True)]
    reduce_sum x2 -> x5, other arithmetic: 0.18 us -> 7.71 us  [the longest x3 4.68 us: body(): alpha = norm_now / (jnp.sum(direction * image, axis=0) + TINY)]
  transfers between devices with their start and end apart: 11 -> 10, of which waited for: 9 -> 10; matrix products, arithmetic and copies ran while one was open for 4% -> 1% of each run, Pallas kernels for 0% -> 0%
where the time goes in v2:
time: 577 us; the launch traced here: 576 us
  waiting for transfers between devices  365 us (63%)
  blocking collectives  83.2 us (14%)
  other arithmetic  42.2 us (7%)
  matrix products  37 us (6%)
  local copies, waits for them, and re-layouts  28.8 us (5%)
  between operations  14.5 us (3%)
  starting transfers between devices  6.11 us (1%)
    all_gather x1, waiting for transfers between devices, exclusive_prefix(): along_x = lax.all_gather(total_z, 'x')  88.4 us
    all_gather x1, waiting for transfers between devices, exclusive_prefix(): along_z = lax.all_gather(mine, 'z')  88.2 us
    all_gather x3, waiting for transfers between devices, body(): lax.all_gather(scale * product + RIDGE * own_dir, 'feat', axis=0, tiled=T...  73.5 us
    all_gather x1, waiting for transfers between devices, body(): rows_x = lax.all_gather(local_x, 'feat', axis=0, tiled=True)  72 us
    all_to_all x1, blocking collectives, body(): lax.all_to_all(sorted_x, TM, split_axis=0, concat_axis=0, tiled=True)  48.7 us
    all_gather x1, waiting for transfers between devices, body(): lax.all_gather(moments[:, width:], 'feat', axis=0, tiled=True)  22.5 us
    dot_general x3, matrix products, body(): jnp.dot(gram_prefix, direction, precision=highest, preferred_element_type...  20.1 us
    all_to_all x1, blocking collectives, body(): lax.all_to_all(predicted.reshape(spans, share, n_targets), TM, split_axis...  17.9 us
  transfers between devices with their start and end apart: 10, of which 10 were waited for; matrix products, arithmetic and copies ran while one was open for 1% of the time, Pallas kernels for 0%

profile of v2, /device:TPU:1, one launch (start us, length us, event | category | flops | bytes accessed | tf_op | source)
XLA Modules:
  0.0 576.4 jit_solution(17117435557100871217)
XLA Ops:
  7.2 5.2 sort.17
  12.5 4.1 gather_fusion
  16.6 5.2 gather.13
  21.9 2.2 broadcast_select_fusion
  24.1 48.7 %all_to_all.15 = bf16[32,20,2048]{2,1,0:T(8,128)(2,1)} all-to-all(bf16[32,20,2048]{2,1,0:T(8,128)(2,1)S(1)} %broadcast_select_fusion), channel_id=1, replica_groups=mesh['x'=4,'z'=4,'c'=2,'feat'=4] {'x','z','c'}, dimensions={0} | all-to-all | bytes 5242880 | tf_op jit(solution)/shard_map/all_to_all | solution.py:57
  72.8 5.2 reshape.74
  78.1 2.0 gather_fusion.1
  80.1 0.9 broadcast_select_fusion.1
  81.0 3.9 all-to-all-start.1
  85.0 8.2 %all-to-all-done.1 = bf16[32,20,128]{2,1,0:T(8,128)(2,1)S(1)} async-done(((bf16[32,20,128]{2,1,0:T(8,128)(2,1)}), bf16[32,20,128]{2,1,0:T(8,128)(2,1)S(1)}, u32[]{:S(2)}, u32[]{:S(2)}) %all-to-all-start.1) | async-done | bytes 163872 | tf_op jit(solution)/shard_map/all_to_all | solution.py:58
  93.3 16.6 %all_gather.31 = bf16[2560,128]{1,0:T(8,128)(2,1)S(1)} all-gather(bf16[640,128]{1,0:T(8,128)(2,1)S(1)} %reshape.75), channel_id=1, replica_groups=mesh['x'=4,'z'=4,'c'=2,'feat'=4] {'feat'}, dimensions={0}, use_global_device_ids=true | all-gather | bytes 819200 | tf_op jit(solution)/shard_map/all_gather | solution.py:64
  109.9 72.0 %all-gather.10.cloned.1.call-done = bf16[2560,2048]{1,0:T(8,128)(2,1)} async-done(((bf16[640,2048]{1,0:T(8,128)(2,1)}), bf16[2560,2048]{1,0:T(8,128)(2,1)}) %all-gather.10.cloned.1.call-update) | async-done | bytes 10485776 | tf_op jit(solution)/shard_map/all_gather | solution.py:63
  181.8 9.1 %fusion.8 = f32[512,2048]{1,0:T(8,128)S(1)} fusion(bf16[2560,2048]{1,0:T(8,128)(2,1)} %all-gather.10.cloned.1.call-done, s32[]{:T(128)S(6)} %select_n.48), kind=kOutput, calls=%fused_computation.18 | convolution fusion | flops 5368709120 | bytes 17301508 | tf_op jit(solution)/shard_map/dot_general | solution.py:66
  191.0 4.1 fusion.6
  195.1 2.5 pad_maximum_fusion
  197.6 0.8 collective-permute-start
  198.4 7.5 %collective-permute-done = f32[512,2176]{1,0:T(8,128)} collective-permute-done((f32[512,2176]{1,0:T(8,128)}, f32[512,2176]{1,0:T(8,128)}, u32[]{:S(2)}, u32[]{:S(2)}) %collective-permute-start) | collective-permute-done | bytes 4456480 | tf_op jit(solution)/shard_map/ppermute | solution.py:27
  205.9 3.9 fusion.11
  209.9 88.2 %all-gather.20.cloned.1.call-done = f32[1024,2176]{1,0:T(8,128)} async-done(((f32[256,2176]{1,0:T(8,128)}), f32[1024,2176]{1,0:T(8,128)}) %all-gather.20.cloned.1.call-update) | async-done | bytes 8912912 | tf_op jit(solution)/shard_map/all_gather | solution.py:31
  298.1 6.4 %select_reduce_fusion = (f32[256,2176]{1,0:T(8,128)S(1)}, f32[256,2176]{1,0:T(8,128)}) fusion(f32[4,256,2176]{2,1,0:T(8,128)} %bitcast.9, pred[4]{0:T(512)(128)(4,1)S(1)} %iota_compare_fusion), kind=kLoop, calls=%fused_computation.3 | loop fusion | flops 5570560 | bytes 13369348 | tf_op jit(solution)/shard_map/reduce_sum | solution.py:18
  304.6 88.4 %all-gather.22.cloned.1.call-done = f32[1024,2176]{1,0:T(8,128)} async-done(((f32[256,2176]{1,0:T(8,128)}), f32[1024,2176]{1,0:T(8,128)}) %all-gather.22.cloned.1.call-update) | async-done | bytes 8912912 | tf_op jit(solution)/shard_map/all_gather | solution.py:34
  393.0 4.5 select_reduce_fusion.1
  397.5 2.5 broadcast_in_dim.63
  400.0 2.4 constant_dynamic-update-slice_fusion.1
  402.3 0.8 collective-permute-start.1
  403.2 4.2 collective-permute-done.1
  407.3 1.6 constant_dynamic-update-slice_fusion
  408.9 4.1 select_add_fusion
  413.0 2.0 copy-done.2
  415.0 0.7 slice.12
  415.8 22.5 %all-gather.12.cloned.1.call-done = f32[2048,128]{1,0:T(8,128)} async-done(((f32[512,128]{1,0:T(8,128)}), f32[2048,128]{1,0:T(8,128)}) %all-gather.12.cloned.1.call-update) | async-done | bytes 1048592 | tf_op jit(solution)/shard_map/all_gather | solution.py:70
  438.4 1.4 broadcast_multiply_fusion
  439.8 6.7 %fusion.15 = f32[512,128]{1,0:T(8,128)} fusion(f32[2048,128]{1,0:T(8,128)S(1)} %broadcast_multiply_fusion, f32[512,2176]{1,0:T(8,128)} %copy-done.2, s32[]{:T(128)S(6)} %select_n.48, f32[]{:T(128)S(6)} %div.44), kind=kOutput, calls=%fused_computation.23 | convolution fusion | flops 1610809344 | bytes 5767176 | tf_op jit(solution)/shard_map/dot_general | solution.py:81
  446.5 24.6 %all-gather.14.cloned.1.call-done = f32[2048,128]{1,0:T(8,128)} async-done(((f32[512,128]{1,0:T(8,128)}), f32[2048,128]{1,0:T(8,128)}) %all-gather.14.cloned.1.call-update) | async-done | bytes 1048592 | tf_op jit(solution)/shard_map/all_gather | solution.py:83
  471.1 1.5 multiply_reduce_fusion.4
  472.6 1.5 multiply_reduce_fusion.3
  474.2 0.9 copy-done.7
  475.2 6.7 %fusion.21 = f32[512,128]{1,0:T(8,128)} fusion(f32[2048,128]{1,0:T(8,128)S(1)} %multiply_add_fusion.1, f32[512,2176]{1,0:T(8,128)} %copy-done.2, s32[]{:T(128)S(6)} %select_n.48, f32[]{:T(128)S(6)} %div.44), kind=kOutput, calls=%fused_computation.25 | convolution fusion | flops 1610809344 | bytes 5767176 | tf_op jit(solution)/shard_map/dot_general | solution.py:81
  482.2 24.3 %all-gather.16.cloned.1.call-done = f32[2048,128]{1,0:T(8,128)} async-done(((f32[512,128]{1,0:T(8,128)}), f32[2048,128]{1,0:T(8,128)}) %all-gather.16.cloned.1.call-update) | async-done | bytes 1048592 | tf_op jit(solution)/shard_map/all_gather | solution.py:83
  506.6 1.7 multiply_reduce_fusion.2
  508.2 1.5 multiply_reduce_fusion.1
  510.0 6.7 %fusion.27 = f32[512,128]{1,0:T(8,128)} fusion(f32[2048,128]{1,0:T(8,128)S(1)} %multiply_add_fusion, f32[512,2176]{1,0:T(8,128)} %copy-done.2, s32[]{:T(128)S(6)} %select_n.48, f32[]{:T(128)S(6)} %div.44), kind=kOutput, calls=%fused_computation.27 | convolution fusion | flops 1610809344 | bytes 5767176 | tf_op jit(solution)/shard_map/dot_general | solution.py:81
  516.8 24.6 %all-gather.18.cloned.1.call-done = f32[2048,128]{1,0:T(8,128)} async-done(((f32[512,128]{1,0:T(8,128)}), f32[2048,128]{1,0:T(8,128)}) %all-gather.18.cloned.1.call-update) | async-done | bytes 1048592 | tf_op jit(solution)/shard_map/all_gather | solution.py:83
  541.4 1.5 multiply_reduce_fusion
  542.9 3.7 convolution_convert_fusion
  546.6 17.9 %all_to_all.16 = bf16[32,20,128]{2,1,0:T(8,128)(2,1)S(1)} all-to-all(bf16[32,20,128]{2,1,0:T(8,128)(2,1)S(1)} %reshape.76), channel_id=1, replica_groups=mesh['x'=4,'z'=4,'c'=2,'feat'=4] {'x','z','c'}, dimensions={0} | all-to-all | bytes 327680 | tf_op jit(solution)/shard_map/all_to_all | solution.py:94
  564.5 4.3 scatter_custom_fusion
  569.0 0.6 broadcast_multiply_fusion.1
  (59 shorter events, 1.5 us)
Async XLA Ops:
  7.2 5.3 copy-start
  7.2 174.7 %all-gather.10.cloned.1.call-start = ((), (), s32[]{:S(2)}) async-start(), calls=%async_computation.3 | async-start | bytes 13107200 | tf_op jit(solution)/shard_map/all_gather | solution.py:63
  72.8 5.3 copy-start.10
  81.0 12.2 %all-to-all-start.1 = ((bf16[32,20,128]{2,1,0:T(8,128)(2,1)}), bf16[32,20,128]{2,1,0:T(8,128)(2,1)S(1)}, u32[]{:S(2)}, u32[]{:S(2)}) async-start(bf16[32,20,128]{2,1,0:T(8,128)(2,1)} %broadcast_select_fusion.1), calls=%async_computation.1 | async-start | bytes 393216 | tf_op jit(solution)/shard_map/all_to_all | solution.py:58
  84.9 213.2 %all-gather.20.cloned.1.call-start = ((), (), s32[]{:S(2)}) async-start(), calls=%async_computation.8 | async-start | bytes 11141120 | tf_op jit(solution)/shard_map/all_gather | solution.py:31
  191.0 6.6 %copy-start.5 = (f32[512,2048]{1,0:T(8,128)}, f32[512,2048]{1,0:T(8,128)S(1)}, u32[]{:S(2)}) copy-start(f32[512,2048]{1,0:T(8,128)S(1)} %fusion.8) | copy-start | bytes 12582916
  197.6 8.3 %collective-permute-start = (f32[512,2176]{1,0:T(8,128)}, f32[512,2176]{1,0:T(8,128)}, u32[]{:S(2)}, u32[]{:S(2)}) collective-permute-start(f32[512,2176]{1,0:T(8,128)} %pad_maximum_fusion), channel_id=1, source_target_pairs={{0,4},{4,0},{1,5},{5,1},{2,6},{6,2},{3,7},{7,3},{8,12},{12,8},{9,1... | collective-permute-start | bytes 13369352 | tf_op jit(solution)/shard_map/ppermute | solution.py:27
  209.8 183.2 %all-gather.22.cloned.1.call-start = ((), (), s32[]{:S(2)}) async-start(), calls=%async_computation.9 | async-start | bytes 11141120 | tf_op jit(solution)/shard_map/all_gather | solution.py:34
  304.5 133.8 %all-gather.12.cloned.1.call-start = ((), (), s32[]{:S(2)}) async-start(), calls=%async_computation.4 | async-start | bytes 1310720 | tf_op jit(solution)/shard_map/all_gather | solution.py:70
  402.3 5.0 collective-permute-start.1
  413.0 2.0 copy-start.2
  415.7 55.4 %all-gather.14.cloned.1.call-start = ((), (), s32[]{:S(2)}) async-start(), calls=%async_computation.5 | async-start | bytes 1310720 | tf_op jit(solution)/shard_map/all_gather | solution.py:83
  438.4 32.7 %copy-start.4 = (f32[2048,128]{1,0:T(8,128)S(1)}, f32[2048,128]{1,0:T(8,128)}, u32[]{:S(2)}) copy-start(f32[2048,128]{1,0:T(8,128)} %all-gather.12.cloned.1.call-done) | copy-start | bytes 3145732
  439.8 34.4 %copy-start.12 = (f32[2048,128]{1,0:T(8,128)}, f32[2048,128]{1,0:T(8,128)S(1)}, u32[]{:S(2)}) copy-start(f32[2048,128]{1,0:T(8,128)S(1)} %broadcast_multiply_fusion) | copy-start | bytes 3145732
  446.5 60.1 %all-gather.16.cloned.1.call-start = ((), (), s32[]{:S(2)}) async-start(), calls=%async_computation.6 | async-start | bytes 1310720 | tf_op jit(solution)/shard_map/all_gather | solution.py:83
  474.1 1.0 copy-start.7
  475.2 34.6 %copy-start.3 = (f32[2048,128]{1,0:T(8,128)}, f32[2048,128]{1,0:T(8,128)S(1)}, u32[]{:S(2)}) copy-start(f32[2048,128]{1,0:T(8,128)S(1)} %multiply_add_fusion.1) | copy-start | bytes 3145732
  475.2 33.0 %copy-start.8 = (f32[2048,128]{1,0:T(8,128)S(1)}, f32[2048,128]{1,0:T(8,128)}, u32[]{:S(2)}) copy-start(f32[2048,128]{1,0:T(8,128)} %copy-done.7) | copy-start | bytes 3145732
  482.0 59.4 %all-gather.18.cloned.1.call-start = ((), (), s32[]{:S(2)}) async-start(), calls=%async_computation.7 | async-start | bytes 1310720 | tf_op jit(solution)/shard_map/all_gather | solution.py:83
  506.6 3.2 copy-start.9
  506.6 3.2 copy-start.11
  510.0 31.3 %copy-start.6 = (f32[2048,128]{1,0:T(8,128)}, f32[2048,128]{1,0:T(8,128)S(1)}, u32[]{:S(2)}) copy-start(f32[2048,128]{1,0:T(8,128)S(1)} %multiply_add_fusion) | copy-start | bytes 3145732
  542.9 26.7 %copy-start.1 = (bf16[640,2048]{1,0:T(8,128)(2,1)S(1)}, bf16[640,2048]{1,0:T(8,128)(2,1)}, u32[]{:S(2)}) copy-start(bf16[640,2048]{1,0:T(8,128)(2,1)} %param.3) | copy-start | bytes 7864324
  568.8 0.8 copy-start.13
Sparse Core Ops, SparseCore 0:
  78.2 103.5 all-gather.9
  209.9 88.1 all-gather.19
  304.7 88.3 all-gather.21
  415.8 22.4 all-gather.11
  446.6 24.4 all-gather.13
  482.1 24.4 all-gather.15
  516.9 24.4 all-gather.17

commit v3 on v2

--- a/solution.py
+++ b/solution.py
@@ -31,8 +31,10 @@
     along_z = lax.all_gather(mine, "z")
     before_z = masked_sum(along_z, zi)
     total_z = jnp.sum(along_z, axis=0)
-    along_x = lax.all_gather(total_z, "x")
-    before_x = masked_sum(along_x, xi)
+    quarter = half // lax.axis_size("z")
+    piece = lax.dynamic_slice_in_dim(total_z, zi * quarter, quarter, 0)
+    along_x = lax.all_gather(piece, "x")
+    before_x = lax.all_gather(masked_sum(along_x, xi), "z", axis=0, tiled=True)
     mine_prefix = before_x + before_z
     other_prefix = lax.ppermute(mine_prefix, "c", SWAP)
     joined = jnp.zeros((rows,) + block.shape[1:], block.dtype)

time: 577 us -> 551 us (0.955)
  waiting for transfers between devices: 365 us -> 340 us
    all_gather x1 -> x2, waiting for transfers between devices: 88.4 us -> 65 us  [the longest x1 32.8 us: exclusive_prefix(): along_x = lax.all_gather(piece, 'x')]
  transfers between devices with their start and end apart: 10 -> 11, of which waited for: 10 -> 11; matrix products, arithmetic and copies ran while one was open for 1% -> 1% of each run, Pallas kernels for 0% -> 0%
where the time goes in v3:
time: 551 us; the launch traced here: 550 us
  waiting for transfers between devices  340 us (62%)
  blocking collectives  83.1 us (15%)
  other arithmetic  39.1 us (7%)
  matrix products  37 us (7%)
  local copies, waits for them, and re-layouts  29.6 us (5%)
  between operations  14.5 us (3%)
  starting transfers between devices  6.34 us (1%)
    all_gather x1, waiting for transfers between devices, exclusive_prefix(): along_z = lax.all_gather(mine, 'z')  88.2 us
    all_gather x3, waiting for transfers between devices, body(): lax.all_gather(scale * product + RIDGE * own_dir, 'feat', axis=0, tiled=T...  73.5 us
    all_gather x1, waiting for transfers between devices, body(): rows_x = lax.all_gather(local_x, 'feat', axis=0, tiled=True)  72 us
    all_to_all x1, blocking collectives, body(): lax.all_to_all(sorted_x, TM, split_axis=0, concat_axis=0, tiled=True)  48.7 us
    all_gather x1, waiting for transfers between devices, exclusive_prefix(): along_x = lax.all_gather(piece, 'x')  32.8 us
    all_gather x1, waiting for transfers between devices, exclusive_prefix(): before_x = lax.all_gather(masked_sum(along_x, xi), 'z', axis=0, tiled=True)  32.2 us
    all_gather x1, waiting for transfers between devices, body(): lax.all_gather(moments[:, width:], 'feat', axis=0, tiled=True)  21.3 us
    dot_general x3, matrix products, body(): jnp.dot(gram_prefix, direction, precision=highest, preferred_element_type...  20.1 us
  transfers between devices with their start and end apart: 11, of which 11 were waited for; matrix products, arithmetic and copies ran while one was open for 1% of the time, Pallas kernels for 0%

profile of v3, /device:TPU:1, one launch (start us, length us, event | category | flops | bytes accessed | tf_op | source)
XLA Modules:
  0.0 549.7 jit_solution(11956748416259935353)
XLA Ops:
  7.2 5.2 sort.17
  12.5 4.1 gather_fusion
  16.6 5.2 gather.13
  21.9 2.2 broadcast_select_fusion
  24.1 48.7 %all_to_all.15 = bf16[32,20,2048]{2,1,0:T(8,128)(2,1)} all-to-all(bf16[32,20,2048]{2,1,0:T(8,128)(2,1)S(1)} %broadcast_select_fusion), channel_id=1, replica_groups=mesh['x'=4,'z'=4,'c'=2,'feat'=4] {'x','z','c'}, dimensions={0} | all-to-all | bytes 5242880 | tf_op jit(solution)/shard_map/all_to_all | solution.py:59
  72.8 5.2 reshape.74
  78.1 2.0 gather_fusion.1
  80.1 0.9 broadcast_select_fusion.1
  81.0 3.9 all-to-all-start.1
  85.0 8.2 %all-to-all-done.1 = bf16[32,20,128]{2,1,0:T(8,128)(2,1)S(1)} async-done(((bf16[32,20,128]{2,1,0:T(8,128)(2,1)}), bf16[32,20,128]{2,1,0:T(8,128)(2,1)S(1)}, u32[]{:S(2)}, u32[]{:S(2)}) %all-to-all-start.1) | async-done | bytes 163872 | tf_op jit(solution)/shard_map/all_to_all | solution.py:60
  93.3 16.6 %all_gather.34 = bf16[2560,128]{1,0:T(8,128)(2,1)S(1)} all-gather(bf16[640,128]{1,0:T(8,128)(2,1)S(1)} %reshape.75), channel_id=1, replica_groups=mesh['x'=4,'z'=4,'c'=2,'feat'=4] {'feat'}, dimensions={0}, use_global_device_ids=true | all-gather | bytes 819200 | tf_op jit(solution)/shard_map/all_gather | solution.py:66
  109.8 72.0 %all-gather.11.cloned.1.call-done = bf16[2560,2048]{1,0:T(8,128)(2,1)} async-done(((bf16[640,2048]{1,0:T(8,128)(2,1)}), bf16[2560,2048]{1,0:T(8,128)(2,1)}) %all-gather.11.cloned.1.call-update) | async-done | bytes 10485776 | tf_op jit(solution)/shard_map/all_gather | solution.py:65
  181.8 9.1 %fusion.8 = f32[512,2048]{1,0:T(8,128)S(1)} fusion(bf16[2560,2048]{1,0:T(8,128)(2,1)} %all-gather.11.cloned.1.call-done, s32[]{:T(128)S(6)} %select_n.52), kind=kOutput, calls=%fused_computation.17 | convolution fusion | flops 5368709120 | bytes 17301508 | tf_op jit(solution)/shard_map/dot_general | solution.py:68
  190.9 4.1 fusion.6
  195.1 2.4 pad_maximum_fusion
  197.5 0.8 collective-permute-start
  198.3 7.5 %collective-permute-done = f32[512,2176]{1,0:T(8,128)} collective-permute-done((f32[512,2176]{1,0:T(8,128)}, f32[512,2176]{1,0:T(8,128)}, u32[]{:S(2)}, u32[]{:S(2)}) %collective-permute-start) | collective-permute-done | bytes 4456480 | tf_op jit(solution)/shard_map/ppermute | solution.py:27
  205.8 3.9 fusion.11
  209.8 88.2 %all-gather.23.cloned.1.call-done = f32[1024,2176]{1,0:T(8,128)} async-done(((f32[256,2176]{1,0:T(8,128)}), f32[1024,2176]{1,0:T(8,128)}) %all-gather.23.cloned.1.call-update) | async-done | bytes 8912912 | tf_op jit(solution)/shard_map/all_gather | solution.py:31
  298.0 5.1 select_reduce_fusion
  303.1 0.8 constant_dynamic-slice_fusion
  304.1 32.8 %all-gather.25.cloned.1.call-done = f32[256,2176]{1,0:T(8,128)} async-done(((f32[64,2176]{1,0:T(8,128)}), f32[256,2176]{1,0:T(8,128)}) %all-gather.25.cloned.1.call-update) | async-done | bytes 2228240 | tf_op jit(solution)/shard_map/all_gather | solution.py:36
  336.9 2.7 select_reduce_fusion.1
  339.6 32.2 %all-gather.13.cloned.1.call-done = f32[256,2176]{1,0:T(8,128)} async-done(((f32[64,2176]{1,0:T(8,128)}), f32[256,2176]{1,0:T(8,128)}) %all-gather.13.cloned.1.call-update) | async-done | bytes 2228240 | tf_op jit(solution)/shard_map/all_gather | solution.py:37
  371.9 2.3 broadcast_in_dim.69
  374.4 2.3 constant_dynamic-update-slice_fusion.1
  376.7 0.8 collective-permute-start.1
  377.6 4.2 collective-permute-done.1
  381.8 1.5 constant_dynamic-update-slice_fusion
  383.3 4.1 select_add_fusion
  387.4 2.0 copy-done.2
  390.4 21.3 %all-gather.15.cloned.1.call-done = f32[2048,128]{1,0:T(8,128)} async-done(((f32[512,128]{1,0:T(8,128)}), f32[2048,128]{1,0:T(8,128)}) %all-gather.15.cloned.1.call-update) | async-done | bytes 1048592 | tf_op jit(solution)/shard_map/all_gather | solution.py:72
  411.7 1.4 broadcast_multiply_fusion
  413.1 6.7 %fusion.15 = f32[512,128]{1,0:T(8,128)} fusion(f32[2048,128]{1,0:T(8,128)S(1)} %broadcast_multiply_fusion, f32[512,2176]{1,0:T(8,128)} %copy-done.2, s32[]{:T(128)S(6)} %select_n.52, f32[]{:T(128)S(6)} %div.44), kind=kOutput, calls=%fused_computation.23 | convolution fusion | flops 1610809344 | bytes 5767176 | tf_op jit(solution)/shard_map/dot_general | solution.py:83
  419.9 24.6 %all-gather.17.cloned.1.call-done = f32[2048,128]{1,0:T(8,128)} async-done(((f32[512,128]{1,0:T(8,128)}), f32[2048,128]{1,0:T(8,128)}) %all-gather.17.cloned.1.call-update) | async-done | bytes 1048592 | tf_op jit(solution)/shard_map/all_gather | solution.py:85
  444.4 1.5 multiply_reduce_fusion.4
  445.9 1.5 multiply_reduce_fusion.3
  447.5 0.9 copy-done.7
  448.6 6.7 %fusion.21 = f32[512,128]{1,0:T(8,128)} fusion(f32[2048,128]{1,0:T(8,128)S(1)} %multiply_add_fusion.1, f32[512,2176]{1,0:T(8,128)} %copy-done.2, s32[]{:T(128)S(6)} %select_n.52, f32[]{:T(128)S(6)} %div.44), kind=kOutput, calls=%fused_computation.25 | convolution fusion | flops 1610809344 | bytes 5767176 | tf_op jit(solution)/shard_map/dot_general | solution.py:83
  455.6 24.3 %all-gather.19.cloned.1.call-done = f32[2048,128]{1,0:T(8,128)} async-done(((f32[512,128]{1,0:T(8,128)}), f32[2048,128]{1,0:T(8,128)}) %all-gather.19.cloned.1.call-update) | async-done | bytes 1048592 | tf_op jit(solution)/shard_map/all_gather | solution.py:85
  479.9 1.7 multiply_reduce_fusion.2
  481.6 1.5 multiply_reduce_fusion.1
  483.4 6.7 %fusion.27 = f32[512,128]{1,0:T(8,128)} fusion(f32[2048,128]{1,0:T(8,128)S(1)} %multiply_add_fusion, f32[512,2176]{1,0:T(8,128)} %copy-done.2, s32[]{:T(128)S(6)} %select_n.52, f32[]{:T(128)S(6)} %div.44), kind=kOutput, calls=%fused_computation.27 | convolution fusion | flops 1610809344 | bytes 5767176 | tf_op jit(solution)/shard_map/dot_general | solution.py:83
  490.1 24.6 %all-gather.21.cloned.1.call-done = f32[2048,128]{1,0:T(8,128)} async-done(((f32[512,128]{1,0:T(8,128)}), f32[2048,128]{1,0:T(8,128)}) %all-gather.21.cloned.1.call-update) | async-done | bytes 1048592 | tf_op jit(solution)/shard_map/all_gather | solution.py:85
  514.7 1.5 multiply_reduce_fusion
  516.2 3.7 convolution_convert_fusion
  519.9 17.8 %all_to_all.16 = bf16[32,20,128]{2,1,0:T(8,128)(2,1)S(1)} all-to-all(bf16[32,20,128]{2,1,0:T(8,128)(2,1)S(1)} %reshape.76), channel_id=1, replica_groups=mesh['x'=4,'z'=4,'c'=2,'feat'=4] {'x','z','c'}, dimensions={0} | all-to-all | bytes 327680 | tf_op jit(solution)/shard_map/all_to_all | solution.py:96
  537.8 4.3 scatter_custom_fusion
  (65 shorter events, 3.3 us)
Async XLA Ops:
  7.2 5.3 copy-start
  7.2 174.6 %all-gather.11.cloned.1.call-start = ((), (), s32[]{:S(2)}) async-start(), calls=%async_computation.3 | async-start | bytes 13107200 | tf_op jit(solution)/shard_map/all_gather | solution.py:65
  72.8 5.3 copy-start.10
  81.0 12.2 %all-to-all-start.1 = ((bf16[32,20,128]{2,1,0:T(8,128)(2,1)}), bf16[32,20,128]{2,1,0:T(8,128)(2,1)S(1)}, u32[]{:S(2)}, u32[]{:S(2)}) async-start(bf16[32,20,128]{2,1,0:T(8,128)(2,1)} %broadcast_select_fusion.1), calls=%async_computation.1 | async-start | bytes 393216 | tf_op jit(solution)/shard_map/all_to_all | solution.py:60
  84.9 213.1 %all-gather.23.cloned.1.call-start = ((), (), s32[]{:S(2)}) async-start(), calls=%async_computation.9 | async-start | bytes 11141120 | tf_op jit(solution)/shard_map/all_gather | solution.py:31
  190.9 6.5 %copy-start.5 = (f32[512,2048]{1,0:T(8,128)}, f32[512,2048]{1,0:T(8,128)S(1)}, u32[]{:S(2)}) copy-start(f32[512,2048]{1,0:T(8,128)S(1)} %fusion.8) | copy-start | bytes 12582916
  197.5 8.3 %collective-permute-start = (f32[512,2176]{1,0:T(8,128)}, f32[512,2176]{1,0:T(8,128)}, u32[]{:S(2)}, u32[]{:S(2)}) collective-permute-start(f32[512,2176]{1,0:T(8,128)} %pad_maximum_fusion), channel_id=1, source_target_pairs={{0,4},{4,0},{1,5},{5,1},{2,6},{6,2},{3,7},{7,3},{8,12},{12,8},{9,1... | collective-permute-start | bytes 13369352 | tf_op jit(solution)/shard_map/ppermute | solution.py:27
  209.7 127.2 %all-gather.25.cloned.1.call-start = ((), (), s32[]{:S(2)}) async-start(), calls=%async_computation.10 | async-start | bytes 2785280 | tf_op jit(solution)/shard_map/all_gather | solution.py:36
  304.0 67.9 %all-gather.13.cloned.1.call-start = ((), (), s32[]{:S(2)}) async-start(), calls=%async_computation.4 | async-start | bytes 2785280 | tf_op jit(solution)/shard_map/all_gather | solution.py:37
  339.6 72.1 %all-gather.15.cloned.1.call-start = ((), (), s32[]{:S(2)}) async-start(), calls=%async_computation.5 | async-start | bytes 1310720 | tf_op jit(solution)/shard_map/all_gather | solution.py:72
  371.9 2.5 copy-start.13
  376.7 5.0 collective-permute-start.1
  387.4 2.0 copy-start.2
  390.1 54.3 %all-gather.17.cloned.1.call-start = ((), (), s32[]{:S(2)}) async-start(), calls=%async_computation.6 | async-start | bytes 1310720 | tf_op jit(solution)/shard_map/all_gather | solution.py:85
  411.7 32.7 %copy-start.4 = (f32[2048,128]{1,0:T(8,128)S(1)}, f32[2048,128]{1,0:T(8,128)}, u32[]{:S(2)}) copy-start(f32[2048,128]{1,0:T(8,128)} %all-gather.15.cloned.1.call-done) | copy-start | bytes 3145732
  413.1 34.4 %copy-start.12 = (f32[2048,128]{1,0:T(8,128)}, f32[2048,128]{1,0:T(8,128)S(1)}, u32[]{:S(2)}) copy-start(f32[2048,128]{1,0:T(8,128)S(1)} %broadcast_multiply_fusion) | copy-start | bytes 3145732
  419.8 60.1 %all-gather.19.cloned.1.call-start = ((), (), s32[]{:S(2)}) async-start(), calls=%async_computation.7 | async-start | bytes 1310720 | tf_op jit(solution)/shard_map/all_gather | solution.py:85
  447.4 1.0 copy-start.7
  448.5 34.6 %copy-start.3 = (f32[2048,128]{1,0:T(8,128)}, f32[2048,128]{1,0:T(8,128)S(1)}, u32[]{:S(2)}) copy-start(f32[2048,128]{1,0:T(8,128)S(1)} %multiply_add_fusion.1) | copy-start | bytes 3145732
  448.5 33.0 %copy-start.8 = (f32[2048,128]{1,0:T(8,128)S(1)}, f32[2048,128]{1,0:T(8,128)}, u32[]{:S(2)}) copy-start(f32[2048,128]{1,0:T(8,128)} %copy-done.7) | copy-start | bytes 3145732
  455.3 59.4 %all-gather.21.cloned.1.call-start = ((), (), s32[]{:S(2)}) async-start(), calls=%async_computation.8 | async-start | bytes 1310720 | tf_op jit(solution)/shard_map/all_gather | solution.py:85
  479.9 3.2 copy-start.9
  479.9 3.2 copy-start.11
  483.4 31.3 %copy-start.6 = (f32[2048,128]{1,0:T(8,128)}, f32[2048,128]{1,0:T(8,128)S(1)}, u32[]{:S(2)}) copy-start(f32[2048,128]{1,0:T(8,128)S(1)} %multiply_add_fusion) | copy-start | bytes 3145732
  516.2 26.7 %copy-start.1 = (bf16[640,2048]{1,0:T(8,128)(2,1)S(1)}, bf16[640,2048]{1,0:T(8,128)(2,1)}, u32[]{:S(2)}) copy-start(bf16[640,2048]{1,0:T(8,128)(2,1)} %param.3) | copy-start | bytes 7864324
  542.1 0.8 copy-start.14
Sparse Core Ops, SparseCore 0:
  78.2 103.5 all-gather.10
  209.8 88.1 all-gather.22
  304.1 32.6 all-gather.24
  339.7 32.1 all-gather.12
  390.3 21.4 all-gather.14
  419.9 24.4 all-gather.16
  455.4 24.4 all-gather.18
  490.2 24.4 all-gather.20

commit v4 on v3

--- a/solution.py
+++ b/solution.py
@@ -16,6 +16,15 @@
 def masked_sum(stack, position):
     keep = jnp.arange(stack.shape[0]) < position
     return jnp.sum(jnp.where(keep.reshape((-1,) + (1,) * (stack.ndim - 1)), stack, 0.0), axis=0)
+
+
+def gather_feat(piece):
+    n = lax.axis_size("feat")
+    f = lax.axis_index("feat")
+    parts = [piece] + [lax.ppermute(piece, "feat", [(i, (i + k) % n) for i in range(n)]) for k in range(1, n)]
+    stacked = jnp.stack(parts)
+    full = jnp.take(stacked, (f - jnp.arange(n)) % n, axis=0)
+    return full.reshape((n * piece.shape[0],) + piece.shape[1:])
 
 
 def exclusive_prefix(block):
@@ -53,23 +62,17 @@
     contract = (((0,), (0,)), ((), ()))
     highest = lax.Precision.HIGHEST
     order = jnp.argsort(span_of, stable=True)
-    sorted_x = jnp.take(activations, order, axis=0).reshape(spans, share, width)
-    sorted_y = jnp.take(targets, order, axis=0).reshape(spans, share, n_targets)
-    moved_x, moved_y = (
-        lax.all_to_all(sorted_x, TM, split_axis=0, concat_axis=0, tiled=True),
-        lax.all_to_all(sorted_y, TM, split_axis=0, concat_axis=0, tiled=True),
-    )
-    local_x = moved_x.reshape(tok_dev, width)
-    local_y = moved_y.reshape(tok_dev, n_targets)
+    joined_in = jnp.concatenate([activations, targets], axis=1)
+    sorted_xy = jnp.take(joined_in, order, axis=0).reshape(spans, share, width + n_targets)
+    moved = lax.all_to_all(sorted_xy, TM, split_axis=0, concat_axis=0, tiled=True)
+    local_xy = moved.reshape(tok_dev, width + n_targets)
+    local_x = local_xy[:, :width]
     col_start = lax.axis_index("feat") * block_rows
-    rows_x = lax.all_gather(local_x, "feat", axis=0, tiled=True)
-    rows_y = lax.all_gather(local_y, "feat", axis=0, tiled=True)
-    own = lax.dynamic_slice_in_dim(rows_x, col_start, block_rows, 1)
-    gram_part = lax.dot_general(own, rows_x, contract, preferred_element_type=jnp.float32)
-    cross_part = lax.dot_general(own, rows_y, contract, preferred_element_type=jnp.float32)
-    moments = exclusive_prefix(jnp.concatenate([gram_part, cross_part], axis=1))
+    rows_xy = lax.all_gather(local_xy, "feat", axis=0, tiled=True)
+    own = lax.dynamic_slice_in_dim(rows_xy, col_start, block_rows, 1)
+    moments = exclusive_prefix(lax.dot_general(own, rows_xy, contract, preferred_element_type=jnp.float32))
     gram_prefix = moments[:, :width]
-    cross_prefix = lax.all_gather(moments[:, width:], "feat", axis=0, tiled=True)
+    cross_prefix = gather_feat(moments[:, width:])
     span = (lax.axis_index("x") * lax.axis_size("z") + lax.axis_index("z")) * lax.axis_size("c") + lax.axis_index("c")
     seen = (span * (tok_dev * feat_count)).astype(jnp.float32)
     scale = 1.0 / jnp.maximum(seen, 1.0)
@@ -82,7 +85,7 @@
     for step in range(ITERS):
         product = jnp.dot(gram_prefix, direction, precision=highest, preferred_element_type=jnp.float32)
         own_dir = lax.dynamic_slice_in_dim(direction, col_start, block_rows, 0)
-        image = lax.all_gather(scale * product + RIDGE * own_dir, "feat", axis=0, tiled=True)
+        image = gather_feat(scale * product + RIDGE * own_dir)
         alpha = norm_now / (jnp.sum(direction * image, axis=0) + TINY)
         update = alpha * direction
         solution = update if solution is None else solution + update

time: 551 us -> 504 us (0.915)
  waiting for transfers between devices: 340 us -> 313 us
  blocking collectives: 83.1 us -> 66.5 us
  starting transfers between devices: 6.34 us -> 19.4 us
  matrix products: 37 us -> 27.4 us
    all_gather x5 -> x1, waiting for transfers between devices: 167 us -> 104 us  [body(): rows_xy = lax.all_gather(local_xy, 'feat', axis=0, tiled=True)]
    ppermute x0 -> x12, waiting for transfers between devices: none -> 43.8 us  [gather_feat(): lax.ppermute(piece, 'feat', [(i, (i + k) % n) for i in range(n)])]
    ppermute x0 -> x12, starting transfers between devices: none -> 17.5 us  [gather_feat(): lax.ppermute(piece, 'feat', [(i, (i + k) % n) for i in range(n)])]
    all_gather x1 -> x0, blocking collectives: 16.6 us -> none  [body(): rows_y = lax.all_gather(local_y, 'feat', axis=0, tiled=True)]
    all_to_all x1 -> x0, waiting for transfers between devices: 8.25 us -> none  [body(): lax.all_to_all(sorted_y, TM, split_axis=0, concat_axis=0, tiled=True)]
    dot_general x3, matrix products: 20.1 us -> 12.5 us  [body(): jnp.dot(gram_prefix, direction, precision=highest, preferred_element_type...]
    gather x4 -> x6, local copies, waits for them, and re-layouts: 11.3 us -> 14.4 us  [the longest x2 7.76 us: body(): jnp.take(joined_in, order, axis=0).reshape(spans, share, width + n_targets)]
    dot_general x2 -> x1, matrix products: 13.2 us -> 12.4 us  [body(): lax.dot_general(own, rows_xy, contract, preferred_element_type=jnp.float32)]
  transfers between devices with their start and end apart: 11 -> 18, of which waited for: 11 -> 16; matrix products, arithmetic and copies ran while one was open for 1% -> 0% of each run, Pallas kernels for 0% -> 0%
where the time goes in v4:
time: 504 us
  waiting for transfers between devices  313 us (62%)
  blocking collectives  66.5 us (13%)
  other arithmetic  34.6 us (7%)
  local copies, waits for them, and re-layouts  29.2 us (6%)
  matrix products  27.4 us (5%)
  starting transfers between devices  19.4 us (4%)
  between operations  14.1 us (3%)
    all_gather x1, waiting for transfers between devices, body(): rows_xy = lax.all_gather(local_xy, 'feat', axis=0, tiled=True)  104 us
    all_gather x1, waiting for transfers between devices, exclusive_prefix(): along_z = lax.all_gather(mine, 'z')  88.2 us
    all_to_all x1, blocking collectives, body(): lax.all_to_all(sorted_xy, TM, split_axis=0, concat_axis=0, tiled=True)  51.2 us
    ppermute x12, waiting for transfers between devices, gather_feat(): lax.ppermute(piece, 'feat', [(i, (i + k) % n) for i in range(n)])  43.8 us
    all_gather x1, waiting for transfers between devices, exclusive_prefix(): along_x = lax.all_gather(piece, 'x')  32.8 us
    all_gather x1, waiting for transfers between devices, exclusive_prefix(): before_x = lax.all_gather(masked_sum(along_x, xi), 'z', axis=0, tiled=True)  32.3 us
    ppermute x12, starting transfers between devices, gather_feat(): lax.ppermute(piece, 'feat', [(i, (i + k) % n) for i in range(n)])  17.5 us
    all_to_all x1, blocking collectives, body(): lax.all_to_all(predicted.reshape(spans, share, n_targets), TM, split_axis...  15.3 us
  transfers between devices with their start and end apart: 18, of which 16 were waited for; matrix products, arithmetic and copies ran while one was open for 0% of the time, Pallas kernels for 0%

profile of v4, /device:TPU:1, one launch (start us, length us, event | category | flops | bytes accessed | tf_op | source)
XLA Modules:
  0.0 503.9 jit_solution(15185255051623306484)
XLA Ops:
  7.2 5.1 %sort.17 = (s32[640]{0:T(1024)}, s32[640]{0:T(1024)S(1)}) sort(s32[640]{0:T(1024)} %param.7, s32[640]{0:T(1024)S(1)} %iota.20), dimensions={0}, to_apply=%region_0.0 | sort | flops 6400 | bytes 10240 | tf_op jit(solution)/shard_map/jit(argsort)/sort | solution.py:64
  12.3 2.1 pad_maximum_fusion
  14.4 4.2 gather_fusion
  18.6 3.6 gather.10
  22.7 51.2 %all_to_all.10 = bf16[32,20,2176]{2,1,0:T(8,128)(2,1)S(1)} all-to-all(bf16[32,20,2176]{2,1,0:T(8,128)(2,1)S(1)} %broadcast_select_fusion), channel_id=1, replica_groups=mesh['x'=4,'z'=4,'c'=2,'feat'=4] {'x','z','c'}, dimensions={0} | all-to-all | bytes 5570560 | tf_op jit(solution)/shard_map/all_to_all | solution.py:67
  73.9 2.3 reshape.125
  76.3 103.8 %all-gather.7.cloned.1.call-done = bf16[2560,2176]{1,0:T(8,128)(2,1)} async-done(((bf16[640,2176]{1,0:T(8,128)(2,1)}), bf16[2560,2176]{1,0:T(8,128)(2,1)}) %all-gather.7.cloned.1.call-update) | async-done | bytes 11141136 | tf_op jit(solution)/shard_map/all_gather | solution.py:71
  180.1 12.4 %fusion.8 = f32[512,2176]{1,0:T(8,128)} fusion(bf16[2560,2176]{1,0:T(8,128)(2,1)} %all-gather.7.cloned.1.call-done, s32[]{:T(128)S(6)} %select_n.67), kind=kOutput, calls=%fused_computation.18 | convolution fusion | flops 5704253440 | bytes 18219012 | tf_op jit(solution)/shard_map/dot_general | solution.py:73
  193.4 7.5 %collective-permute-done = f32[512,2176]{1,0:T(8,128)} collective-permute-done((f32[512,2176]{1,0:T(8,128)}, f32[512,2176]{1,0:T(8,128)}, u32[]{:S(2)}, u32[]{:S(2)}) %collective-permute-start) | collective-permute-done | bytes 4456480 | tf_op jit(solution)/shard_map/ppermute | solution.py:36
  200.9 3.9 dynamic-slice_add_fusion
  204.9 88.2 %all-gather.11.cloned.1.call-done = f32[1024,2176]{1,0:T(8,128)} async-done(((f32[256,2176]{1,0:T(8,128)}), f32[1024,2176]{1,0:T(8,128)}) %all-gather.11.cloned.1.call-update) | async-done | bytes 8912912 | tf_op jit(solution)/shard_map/all_gather | solution.py:40
  293.1 5.1 %select_reduce_fusion = (f32[256,2176]{1,0:T(8,128)S(1)}, f32[256,2176]{1,0:T(8,128)S(1)}) fusion(f32[4,256,2176]{2,1,0:T(8,128)} %bitcast.48, pred[4]{0:T(512)(128)(4,1)S(1)} %iota_compare_fusion), kind=kLoop, calls=%fused_computation.6 | loop fusion | flops 5570560 | bytes 13369348 | tf_op jit(solution)/shard_map/reduce_sum | solution.py:18
  299.2 32.8 %all-gather.13.cloned.1.call-done = f32[256,2176]{1,0:T(8,128)} async-done(((f32[64,2176]{1,0:T(8,128)}), f32[256,2176]{1,0:T(8,128)}) %all-gather.13.cloned.1.call-update) | async-done | bytes 2228240 | tf_op jit(solution)/shard_map/all_gather | solution.py:45
  332.0 2.7 select_reduce_fusion.1
  334.7 32.3 %all-gather.9.cloned.1.call-done = f32[256,2176]{1,0:T(8,128)} async-done(((f32[64,2176]{1,0:T(8,128)}), f32[256,2176]{1,0:T(8,128)}) %all-gather.9.cloned.1.call-update) | async-done | bytes 2228240 | tf_op jit(solution)/shard_map/all_gather | solution.py:46
  367.0 2.3 broadcast_in_dim.68
  369.5 2.3 constant_dynamic-update-slice_fusion.1
  372.7 4.2 collective-permute-done.1
  378.4 4.1 select_add_fusion
  382.5 2.0 copy-done
  385.9 2.4 collective-permute-start.3
  389.6 3.8 collective-permute-done.2
  393.3 6.6 %collective-permute-done.3 = f32[512,128]{1,0:T(8,128)S(1)} collective-permute-done((f32[512,128]{1,0:T(8,128)S(1)}, f32[512,128]{1,0:T(8,128)S(1)}, u32[]{:S(2)}, u32[]{:S(2)}) %collective-permute-start.3) | collective-permute-done | bytes 262176 | tf_op jit(solution)/shard_map/ppermute | solution.py:24
  400.8 5.6 %fusion.13 = f32[512,128]{1,0:T(8,128)S(1)} fusion(f32[2048,128]{1,0:T(8,128)S(1)} %bitcast.46, f32[512,2176]{1,0:T(8,128)} %copy-done, s32[]{:T(128)S(6)} %select_n.76, f32[]{:T(128)S(6)} %div.44), kind=kOutput, calls=%fused_computation.23 | convolution fusion | flops 1610809344 | bytes 5767176 | tf_op jit(solution)/shard_map/dot_general | solution.py:86
  406.4 2.6 collective-permute-start.7
  410.6 4.1 collective-permute-done.7
  414.7 3.9 collective-permute-done.5
  418.6 3.4 collective-permute-done.6
  422.1 1.6 gather_fusion.2
  423.7 1.7 multiply_reduce_fusion.3
  426.2 3.4 fusion.19
  429.7 1.9 collective-permute-start.9
  431.6 1.8 collective-permute-start.10
  433.4 2.9 collective-permute-done.8
  436.3 5.5 %collective-permute-done.9 = f32[512,128]{1,0:T(8,128)S(1)} collective-permute-done((f32[512,128]{1,0:T(8,128)S(1)}, f32[512,128]{1,0:T(8,128)S(1)}, u32[]{:S(2)}, u32[]{:S(2)}) %collective-permute-start.9) | collective-permute-done | bytes 262176 | tf_op jit(solution)/shard_map/ppermute | solution.py:24
  441.8 2.3 collective-permute-done.10
  444.2 1.6 gather_fusion.3
  445.8 1.8 multiply_reduce_fusion.1
  448.6 3.4 fusion.25
  452.1 2.1 collective-permute-start.11
  454.2 2.5 collective-permute-start.12
  456.7 4.2 collective-permute-done.11
  461.0 7.1 %collective-permute-done.12 = f32[512,128]{1,0:T(8,128)S(1)} collective-permute-done((f32[512,128]{1,0:T(8,128)S(1)}, f32[512,128]{1,0:T(8,128)S(1)}, u32[]{:S(2)}, u32[]{:S(2)}) %collective-permute-start.12) | collective-permute-done | bytes 262176 | tf_op jit(solution)/shard_map/ppermute | solution.py:24
  469.2 2.8 gather_fusion.4
  472.0 1.9 fusion.34
  474.4 2.5 fusion.28
  477.0 15.3 %all_to_all.11 = bf16[32,20,128]{2,1,0:T(8,128)(2,1)S(1)} all-to-all(bf16[32,20,128]{2,1,0:T(8,128)(2,1)S(1)} %reshape.128), channel_id=1, replica_groups=mesh['x'=4,'z'=4,'c'=2,'feat'=4] {'x','z','c'}, dimensions={0} | all-to-all | bytes 327680 | tf_op jit(solution)/shard_map/all_to_all | solution.py:99
  492.3 4.3 scatter_custom_fusion
  (80 shorter events, 14.5 us)
Async XLA Ops:
  7.2 172.9 %all-gather.7.cloned.1.call-start = ((), (), s32[]{:S(2)}) async-start(), calls=%async_computation.2 | async-start | bytes 13926400 | tf_op jit(solution)/shard_map/all_gather | solution.py:71
  76.2 216.9 %all-gather.11.cloned.1.call-start = ((), (), s32[]{:S(2)}) async-start(), calls=%async_computation.4 | async-start | bytes 11141120 | tf_op jit(solution)/shard_map/all_gather | solution.py:40
  192.5 8.3 %collective-permute-start = (f32[512,2176]{1,0:T(8,128)}, f32[512,2176]{1,0:T(8,128)}, u32[]{:S(2)}, u32[]{:S(2)}) collective-permute-start(f32[512,2176]{1,0:T(8,128)} %fusion.8), channel_id=1, source_target_pairs={{0,4},{4,0},{1,5},{5,1},{2,6},{6,2},{3,7},{7,3},{8,12},{12,8},{9,1... | collective-permute-start | bytes 13369352 | tf_op jit(solution)/shard_map/ppermute | solution.py:36
  204.8 127.2 %all-gather.13.cloned.1.call-start = ((), (), s32[]{:S(2)}) async-start(), calls=%async_computation.5 | async-start | bytes 2785280 | tf_op jit(solution)/shard_map/all_gather | solution.py:45
  299.1 67.9 %all-gather.9.cloned.1.call-start = ((), (), s32[]{:S(2)}) async-start(), calls=%async_computation.3 | async-start | bytes 2785280 | tf_op jit(solution)/shard_map/all_gather | solution.py:46
  367.0 2.5 copy-start.7
  371.9 5.0 collective-permute-start.1
  382.5 2.0 copy-start
  384.6 8.7 %collective-permute-start.2 = (f32[512,128]{1,0:T(8,128)S(1)}, f32[512,128]{1,0:T(8,128)S(1)}, u32[]{:S(2)}, u32[]{:S(2)}) collective-permute-start(f32[512,128]{1,0:T(8,128)S(1)} %get-tuple-element.15), channel_id=1, source_target_pairs={{0,1},{1,2},{2,3},{3,0},{4,5},{5,6},{6,7},{7,4},{8,9},{9,10},{10,1... | collective-permute-start | bytes 786440 | tf_op jit(solution)/shard_map/ppermute | solution.py:24
  385.9 14.1 %collective-permute-start.3 = (f32[512,128]{1,0:T(8,128)S(1)}, f32[512,128]{1,0:T(8,128)S(1)}, u32[]{:S(2)}, u32[]{:S(2)}) collective-permute-start(f32[512,128]{1,0:T(8,128)S(1)} %get-tuple-element.15), channel_id=1, source_target_pairs={{0,2},{1,3},{2,0},{3,1},{4,6},{5,7},{6,4},{7,5},{8,10},{9,11},{10,... | collective-permute-start | bytes 786440 | tf_op jit(solution)/shard_map/ppermute | solution.py:24
  388.3 11.6 %collective-permute-start.4 = (f32[512,128]{1,0:T(8,128)S(1)}, f32[512,128]{1,0:T(8,128)S(1)}, u32[]{:S(2)}, u32[]{:S(2)}) collective-permute-start(f32[512,128]{1,0:T(8,128)S(1)} %get-tuple-element.15), channel_id=1, source_target_pairs={{0,3},{1,0},{2,1},{3,2},{4,7},{5,4},{6,5},{7,6},{8,11},{9,8},{10,9... | collective-permute-start | bytes 786440 | tf_op jit(solution)/shard_map/ppermute | solution.py:24
  400.8 25.0 %copy-start.1 = (f32[4,512,128]{2,1,0:T(8,128)}, f32[4,512,128]{2,1,0:T(8,128)S(1)}, u32[]{:S(2)}) copy-start(f32[4,512,128]{2,1,0:T(8,128)S(1)} %select_multiply_fusion.1) | copy-start | bytes 3145732
  406.4 8.3 %collective-permute-start.7 = (f32[512,128]{1,0:T(8,128)S(1)}, f32[512,128]{1,0:T(8,128)S(1)}, u32[]{:S(2)}, u32[]{:S(2)}) collective-permute-start(f32[512,128]{1,0:T(8,128)S(1)} %fusion.13), channel_id=1, source_target_pairs={{0,3},{1,0},{2,1},{3,2},{4,7},{5,4},{6,5},{7,6},{8,11},{9,8},{10,9... | collective-permute-start | bytes 786440 | tf_op jit(solution)/shard_map/ppermute | solution.py:24
  409.0 9.5 %collective-permute-start.5 = (f32[512,128]{1,0:T(8,128)S(1)}, f32[512,128]{1,0:T(8,128)S(1)}, u32[]{:S(2)}, u32[]{:S(2)}) collective-permute-start(f32[512,128]{1,0:T(8,128)S(1)} %fusion.13), channel_id=1, source_target_pairs={{0,1},{1,2},{2,3},{3,0},{4,5},{5,6},{6,7},{7,4},{8,9},{9,10},{10,1... | collective-permute-start | bytes 786440 | tf_op jit(solution)/shard_map/ppermute | solution.py:24
  409.0 12.9 %collective-permute-start.6 = (f32[512,128]{1,0:T(8,128)S(1)}, f32[512,128]{1,0:T(8,128)S(1)}, u32[]{:S(2)}, u32[]{:S(2)}) collective-permute-start(f32[512,128]{1,0:T(8,128)S(1)} %fusion.13), channel_id=1, source_target_pairs={{0,2},{1,3},{2,0},{3,1},{4,6},{5,7},{6,4},{7,5},{8,10},{9,11},{10,... | collective-permute-start | bytes 786440 | tf_op jit(solution)/shard_map/ppermute | solution.py:24
  422.0 4.0 slice-start
  423.7 2.5 slice-start.1
  426.2 18.0 %copy-start.5 = (f32[2048,128]{1,0:T(8,128)}, f32[2048,128]{1,0:T(8,128)S(1)}, u32[]{:S(2)}) copy-start(f32[2048,128]{1,0:T(8,128)S(1)} %multiply_add_fusion) | copy-start | bytes 3145732
  429.6 6.7 %collective-permute-start.8 = (f32[512,128]{1,0:T(8,128)S(1)}, f32[512,128]{1,0:T(8,128)S(1)}, u32[]{:S(2)}, u32[]{:S(2)}) collective-permute-start(f32[512,128]{1,0:T(8,128)S(1)} %fusion.19), channel_id=1, source_target_pairs={{0,1},{1,2},{2,3},{3,0},{4,5},{5,6},{6,7},{7,4},{8,9},{9,10},{10,1... | collective-permute-start | bytes 786440 | tf_op jit(solution)/shard_map/ppermute | solution.py:24
  429.7 12.1 %collective-permute-start.9 = (f32[512,128]{1,0:T(8,128)S(1)}, f32[512,128]{1,0:T(8,128)S(1)}, u32[]{:S(2)}, u32[]{:S(2)}) collective-permute-start(f32[512,128]{1,0:T(8,128)S(1)} %fusion.19), channel_id=1, source_target_pairs={{0,2},{1,3},{2,0},{3,1},{4,6},{5,7},{6,4},{7,5},{8,10},{9,11},{10,... | collective-permute-start | bytes 786440 | tf_op jit(solution)/shard_map/ppermute | solution.py:24
  431.6 12.5 %collective-permute-start.10 = (f32[512,128]{1,0:T(8,128)S(1)}, f32[512,128]{1,0:T(8,128)S(1)}, u32[]{:S(2)}, u32[]{:S(2)}) collective-permute-start(f32[512,128]{1,0:T(8,128)S(1)} %fusion.19), channel_id=1, source_target_pairs={{0,3},{1,0},{2,1},{3,2},{4,7},{5,4},{6,5},{7,6},{8,11},{9,8},{10,9... | collective-permute-start | bytes 786440 | tf_op jit(solution)/shard_map/ppermute | solution.py:24
  444.1 4.1 slice-start.2
  445.8 2.1 copy-start.2
  445.8 2.8 slice-start.3
  448.6 3.4 copy-start.6
  452.1 8.9 %collective-permute-start.11 = (f32[512,128]{1,0:T(8,128)S(1)}, f32[512,128]{1,0:T(8,128)S(1)}, u32[]{:S(2)}, u32[]{:S(2)}) collective-permute-start(f32[512,128]{1,0:T(8,128)S(1)} %fusion.25), channel_id=1, source_target_pairs={{0,1},{1,2},{2,3},{3,0},{4,5},{5,6},{6,7},{7,4},{8,9},{9,10},{10,1... | collective-permute-start | bytes 786440 | tf_op jit(solution)/shard_map/ppermute | solution.py:24
  454.2 13.9 %collective-permute-start.12 = (f32[512,128]{1,0:T(8,128)S(1)}, f32[512,128]{1,0:T(8,128)S(1)}, u32[]{:S(2)}, u32[]{:S(2)}) collective-permute-start(f32[512,128]{1,0:T(8,128)S(1)} %fusion.25), channel_id=1, source_target_pairs={{0,2},{1,3},{2,0},{3,1},{4,6},{5,7},{6,4},{7,5},{8,10},{9,11},{10,... | collective-permute-start | bytes 786440 | tf_op jit(solution)/shard_map/ppermute | solution.py:24
  456.7 11.4 %collective-permute-start.13 = (f32[512,128]{1,0:T(8,128)S(1)}, f32[512,128]{1,0:T(8,128)S(1)}, u32[]{:S(2)}, u32[]{:S(2)}) collective-permute-start(f32[512,128]{1,0:T(8,128)S(1)} %fusion.25), channel_id=1, source_target_pairs={{0,3},{1,0},{2,1},{3,2},{4,7},{5,4},{6,5},{7,6},{8,11},{9,8},{10,9... | collective-permute-start | bytes 786440 | tf_op jit(solution)/shard_map/ppermute | solution.py:24
  472.0 1.9 copy-start.3
  472.0 2.4 copy-start.4
  474.4 22.1 %copy-start.8 = (bf16[640,128]{1,0:T(8,128)(2,1)S(1)}, bf16[640,128]{1,0:T(8,128)(2,1)}, u32[]{:S(2)}) copy-start(bf16[640,128]{1,0:T(8,128)(2,1)} %param.6) | copy-start | bytes 491524
  496.6 0.8 copy-start.9
Sparse Core Ops, SparseCore 0:
  76.4 103.6 all-gather.6
  204.9 88.1 all-gather.10
  299.2 32.6 all-gather.12
  334.8 32.1 all-gather.8

commit v5 on v4

--- a/solution.py
+++ b/solution.py
@@ -64,13 +64,19 @@
     order = jnp.argsort(span_of, stable=True)
     joined_in = jnp.concatenate([activations, targets], axis=1)
     sorted_xy = jnp.take(joined_in, order, axis=0).reshape(spans, share, width + n_targets)
-    moved = lax.all_to_all(sorted_xy, TM, split_axis=0, concat_axis=0, tiled=True)
-    local_xy = moved.reshape(tok_dev, width + n_targets)
-    local_x = local_xy[:, :width]
     col_start = lax.axis_index("feat") * block_rows
-    rows_xy = lax.all_gather(local_xy, "feat", axis=0, tiled=True)
-    own = lax.dynamic_slice_in_dim(rows_xy, col_start, block_rows, 1)
-    moments = exclusive_prefix(lax.dot_general(own, rows_xy, contract, preferred_element_type=jnp.float32))
+    cut = share // 2
+    locals_x = []
+    moments = None
+    for piece in (sorted_xy[:, :cut], sorted_xy[:, cut:]):
+        moved = lax.all_to_all(piece, TM, split_axis=0, concat_axis=0, tiled=True)
+        local_xy = moved.reshape(-1, width + n_targets)
+        locals_x.append(local_xy[:, :width])
+        rows_xy = lax.all_gather(local_xy, "feat", axis=0, tiled=True)
+        own = lax.dynamic_slice_in_dim(rows_xy, col_start, block_rows, 1)
+        part = lax.dot_general(own, rows_xy, contract, preferred_element_type=jnp.float32)
+        moments = part if moments is None else moments + part
+    moments = exclusive_prefix(moments)
     gram_prefix = moments[:, :width]
     cross_prefix = gather_feat(moments[:, width:])
     span = (lax.axis_index("x") * lax.axis_size("z") + lax.axis_index("z")) * lax.axis_size("c") + lax.axis_index("c")
@@ -95,9 +101,12 @@
             direction = residual + norm_next / (norm_now + TINY) * direction
             norm_now = norm_next
     weights = solution.astype(jnp.bfloat16)
-    predicted = jnp.dot(local_x, weights, preferred_element_type=jnp.float32).astype(jnp.bfloat16)
+    predicted = [
+        jnp.dot(lx, weights, preferred_element_type=jnp.float32).astype(jnp.bfloat16).reshape(spans, -1, n_targets)
+        for lx in locals_x
+    ]
     returned = lax.all_to_all(
-        predicted.reshape(spans, share, n_targets), TM, split_axis=0, concat_axis=0, tiled=True
+        jnp.concatenate(predicted, axis=1), TM, split_axis=0, concat_axis=0, tiled=True
     )
     in_order = returned.reshape(tok_dev, n_targets)
     predictions = jnp.zeros_like(in_order).at[order].set(in_order)

time: 504 us -> 508 us (level)
  waiting for transfers between devices: 313 us -> 281 us
  blocking collectives: 66.5 us -> 88.7 us
  local copies, waits for them, and re-layouts: 29.2 us -> 36.4 us
    all_gather x1 -> x2, waiting for transfers between devices: 104 us -> 73 us  [body(): rows_xy = lax.all_gather(local_xy, 'feat', axis=0, tiled=True)]
    all_to_all x2 -> x3, blocking collectives: 66.5 us -> 88.7 us  [the longest x2 73.5 us: body(): moved = lax.all_to_all(piece, TM, split_axis=0, concat_axis=0, tiled=True)]
    dot_general x1 -> x2, matrix products: 12.4 us -> 17.9 us  [body(): lax.dot_general(own, rows_xy, contract, preferred_element_type=jnp.float32)]
    reshape x2 -> x4, local copies, waits for them, and re-layouts: 2.3 us -> 7.39 us  [the longest x2 7.33 us: body(): local_xy = moved.reshape(-1, width + n_targets)]
  transfers between devices with their start and end apart: 18 -> 19, of which waited for: 16 -> 17; matrix products, arithmetic and copies ran while one was open for 0% -> 2% of each run, Pallas kernels for 0% -> 0%
where the time goes in v5:
time: 508 us
  waiting for transfers between devices  281 us (55%)
  blocking collectives  88.7 us (17%)
  local copies, waits for them, and re-layouts  36.4 us (7%)
  other arithmetic  36.3 us (7%)
  matrix products  31 us (6%)
  starting transfers between devices  19.6 us (4%)
  between operations  14.2 us (3%)
    all_gather x1, waiting for transfers between devices, exclusive_prefix(): along_z = lax.all_gather(mine, 'z')  87.6 us
    all_to_all x2, blocking collectives, body(): moved = lax.all_to_all(piece, TM, split_axis=0, concat_axis=0, tiled=True)  73.5 us
    all_gather x2, waiting for transfers between devices, body(): rows_xy = lax.all_gather(local_xy, 'feat', axis=0, tiled=True)  73 us
    ppermute x12, waiting for transfers between devices, gather_feat(): lax.ppermute(piece, 'feat', [(i, (i + k) % n) for i in range(n)])  43.9 us
    all_gather x1, waiting for transfers between devices, exclusive_prefix(): along_x = lax.all_gather(piece, 'x')  32.8 us
    all_gather x1, waiting for transfers between devices, exclusive_prefix(): before_x = lax.all_gather(masked_sum(along_x, xi), 'z', axis=0, tiled=True)  32.3 us
    dot_general x2, matrix products, body(): lax.dot_general(own, rows_xy, contract, preferred_element_type=jnp.float32)  17.9 us
    ppermute x12, starting transfers between devices, gather_feat(): lax.ppermute(piece, 'feat', [(i, (i + k) % n) for i in range(n)])  17.5 us
  transfers between devices with their start and end apart: 19, of which 17 were waited for; matrix products, arithmetic and copies ran while one was open for 2% of the time, Pallas kernels for 0%

profile of v5, /device:TPU:1, one launch (start us, length us, event | category | flops | bytes accessed | tf_op | source)
XLA Modules:
  0.0 507.6 jit_solution(9705571603082384308)
XLA Ops:
  7.2 5.1 sort.17
  12.3 2.1 pad_maximum_fusion
  14.4 4.2 gather_fusion
  18.6 3.6 gather.10
  23.4 39.5 %all_to_all.15 = bf16[32,10,2176]{2,1,0:T(8,128)(2,1)} all-to-all(bf16[32,10,2176]{2,1,0:T(8,128)(2,1)S(1)} %get-tuple-element.17), channel_id=1, replica_groups=mesh['x'=4,'z'=4,'c'=2,'feat'=4] {'x','z','c'}, dimensions={0} | all-to-all | bytes 2785280 | tf_op jit(solution)/shard_map/all_to_all | solution.py:72
  62.9 3.7 reshape.131
  66.7 34.0 %all_to_all.16 = bf16[32,10,2176]{2,1,0:T(8,128)(2,1)} all-to-all(bf16[32,10,2176]{2,1,0:T(8,128)(2,1)S(1)} %get-tuple-element.16), channel_id=1, replica_groups=mesh['x'=4,'z'=4,'c'=2,'feat'=4] {'x','z','c'}, dimensions={0} | all-to-all | bytes 2785280 | tf_op jit(solution)/shard_map/all_to_all | solution.py:72
  100.7 3.7 reshape.132
  104.4 19.4 %all-gather.8.cloned.1.call-done = bf16[1280,2176]{1,0:T(8,128)(2,1)} async-done(((bf16[320,2176]{1,0:T(8,128)(2,1)}), bf16[1280,2176]{1,0:T(8,128)(2,1)}) %all-gather.8.cloned.1.call-update) | async-done | bytes 5570576 | tf_op jit(solution)/shard_map/all_gather | solution.py:75
  123.8 8.3 %fusion.11 = f32[512,2176]{1,0:T(8,128)} fusion(bf16[1280,2176]{1,0:T(8,128)(2,1)} %all-gather.8.cloned.1.call-done, s32[]{:T(128)S(6)} %select_n.68), kind=kOutput, calls=%fused_computation.24 | convolution fusion | flops 2852126720 | bytes 11337732 | tf_op jit(solution)/shard_map/dot_general | solution.py:77
  132.1 53.6 %all-gather.10.cloned.1.call-done = bf16[1280,2176]{1,0:T(8,128)(2,1)} async-done(((bf16[320,2176]{1,0:T(8,128)(2,1)}), bf16[1280,2176]{1,0:T(8,128)(2,1)}) %all-gather.10.cloned.1.call-update) | async-done | bytes 5570576 | tf_op jit(solution)/shard_map/all_gather | solution.py:75
  185.7 9.6 %convolution_add_fusion = f32[512,2176]{1,0:T(8,128)} fusion(f32[512,2176]{1,0:T(8,128)} %fusion.11, bf16[1280,2176]{1,0:T(8,128)(2,1)} %all-gather.10.cloned.1.call-done, s32[]{:T(128)S(6)} %select_n.68), kind=kOutput, calls=%fused_computation.7 | convolution fusion | flops 2853240832 | bytes 15794180 | tf_op jit(solution)/shard_map/dot_general | solution.py:77
  196.1 7.5 %collective-permute-done = f32[512,2176]{1,0:T(8,128)} collective-permute-done((f32[512,2176]{1,0:T(8,128)}, f32[512,2176]{1,0:T(8,128)}, u32[]{:S(2)}, u32[]{:S(2)}) %collective-permute-start) | collective-permute-done | bytes 4456480 | tf_op jit(solution)/shard_map/ppermute | solution.py:36
  203.6 3.9 dynamic-slice_add_fusion
  207.8 87.6 %all-gather.14.cloned.1.call-done = f32[1024,2176]{1,0:T(8,128)} async-done(((f32[256,2176]{1,0:T(8,128)}), f32[1024,2176]{1,0:T(8,128)}) %all-gather.14.cloned.1.call-update) | async-done | bytes 8912912 | tf_op jit(solution)/shard_map/all_gather | solution.py:40
  295.4 5.1 %select_reduce_fusion = (f32[256,2176]{1,0:T(8,128)S(1)}, f32[256,2176]{1,0:T(8,128)S(1)}) fusion(f32[4,256,2176]{2,1,0:T(8,128)} %bitcast.53, pred[4]{0:T(512)(128)(4,1)S(1)} %iota_compare_fusion), kind=kLoop, calls=%fused_computation.6 | loop fusion | flops 5570560 | bytes 13369348 | tf_op jit(solution)/shard_map/reduce_sum | solution.py:18
  301.5 32.8 %all-gather.16.cloned.1.call-done = f32[256,2176]{1,0:T(8,128)} async-done(((f32[64,2176]{1,0:T(8,128)}), f32[256,2176]{1,0:T(8,128)}) %all-gather.16.cloned.1.call-update) | async-done | bytes 2228240 | tf_op jit(solution)/shard_map/all_gather | solution.py:45
  334.2 2.7 select_reduce_fusion.1
  337.0 32.3 %all-gather.12.cloned.1.call-done = f32[256,2176]{1,0:T(8,128)} async-done(((f32[64,2176]{1,0:T(8,128)}), f32[256,2176]{1,0:T(8,128)}) %all-gather.12.cloned.1.call-update) | async-done | bytes 2228240 | tf_op jit(solution)/shard_map/all_gather | solution.py:46
  369.3 2.3 broadcast_in_dim.68
  371.8 2.3 constant_dynamic-update-slice_fusion.1
  375.0 4.2 collective-permute-done.1
  380.7 4.1 select_add_fusion
  384.8 2.0 copy-done
  388.1 2.4 collective-permute-start.3
  391.8 3.8 collective-permute-done.2
  395.6 6.6 %collective-permute-done.3 = f32[512,128]{1,0:T(8,128)S(1)} collective-permute-done((f32[512,128]{1,0:T(8,128)S(1)}, f32[512,128]{1,0:T(8,128)S(1)}, u32[]{:S(2)}, u32[]{:S(2)}) %collective-permute-start.3) | collective-permute-done | bytes 262176 | tf_op jit(solution)/shard_map/ppermute | solution.py:24
  403.0 5.3 %fusion.16 = f32[512,128]{1,0:T(8,128)S(1)} fusion(f32[2048,128]{1,0:T(8,128)S(1)} %bitcast.52, f32[512,2176]{1,0:T(8,128)} %copy-done, s32[]{:T(128)S(6)} %select_n.77, f32[]{:T(128)S(6)} %div.44), kind=kOutput, calls=%fused_computation.27 | convolution fusion | flops 1610809344 | bytes 5767176 | tf_op jit(solution)/shard_map/dot_general | solution.py:92
  408.3 2.6 collective-permute-start.7
  412.5 4.0 collective-permute-done.7
  416.5 3.9 collective-permute-done.5
  420.4 3.4 collective-permute-done.6
  428.1 3.4 fusion.22
  431.6 1.9 collective-permute-start.9
  433.5 1.8 collective-permute-start.10
  435.3 3.4 collective-permute-done.8
  438.7 5.0 collective-permute-done.9
  443.6 2.4 collective-permute-done.10
  447.2 2.8 gather_fusion.3
  453.1 3.4 fusion.28
  456.6 2.1 collective-permute-start.11
  458.7 2.5 collective-permute-start.12
  461.2 4.3 collective-permute-done.11
  465.5 7.1 %collective-permute-done.12 = f32[512,128]{1,0:T(8,128)S(1)} collective-permute-done((f32[512,128]{1,0:T(8,128)S(1)}, f32[512,128]{1,0:T(8,128)S(1)}, u32[]{:S(2)}, u32[]{:S(2)}) %collective-permute-start.12) | collective-permute-done | bytes 262176 | tf_op jit(solution)/shard_map/ppermute | solution.py:24
  473.6 2.8 gather_fusion.4
  476.5 2.2 fusion.40
  480.7 15.3 %all_to_all.17 = bf16[32,20,128]{2,1,0:T(8,128)(2,1)S(1)} all-to-all(bf16[32,20,128]{2,1,0:T(8,128)(2,1)S(1)} %pad_maximum_fusion.5), channel_id=1, replica_groups=mesh['x'=4,'z'=4,'c'=2,'feat'=4] {'x','z','c'}, dimensions={0} | all-to-all | bytes 327680 | tf_op jit(solution)/shard_map/all_to_all | solution.py:108
  496.0 4.3 scatter_custom_fusion
  (89 shorter events, 23.2 us)
Async XLA Ops:
  7.2 116.6 %all-gather.8.cloned.1.call-start = ((), (), s32[]{:S(2)}) async-start(), calls=%async_computation.3 | async-start | bytes 6963200 | tf_op jit(solution)/shard_map/all_gather | solution.py:75
  66.6 119.1 %all-gather.10.cloned.1.call-start = ((), (), s32[]{:S(2)}) async-start(), calls=%async_computation.4 | async-start | bytes 6963200 | tf_op jit(solution)/shard_map/all_gather | solution.py:75
  104.3 191.1 %all-gather.14.cloned.1.call-start = ((), (), s32[]{:S(2)}) async-start(), calls=%async_computation.6 | async-start | bytes 11141120 | tf_op jit(solution)/shard_map/all_gather | solution.py:40
  195.3 8.3 %collective-permute-start = (f32[512,2176]{1,0:T(8,128)}, f32[512,2176]{1,0:T(8,128)}, u32[]{:S(2)}, u32[]{:S(2)}) collective-permute-start(f32[512,2176]{1,0:T(8,128)} %convolution_add_fusion), channel_id=1, source_target_pairs={{0,4},{4,0},{1,5},{5,1},{2,6},{6,2},{3,7},{7,3},{8,12},{12,8},{9,1... | collective-permute-start | bytes 13369352 | tf_op jit(solution)/shard_map/ppermute | solution.py:36
  207.5 126.7 %all-gather.16.cloned.1.call-start = ((), (), s32[]{:S(2)}) async-start(), calls=%async_computation.7 | async-start | bytes 2785280 | tf_op jit(solution)/shard_map/all_gather | solution.py:45
  301.4 67.9 %all-gather.12.cloned.1.call-start = ((), (), s32[]{:S(2)}) async-start(), calls=%async_computation.5 | async-start | bytes 2785280 | tf_op jit(solution)/shard_map/all_gather | solution.py:46
  369.3 2.5 copy-start.6
  374.1 5.0 collective-permute-start.1
  384.8 2.0 copy-start
  386.8 8.8 %collective-permute-start.2 = (f32[512,128]{1,0:T(8,128)S(1)}, f32[512,128]{1,0:T(8,128)S(1)}, u32[]{:S(2)}, u32[]{:S(2)}) collective-permute-start(f32[512,128]{1,0:T(8,128)S(1)} %get-tuple-element.15), channel_id=1, source_target_pairs={{0,1},{1,2},{2,3},{3,0},{4,5},{5,6},{6,7},{7,4},{8,9},{9,10},{10,1... | collective-permute-start | bytes 786440 | tf_op jit(solution)/shard_map/ppermute | solution.py:24
  388.1 14.1 %collective-permute-start.3 = (f32[512,128]{1,0:T(8,128)S(1)}, f32[512,128]{1,0:T(8,128)S(1)}, u32[]{:S(2)}, u32[]{:S(2)}) collective-permute-start(f32[512,128]{1,0:T(8,128)S(1)} %get-tuple-element.15), channel_id=1, source_target_pairs={{0,2},{1,3},{2,0},{3,1},{4,6},{5,7},{6,4},{7,5},{8,10},{9,11},{10,... | collective-permute-start | bytes 786440 | tf_op jit(solution)/shard_map/ppermute | solution.py:24
  390.6 11.6 %collective-permute-start.4 = (f32[512,128]{1,0:T(8,128)S(1)}, f32[512,128]{1,0:T(8,128)S(1)}, u32[]{:S(2)}, u32[]{:S(2)}) collective-permute-start(f32[512,128]{1,0:T(8,128)S(1)} %get-tuple-element.15), channel_id=1, source_target_pairs={{0,3},{1,0},{2,1},{3,2},{4,7},{5,4},{6,5},{7,6},{8,11},{9,8},{10,9... | collective-permute-start | bytes 786440 | tf_op jit(solution)/shard_map/ppermute | solution.py:24
  408.3 8.3 %collective-permute-start.7 = (f32[512,128]{1,0:T(8,128)S(1)}, f32[512,128]{1,0:T(8,128)S(1)}, u32[]{:S(2)}, u32[]{:S(2)}) collective-permute-start(f32[512,128]{1,0:T(8,128)S(1)} %fusion.16), channel_id=1, source_target_pairs={{0,3},{1,0},{2,1},{3,2},{4,7},{5,4},{6,5},{7,6},{8,11},{9,8},{10,9... | collective-permute-start | bytes 786440 | tf_op jit(solution)/shard_map/ppermute | solution.py:24
  410.9 9.5 %collective-permute-start.5 = (f32[512,128]{1,0:T(8,128)S(1)}, f32[512,128]{1,0:T(8,128)S(1)}, u32[]{:S(2)}, u32[]{:S(2)}) collective-permute-start(f32[512,128]{1,0:T(8,128)S(1)} %fusion.16), channel_id=1, source_target_pairs={{0,1},{1,2},{2,3},{3,0},{4,5},{5,6},{6,7},{7,4},{8,9},{9,10},{10,1... | collective-permute-start | bytes 786440 | tf_op jit(solution)/shard_map/ppermute | solution.py:24
  410.9 13.0 %collective-permute-start.6 = (f32[512,128]{1,0:T(8,128)S(1)}, f32[512,128]{1,0:T(8,128)S(1)}, u32[]{:S(2)}, u32[]{:S(2)}) collective-permute-start(f32[512,128]{1,0:T(8,128)S(1)} %fusion.16), channel_id=1, source_target_pairs={{0,2},{1,3},{2,0},{3,1},{4,6},{5,7},{6,4},{7,5},{8,10},{9,11},{10,... | collective-permute-start | bytes 786440 | tf_op jit(solution)/shard_map/ppermute | solution.py:24
  423.9 4.0 slice-start
  425.6 2.5 slice-start.1
  431.5 7.2 %collective-permute-start.8 = (f32[512,128]{1,0:T(8,128)S(1)}, f32[512,128]{1,0:T(8,128)S(1)}, u32[]{:S(2)}, u32[]{:S(2)}) collective-permute-start(f32[512,128]{1,0:T(8,128)S(1)} %fusion.22), channel_id=1, source_target_pairs={{0,1},{1,2},{2,3},{3,0},{4,5},{5,6},{6,7},{7,4},{8,9},{9,10},{10,1... | collective-permute-start | bytes 786440 | tf_op jit(solution)/shard_map/ppermute | solution.py:24
  431.6 12.0 %collective-permute-start.9 = (f32[512,128]{1,0:T(8,128)S(1)}, f32[512,128]{1,0:T(8,128)S(1)}, u32[]{:S(2)}, u32[]{:S(2)}) collective-permute-start(f32[512,128]{1,0:T(8,128)S(1)} %fusion.22), channel_id=1, source_target_pairs={{0,2},{1,3},{2,0},{3,1},{4,6},{5,7},{6,4},{7,5},{8,10},{9,11},{10,... | collective-permute-start | bytes 786440 | tf_op jit(solution)/shard_map/ppermute | solution.py:24
  433.5 12.6 %collective-permute-start.10 = (f32[512,128]{1,0:T(8,128)S(1)}, f32[512,128]{1,0:T(8,128)S(1)}, u32[]{:S(2)}, u32[]{:S(2)}) collective-permute-start(f32[512,128]{1,0:T(8,128)S(1)} %fusion.22), channel_id=1, source_target_pairs={{0,3},{1,0},{2,1},{3,2},{4,7},{5,4},{6,5},{7,6},{8,11},{9,8},{10,9... | collective-permute-start | bytes 786440 | tf_op jit(solution)/shard_map/ppermute | solution.py:24
  446.1 7.0 %slice-start.2 = ((s8[4456448]{0:T(1024)(128)(4,1)}), s8[262144]{0:T(1024)(128)(4,1)S(1)}, s32[]{:S(2)}) async-start(s8[4456448]{0:T(1024)(128)(4,1)} %bitcast.50), calls=%async_computation.10 | async-start | bytes 524288
  450.0 3.1 slice-start.3
  451.7 1.0 copy-start.1
  453.1 3.5 copy-start.2
  456.6 8.9 %collective-permute-start.11 = (f32[512,128]{1,0:T(8,128)S(1)}, f32[512,128]{1,0:T(8,128)S(1)}, u32[]{:S(2)}, u32[]{:S(2)}) collective-permute-start(f32[512,128]{1,0:T(8,128)S(1)} %fusion.28), channel_id=1, source_target_pairs={{0,1},{1,2},{2,3},{3,0},{4,5},{5,6},{6,7},{7,4},{8,9},{9,10},{10,1... | collective-permute-start | bytes 786440 | tf_op jit(solution)/shard_map/ppermute | solution.py:24
  458.7 13.9 %collective-permute-start.12 = (f32[512,128]{1,0:T(8,128)S(1)}, f32[512,128]{1,0:T(8,128)S(1)}, u32[]{:S(2)}, u32[]{:S(2)}) collective-permute-start(f32[512,128]{1,0:T(8,128)S(1)} %fusion.28), channel_id=1, source_target_pairs={{0,2},{1,3},{2,0},{3,1},{4,6},{5,7},{6,4},{7,5},{8,10},{9,11},{10,... | collective-permute-start | bytes 786440 | tf_op jit(solution)/shard_map/ppermute | solution.py:24
  461.2 11.4 %collective-permute-start.13 = (f32[512,128]{1,0:T(8,128)S(1)}, f32[512,128]{1,0:T(8,128)S(1)}, u32[]{:S(2)}, u32[]{:S(2)}) collective-permute-start(f32[512,128]{1,0:T(8,128)S(1)} %fusion.28), channel_id=1, source_target_pairs={{0,3},{1,0},{2,1},{3,2},{4,7},{5,4},{6,5},{7,6},{8,11},{9,8},{10,9... | collective-permute-start | bytes 786440 | tf_op jit(solution)/shard_map/ppermute | solution.py:24
  476.5 2.2 copy-start.3
  476.5 2.6 copy-start.4
  478.7 1.4 copy-start.5
  479.1 21.2 %copy-start.7 = (bf16[640,128]{1,0:T(8,128)(2,1)S(1)}, bf16[640,128]{1,0:T(8,128)(2,1)}, u32[]{:S(2)}) copy-start(bf16[640,128]{1,0:T(8,128)(2,1)} %param.6) | copy-start | bytes 491524
  500.3 0.8 copy-start.8
Sparse Core Ops, SparseCore 0:
  66.7 57.0 all-gather.7
  125.5 60.1 all-gather.9
  207.7 87.6 all-gather.13
  301.5 32.6 all-gather.15
  337.1 32.1 all-gather.11

commit v6 on v4

--- a/solution.py
+++ b/solution.py
@@ -46,10 +46,10 @@
     before_x = lax.all_gather(masked_sum(along_x, xi), "z", axis=0, tiled=True)
     mine_prefix = before_x + before_z
     other_prefix = lax.ppermute(mine_prefix, "c", SWAP)
-    joined = jnp.zeros((rows,) + block.shape[1:], block.dtype)
-    joined = lax.dynamic_update_slice_in_dim(joined, mine_prefix, ci * half, 0)
-    joined = lax.dynamic_update_slice_in_dim(joined, other_prefix, (1 - ci) * half, 0)
-    return joined + below
+    first = ci == 0
+    top = jnp.where(first, mine_prefix, other_prefix)
+    bottom = jnp.where(first, other_prefix, mine_prefix)
+    return jnp.concatenate([top, bottom], axis=0) + below
 
 
 def body(activations, targets, span_of):
@@ -64,11 +64,16 @@
     order = jnp.argsort(span_of, stable=True)
     joined_in = jnp.concatenate([activations, targets], axis=1)
     sorted_xy = jnp.take(joined_in, order, axis=0).reshape(spans, share, width + n_targets)
-    moved = lax.all_to_all(sorted_xy, TM, split_axis=0, concat_axis=0, tiled=True)
-    local_xy = moved.reshape(tok_dev, width + n_targets)
-    local_x = local_xy[:, :width]
-    col_start = lax.axis_index("feat") * block_rows
-    rows_xy = lax.all_gather(local_xy, "feat", axis=0, tiled=True)
+    fanned = jnp.broadcast_to(sorted_xy[:, None], (spans, feat_count, share, width + n_targets))
+    moved = lax.all_to_all(
+        fanned.reshape(spans * feat_count, share, width + n_targets),
+        TM + ("feat",), split_axis=0, concat_axis=0, tiled=True,
+    )
+    rows_xy = moved.reshape(spans * feat_count * share, width + n_targets)
+    fi = lax.axis_index("feat")
+    by_source = moved.reshape(spans, feat_count, share, width + n_targets)
+    local_x = lax.dynamic_index_in_dim(by_source, fi, axis=1, keepdims=False)[:, :, :width].reshape(tok_dev, width)
+    col_start = fi * block_rows
     own = lax.dynamic_slice_in_dim(rows_xy, col_start, block_rows, 1)
     moments = exclusive_prefix(lax.dot_general(own, rows_xy, contract, preferred_element_type=jnp.float32))
     gram_prefix = moments[:, :width]

time: 504 us -> 557 us (1.11)
  waiting for transfers between devices: 313 us -> 383 us
  blocking collectives: 66.5 us -> 14.2 us
  local copies, waits for them, and re-layouts: 29.2 us -> 55.9 us
  other arithmetic: 34.6 us -> 40.5 us
    all_to_all x0 -> x1, waiting for transfers between devices: none -> 172 us  [body(): lax.all_to_all(fanned.reshape(spans * feat_count, share, width + n_target...]
    all_gather x1 -> x0, waiting for transfers between devices: 104 us -> none  [body(): rows_xy = lax.all_gather(local_xy, 'feat', axis=0, tiled=True)]
    all_to_all x1 -> x0, blocking collectives: 51.2 us -> none  [body(): lax.all_to_all(sorted_xy, TM, split_axis=0, concat_axis=0, tiled=True)]
    reshape x1 -> x2, local copies, waits for them, and re-layouts: 2.26 us -> 22 us  [the longest x1 16.8 us: body(): rows_xy = moved.reshape(spans * feat_count * share, width + n_targets)]
    all_to_all x0 -> x1, starting transfers between devices: none -> 11.9 us  [body(): lax.all_to_all(fanned.reshape(spans * feat_count, share, width + n_target...]
    ppermute x12, starting transfers between devices: 17.5 us -> 8.21 us  [gather_feat(): lax.ppermute(piece, 'feat', [(i, (i + k) % n) for i in range(n)])]
  transfers between devices with their start and end apart: 18 -> 18, of which waited for: 16 -> 15; matrix products, arithmetic and copies ran while one was open for 0% -> 2% of each run, Pallas kernels for 0% -> 0%
where the time goes in v6:
time: 557 us; the launch traced here: 556 us
  waiting for transfers between devices  383 us (69%)
  local copies, waits for them, and re-layouts  55.9 us (10%)
  other arithmetic  40.5 us (7%)
  matrix products  26.2 us (5%)
  starting transfers between devices  22 us (4%)
  blocking collectives  14.2 us (3%)
  between operations  14.1 us (3%)
    all_to_all x1, waiting for transfers between devices, body(): lax.all_to_all(fanned.reshape(spans * feat_count, share, width + n_target...  172 us
    all_gather x1, waiting for transfers between devices, exclusive_prefix(): along_z = lax.all_gather(mine, 'z')  87.6 us
    ppermute x12, waiting for transfers between devices, gather_feat(): lax.ppermute(piece, 'feat', [(i, (i + k) % n) for i in range(n)])  45.8 us
    all_gather x1, waiting for transfers between devices, exclusive_prefix(): along_x = lax.all_gather(piece, 'x')  32.8 us
    all_gather x1, waiting for transfers between devices, exclusive_prefix(): before_x = lax.all_gather(masked_sum(along_x, xi), 'z', axis=0, tiled=True)  32.3 us
    reshape x1, local copies, waits for them, and re-layouts, body(): rows_xy = moved.reshape(spans * feat_count * share, width + n_targets)  16.8 us
    all_to_all x1, blocking collectives, body(): lax.all_to_all(predicted.reshape(spans, share, n_targets), TM, split_axis...  14.2 us
    dot_general x3, matrix products, body(): jnp.dot(gram_prefix, direction, precision=highest, preferred_element_type...  12.8 us
  transfers between devices with their start and end apart: 18, of which 15 were waited for; matrix products, arithmetic and copies ran while one was open for 2% of the time, Pallas kernels for 0%

profile of v6, /device:TPU:1, one launch (start us, length us, event | category | flops | bytes accessed | tf_op | source)
XLA Modules:
  0.0 555.6 jit_solution(915325174221495009)
XLA Ops:
  7.2 5.1 sort.17
  12.3 2.1 pad_maximum_fusion
  14.3 4.2 gather_fusion
  18.5 3.6 gather.10
  22.7 5.5 broadcast_in_dim.72
  28.2 11.9 %all-to-all-start = ((bf16[128,20,2176]{2,1,0:T(8,128)(2,1)}), bf16[128,20,2176]{2,1,0:T(8,128)(2,1)}, u32[]{:S(2)}, u32[]{:S(2)}) async-start(bf16[128,20,2176]{2,1,0:T(8,128)(2,1)} %bitcast.53), calls=%async_computation | async-start | bytes 26738688 | tf_op jit(solution)/shard_map/all_to_all | solution.py:68
  40.1 172.4 %all-to-all-done = bf16[128,20,2176]{2,1,0:T(8,128)(2,1)} async-done(((bf16[128,20,2176]{2,1,0:T(8,128)(2,1)}), bf16[128,20,2176]{2,1,0:T(8,128)(2,1)}, u32[]{:S(2)}, u32[]{:S(2)}) %all-to-all-start) | async-done | bytes 11141152 | tf_op jit(solution)/shard_map/all_to_all | solution.py:68
  212.5 16.8 %reshape.178 = bf16[2560,2176]{1,0:T(8,128)(2,1)} reshape(bf16[128,20,2176]{2,1,0:T(8,128)(2,1)} %all-to-all-done) | data formatting | bytes 22282240 | tf_op jit(solution)/shard_map/reshape | solution.py:72
  229.3 12.5 %fusion.6 = f32[512,2176]{1,0:T(8,128)} fusion(bf16[2560,2176]{1,0:T(8,128)(2,1)} %reshape.178, s32[]{:T(128)S(6)} %select_n.84), kind=kOutput, calls=%fused_computation.17 | convolution fusion | flops 5704253440 | bytes 18219012 | tf_op jit(solution)/shard_map/dot_general | solution.py:78
  241.9 1.0 collective-permute-start
  242.8 7.5 %collective-permute-done = f32[512,2176]{1,0:T(8,128)} collective-permute-done((f32[512,2176]{1,0:T(8,128)}, f32[512,2176]{1,0:T(8,128)}, u32[]{:S(2)}, u32[]{:S(2)}) %collective-permute-start) | collective-permute-done | bytes 4456480 | tf_op jit(solution)/shard_map/ppermute | solution.py:36
  250.3 3.9 dynamic-slice_add_fusion
  254.3 87.6 %all-gather.8.cloned.1.call-done = f32[1024,2176]{1,0:T(8,128)} async-done(((f32[256,2176]{1,0:T(8,128)}), f32[1024,2176]{1,0:T(8,128)}) %all-gather.8.cloned.1.call-update) | async-done | bytes 8912912 | tf_op jit(solution)/shard_map/all_gather | solution.py:40
  341.9 5.1 select_reduce_fusion
  348.0 32.8 %all-gather.10.cloned.1.call-done = f32[256,2176]{1,0:T(8,128)} async-done(((f32[64,2176]{1,0:T(8,128)}), f32[256,2176]{1,0:T(8,128)}) %all-gather.10.cloned.1.call-update) | async-done | bytes 2228240 | tf_op jit(solution)/shard_map/all_gather | solution.py:45
  380.8 2.7 select_reduce_fusion.1
  383.5 32.3 %all-gather.6.cloned.1.call-done = f32[256,2176]{1,0:T(8,128)} async-done(((f32[64,2176]{1,0:T(8,128)}), f32[256,2176]{1,0:T(8,128)}) %all-gather.6.cloned.1.call-update) | async-done | bytes 2228240 | tf_op jit(solution)/shard_map/all_gather | solution.py:46
  415.8 3.2 add.134
  419.9 4.2 collective-permute-done.1
  424.0 1.9 broadcast_select_fusion.2
  426.0 2.7 maximum_add_fusion
  428.7 2.0 copy-done
  430.7 2.5 collective-permute-start.4
  434.5 9.1 %collective-permute-done.4 = f32[512,128]{1,0:T(8,128)S(1)} collective-permute-done((f32[512,128]{1,0:T(8,128)S(1)}, f32[512,128]{1,0:T(8,128)S(1)}, u32[]{:S(2)}, u32[]{:S(2)}) %collective-permute-start.4) | collective-permute-done | bytes 262176 | tf_op jit(solution)/shard_map/ppermute | solution.py:24
  443.6 3.9 collective-permute-done.2
  448.3 5.2 fusion.11
  455.1 6.0 %collective-permute-done.7 = f32[512,128]{1,0:T(8,128)S(1)} collective-permute-done((f32[512,128]{1,0:T(8,128)S(1)}, f32[512,128]{1,0:T(8,128)S(1)}, u32[]{:S(2)}, u32[]{:S(2)}) %collective-permute-start.7) | collective-permute-done | bytes 262176 | tf_op jit(solution)/shard_map/ppermute | solution.py:24
  461.1 1.7 collective-permute-done.6
  462.8 6.3 %collective-permute-done.5 = f32[512,128]{1,0:T(8,128)S(1)} collective-permute-done((f32[512,128]{1,0:T(8,128)S(1)}, f32[512,128]{1,0:T(8,128)S(1)}, u32[]{:S(2)}, u32[]{:S(2)}) %collective-permute-start.5) | collective-permute-done | bytes 262176 | tf_op jit(solution)/shard_map/ppermute | solution.py:24
  469.2 1.6 gather_fusion.2
  470.8 1.7 multiply_reduce_fusion.3
  473.3 4.1 fusion.17
  478.9 6.2 %collective-permute-done.10 = f32[512,128]{1,0:T(8,128)S(1)} collective-permute-done((f32[512,128]{1,0:T(8,128)}, f32[512,128]{1,0:T(8,128)S(1)}, u32[]{:S(2)}, u32[]{:S(2)}) %collective-permute-start.10) | collective-permute-done | bytes 262176 | tf_op jit(solution)/shard_map/ppermute | solution.py:24
  485.7 7.5 %collective-permute-done.8 = f32[512,128]{1,0:T(8,128)} collective-permute-done((f32[512,128]{1,0:T(8,128)}, f32[512,128]{1,0:T(8,128)}, u32[]{:S(2)}, u32[]{:S(2)}) %collective-permute-start.8) | collective-permute-done | bytes 262176 | tf_op jit(solution)/shard_map/ppermute | solution.py:24
  493.2 2.2 pad_maximum_fusion.3
  495.4 2.8 gather_fusion.3
  498.2 1.6 multiply_reduce_fusion.1
  499.8 1.4 multiply_reduce_fusion
  502.4 3.4 fusion.23
  507.3 2.2 dynamic-slice_bitcast_fusion
  509.5 2.1 slice.22
  511.6 5.2 reshape.177
  516.8 4.6 collective-permute-done.11
  521.4 2.1 pad_maximum_fusion.4
  523.6 2.8 gather_fusion.4
  526.4 1.8 fusion.29
  529.7 14.2 %all_to_all.10 = bf16[32,20,128]{2,1,0:T(8,128)(2,1)S(1)} all-to-all(bf16[32,20,128]{2,1,0:T(8,128)(2,1)S(1)} %reshape.181), channel_id=1, replica_groups=mesh['x'=4,'z'=4,'c'=2,'feat'=4] {'x','z','c'}, dimensions={0} | all-to-all | bytes 327680 | tf_op jit(solution)/shard_map/all_to_all | solution.py:104
  544.0 4.3 scatter_custom_fusion
  (72 shorter events, 13.8 us)
Async XLA Ops:
  28.2 184.3 %all-to-all-start = ((bf16[128,20,2176]{2,1,0:T(8,128)(2,1)}), bf16[128,20,2176]{2,1,0:T(8,128)(2,1)}, u32[]{:S(2)}, u32[]{:S(2)}) async-start(bf16[128,20,2176]{2,1,0:T(8,128)(2,1)} %bitcast.53), calls=%async_computation | async-start | bytes 26738688 | tf_op jit(solution)/shard_map/all_to_all | solution.py:68
  40.1 301.8 %all-gather.8.cloned.1.call-start = ((), (), s32[]{:S(2)}) async-start(), calls=%async_computation.3 | async-start | bytes 11141120 | tf_op jit(solution)/shard_map/all_gather | solution.py:40
  241.9 8.5 %collective-permute-start = (f32[512,2176]{1,0:T(8,128)}, f32[512,2176]{1,0:T(8,128)}, u32[]{:S(2)}, u32[]{:S(2)}) collective-permute-start(f32[512,2176]{1,0:T(8,128)} %fusion.6), channel_id=1, source_target_pairs={{0,4},{4,0},{1,5},{5,1},{2,6},{6,2},{3,7},{7,3},{8,12},{12,8},{9,1... | collective-permute-start | bytes 13369352 | tf_op jit(solution)/shard_map/ppermute | solution.py:36
  254.2 126.6 %all-gather.10.cloned.1.call-start = ((), (), s32[]{:S(2)}) async-start(), calls=%async_computation.4 | async-start | bytes 2785280 | tf_op jit(solution)/shard_map/all_gather | solution.py:45
  347.9 67.9 %all-gather.6.cloned.1.call-start = ((), (), s32[]{:S(2)}) async-start(), calls=%async_computation.2 | async-start | bytes 2785280 | tf_op jit(solution)/shard_map/all_gather | solution.py:46
  419.0 5.0 collective-permute-start.1
  428.7 2.0 copy-start
  430.7 12.9 %collective-permute-start.4 = (f32[512,128]{1,0:T(8,128)S(1)}, f32[512,128]{1,0:T(8,128)S(1)}, u32[]{:S(2)}, u32[]{:S(2)}) collective-permute-start(f32[512,128]{1,0:T(8,128)S(1)} %get-tuple-element.15), channel_id=1, source_target_pairs={{0,3},{1,0},{2,1},{3,2},{4,7},{5,4},{6,5},{7,6},{8,11},{9,8},{10,9... | collective-permute-start | bytes 786440 | tf_op jit(solution)/shard_map/ppermute | solution.py:24
  433.3 10.3 %collective-permute-start.3 = (f32[512,128]{1,0:T(8,128)S(1)}, f32[512,128]{1,0:T(8,128)S(1)}, u32[]{:S(2)}, u32[]{:S(2)}) collective-permute-start(f32[512,128]{1,0:T(8,128)S(1)} %get-tuple-element.15), channel_id=1, source_target_pairs={{0,2},{1,3},{2,0},{3,1},{4,6},{5,7},{6,4},{7,5},{8,10},{9,11},{10,... | collective-permute-start | bytes 786440 | tf_op jit(solution)/shard_map/ppermute | solution.py:24
  433.8 13.7 %collective-permute-start.2 = (f32[512,128]{1,0:T(8,128)S(1)}, f32[512,128]{1,0:T(8,128)S(1)}, u32[]{:S(2)}, u32[]{:S(2)}) collective-permute-start(f32[512,128]{1,0:T(8,128)S(1)} %get-tuple-element.15), channel_id=1, source_target_pairs={{0,1},{1,2},{2,3},{3,0},{4,5},{5,6},{6,7},{7,4},{8,9},{9,10},{10,1... | collective-permute-start | bytes 786440 | tf_op jit(solution)/shard_map/ppermute | solution.py:24
  453.6 7.5 %collective-permute-start.7 = (f32[512,128]{1,0:T(8,128)S(1)}, f32[512,128]{1,0:T(8,128)S(1)}, u32[]{:S(2)}, u32[]{:S(2)}) collective-permute-start(f32[512,128]{1,0:T(8,128)S(1)} %fusion.11), channel_id=1, source_target_pairs={{0,3},{1,0},{2,1},{3,2},{4,7},{5,4},{6,5},{7,6},{8,11},{9,8},{10,9... | collective-permute-start | bytes 786440 | tf_op jit(solution)/shard_map/ppermute | solution.py:24
  453.8 9.0 %collective-permute-start.6 = (f32[512,128]{1,0:T(8,128)S(1)}, f32[512,128]{1,0:T(8,128)S(1)}, u32[]{:S(2)}, u32[]{:S(2)}) collective-permute-start(f32[512,128]{1,0:T(8,128)S(1)} %fusion.11), channel_id=1, source_target_pairs={{0,2},{1,3},{2,0},{3,1},{4,6},{5,7},{6,4},{7,5},{8,10},{9,11},{10,... | collective-permute-start | bytes 786440 | tf_op jit(solution)/shard_map/ppermute | solution.py:24
  454.3 14.8 %collective-permute-start.5 = (f32[512,128]{1,0:T(8,128)S(1)}, f32[512,128]{1,0:T(8,128)S(1)}, u32[]{:S(2)}, u32[]{:S(2)}) collective-permute-start(f32[512,128]{1,0:T(8,128)S(1)} %fusion.11), channel_id=1, source_target_pairs={{0,1},{1,2},{2,3},{3,0},{4,5},{5,6},{6,7},{7,4},{8,9},{9,10},{10,1... | collective-permute-start | bytes 786440 | tf_op jit(solution)/shard_map/ppermute | solution.py:24
  469.1 4.0 slice-start
  470.8 2.5 slice-start.1
  477.5 7.7 %collective-permute-start.10 = (f32[512,128]{1,0:T(8,128)}, f32[512,128]{1,0:T(8,128)S(1)}, u32[]{:S(2)}, u32[]{:S(2)}) collective-permute-start(f32[512,128]{1,0:T(8,128)} %fusion.17), channel_id=1, source_target_pairs={{0,3},{1,0},{2,1},{3,2},{4,7},{5,4},{6,5},{7,6},{8,11},{9,8},{10,9... | collective-permute-start | bytes 786440 | tf_op jit(solution)/shard_map/ppermute | solution.py:24
  477.5 8.2 %collective-permute-start.9 = (f32[512,128]{1,0:T(8,128)}, f32[512,128]{1,0:T(8,128)}, u32[]{:S(2)}, u32[]{:S(2)}) collective-permute-start(f32[512,128]{1,0:T(8,128)} %fusion.17), channel_id=1, source_target_pairs={{0,2},{1,3},{2,0},{3,1},{4,6},{5,7},{6,4},{7,5},{8,10},{9,11},{10,... | collective-permute-start | bytes 786440 | tf_op jit(solution)/shard_map/ppermute | solution.py:24
  478.0 15.1 %collective-permute-start.8 = (f32[512,128]{1,0:T(8,128)}, f32[512,128]{1,0:T(8,128)}, u32[]{:S(2)}, u32[]{:S(2)}) collective-permute-start(f32[512,128]{1,0:T(8,128)} %fusion.17), channel_id=1, source_target_pairs={{0,1},{1,2},{2,3},{3,0},{4,5},{5,6},{6,7},{7,4},{8,9},{9,10},{10,1... | collective-permute-start | bytes 786440 | tf_op jit(solution)/shard_map/ppermute | solution.py:24
  499.8 2.6 slice-start.2
  499.8 2.6 slice-start.3
  505.8 11.0 %collective-permute-start.13 = (f32[512,128]{1,0:T(8,128)S(1)}, f32[512,128]{1,0:T(8,128)}, u32[]{:S(2)}, u32[]{:S(2)}) collective-permute-start(f32[512,128]{1,0:T(8,128)S(1)} %fusion.23), channel_id=1, source_target_pairs={{0,3},{1,0},{2,1},{3,2},{4,7},{5,4},{6,5},{7,6},{8,11},{9,8},{10,9... | collective-permute-start | bytes 786440 | tf_op jit(solution)/shard_map/ppermute | solution.py:24
  505.9 10.9 %collective-permute-start.12 = (f32[512,128]{1,0:T(8,128)S(1)}, f32[512,128]{1,0:T(8,128)}, u32[]{:S(2)}, u32[]{:S(2)}) collective-permute-start(f32[512,128]{1,0:T(8,128)S(1)} %fusion.23), channel_id=1, source_target_pairs={{0,2},{1,3},{2,0},{3,1},{4,6},{5,7},{6,4},{7,5},{8,10},{9,11},{10,... | collective-permute-start | bytes 786440 | tf_op jit(solution)/shard_map/ppermute | solution.py:24
  506.5 14.9 %collective-permute-start.11 = (f32[512,128]{1,0:T(8,128)S(1)}, f32[512,128]{1,0:T(8,128)}, u32[]{:S(2)}, u32[]{:S(2)}) collective-permute-start(f32[512,128]{1,0:T(8,128)S(1)} %fusion.23), channel_id=1, source_target_pairs={{0,1},{1,2},{2,3},{3,0},{4,5},{5,6},{6,7},{7,4},{8,9},{9,10},{10,1... | collective-permute-start | bytes 786440 | tf_op jit(solution)/shard_map/ppermute | solution.py:24
  516.8 9.6 %copy-start.1 = (f32[4,512,128]{2,1,0:T(8,128)S(1)}, f32[4,512,128]{2,1,0:T(8,128)}, u32[]{:S(2)}) copy-start(f32[4,512,128]{2,1,0:T(8,128)} %get-tuple-element.10) | copy-start | bytes 3145732
  526.4 2.4 copy-start.2
  528.8 19.4 %copy-start.3 = (bf16[640,128]{1,0:T(8,128)(2,1)S(1)}, bf16[640,128]{1,0:T(8,128)(2,1)}, u32[]{:S(2)}) copy-start(bf16[640,128]{1,0:T(8,128)(2,1)} %param.6) | copy-start | bytes 491524
  548.3 0.8 copy-start.4
Sparse Core Ops, SparseCore 0:
  254.4 87.5 all-gather.7
  348.1 32.6 all-gather.9
  383.7 32.1 all-gather.5

commit v7 on v4

--- a/solution.py
+++ b/solution.py
@@ -46,10 +46,10 @@
     before_x = lax.all_gather(masked_sum(along_x, xi), "z", axis=0, tiled=True)
     mine_prefix = before_x + before_z
     other_prefix = lax.ppermute(mine_prefix, "c", SWAP)
-    joined = jnp.zeros((rows,) + block.shape[1:], block.dtype)
-    joined = lax.dynamic_update_slice_in_dim(joined, mine_prefix, ci * half, 0)
-    joined = lax.dynamic_update_slice_in_dim(joined, other_prefix, (1 - ci) * half, 0)
-    return joined + below
+    first = ci == 0
+    top = jnp.where(first, mine_prefix, other_prefix)
+    bottom = jnp.where(first, other_prefix, mine_prefix)
+    return jnp.concatenate([top, bottom], axis=0) + below
 
 
 def body(activations, targets, span_of):
@@ -78,22 +78,26 @@
     scale = 1.0 / jnp.maximum(seen, 1.0)
     rhs = scale * cross_prefix
 
-    residual = rhs
-    direction = rhs
-    norm_now = jnp.sum(residual * residual, axis=0)
-    solution = None
+    chains = 2
+    step_cols = n_targets // chains
+    residual = [rhs[:, k * step_cols:(k + 1) * step_cols] for k in range(chains)]
+    direction = list(residual)
+    norm_now = [jnp.sum(r * r, axis=0) for r in residual]
+    solution = [None] * chains
     for step in range(ITERS):
-        product = jnp.dot(gram_prefix, direction, precision=highest, preferred_element_type=jnp.float32)
-        own_dir = lax.dynamic_slice_in_dim(direction, col_start, block_rows, 0)
-        image = gather_feat(scale * product + RIDGE * own_dir)
-        alpha = norm_now / (jnp.sum(direction * image, axis=0) + TINY)
-        update = alpha * direction
-        solution = update if solution is None else solution + update
-        if step + 1 < ITERS:
-            residual = residual - alpha * image
-            norm_next = jnp.sum(residual * residual, axis=0)
-            direction = residual + norm_next / (norm_now + TINY) * direction
-            norm_now = norm_next
+        for k in range(chains):
+            product = jnp.dot(gram_prefix, direction[k], precision=lax.Precision.HIGH, preferred_element_type=jnp.float32)
+            own_dir = lax.dynamic_slice_in_dim(direction[k], col_start, block_rows, 0)
+            image = gather_feat(scale * product + RIDGE * own_dir)
+            alpha = norm_now[k] / (jnp.sum(direction[k] * image, axis=0) + TINY)
+            update = alpha * direction[k]
+            solution[k] = update if solution[k] is None else solution[k] + update
+            if step + 1 < ITERS:
+                residual[k] = residual[k] - alpha * image
+                norm_next = jnp.sum(residual[k] * residual[k], axis=0)
+                direction[k] = residual[k] + norm_next / (norm_now[k] + TINY) * direction[k]
+                norm_now[k] = norm_next
+    solution = jnp.concatenate(solution, axis=1)
     weights = solution.astype(jnp.bfloat16)
     predicted = jnp.dot(local_x, weights, preferred_element_type=jnp.float32).astype(jnp.bfloat16)
     returned = lax.all_to_all(

time: 504 us -> 510 us (1.012)
  waiting for transfers between devices: 313 us -> 299 us
  starting transfers between devices: 19.4 us -> 29.7 us
  matrix products: 27.4 us -> 34.4 us
  blocking collectives: 66.5 us -> 71.7 us
    ppermute x12 -> x21, waiting for transfers between devices: 43.8 us -> 30.1 us  [gather_feat(): lax.ppermute(piece, 'feat', [(i, (i + k) % n) for i in range(n)])]
    ppermute x12 -> x21, starting transfers between devices: 17.5 us -> 27.9 us  [gather_feat(): lax.ppermute(piece, 'feat', [(i, (i + k) % n) for i in range(n)])]
    dot_general x3 -> x6, matrix products: 12.5 us -> 21.1 us  [body(): jnp.dot(gram_prefix, direction[k], precision=lax.Precision.HIGH, preferre...]
    all_to_all x1, blocking collectives: 15.3 us -> 20.5 us  [body(): lax.all_to_all(predicted.reshape(spans, share, n_targets), TM, split_axis...]
  transfers between devices with their start and end apart: 18 -> 27, of which waited for: 16 -> 21; matrix products, arithmetic and copies ran while one was open for 0% -> 1% of each run, Pallas kernels for 0% -> 0%
where the time goes in v7:
time: 510 us; the launch traced here: 509 us
  waiting for transfers between devices  299 us (59%)
  blocking collectives  71.7 us (14%)
  matrix products  34.4 us (7%)
  other arithmetic  33.9 us (7%)
  starting transfers between devices  29.7 us (6%)
  local copies, waits for them, and re-layouts  26.5 us (5%)
  between operations  14.3 us (3%)
    all_gather x1, waiting for transfers between devices, body(): rows_xy = lax.all_gather(local_xy, 'feat', axis=0, tiled=True)  104 us
    all_gather x1, waiting for transfers between devices, exclusive_prefix(): along_z = lax.all_gather(mine, 'z')  88.2 us
    all_to_all x1, blocking collectives, body(): lax.all_to_all(sorted_xy, TM, split_axis=0, concat_axis=0, tiled=True)  51.2 us
    all_gather x1, waiting for transfers between devices, exclusive_prefix(): along_x = lax.all_gather(piece, 'x')  32.8 us
    all_gather x1, waiting for transfers between devices, exclusive_prefix(): before_x = lax.all_gather(masked_sum(along_x, xi), 'z', axis=0, tiled=True)  32.3 us
    ppermute x21, waiting for transfers between devices, gather_feat(): lax.ppermute(piece, 'feat', [(i, (i + k) % n) for i in range(n)])  30.1 us
    ppermute x21, starting transfers between devices, gather_feat(): lax.ppermute(piece, 'feat', [(i, (i + k) % n) for i in range(n)])  27.9 us
    dot_general x6, matrix products, body(): jnp.dot(gram_prefix, direction[k], precision=lax.Precision.HIGH, preferre...  21.1 us
  transfers between devices with their start and end apart: 27, of which 21 were waited for; matrix products, arithmetic and copies ran while one was open for 1% of the time, Pallas kernels for 0%

profile of v7, /device:TPU:1, one launch (start us, length us, event | category | flops | bytes accessed | tf_op | source)
XLA Modules:
  0.0 509.4 jit_solution(550474690311861463)
XLA Ops:
  7.2 5.1 sort.17
  12.3 2.1 pad_maximum_fusion
  14.4 4.2 gather_fusion
  18.6 3.6 gather.16
  22.7 51.2 %all_to_all.10 = bf16[32,20,2176]{2,1,0:T(8,128)(2,1)S(1)} all-to-all(bf16[32,20,2176]{2,1,0:T(8,128)(2,1)S(1)} %broadcast_select_fusion), channel_id=1, replica_groups=mesh['x'=4,'z'=4,'c'=2,'feat'=4] {'x','z','c'}, dimensions={0} | all-to-all | bytes 5570560 | tf_op jit(solution)/shard_map/all_to_all | solution.py:67
  73.9 2.3 reshape.175
  76.3 103.8 %all-gather.7.cloned.1.call-done = bf16[2560,2176]{1,0:T(8,128)(2,1)} async-done(((bf16[640,2176]{1,0:T(8,128)(2,1)}), bf16[2560,2176]{1,0:T(8,128)(2,1)}) %all-gather.7.cloned.1.call-update) | async-done | bytes 11141136 | tf_op jit(solution)/shard_map/all_gather | solution.py:71
  180.1 12.5 %fusion.14 = f32[512,2176]{1,0:T(8,128)} fusion(bf16[2560,2176]{1,0:T(8,128)(2,1)} %all-gather.7.cloned.1.call-done, s32[]{:T(128)S(6)} %select_n.118), kind=kOutput, calls=%fused_computation.27 | convolution fusion | flops 5704253440 | bytes 18219012 | tf_op jit(solution)/shard_map/dot_general | solution.py:73
  193.4 7.5 %collective-permute-done = f32[512,2176]{1,0:T(8,128)} collective-permute-done((f32[512,2176]{1,0:T(8,128)}, f32[512,2176]{1,0:T(8,128)}, u32[]{:S(2)}, u32[]{:S(2)}) %collective-permute-start) | collective-permute-done | bytes 4456480 | tf_op jit(solution)/shard_map/ppermute | solution.py:36
  200.9 3.9 dynamic-slice_add_fusion
  204.9 88.2 %all-gather.11.cloned.1.call-done = f32[1024,2176]{1,0:T(8,128)} async-done(((f32[256,2176]{1,0:T(8,128)}), f32[1024,2176]{1,0:T(8,128)}) %all-gather.11.cloned.1.call-update) | async-done | bytes 8912912 | tf_op jit(solution)/shard_map/all_gather | solution.py:40
  293.2 5.1 %select_reduce_fusion = (f32[256,2176]{1,0:T(8,128)S(1)}, f32[256,2176]{1,0:T(8,128)S(1)}) fusion(f32[4,256,2176]{2,1,0:T(8,128)} %bitcast.66, pred[4]{0:T(512)(128)(4,1)S(1)} %iota_compare_fusion), kind=kLoop, calls=%fused_computation.9 | loop fusion | flops 5570560 | bytes 13369348 | tf_op jit(solution)/shard_map/reduce_sum | solution.py:18
  299.2 32.8 %all-gather.13.cloned.1.call-done = f32[256,2176]{1,0:T(8,128)} async-done(((f32[64,2176]{1,0:T(8,128)}), f32[256,2176]{1,0:T(8,128)}) %all-gather.13.cloned.1.call-update) | async-done | bytes 2228240 | tf_op jit(solution)/shard_map/all_gather | solution.py:45
  332.0 2.7 select_reduce_fusion.1
  334.8 32.3 %all-gather.9.cloned.1.call-done = f32[256,2176]{1,0:T(8,128)} async-done(((f32[64,2176]{1,0:T(8,128)}), f32[256,2176]{1,0:T(8,128)}) %all-gather.9.cloned.1.call-update) | async-done | bytes 2228240 | tf_op jit(solution)/shard_map/all_gather | solution.py:46
  367.1 3.2 add.211
  371.2 4.1 collective-permute-done.1
  375.3 1.9 broadcast_select_fusion.2
  377.2 2.7 maximum_add_fusion
  380.0 2.0 copy-done
  383.3 2.4 collective-permute-start.3
  387.0 3.7 collective-permute-done.2
  390.7 5.8 %collective-permute-done.3 = f32[512,128]{1,0:T(8,128)S(1)} collective-permute-done((f32[512,128]{1,0:T(8,128)S(1)}, f32[512,128]{1,0:T(8,128)S(1)}, u32[]{:S(2)}, u32[]{:S(2)}) %collective-permute-start.3) | collective-permute-done | bytes 262176 | tf_op jit(solution)/shard_map/ppermute | solution.py:24
  397.7 4.4 fusion.40
  402.1 1.7 collective-permute-start.14
  403.8 2.0 collective-permute-start.15
  406.9 2.0 fusion.22
  409.4 2.5 collective-permute-start.7
  412.5 2.7 collective-permute-done.6
  415.2 2.0 collective-permute-done.7
  419.2 1.3 slice-done.3
  420.6 2.0 fusion.28
  423.9 2.3 collective-permute-start.9
  427.7 4.0 collective-permute-done.9
  431.7 1.4 gather_fusion.3
  435.0 4.2 fusion.34
  440.8 1.8 collective-permute-start.13
  442.6 3.6 collective-permute-done.11
  446.6 1.4 gather_fusion.4
  449.6 4.2 fusion.46
  454.3 3.2 collective-permute-start.18
  457.5 1.4 collective-permute-done.17
  458.9 2.3 collective-permute-done.18
  462.7 4.2 fusion.52
  467.6 2.6 collective-permute-start.21
  472.0 1.9 collective-permute-done.21
  477.3 20.5 %all_to_all.11 = bf16[32,20,128]{2,1,0:T(8,128)(2,1)S(1)} all-to-all(bf16[32,20,128]{2,1,0:T(8,128)(2,1)S(1)} %reshape.182), channel_id=1, replica_groups=mesh['x'=4,'z'=4,'c'=2,'feat'=4] {'x','z','c'}, dimensions={0} | all-to-all | bytes 327680 | tf_op jit(solution)/shard_map/all_to_all | solution.py:103
  497.8 4.3 scatter_custom_fusion
  (121 shorter events, 28.0 us)
Async XLA Ops:
  7.2 172.9 %all-gather.7.cloned.1.call-start = ((), (), s32[]{:S(2)}) async-start(), calls=%async_computation.2 | async-start | bytes 13926400 | tf_op jit(solution)/shard_map/all_gather | solution.py:71
  76.3 216.9 %all-gather.11.cloned.1.call-start = ((), (), s32[]{:S(2)}) async-start(), calls=%async_computation.4 | async-start | bytes 11141120 | tf_op jit(solution)/shard_map/all_gather | solution.py:40
  192.6 8.3 %collective-permute-start = (f32[512,2176]{1,0:T(8,128)}, f32[512,2176]{1,0:T(8,128)}, u32[]{:S(2)}, u32[]{:S(2)}) collective-permute-start(f32[512,2176]{1,0:T(8,128)} %fusion.14), channel_id=1, source_target_pairs={{0,4},{4,0},{1,5},{5,1},{2,6},{6,2},{3,7},{7,3},{8,12},{12,8},{9,1... | collective-permute-start | bytes 13369352 | tf_op jit(solution)/shard_map/ppermute | solution.py:36
  204.9 127.2 %all-gather.13.cloned.1.call-start = ((), (), s32[]{:S(2)}) async-start(), calls=%async_computation.5 | async-start | bytes 2785280 | tf_op jit(solution)/shard_map/all_gather | solution.py:45
  299.2 67.9 %all-gather.9.cloned.1.call-start = ((), (), s32[]{:S(2)}) async-start(), calls=%async_computation.3 | async-start | bytes 2785280 | tf_op jit(solution)/shard_map/all_gather | solution.py:46
  370.3 5.0 collective-permute-start.1
  379.9 2.0 copy-start
  382.0 8.6 %collective-permute-start.2 = (f32[512,128]{1,0:T(8,128)S(1)}, f32[512,128]{1,0:T(8,128)S(1)}, u32[]{:S(2)}, u32[]{:S(2)}) collective-permute-start(f32[512,128]{1,0:T(8,128)S(1)} %get-tuple-element.16), channel_id=1, source_target_pairs={{0,1},{1,2},{2,3},{3,0},{4,5},{5,6},{6,7},{7,4},{8,9},{9,10},{10,1... | collective-permute-start | bytes 786440 | tf_op jit(solution)/shard_map/ppermute | solution.py:24
  383.3 13.2 %collective-permute-start.3 = (f32[512,128]{1,0:T(8,128)S(1)}, f32[512,128]{1,0:T(8,128)S(1)}, u32[]{:S(2)}, u32[]{:S(2)}) collective-permute-start(f32[512,128]{1,0:T(8,128)S(1)} %get-tuple-element.16), channel_id=1, source_target_pairs={{0,2},{1,3},{2,0},{3,1},{4,6},{5,7},{6,4},{7,5},{8,10},{9,11},{10,... | collective-permute-start | bytes 786440 | tf_op jit(solution)/shard_map/ppermute | solution.py:24
  385.7 10.8 %collective-permute-start.4 = (f32[512,128]{1,0:T(8,128)S(1)}, f32[512,128]{1,0:T(8,128)S(1)}, u32[]{:S(2)}, u32[]{:S(2)}) collective-permute-start(f32[512,128]{1,0:T(8,128)S(1)} %get-tuple-element.16), channel_id=1, source_target_pairs={{0,3},{1,0},{2,1},{3,2},{4,7},{5,4},{6,5},{7,6},{8,11},{9,8},{10,9... | collective-permute-start | bytes 786440 | tf_op jit(solution)/shard_map/ppermute | solution.py:24
  396.5 10.4 %slice-start = ((s8[4456448]{0:T(1024)(128)(4,1)}), s8[262144]{0:T(1024)(128)(4,1)S(1)}, s32[]{:S(2)}) async-start(s8[4456448]{0:T(1024)(128)(4,1)} %bitcast.62), calls=%async_computation.6 | async-start | bytes 524288
  397.5 9.4 %slice-start.1 = ((s8[4456448]{0:T(1024)(128)(4,1)}), s8[4194304]{0:T(1024)(128)(4,1)S(1)}, s32[]{:S(2)}) async-start(s8[4456448]{0:T(1024)(128)(4,1)} %bitcast.62), calls=%async_computation.7 | async-start | bytes 8388608
  402.1 9.7 %collective-permute-start.14 = (f32[512,64]{0,1:T(8,128)S(1)}, f32[512,64]{0,1:T(8,128)S(1)}, u32[]{:S(2)}, u32[]{:S(2)}) collective-permute-start(f32[512,64]{0,1:T(8,128)S(1)} %fusion.40), channel_id=1, source_target_pairs={{0,1},{1,2},{2,3},{3,0},{4,5},{5,6},{6,7},{7,4},{8,9},{9,10},{10,1... | collective-permute-start | bytes 393224 | tf_op jit(solution)/shard_map/ppermute | solution.py:24
  403.8 8.0 %collective-permute-start.15 = (f32[512,64]{0,1:T(8,128)S(1)}, f32[512,64]{0,1:T(8,128)S(1)}, u32[]{:S(2)}, u32[]{:S(2)}) collective-permute-start(f32[512,64]{0,1:T(8,128)S(1)} %fusion.40), channel_id=1, source_target_pairs={{0,2},{1,3},{2,0},{3,1},{4,6},{5,7},{6,4},{7,5},{8,10},{9,11},{10,... | collective-permute-start | bytes 393224 | tf_op jit(solution)/shard_map/ppermute | solution.py:24
  405.9 6.0 %collective-permute-start.16 = (f32[512,64]{0,1:T(8,128)S(1)}, f32[512,64]{0,1:T(8,128)S(1)}, u32[]{:S(2)}, u32[]{:S(2)}) collective-permute-start(f32[512,64]{0,1:T(8,128)S(1)} %fusion.40), channel_id=1, source_target_pairs={{0,3},{1,0},{2,1},{3,2},{4,7},{5,4},{6,5},{7,6},{8,11},{9,8},{10,9... | collective-permute-start | bytes 393224 | tf_op jit(solution)/shard_map/ppermute | solution.py:24
  409.0 6.2 %collective-permute-start.6 = (f32[512,64]{0,1:T(8,128)S(1)}, f32[512,64]{0,1:T(8,128)S(1)}, u32[]{:S(2)}, u32[]{:S(2)}) collective-permute-start(f32[512,64]{0,1:T(8,128)S(1)} %fusion.22), channel_id=1, source_target_pairs={{0,2},{1,3},{2,0},{3,1},{4,6},{5,7},{6,4},{7,5},{8,10},{9,11},{10,... | collective-permute-start | bytes 393224 | tf_op jit(solution)/shard_map/ppermute | solution.py:24
  409.4 7.8 %collective-permute-start.7 = (f32[512,64]{0,1:T(8,128)S(1)}, f32[512,64]{0,1:T(8,128)S(1)}, u32[]{:S(2)}, u32[]{:S(2)}) collective-permute-start(f32[512,64]{0,1:T(8,128)S(1)} %fusion.22), channel_id=1, source_target_pairs={{0,3},{1,0},{2,1},{3,2},{4,7},{5,4},{6,5},{7,6},{8,11},{9,8},{10,9... | collective-permute-start | bytes 393224 | tf_op jit(solution)/shard_map/ppermute | solution.py:24
  411.9 5.6 %collective-permute-start.5 = (f32[512,64]{0,1:T(8,128)S(1)}, f32[512,64]{0,1:T(8,128)S(1)}, u32[]{:S(2)}, u32[]{:S(2)}) collective-permute-start(f32[512,64]{0,1:T(8,128)S(1)} %fusion.22), channel_id=1, source_target_pairs={{0,1},{1,2},{2,3},{3,0},{4,5},{5,6},{6,7},{7,4},{8,9},{9,10},{10,1... | collective-permute-start | bytes 393224 | tf_op jit(solution)/shard_map/ppermute | solution.py:24
  417.5 1.7 slice-start.2
  418.4 2.2 slice-start.3
  422.6 5.1 %collective-permute-start.8 = (f32[512,64]{0,1:T(8,128)S(1)}, f32[512,64]{0,1:T(8,128)S(1)}, u32[]{:S(2)}, u32[]{:S(2)}) collective-permute-start(f32[512,64]{0,1:T(8,128)S(1)} %fusion.28), channel_id=1, source_target_pairs={{0,1},{1,2},{2,3},{3,0},{4,5},{5,6},{6,7},{7,4},{8,9},{9,10},{10,1... | collective-permute-start | bytes 393224 | tf_op jit(solution)/shard_map/ppermute | solution.py:24
  423.9 7.8 %collective-permute-start.9 = (f32[512,64]{0,1:T(8,128)S(1)}, f32[512,64]{0,1:T(8,128)S(1)}, u32[]{:S(2)}, u32[]{:S(2)}) collective-permute-start(f32[512,64]{0,1:T(8,128)S(1)} %fusion.28), channel_id=1, source_target_pairs={{0,2},{1,3},{2,0},{3,1},{4,6},{5,7},{6,4},{7,5},{8,10},{9,11},{10,... | collective-permute-start | bytes 393224 | tf_op jit(solution)/shard_map/ppermute | solution.py:24
  426.2 5.5 %collective-permute-start.10 = (f32[512,64]{0,1:T(8,128)S(1)}, f32[512,64]{0,1:T(8,128)S(1)}, u32[]{:S(2)}, u32[]{:S(2)}) collective-permute-start(f32[512,64]{0,1:T(8,128)S(1)} %fusion.28), channel_id=1, source_target_pairs={{0,3},{1,0},{2,1},{3,2},{4,7},{5,4},{6,5},{7,6},{8,11},{9,8},{10,9... | collective-permute-start | bytes 393224 | tf_op jit(solution)/shard_map/ppermute | solution.py:24
  439.2 7.1 %collective-permute-start.11 = (f32[512,64]{0,1:T(8,128)S(1)}, f32[512,64]{0,1:T(8,128)S(1)}, u32[]{:S(2)}, u32[]{:S(2)}) collective-permute-start(f32[512,64]{0,1:T(8,128)S(1)} %fusion.34), channel_id=1, source_target_pairs={{0,1},{1,2},{2,3},{3,0},{4,5},{5,6},{6,7},{7,4},{8,9},{9,10},{10,1... | collective-permute-start | bytes 393224 | tf_op jit(solution)/shard_map/ppermute | solution.py:24
  439.5 6.7 %collective-permute-start.12 = (f32[512,64]{0,1:T(8,128)S(1)}, f32[512,64]{0,1:T(8,128)S(1)}, u32[]{:S(2)}, u32[]{:S(2)}) collective-permute-start(f32[512,64]{0,1:T(8,128)S(1)} %fusion.34), channel_id=1, source_target_pairs={{0,2},{1,3},{2,0},{3,1},{4,6},{5,7},{6,4},{7,5},{8,10},{9,11},{10,... | collective-permute-start | bytes 393224 | tf_op jit(solution)/shard_map/ppermute | solution.py:24
  440.8 5.8 %collective-permute-start.13 = (f32[512,64]{0,1:T(8,128)S(1)}, f32[512,64]{0,1:T(8,128)S(1)}, u32[]{:S(2)}, u32[]{:S(2)}) collective-permute-start(f32[512,64]{0,1:T(8,128)S(1)} %fusion.34), channel_id=1, source_target_pairs={{0,3},{1,0},{2,1},{3,2},{4,7},{5,4},{6,5},{7,6},{8,11},{9,8},{10,9... | collective-permute-start | bytes 393224 | tf_op jit(solution)/shard_map/ppermute | solution.py:24
  453.8 5.1 %collective-permute-start.17 = (f32[512,64]{0,1:T(8,128)S(1)}, f32[512,64]{0,1:T(8,128)S(1)}, u32[]{:S(2)}, u32[]{:S(2)}) collective-permute-start(f32[512,64]{0,1:T(8,128)S(1)} %fusion.46), channel_id=1, source_target_pairs={{0,1},{1,2},{2,3},{3,0},{4,5},{5,6},{6,7},{7,4},{8,9},{9,10},{10,1... | collective-permute-start | bytes 393224 | tf_op jit(solution)/shard_map/ppermute | solution.py:24
  454.3 6.9 %collective-permute-start.18 = (f32[512,64]{0,1:T(8,128)S(1)}, f32[512,64]{0,1:T(8,128)S(1)}, u32[]{:S(2)}, u32[]{:S(2)}) collective-permute-start(f32[512,64]{0,1:T(8,128)S(1)} %fusion.46), channel_id=1, source_target_pairs={{0,2},{1,3},{2,0},{3,1},{4,6},{5,7},{6,4},{7,5},{8,10},{9,11},{10,... | collective-permute-start | bytes 393224 | tf_op jit(solution)/shard_map/ppermute | solution.py:24
  457.4 3.8 collective-permute-start.19
  466.9 5.1 collective-permute-start.20
  467.6 6.3 %collective-permute-start.21 = (f32[512,64]{0,1:T(8,128)S(1)}, f32[512,64]{0,1:T(8,128)S(1)}, u32[]{:S(2)}, u32[]{:S(2)}) collective-permute-start(f32[512,64]{0,1:T(8,128)S(1)} %fusion.52), channel_id=1, source_target_pairs={{0,2},{1,3},{2,0},{3,1},{4,6},{5,7},{6,4},{7,5},{8,10},{9,11},{10,... | collective-permute-start | bytes 393224 | tf_op jit(solution)/shard_map/ppermute | solution.py:24
  470.2 3.8 collective-permute-start.22
  474.6 1.8 copy-start.1
  476.4 25.7 %copy-start.2 = (bf16[640,128]{1,0:T(8,128)(2,1)S(1)}, bf16[640,128]{1,0:T(8,128)(2,1)}, u32[]{:S(2)}) copy-start(bf16[640,128]{1,0:T(8,128)(2,1)} %param.6) | copy-start | bytes 491524
  502.1 0.8 copy-start.3
Sparse Core Ops, SparseCore 0:
  76.4 103.6 all-gather.6
  205.0 88.1 all-gather.10
  299.3 32.6 all-gather.12
  334.9 32.1 all-gather.8

commit v8 on v4

--- a/solution.py
+++ b/solution.py
@@ -46,10 +46,55 @@
     before_x = lax.all_gather(masked_sum(along_x, xi), "z", axis=0, tiled=True)
     mine_prefix = before_x + before_z
     other_prefix = lax.ppermute(mine_prefix, "c", SWAP)
-    joined = jnp.zeros((rows,) + block.shape[1:], block.dtype)
-    joined = lax.dynamic_update_slice_in_dim(joined, mine_prefix, ci * half, 0)
-    joined = lax.dynamic_update_slice_in_dim(joined, other_prefix, (1 - ci) * half, 0)
-    return joined + below
+    first = ci == 0
+    top = jnp.where(first, mine_prefix, other_prefix)
+    bottom = jnp.where(first, other_prefix, mine_prefix)
+    return jnp.concatenate([top, bottom], axis=0) + below
+
+
+def pack_unique(moments, width):
+    f = lax.axis_index("feat")
+    rows = moments.shape[0]
+    blocks = 8
+    b = width // blocks
+    far_row = f // 2
+    gram = moments[:, :width].reshape(rows, blocks, b)
+    picked = jnp.take(gram, (2 * f + jnp.arange(6)) % blocks, axis=1)
+    row0 = picked[:b]
+    row1 = picked[b:]
+    q0 = row0[:, 0:4].reshape(b, 4 * b)
+    q1 = row1[:, 1:5].reshape(b, 4 * b)
+    q4 = jnp.where(far_row == 0, row0[:, 4], row1[:, 5])
+    cross = moments[:, width:].reshape(b, -1)
+    return jnp.concatenate([q0, q1, q4, cross], axis=1)
+
+
+def unpack_unique(packed, width, n_targets):
+    n = lax.axis_size("feat")
+    f = lax.axis_index("feat")
+    blocks = 8
+    b = width // blocks
+    far_row = f // 2
+    q0 = packed[:, : 4 * b].reshape(b, 4, b)
+    q1 = packed[:, 4 * b : 8 * b].reshape(b, 4, b)
+    q4 = packed[:, 8 * b : 9 * b]
+    cross = packed[:, 9 * b :].reshape(2 * b, n_targets)
+    prev = lax.ppermute(
+        jnp.stack([q0[:, 2], q1[:, 1], q0[:, 3], q1[:, 2]]), "feat", [(i, (i + 1) % n) for i in range(n)]
+    )
+    far = lax.ppermute(jnp.stack([q1[:, 3], q4]), "feat", [(i, (i + 2) % n) for i in range(n)])
+    far_q4 = far[1].T
+    rel0 = jnp.concatenate(
+        [q0[:, 0], q0[:, 1], q0[:, 2], q0[:, 3], jnp.where(far_row == 0, q4, far_q4), far[0].T, prev[0].T, prev[1].T],
+        axis=1,
+    )
+    rel1 = jnp.concatenate(
+        [q1[:, 0], q1[:, 1], q1[:, 2], q1[:, 3], jnp.where(far_row == 1, q4, far_q4), prev[2].T, prev[3].T, q0[:, 1].T],
+        axis=1,
+    )
+    abs0 = lax.dynamic_slice_in_dim(jnp.concatenate([rel0, rel0], axis=1), ((blocks - 2 * f) % blocks) * b, width, 1)
+    abs1 = lax.dynamic_slice_in_dim(jnp.concatenate([rel1, rel1], axis=1), ((blocks - 1 - 2 * f) % blocks) * b, width, 1)
+    return jnp.concatenate([abs0, abs1], axis=0), cross
 
 
 def body(activations, targets, span_of):
@@ -70,9 +115,9 @@
     col_start = lax.axis_index("feat") * block_rows
     rows_xy = lax.all_gather(local_xy, "feat", axis=0, tiled=True)
     own = lax.dynamic_slice_in_dim(rows_xy, col_start, block_rows, 1)
-    moments = exclusive_prefix(lax.dot_general(own, rows_xy, contract, preferred_element_type=jnp.float32))
-    gram_prefix = moments[:, :width]
-    cross_prefix = gather_feat(moments[:, width:])
+    moments = lax.dot_general(own, rows_xy, contract, preferred_element_type=jnp.float32)
+    gram_prefix, cross_block = unpack_unique(exclusive_prefix(pack_unique(moments, width)), width, n_targets)
+    cross_prefix = gather_feat(cross_block)
     span = (lax.axis_index("x") * lax.axis_size("z") + lax.axis_index("z")) * lax.axis_size("c") + lax.axis_index("c")
     seen = (span * (tok_dev * feat_count)).astype(jnp.float32)
     scale = 1.0 / jnp.maximum(seen, 1.0)

time: 504 us -> 567 us (1.12); the launches traced: 504 us -> 560 us
  local copies, waits for them, and re-layouts: 29.2 us -> 80.9 us
  waiting for transfers between devices: 313 us -> 276 us
  other arithmetic: 34.6 us -> 59.7 us
  matrix products: 27.4 us -> 34.7 us
  starting transfers between devices: 19.4 us -> 26.6 us
    all_gather x1, waiting for transfers between devices: 88.2 us -> 59.4 us  [exclusive_prefix(): along_z = lax.all_gather(mine, 'z')]
    ppermute x0 -> x2, waiting for transfers between devices: none -> 26.6 us  [the longest x1 26.6 us: unpack_unique(): lax.ppermute(jnp.stack([q1[:, 3], q4]), 'feat', [(i, (i + 2) % n) for i i...]
    unnamed x28 -> x69, local copies, waits for them, and re-layouts: 3.36 us -> 26.7 us
    ppermute x12, waiting for transfers between devices: 43.8 us -> 27.3 us  [gather_feat(): lax.ppermute(piece, 'feat', [(i, (i + k) % n) for i in range(n)])]
    reduce_sum x2, other arithmetic: 7.85 us -> 20.5 us  [masked_sum(): jnp.sum(jnp.where(keep.reshape((-1,) + (1,) * (stack.ndim - 1)), stack, 0...]
    all_gather x0 -> x2, local copies, waits for them, and re-layouts: none -> 10.1 us  [the longest x1 7.26 us: exclusive_prefix(): along_z = lax.all_gather(mine, 'z')]
    dot_general x3, matrix products: 12.5 us -> 22.2 us  [body(): jnp.dot(gram_prefix, direction, precision=highest, preferred_element_type...]
    all_gather x1, waiting for transfers between devices: 32.8 us -> 25.7 us  [exclusive_prefix(): along_x = lax.all_gather(piece, 'x')]
  transfers between devices with their start and end apart: 18 -> 20, of which waited for: 16 -> 14; matrix products, arithmetic and copies ran while one was open for 0% -> 5% of each run, Pallas kernels for 0% -> 0%
where the time goes in v8:
time: 567 us; the launch traced here: 560 us
  waiting for transfers between devices  276 us (49%)
  local copies, waits for them, and re-layouts  80.9 us (14%)
  blocking collectives  67.3 us (12%)
  other arithmetic  59.7 us (11%)
  matrix products  34.7 us (6%)
  starting transfers between devices  26.6 us (5%)
  between operations  14.5 us (3%)
    all_gather x1, waiting for transfers between devices, body(): rows_xy = lax.all_gather(local_xy, 'feat', axis=0, tiled=True)  104 us
    all_gather x1, waiting for transfers between devices, exclusive_prefix(): along_z = lax.all_gather(mine, 'z')  59.4 us
    all_to_all x1, blocking collectives, body(): lax.all_to_all(sorted_xy, TM, split_axis=0, concat_axis=0, tiled=True)  51.2 us
    ppermute x12, waiting for transfers between devices, gather_feat(): lax.ppermute(piece, 'feat', [(i, (i + k) % n) for i in range(n)])  27.3 us
    unnamed x69, local copies, waits for them, and re-layouts  26.7 us
    ppermute x1, waiting for transfers between devices, unpack_unique(): lax.ppermute(jnp.stack([q1[:, 3], q4]), 'feat', [(i, (i + 2) % n) for i i...  26.6 us
    all_gather x1, waiting for transfers between devices, exclusive_prefix(): before_x = lax.all_gather(masked_sum(along_x, xi), 'z', axis=0, tiled=True)  25.7 us
    all_gather x1, waiting for transfers between devices, exclusive_prefix(): along_x = lax.all_gather(piece, 'x')  25.7 us
  transfers between devices with their start and end apart: 20, of which 14 were waited for; matrix products, arithmetic and copies ran while one was open for 5% of the time, Pallas kernels for 0%

profile of v8, /device:TPU:1, one launch (start us, length us, event | category | flops | bytes accessed | tf_op | source)
XLA Modules:
  0.0 559.9 jit_solution(761061138356884409)
XLA Ops:
  7.2 5.1 sort.17
  12.3 2.1 pad_maximum_fusion.1
  14.4 4.2 gather_fusion
  18.6 3.6 gather.14
  22.7 51.2 %all_to_all.10 = bf16[32,20,2176]{2,1,0:T(8,128)(2,1)S(1)} all-to-all(bf16[32,20,2176]{2,1,0:T(8,128)(2,1)S(1)} %broadcast_select_fusion), channel_id=1, replica_groups=mesh['x'=4,'z'=4,'c'=2,'feat'=4] {'x','z','c'}, dimensions={0} | all-to-all | bytes 5570560 | tf_op jit(solution)/shard_map/all_to_all | solution.py:112
  74.0 2.3 reshape.202
  76.4 103.7 %all-gather.7.cloned.1.call-done = bf16[2560,2176]{1,0:T(8,128)(2,1)} async-done(((bf16[640,2176]{1,0:T(8,128)(2,1)}), bf16[2560,2176]{1,0:T(8,128)(2,1)}) %all-gather.7.cloned.1.call-update) | async-done | bytes 11141136 | tf_op jit(solution)/shard_map/all_gather | solution.py:116
  180.1 10.0 %fusion.5 = f32[512,2176]{1,0:T(8,128)S(1)} fusion(bf16[2560,2176]{1,0:T(8,128)(2,1)} %all-gather.7.cloned.1.call-done, s32[]{:T(128)S(6)} %select_n.159), kind=kOutput, calls=%fused_computation.20 | convolution fusion | flops 5704253440 | bytes 18219012 | tf_op jit(solution)/shard_map/dot_general | solution.py:118
  192.2 2.5 copy.161
  194.7 2.9 gather_fusion.1
  200.0 2.7 pad_maximum_fusion.5
  203.5 4.7 collective-permute-done
  208.3 2.6 dynamic-slice_add_fusion
  211.2 59.4 %all-gather.11.cloned.1.call-done = f32[512,2560]{0,1:T(8,128)} async-done(((f32[128,2560]{0,1:T(8,128)}), f32[512,2560]{0,1:T(8,128)}) %all-gather.11.cloned.1.call-update) | async-done | bytes 5242896 | tf_op jit(solution)/shard_map/all_gather | solution.py:40
  270.6 7.3 %reshape.270 = f32[4,128,2560]{1,0,2:T(4,128)} reshape(f32[512,2560]{0,1:T(8,128)} %all-gather.11.cloned.1.call-done) | data formatting | bytes 10485760 | tf_op jit(solution)/shard_map/all_gather | solution.py:40
  277.9 18.3 %select_reduce_fusion = (f32[128,2560]{0,1:T(8,128)}, f32[128,2560]{0,1:T(8,128)S(1)}) fusion(f32[4,128,2560]{1,0,2:T(4,128)} %reshape.270, pred[4]{0:T(512)(128)(4,1)S(1)} %iota_compare_fusion), kind=kLoop, calls=%fused_computation.7 | loop fusion | flops 3276800 | bytes 7864324 | tf_op jit(solution)/shard_map/reduce_sum | solution.py:18
  297.7 2.4 copy.127
  300.2 25.7 %all-gather.13.cloned.1.call-done = f32[128,2560]{1,0:T(8,128)} async-done(((f32[32,2560]{1,0:T(8,128)}), f32[128,2560]{1,0:T(8,128)}) %all-gather.13.cloned.1.call-update) | async-done | bytes 1310736 | tf_op jit(solution)/shard_map/all_gather | solution.py:45
  325.9 2.2 select_reduce_fusion.1
  328.2 25.7 %all-gather.9.cloned.1.call-done = f32[128,2560]{1,0:T(8,128)} async-done(((f32[32,2560]{1,0:T(8,128)}), f32[128,2560]{1,0:T(8,128)}) %all-gather.9.cloned.1.call-update) | async-done | bytes 1310736 | tf_op jit(solution)/shard_map/all_gather | solution.py:46
  353.9 2.8 copy.128
  356.7 3.0 add.198
  361.4 2.9 collective-permute-done.1
  364.3 1.9 broadcast_select_fusion.2
  373.2 2.0 pad_maximum_fusion.19
  379.1 1.9 pad_maximum_fusion.23
  381.0 2.4 collective-permute-start.5
  386.7 26.6 %collective-permute-done.5 = f32[2,256,256]{2,1,0:T(8,128)} collective-permute-done((f32[2,256,256]{2,1,0:T(8,128)}, f32[2,256,256]{2,1,0:T(8,128)}, u32[]{:S(2)}, u32[]{:S(2)}) %collective-permute-start.5) | collective-permute-done | bytes 524320 | tf_op jit(solution)/shard_map/ppermute | solution.py:85
  424.4 2.4 collective-permute-start.4
  438.5 3.3 constant_dynamic-slice_fusion
  441.9 2.8 pad_maximum_fusion.18
  446.6 8.7 %fusion.12 = f32[512,128]{1,0:T(8,128)S(1)} fusion(f32[2048,128]{1,0:T(8,128)S(1)} %bitcast.157, f32[256,2048]{0,1:T(8,128)S(1)} %get-tuple-element.31, f32[256,2048]{0,1:T(8,128)} %get-tuple-element.32, s32[]{:T(128)S(6)} %select_n.184, f32[]{:T(128)S(6)} %div.53), kind=kOutput, calls=%fused_computation.29 | convolution fusion | flops 1611857920 | bytes 5767176 | tf_op jit(solution)/shard_map/dot_general | solution.py:131
  457.8 2.4 collective-permute-start.9
  460.2 2.3 collective-permute-done.7
  462.5 5.5 collective-permute-done.8
  473.3 6.8 %fusion.11 = f32[512,128]{1,0:T(8,128)S(1)} fusion(f32[2048,128]{1,0:T(8,128)S(1)} %multiply_add_fusion, f32[256,2048]{0,1:T(8,128)S(1)} %copy-done.1, f32[256,2048]{0,1:T(8,128)S(1)} %copy-done.3, s32[]{:T(128)S(6)} %select_n.184, f32[]{:T(128)S(6)} %div.53), kind=kOutput, calls=%fused_computation.28 | convolution fusion | flops 1611857920 | bytes 5767176 | tf_op jit(solution)/shard_map/dot_general | solution.py:131
  480.0 3.7 collective-permute-start.10
  486.4 2.4 collective-permute-done.10
  488.8 6.4 %collective-permute-done.11 = f32[512,128]{1,0:T(8,128)S(1)} collective-permute-done((f32[512,128]{1,0:T(8,128)S(1)}, f32[512,128]{1,0:T(8,128)S(1)}, u32[]{:S(2)}, u32[]{:S(2)}) %collective-permute-start.11) | collective-permute-done | bytes 262176 | tf_op jit(solution)/shard_map/ppermute | solution.py:24
  500.8 6.8 %fusion.10 = f32[512,128]{1,0:T(8,128)S(1)} fusion(f32[2048,128]{1,0:T(8,128)S(1)} %fusion.17, f32[256,2048]{0,1:T(8,128)S(1)} %copy-done.2, f32[256,2048]{0,1:T(8,128)S(1)} %copy-done.4, s32[]{:T(128)S(6)} %select_n.184, f32[]{:T(128)S(6)} %div.53), kind=kOutput, calls=%fused_computation.27 | convolution fusion | flops 1611857920 | bytes 5767176 | tf_op jit(solution)/shard_map/dot_general | solution.py:131
  507.6 3.5 collective-permute-start.13
  513.6 2.4 collective-permute-done.13
  516.0 7.2 %collective-permute-done.14 = f32[512,128]{1,0:T(8,128)S(1)} collective-permute-done((f32[512,128]{1,0:T(8,128)S(1)}, f32[512,128]{1,0:T(8,128)S(1)}, u32[]{:S(2)}, u32[]{:S(2)}) %collective-permute-start.14) | collective-permute-done | bytes 262176 | tf_op jit(solution)/shard_map/ppermute | solution.py:24
  524.2 2.8 gather_fusion.5
  527.1 1.9 fusion.19
  529.5 2.5 fusion.13
  532.0 16.0 %all_to_all.11 = bf16[32,20,128]{2,1,0:T(8,128)(2,1)S(1)} all-to-all(bf16[32,20,128]{2,1,0:T(8,128)(2,1)S(1)} %reshape.212), channel_id=1, replica_groups=mesh['x'=4,'z'=4,'c'=2,'feat'=4] {'x','z','c'}, dimensions={0} | all-to-all | bytes 327680 | tf_op jit(solution)/shard_map/all_to_all | solution.py:144
  548.1 4.3 scatter_custom_fusion
  (159 shorter events, 69.2 us)
Async XLA Ops:
  7.2 172.9 %all-gather.7.cloned.1.call-start = ((), (), s32[]{:S(2)}) async-start(), calls=%async_computation.2 | async-start | bytes 13926400 | tf_op jit(solution)/shard_map/all_gather | solution.py:116
  76.3 194.4 %all-gather.11.cloned.1.call-start = ((), (), s32[]{:S(2)}) async-start(), calls=%async_computation.4 | async-start | bytes 6553600 | tf_op jit(solution)/shard_map/all_gather | solution.py:40
  190.1 2.1 copy-start.13
  198.0 1.8 slice-start.1
  202.7 5.6 collective-permute-start
  211.0 114.9 %all-gather.13.cloned.1.call-start = ((), (), s32[]{:S(2)}) async-start(), calls=%async_computation.5 | async-start | bytes 1638400 | tf_op jit(solution)/shard_map/all_gather | solution.py:45
  300.1 53.8 %all-gather.9.cloned.1.call-start = ((), (), s32[]{:S(2)}) async-start(), calls=%async_computation.3 | async-start | bytes 1638400 | tf_op jit(solution)/shard_map/all_gather | solution.py:46
  359.7 4.6 collective-permute-start.1
  366.5 2.5 copy-start.9
  369.8 8.5 %slice-start = ((f32[256,2560]{0,1:T(8,128)}), f32[256,256]{0,1:T(8,128)S(1)}, s32[]{:S(2)}) async-start(f32[256,2560]{0,1:T(8,128)} %copy-done.9), calls=%async_computation.6 | async-start | bytes 524288 | tf_op jit(solution)/shard_map/slice | solution.py:80
  375.2 41.5 %collective-permute-start.6 = (f32[4,256,256]{2,1,0:T(8,128)}, f32[4,256,256]{2,1,0:T(8,128)S(1)}, u32[]{:S(2)}, u32[]{:S(2)}) collective-permute-start(f32[4,256,256]{2,1,0:T(8,128)} %pad_maximum_fusion.19), channel_id=1, source_target_pairs={{0,1},{1,2},{2,3},{3,0},{4,5},{5,6},{6,7},{7,4},{8,9},{9,10},{10,1... | collective-permute-start | bytes 3145736 | tf_op jit(solution)/shard_map/ppermute | solution.py:82
  381.0 32.4 %collective-permute-start.5 = (f32[2,256,256]{2,1,0:T(8,128)}, f32[2,256,256]{2,1,0:T(8,128)}, u32[]{:S(2)}, u32[]{:S(2)}) collective-permute-start(f32[2,256,256]{2,1,0:T(8,128)} %pad_maximum_fusion.23), channel_id=1, source_target_pairs={{0,2},{1,3},{2,0},{3,1},{4,6},{5,7},{6,4},{7,5},{8,10},{9,11},{10,... | collective-permute-start | bytes 1572872 | tf_op jit(solution)/shard_map/ppermute | solution.py:85
  385.2 35.9 %copy-start.10 = (f32[256,2560]{0,1:T(8,128)S(1)}, f32[256,2560]{0,1:T(8,128)}, u32[]{:S(2)}) copy-start(f32[256,2560]{0,1:T(8,128)} %copy-done.9) | copy-start | bytes 7864324
  423.8 18.0 %collective-permute-start.2 = (f32[512,128]{1,0:T(8,128)}, f32[512,128]{1,0:T(8,128)}, u32[]{:S(2)}, u32[]{:S(2)}) collective-permute-start(f32[512,128]{1,0:T(8,128)} %reshape.207), channel_id=1, source_target_pairs={{0,1},{1,2},{2,3},{3,0},{4,5},{5,6},{6,7},{7,4},{8,9},{9,10},{10,1... | collective-permute-start | bytes 786440 | tf_op jit(solution)/shard_map/ppermute | solution.py:24
  423.8 18.0 %collective-permute-start.3 = (f32[512,128]{1,0:T(8,128)}, f32[512,128]{1,0:T(8,128)}, u32[]{:S(2)}, u32[]{:S(2)}) collective-permute-start(f32[512,128]{1,0:T(8,128)} %reshape.207), channel_id=1, source_target_pairs={{0,2},{1,3},{2,0},{3,1},{4,6},{5,7},{6,4},{7,5},{8,10},{9,11},{10,... | collective-permute-start | bytes 786440 | tf_op jit(solution)/shard_map/ppermute | solution.py:24
  424.4 17.5 %collective-permute-start.4 = (f32[512,128]{1,0:T(8,128)}, f32[512,128]{1,0:T(8,128)}, u32[]{:S(2)}, u32[]{:S(2)}) collective-permute-start(f32[512,128]{1,0:T(8,128)} %reshape.207), channel_id=1, source_target_pairs={{0,3},{1,0},{2,1},{3,2},{4,7},{5,4},{6,5},{7,6},{8,11},{9,8},{10,9... | collective-permute-start | bytes 786440 | tf_op jit(solution)/shard_map/ppermute | solution.py:24
  427.5 7.2 %copy-start.11 = (f32[256,2560]{0,1:T(8,128)S(1)}, f32[256,2560]{0,1:T(8,128)}, u32[]{:S(2)}) copy-start(f32[256,2560]{0,1:T(8,128)} %copy-done.9) | copy-start | bytes 7864324
  431.0 7.6 %copy-start.16 = (f32[256,4096]{0,1:T(8,128)S(1)}, f32[256,4096]{0,1:T(8,128)}, u32[]{:S(2)}) copy-start(f32[256,4096]{0,1:T(8,128)} %get-tuple-element.21) | copy-start | bytes 12582916
  438.5 3.3 copy-start.17
  441.8 13.4 %copy-start = (f32[256,2048]{0,1:T(8,128)}, f32[256,2048]{0,1:T(8,128)S(1)}, u32[]{:S(2)}) copy-start(f32[256,2048]{0,1:T(8,128)S(1)} %get-tuple-element.31) | copy-start | bytes 6291460
  446.6 9.3 %copy-start.5 = (f32[4,512,128]{2,1,0:T(8,128)}, f32[4,512,128]{2,1,0:T(8,128)S(1)}, u32[]{:S(2)}) copy-start(f32[4,512,128]{2,1,0:T(8,128)S(1)} %select_multiply_fusion.1) | copy-start | bytes 3145732
  455.3 7.2 %collective-permute-start.7 = (f32[512,128]{1,0:T(8,128)S(1)}, f32[512,128]{1,0:T(8,128)S(1)}, u32[]{:S(2)}, u32[]{:S(2)}) collective-permute-start(f32[512,128]{1,0:T(8,128)S(1)} %fusion.12), channel_id=1, source_target_pairs={{0,1},{1,2},{2,3},{3,0},{4,5},{5,6},{6,7},{7,4},{8,9},{9,10},{10,1... | collective-permute-start | bytes 786440 | tf_op jit(solution)/shard_map/ppermute | solution.py:24
  456.0 12.0 %collective-permute-start.8 = (f32[512,128]{1,0:T(8,128)S(1)}, f32[512,128]{1,0:T(8,128)S(1)}, u32[]{:S(2)}, u32[]{:S(2)}) collective-permute-start(f32[512,128]{1,0:T(8,128)S(1)} %fusion.12), channel_id=1, source_target_pairs={{0,2},{1,3},{2,0},{3,1},{4,6},{5,7},{6,4},{7,5},{8,10},{9,11},{10,... | collective-permute-start | bytes 786440 | tf_op jit(solution)/shard_map/ppermute | solution.py:24
  457.8 11.2 %collective-permute-start.9 = (f32[512,128]{1,0:T(8,128)S(1)}, f32[512,128]{1,0:T(8,128)S(1)}, u32[]{:S(2)}, u32[]{:S(2)}) collective-permute-start(f32[512,128]{1,0:T(8,128)S(1)} %fusion.12), channel_id=1, source_target_pairs={{0,3},{1,0},{2,1},{3,2},{4,7},{5,4},{6,5},{7,6},{8,11},{9,8},{10,9... | collective-permute-start | bytes 786440 | tf_op jit(solution)/shard_map/ppermute | solution.py:24
  469.1 3.8 copy-start.6
  470.7 2.3 copy-start.1
  470.7 2.5 copy-start.3
  473.2 22.0 %copy-start.14 = (f32[2048,128]{1,0:T(8,128)}, f32[2048,128]{1,0:T(8,128)S(1)}, u32[]{:S(2)}) copy-start(f32[2048,128]{1,0:T(8,128)S(1)} %multiply_add_fusion) | copy-start | bytes 3145732
  480.0 8.8 %collective-permute-start.10 = (f32[512,128]{1,0:T(8,128)S(1)}, f32[512,128]{1,0:T(8,128)S(1)}, u32[]{:S(2)}, u32[]{:S(2)}) collective-permute-start(f32[512,128]{1,0:T(8,128)S(1)} %fusion.11), channel_id=1, source_target_pairs={{0,1},{1,2},{2,3},{3,0},{4,5},{5,6},{6,7},{7,4},{8,9},{9,10},{10,1... | collective-permute-start | bytes 786440 | tf_op jit(solution)/shard_map/ppermute | solution.py:24
  483.7 11.5 %collective-permute-start.11 = (f32[512,128]{1,0:T(8,128)S(1)}, f32[512,128]{1,0:T(8,128)S(1)}, u32[]{:S(2)}, u32[]{:S(2)}) collective-permute-start(f32[512,128]{1,0:T(8,128)S(1)} %fusion.11), channel_id=1, source_target_pairs={{0,2},{1,3},{2,0},{3,1},{4,6},{5,7},{6,4},{7,5},{8,10},{9,11},{10,... | collective-permute-start | bytes 786440 | tf_op jit(solution)/shard_map/ppermute | solution.py:24
  484.7 10.6 %collective-permute-start.12 = (f32[512,128]{1,0:T(8,128)S(1)}, f32[512,128]{1,0:T(8,128)S(1)}, u32[]{:S(2)}, u32[]{:S(2)}) collective-permute-start(f32[512,128]{1,0:T(8,128)S(1)} %fusion.11), channel_id=1, source_target_pairs={{0,3},{1,0},{2,1},{3,2},{4,7},{5,4},{6,5},{7,6},{8,11},{9,8},{10,9... | collective-permute-start | bytes 786440 | tf_op jit(solution)/shard_map/ppermute | solution.py:24
  496.9 2.1 copy-start.7
  498.6 1.6 copy-start.2
  498.6 2.2 copy-start.4
  500.8 6.8 %copy-start.15 = (f32[2048,128]{1,0:T(8,128)}, f32[2048,128]{1,0:T(8,128)S(1)}, u32[]{:S(2)}) copy-start(f32[2048,128]{1,0:T(8,128)S(1)} %fusion.17) | copy-start | bytes 3145732
  507.6 8.4 %collective-permute-start.13 = (f32[512,128]{1,0:T(8,128)S(1)}, f32[512,128]{1,0:T(8,128)S(1)}, u32[]{:S(2)}, u32[]{:S(2)}) collective-permute-start(f32[512,128]{1,0:T(8,128)S(1)} %fusion.10), channel_id=1, source_target_pairs={{0,1},{1,2},{2,3},{3,0},{4,5},{5,6},{6,7},{7,4},{8,9},{9,10},{10,1... | collective-permute-start | bytes 786440 | tf_op jit(solution)/shard_map/ppermute | solution.py:24
  511.1 12.1 %collective-permute-start.14 = (f32[512,128]{1,0:T(8,128)S(1)}, f32[512,128]{1,0:T(8,128)S(1)}, u32[]{:S(2)}, u32[]{:S(2)}) collective-permute-start(f32[512,128]{1,0:T(8,128)S(1)} %fusion.10), channel_id=1, source_target_pairs={{0,2},{1,3},{2,0},{3,1},{4,6},{5,7},{6,4},{7,5},{8,10},{9,11},{10,... | collective-permute-start | bytes 786440 | tf_op jit(solution)/shard_map/ppermute | solution.py:24
  512.1 11.1 %collective-permute-start.15 = (f32[512,128]{1,0:T(8,128)S(1)}, f32[512,128]{1,0:T(8,128)S(1)}, u32[]{:S(2)}, u32[]{:S(2)}) collective-permute-start(f32[512,128]{1,0:T(8,128)S(1)} %fusion.10), channel_id=1, source_target_pairs={{0,3},{1,0},{2,1},{3,2},{4,7},{5,4},{6,5},{7,6},{8,11},{9,8},{10,9... | collective-permute-start | bytes 786440 | tf_op jit(solution)/shard_map/ppermute | solution.py:24
  527.1 1.9 copy-start.8
  527.1 2.4 copy-start.12
  529.5 22.9 %copy-start.18 = (bf16[640,128]{1,0:T(8,128)(2,1)S(1)}, bf16[640,128]{1,0:T(8,128)(2,1)}, u32[]{:S(2)}) copy-start(bf16[640,128]{1,0:T(8,128)(2,1)} %param.6) | copy-start | bytes 491524
  552.4 0.8 copy-start.19
Sparse Core Ops, SparseCore 0:
  76.4 103.6 all-gather.6
  211.1 59.4 all-gather.10
  300.2 25.6 all-gather.12
  328.3 25.5 all-gather.8

commit v9 on v4

--- a/solution.py
+++ b/solution.py
@@ -46,10 +46,10 @@
     before_x = lax.all_gather(masked_sum(along_x, xi), "z", axis=0, tiled=True)
     mine_prefix = before_x + before_z
     other_prefix = lax.ppermute(mine_prefix, "c", SWAP)
-    joined = jnp.zeros((rows,) + block.shape[1:], block.dtype)
-    joined = lax.dynamic_update_slice_in_dim(joined, mine_prefix, ci * half, 0)
-    joined = lax.dynamic_update_slice_in_dim(joined, other_prefix, (1 - ci) * half, 0)
-    return joined + below
+    first = ci == 0
+    top = jnp.where(first, mine_prefix, other_prefix)
+    bottom = jnp.where(first, other_prefix, mine_prefix)
+    return jnp.concatenate([top, bottom], axis=0) + below
 
 
 def body(activations, targets, span_of):
@@ -61,9 +61,15 @@
     share = tok_dev // spans
     contract = (((0,), (0,)), ((), ()))
     highest = lax.Precision.HIGHEST
-    order = jnp.argsort(span_of, stable=True)
+    hot = (span_of[:, None] == jnp.arange(spans)[None, :]).astype(jnp.float32)
+    earlier = (jnp.arange(tok_dev)[:, None] > jnp.arange(tok_dev)[None, :]).astype(jnp.float32)
+    before = jnp.dot(earlier, hot, precision=highest, preferred_element_type=jnp.float32)
+    rank = jnp.sum(before * hot, axis=1).astype(jnp.int32)
+    dest = span_of * share + rank
+    permute = (dest[None, :] == jnp.arange(tok_dev)[:, None]).astype(jnp.bfloat16)
     joined_in = jnp.concatenate([activations, targets], axis=1)
-    sorted_xy = jnp.take(joined_in, order, axis=0).reshape(spans, share, width + n_targets)
+    sorted_xy = jnp.dot(permute, joined_in, preferred_element_type=jnp.float32).astype(jnp.bfloat16)
+    sorted_xy = sorted_xy.reshape(spans, share, width + n_targets)
     moved = lax.all_to_all(sorted_xy, TM, split_axis=0, concat_axis=0, tiled=True)
     local_xy = moved.reshape(tok_dev, width + n_targets)
     local_x = local_xy[:, :width]
@@ -83,7 +89,7 @@
     norm_now = jnp.sum(residual * residual, axis=0)
     solution = None
     for step in range(ITERS):
-        product = jnp.dot(gram_prefix, direction, precision=highest, preferred_element_type=jnp.float32)
+        product = jnp.dot(gram_prefix, direction, precision=lax.Precision.HIGH, preferred_element_type=jnp.float32)
         own_dir = lax.dynamic_slice_in_dim(direction, col_start, block_rows, 0)
         image = gather_feat(scale * product + RIDGE * own_dir)
         alpha = norm_now / (jnp.sum(direction * image, axis=0) + TINY)
@@ -100,7 +106,9 @@
         predicted.reshape(spans, share, n_targets), TM, split_axis=0, concat_axis=0, tiled=True
     )
     in_order = returned.reshape(tok_dev, n_targets)
-    predictions = jnp.zeros_like(in_order).at[order].set(in_order)
+    predictions = lax.dot_general(
+        permute, in_order, (((0,), (0,)), ((), ())), preferred_element_type=jnp.float32
+    ).astype(jnp.bfloat16)
     error = targets.astype(jnp.float32) - predictions.astype(jnp.float32)
     surprise = jnp.mean(error * error, axis=1)
     return (predictions, surprise)

time: 504 us -> 494 us (0.980)
  blocking collectives: 66.5 us -> 51.3 us
  waiting for transfers between devices: 313 us -> 322 us
  local copies, waits for them, and re-layouts: 29.2 us -> 21.3 us
  starting transfers between devices: 19.4 us -> 25.6 us
  other arithmetic: 34.6 us -> 28.9 us
    all_to_all x1 -> x0, blocking collectives: 15.3 us -> none  [body(): lax.all_to_all(predicted.reshape(spans, share, n_targets), TM, split_axis...]
    all_to_all x0 -> x1, waiting for transfers between devices: none -> 8.13 us  [body(): lax.all_to_all(predicted.reshape(spans, share, n_targets), TM, split_axis...]
    gather x2 -> x0, local copies, waits for them, and re-layouts: 7.76 us -> none  [body(): jnp.take(joined_in, order, axis=0).reshape(spans, share, width + n_targets)]
    all_to_all x0 -> x1, starting transfers between devices: none -> 6.97 us  [body(): lax.all_to_all(predicted.reshape(spans, share, n_targets), TM, split_axis...]
    sort x1 -> x0, other arithmetic: 5.06 us -> none  [body(): order = jnp.argsort(span_of, stable=True)]
    dot_general x3 -> x6, matrix products: 12.5 us -> 15.3 us  [the longest x3 8.02 us: body(): jnp.dot(gram_prefix, direction, precision=lax.Precision.HIGH, preferred_e...]
  transfers between devices with their start and end apart: 18 -> 19, of which waited for: 16 -> 17; matrix products, arithmetic and copies ran while one was open for 0% -> 0% of each run, Pallas kernels for 0% -> 0%
where the time goes in v9:
time: 494 us; the launch traced here: 493 us
  waiting for transfers between devices  322 us (65%)
  blocking collectives  51.3 us (10%)
  matrix products  30.3 us (6%)
  other arithmetic  28.9 us (6%)
  starting transfers between devices  25.6 us (5%)
  local copies, waits for them, and re-layouts  21.3 us (4%)
  between operations  14.1 us (3%)
    all_gather x1, waiting for transfers between devices, body(): rows_xy = lax.all_gather(local_xy, 'feat', axis=0, tiled=True)  104 us
    all_gather x1, waiting for transfers between devices, exclusive_prefix(): along_z = lax.all_gather(mine, 'z')  88.4 us
    all_to_all x1, blocking collectives, body(): lax.all_to_all(sorted_xy, TM, split_axis=0, concat_axis=0, tiled=True)  51.3 us
    ppermute x12, waiting for transfers between devices, gather_feat(): lax.ppermute(piece, 'feat', [(i, (i + k) % n) for i in range(n)])  44.7 us
    all_gather x1, waiting for transfers between devices, exclusive_prefix(): along_x = lax.all_gather(piece, 'x')  32.8 us
    all_gather x1, waiting for transfers between devices, exclusive_prefix(): before_x = lax.all_gather(masked_sum(along_x, xi), 'z', axis=0, tiled=True)  32.3 us
    ppermute x12, starting transfers between devices, gather_feat(): lax.ppermute(piece, 'feat', [(i, (i + k) % n) for i in range(n)])  16.8 us
    dot_general x1, matrix products, body(): lax.dot_general(own, rows_xy, contract, preferred_element_type=jnp.float32)  12.5 us
  transfers between devices with their start and end apart: 19, of which 17 were waited for; matrix products, arithmetic and copies ran while one was open for 0% of the time, Pallas kernels for 0%

profile of v9, /device:TPU:1, one launch (start us, length us, event | category | flops | bytes accessed | tf_op | source)
XLA Modules:
  0.0 493.3 jit_solution(9516182229129319183)
XLA Ops:
  9.0 5.8 %convolution_convert_fusion = bf16[640,2176]{1,0:T(8,128)(2,1)} fusion(bf16[640,128]{1,0:T(8,128)(2,1)} %param.6, bf16[640,2048]{1,0:T(8,128)(2,1)} %param.5, s32[640]{0:T(1024)S(1)} %convert_add_fusion), kind=kOutput, calls=%fused_computation.5 | convolution fusion | flops 1789952000 | bytes 5573120 | tf_op jit(solution)/shard_map/dot_general | solution.py:71
  14.8 3.6 reshape.118
  18.3 51.3 %all_to_all.10 = bf16[32,20,2176]{2,1,0:T(8,128)(2,1)} all-to-all(bf16[32,20,2176]{2,1,0:T(8,128)(2,1)S(1)} %reshape.118), channel_id=1, replica_groups=mesh['x'=4,'z'=4,'c'=2,'feat'=4] {'x','z','c'}, dimensions={0} | all-to-all | bytes 5570560 | tf_op jit(solution)/shard_map/all_to_all | solution.py:73
  69.7 5.3 %reshape.119 = bf16[640,2176]{1,0:T(8,128)(2,1)} reshape(bf16[32,20,2176]{2,1,0:T(8,128)(2,1)} %all_to_all.10) | data formatting | bytes 5570560 | tf_op jit(solution)/shard_map/reshape | solution.py:74
  75.1 103.8 %all-gather.7.cloned.1.call-done = bf16[2560,2176]{1,0:T(8,128)(2,1)} async-done(((bf16[640,2176]{1,0:T(8,128)(2,1)}), bf16[2560,2176]{1,0:T(8,128)(2,1)}) %all-gather.7.cloned.1.call-update) | async-done | bytes 11141136 | tf_op jit(solution)/shard_map/all_gather | solution.py:77
  178.8 12.5 %fusion.11 = f32[512,2176]{1,0:T(8,128)} fusion(bf16[2560,2176]{1,0:T(8,128)(2,1)} %all-gather.7.cloned.1.call-done, s32[]{:T(128)S(6)} %select_n.63), kind=kOutput, calls=%fused_computation.18 | convolution fusion | flops 5704253440 | bytes 18219012 | tf_op jit(solution)/shard_map/dot_general | solution.py:79
  192.2 7.5 %collective-permute-done = f32[512,2176]{1,0:T(8,128)} collective-permute-done((f32[512,2176]{1,0:T(8,128)}, f32[512,2176]{1,0:T(8,128)}, u32[]{:S(2)}, u32[]{:S(2)}) %collective-permute-start) | collective-permute-done | bytes 4456480 | tf_op jit(solution)/shard_map/ppermute | solution.py:36
  199.7 3.9 dynamic-slice_add_fusion
  203.6 88.4 %all-gather.11.cloned.1.call-done = f32[1024,2176]{1,0:T(8,128)} async-done(((f32[256,2176]{1,0:T(8,128)}), f32[1024,2176]{1,0:T(8,128)}) %all-gather.11.cloned.1.call-update) | async-done | bytes 8912912 | tf_op jit(solution)/shard_map/all_gather | solution.py:40
  292.0 5.1 %select_reduce_fusion = (f32[256,2176]{1,0:T(8,128)S(1)}, f32[256,2176]{1,0:T(8,128)S(1)}) fusion(f32[4,256,2176]{2,1,0:T(8,128)} %bitcast.49, pred[4]{0:T(512)(128)(4,1)S(1)} %iota_compare_fusion.13), kind=kLoop, calls=%fused_computation.4 | loop fusion | flops 5570560 | bytes 13369348 | tf_op jit(solution)/shard_map/reduce_sum | solution.py:18
  298.1 32.8 %all-gather.13.cloned.1.call-done = f32[256,2176]{1,0:T(8,128)} async-done(((f32[64,2176]{1,0:T(8,128)}), f32[256,2176]{1,0:T(8,128)}) %all-gather.13.cloned.1.call-update) | async-done | bytes 2228240 | tf_op jit(solution)/shard_map/all_gather | solution.py:45
  330.9 2.7 select_reduce_fusion.1
  333.7 32.3 %all-gather.9.cloned.1.call-done = f32[256,2176]{1,0:T(8,128)} async-done(((f32[64,2176]{1,0:T(8,128)}), f32[256,2176]{1,0:T(8,128)}) %all-gather.9.cloned.1.call-update) | async-done | bytes 2228240 | tf_op jit(solution)/shard_map/all_gather | solution.py:46
  366.0 3.2 add.117
  370.0 4.2 collective-permute-done.1
  374.2 1.9 broadcast_select_fusion.1
  376.1 2.7 maximum_add_fusion
  378.9 2.0 copy-done
  380.9 1.3 collective-permute-start.2
  382.2 2.4 collective-permute-start.3
  385.9 3.7 collective-permute-done.2
  389.6 5.8 %collective-permute-done.3 = f32[512,128]{1,0:T(8,128)S(1)} collective-permute-done((f32[512,128]{1,0:T(8,128)S(1)}, f32[512,128]{1,0:T(8,128)S(1)}, u32[]{:S(2)}, u32[]{:S(2)}) %collective-permute-start.3) | collective-permute-done | bytes 262176 | tf_op jit(solution)/shard_map/ppermute | solution.py:24
  396.3 4.4 fusion.18
  400.7 2.6 collective-permute-start.7
  403.2 1.6 collective-permute-start.6
  404.9 4.0 collective-permute-done.7
  408.8 3.2 collective-permute-done.5
  412.0 4.9 collective-permute-done.6
  417.0 1.6 gather_fusion.1
  418.6 1.7 multiply_reduce_fusion.3
  421.1 1.8 fusion.24
  423.0 1.8 collective-permute-start.9
  424.8 1.2 collective-permute-start.10
  426.0 4.5 collective-permute-done.8
  430.4 5.2 %collective-permute-done.9 = f32[512,128]{1,0:T(8,128)S(1)} collective-permute-done((f32[512,128]{1,0:T(8,128)S(1)}, f32[512,128]{1,0:T(8,128)S(1)}, u32[]{:S(2)}, u32[]{:S(2)}) %collective-permute-start.9) | collective-permute-done | bytes 262176 | tf_op jit(solution)/shard_map/ppermute | solution.py:24
  435.6 2.0 collective-permute-done.10
  437.7 1.6 gather_fusion.2
  439.3 1.8 multiply_reduce_fusion.1
  442.1 1.8 fusion.30
  443.9 1.2 collective-permute-start.11
  445.2 3.4 collective-permute-start.12
  448.6 4.4 collective-permute-done.11
  453.0 7.1 %collective-permute-done.12 = f32[512,128]{1,0:T(8,128)S(1)} collective-permute-done((f32[512,128]{1,0:T(8,128)S(1)}, f32[512,128]{1,0:T(8,128)S(1)}, u32[]{:S(2)}, u32[]{:S(2)}) %collective-permute-start.12) | collective-permute-done | bytes 262176 | tf_op jit(solution)/shard_map/ppermute | solution.py:24
  461.2 2.8 gather_fusion.3
  464.0 1.9 fusion.42
  466.4 2.5 fusion.33
  469.6 7.0 %all-to-all-start.1 = ((bf16[32,20,128]{2,1,0:T(8,128)(2,1)}), bf16[32,20,128]{2,1,0:T(8,128)(2,1)S(1)}, u32[]{:S(2)}, u32[]{:S(2)}) async-start(bf16[32,20,128]{2,1,0:T(8,128)(2,1)} %reshape.122), calls=%async_computation.1 | async-start | bytes 393216 | tf_op jit(solution)/shard_map/all_to_all | solution.py:105
  476.8 8.1 %all-to-all-done.1 = bf16[32,20,128]{2,1,0:T(8,128)(2,1)S(1)} async-done(((bf16[32,20,128]{2,1,0:T(8,128)(2,1)}), bf16[32,20,128]{2,1,0:T(8,128)(2,1)S(1)}, u32[]{:S(2)}, u32[]{:S(2)}) %all-to-all-start.1) | async-done | bytes 163872 | tf_op jit(solution)/shard_map/all_to_all | solution.py:105
  (71 shorter events, 13.0 us)
Async XLA Ops:
  7.2 171.7 %all-gather.7.cloned.1.call-start = ((), (), s32[]{:S(2)}) async-start(), calls=%async_computation.2 | async-start | bytes 13926400 | tf_op jit(solution)/shard_map/all_gather | solution.py:77
  75.0 217.0 %all-gather.11.cloned.1.call-start = ((), (), s32[]{:S(2)}) async-start(), calls=%async_computation.4 | async-start | bytes 11141120 | tf_op jit(solution)/shard_map/all_gather | solution.py:40
  191.3 8.3 %collective-permute-start = (f32[512,2176]{1,0:T(8,128)}, f32[512,2176]{1,0:T(8,128)}, u32[]{:S(2)}, u32[]{:S(2)}) collective-permute-start(f32[512,2176]{1,0:T(8,128)} %fusion.11), channel_id=1, source_target_pairs={{0,4},{4,0},{1,5},{5,1},{2,6},{6,2},{3,7},{7,3},{8,12},{12,8},{9,1... | collective-permute-start | bytes 13369352 | tf_op jit(solution)/shard_map/ppermute | solution.py:36
  203.6 127.4 %all-gather.13.cloned.1.call-start = ((), (), s32[]{:S(2)}) async-start(), calls=%async_computation.5 | async-start | bytes 2785280 | tf_op jit(solution)/shard_map/all_gather | solution.py:45
  298.1 67.9 %all-gather.9.cloned.1.call-start = ((), (), s32[]{:S(2)}) async-start(), calls=%async_computation.3 | async-start | bytes 2785280 | tf_op jit(solution)/shard_map/all_gather | solution.py:46
  369.2 5.0 %collective-permute-start.1 = (f32[256,2176]{1,0:T(8,128)}, f32[256,2176]{1,0:T(8,128)S(1)}, u32[]{:S(2)}, u32[]{:S(2)}) collective-permute-start(f32[256,2176]{1,0:T(8,128)} %add.117), channel_id=1, source_target_pairs={{0,4},{4,0},{1,5},{5,1},{2,6},{6,2},{3,7},{7,3},{8,12},{12,8},{9,1... | collective-permute-start | bytes 6684680 | tf_op jit(solution)/shard_map/ppermute | solution.py:48
  378.9 2.0 copy-start
  380.9 8.6 %collective-permute-start.2 = (f32[512,128]{1,0:T(8,128)S(1)}, f32[512,128]{1,0:T(8,128)S(1)}, u32[]{:S(2)}, u32[]{:S(2)}) collective-permute-start(f32[512,128]{1,0:T(8,128)S(1)} %get-tuple-element.17), channel_id=1, source_target_pairs={{0,1},{1,2},{2,3},{3,0},{4,5},{5,6},{6,7},{7,4},{8,9},{9,10},{10,1... | collective-permute-start | bytes 786440 | tf_op jit(solution)/shard_map/ppermute | solution.py:24
  382.2 13.2 %collective-permute-start.3 = (f32[512,128]{1,0:T(8,128)S(1)}, f32[512,128]{1,0:T(8,128)S(1)}, u32[]{:S(2)}, u32[]{:S(2)}) collective-permute-start(f32[512,128]{1,0:T(8,128)S(1)} %get-tuple-element.17), channel_id=1, source_target_pairs={{0,2},{1,3},{2,0},{3,1},{4,6},{5,7},{6,4},{7,5},{8,10},{9,11},{10,... | collective-permute-start | bytes 786440 | tf_op jit(solution)/shard_map/ppermute | solution.py:24
  384.7 10.8 %collective-permute-start.4 = (f32[512,128]{1,0:T(8,128)S(1)}, f32[512,128]{1,0:T(8,128)S(1)}, u32[]{:S(2)}, u32[]{:S(2)}) collective-permute-start(f32[512,128]{1,0:T(8,128)S(1)} %get-tuple-element.17), channel_id=1, source_target_pairs={{0,3},{1,0},{2,1},{3,2},{4,7},{5,4},{6,5},{7,6},{8,11},{9,8},{10,9... | collective-permute-start | bytes 786440 | tf_op jit(solution)/shard_map/ppermute | solution.py:24
  396.3 24.4 %copy-start.1 = (f32[4,512,128]{2,1,0:T(8,128)}, f32[4,512,128]{2,1,0:T(8,128)S(1)}, u32[]{:S(2)}) copy-start(f32[4,512,128]{2,1,0:T(8,128)S(1)} %select_multiply_fusion.1) | copy-start | bytes 3145732
  400.7 8.2 %collective-permute-start.7 = (f32[512,128]{1,0:T(8,128)S(1)}, f32[512,128]{1,0:T(8,128)S(1)}, u32[]{:S(2)}, u32[]{:S(2)}) collective-permute-start(f32[512,128]{1,0:T(8,128)S(1)} %fusion.18), channel_id=1, source_target_pairs={{0,3},{1,0},{2,1},{3,2},{4,7},{5,4},{6,5},{7,6},{8,11},{9,8},{10,9... | collective-permute-start | bytes 786440 | tf_op jit(solution)/shard_map/ppermute | solution.py:24
  403.2 8.8 %collective-permute-start.5 = (f32[512,128]{1,0:T(8,128)S(1)}, f32[512,128]{1,0:T(8,128)S(1)}, u32[]{:S(2)}, u32[]{:S(2)}) collective-permute-start(f32[512,128]{1,0:T(8,128)S(1)} %fusion.18), channel_id=1, source_target_pairs={{0,1},{1,2},{2,3},{3,0},{4,5},{5,6},{6,7},{7,4},{8,9},{9,10},{10,1... | collective-permute-start | bytes 786440 | tf_op jit(solution)/shard_map/ppermute | solution.py:24
  403.2 13.7 %collective-permute-start.6 = (f32[512,128]{1,0:T(8,128)S(1)}, f32[512,128]{1,0:T(8,128)S(1)}, u32[]{:S(2)}, u32[]{:S(2)}) collective-permute-start(f32[512,128]{1,0:T(8,128)S(1)} %fusion.18), channel_id=1, source_target_pairs={{0,2},{1,3},{2,0},{3,1},{4,6},{5,7},{6,4},{7,5},{8,10},{9,11},{10,... | collective-permute-start | bytes 786440 | tf_op jit(solution)/shard_map/ppermute | solution.py:24
  416.9 4.0 slice-start
  418.6 2.5 slice-start.1
  421.1 16.5 %copy-start.5 = (f32[2048,128]{1,0:T(8,128)}, f32[2048,128]{1,0:T(8,128)S(1)}, u32[]{:S(2)}) copy-start(f32[2048,128]{1,0:T(8,128)S(1)} %multiply_add_fusion) | copy-start | bytes 3145732
  422.9 7.5 %collective-permute-start.8 = (f32[512,128]{1,0:T(8,128)S(1)}, f32[512,128]{1,0:T(8,128)S(1)}, u32[]{:S(2)}, u32[]{:S(2)}) collective-permute-start(f32[512,128]{1,0:T(8,128)S(1)} %fusion.24), channel_id=1, source_target_pairs={{0,1},{1,2},{2,3},{3,0},{4,5},{5,6},{6,7},{7,4},{8,9},{9,10},{10,1... | collective-permute-start | bytes 786440 | tf_op jit(solution)/shard_map/ppermute | solution.py:24
  423.0 12.6 %collective-permute-start.9 = (f32[512,128]{1,0:T(8,128)S(1)}, f32[512,128]{1,0:T(8,128)S(1)}, u32[]{:S(2)}, u32[]{:S(2)}) collective-permute-start(f32[512,128]{1,0:T(8,128)S(1)} %fusion.24), channel_id=1, source_target_pairs={{0,2},{1,3},{2,0},{3,1},{4,6},{5,7},{6,4},{7,5},{8,10},{9,11},{10,... | collective-permute-start | bytes 786440 | tf_op jit(solution)/shard_map/ppermute | solution.py:24
  424.8 12.8 %collective-permute-start.10 = (f32[512,128]{1,0:T(8,128)S(1)}, f32[512,128]{1,0:T(8,128)S(1)}, u32[]{:S(2)}, u32[]{:S(2)}) collective-permute-start(f32[512,128]{1,0:T(8,128)S(1)} %fusion.24), channel_id=1, source_target_pairs={{0,3},{1,0},{2,1},{3,2},{4,7},{5,4},{6,5},{7,6},{8,11},{9,8},{10,9... | collective-permute-start | bytes 786440 | tf_op jit(solution)/shard_map/ppermute | solution.py:24
  437.6 4.1 slice-start.2
  439.3 2.1 copy-start.2
  439.3 2.8 slice-start.3
  442.1 1.8 copy-start.6
  443.9 9.1 %collective-permute-start.11 = (f32[512,128]{1,0:T(8,128)S(1)}, f32[512,128]{1,0:T(8,128)S(1)}, u32[]{:S(2)}, u32[]{:S(2)}) collective-permute-start(f32[512,128]{1,0:T(8,128)S(1)} %fusion.30), channel_id=1, source_target_pairs={{0,1},{1,2},{2,3},{3,0},{4,5},{5,6},{6,7},{7,4},{8,9},{9,10},{10,1... | collective-permute-start | bytes 786440 | tf_op jit(solution)/shard_map/ppermute | solution.py:24
  445.2 14.9 %collective-permute-start.12 = (f32[512,128]{1,0:T(8,128)S(1)}, f32[512,128]{1,0:T(8,128)S(1)}, u32[]{:S(2)}, u32[]{:S(2)}) collective-permute-start(f32[512,128]{1,0:T(8,128)S(1)} %fusion.30), channel_id=1, source_target_pairs={{0,2},{1,3},{2,0},{3,1},{4,6},{5,7},{6,4},{7,5},{8,10},{9,11},{10,... | collective-permute-start | bytes 786440 | tf_op jit(solution)/shard_map/ppermute | solution.py:24
  448.6 11.5 %collective-permute-start.13 = (f32[512,128]{1,0:T(8,128)S(1)}, f32[512,128]{1,0:T(8,128)S(1)}, u32[]{:S(2)}, u32[]{:S(2)}) collective-permute-start(f32[512,128]{1,0:T(8,128)S(1)} %fusion.30), channel_id=1, source_target_pairs={{0,3},{1,0},{2,1},{3,2},{4,7},{5,4},{6,5},{7,6},{8,11},{9,8},{10,9... | collective-permute-start | bytes 786440 | tf_op jit(solution)/shard_map/ppermute | solution.py:24
  464.0 1.9 copy-start.3
  464.0 2.4 copy-start.4
  466.4 10.2 %copy-start.7 = (bf16[640,128]{1,0:T(8,128)(2,1)S(1)}, bf16[640,128]{1,0:T(8,128)(2,1)}, u32[]{:S(2)}) copy-start(bf16[640,128]{1,0:T(8,128)(2,1)} %param.6) | copy-start | bytes 491524
  469.6 15.3 %all-to-all-start.1 = ((bf16[32,20,128]{2,1,0:T(8,128)(2,1)}), bf16[32,20,128]{2,1,0:T(8,128)(2,1)S(1)}, u32[]{:S(2)}, u32[]{:S(2)}) async-start(bf16[32,20,128]{2,1,0:T(8,128)(2,1)} %reshape.122), calls=%async_computation.1 | async-start | bytes 393216 | tf_op jit(solution)/shard_map/all_to_all | solution.py:105
Sparse Core Ops, SparseCore 0:
  75.1 103.6 all-gather.6
  203.7 88.3 all-gather.10
  298.2 32.6 all-gather.12
  333.8 32.1 all-gather.8

commit v10 on v9

--- a/solution.py
+++ b/solution.py
@@ -18,13 +18,17 @@
     return jnp.sum(jnp.where(keep.reshape((-1,) + (1,) * (stack.ndim - 1)), stack, 0.0), axis=0)
 
 
-def gather_feat(piece):
-    n = lax.axis_size("feat")
-    f = lax.axis_index("feat")
-    parts = [piece] + [lax.ppermute(piece, "feat", [(i, (i + k) % n) for i in range(n)]) for k in range(1, n)]
+def stack_over(piece, axis):
+    n = lax.axis_size(axis)
+    f = lax.axis_index(axis)
+    parts = [piece] + [lax.ppermute(piece, axis, [(i, (i + k) % n) for i in range(n)]) for k in range(1, n)]
     stacked = jnp.stack(parts)
-    full = jnp.take(stacked, (f - jnp.arange(n)) % n, axis=0)
-    return full.reshape((n * piece.shape[0],) + piece.shape[1:])
+    return jnp.take(stacked, (f - jnp.arange(n)) % n, axis=0)
+
+
+def gather_feat(piece, axis="feat"):
+    full = stack_over(piece, axis)
+    return full.reshape((full.shape[0] * piece.shape[0],) + piece.shape[1:])
 
 
 def exclusive_prefix(block):
@@ -42,8 +46,8 @@
     total_z = jnp.sum(along_z, axis=0)
     quarter = half // lax.axis_size("z")
     piece = lax.dynamic_slice_in_dim(total_z, zi * quarter, quarter, 0)
-    along_x = lax.all_gather(piece, "x")
-    before_x = lax.all_gather(masked_sum(along_x, xi), "z", axis=0, tiled=True)
+    along_x = stack_over(piece, "x")
+    before_x = gather_feat(masked_sum(along_x, xi), "z")
     mine_prefix = before_x + before_z
     other_prefix = lax.ppermute(mine_prefix, "c", SWAP)
     first = ci == 0

time: 494 us -> 495 us (level)
  waiting for transfers between devices: 322 us -> 300 us
  starting transfers between devices: 25.6 us -> 39 us
  local copies, waits for them, and re-layouts: 21.3 us -> 28.3 us
    all_gather x2 -> x0, waiting for transfers between devices: 65.1 us -> none  [the longest x1 32.8 us: exclusive_prefix(): along_x = lax.all_gather(piece, 'x')]
    ppermute x12 -> x18, waiting for transfers between devices: 44.7 us -> 87.5 us  [stack_over(): lax.ppermute(piece, axis, [(i, (i + k) % n) for i in range(n)])]
    ppermute x12 -> x18, starting transfers between devices: 16.8 us -> 28 us  [stack_over(): lax.ppermute(piece, axis, [(i, (i + k) % n) for i in range(n)])]
    gather x4 -> x6, local copies, waits for them, and re-layouts: 6.6 us -> 13.9 us  [stack_over(): return jnp.take(stacked, (f - jnp.arange(n)) % n, axis=0)]
    reduce_sum x2 -> x1, other arithmetic: 7.86 us -> 1.99 us  [masked_sum(): jnp.sum(jnp.where(keep.reshape((-1,) + (1,) * (stack.ndim - 1)), stack, 0...]
    reduce_sum x0 -> x1, other arithmetic: none -> 5.06 us  [exclusive_prefix(): total_z = jnp.sum(along_z, axis=0)]
  transfers between devices with their start and end apart: 19 -> 23, of which waited for: 17 -> 18; matrix products, arithmetic and copies ran while one was open for 0% -> 0% of each run, Pallas kernels for 0% -> 0%
where the time goes in v10:
time: 495 us; the launch traced here: 494 us
  waiting for transfers between devices  300 us (61%)
  blocking collectives  51.3 us (10%)
  starting transfers between devices  39 us (8%)
  other arithmetic  31.3 us (6%)
  matrix products  30.3 us (6%)
  local copies, waits for them, and re-layouts  28.3 us (6%)
  between operations  14.4 us (3%)
    all_gather x1, waiting for transfers between devices, body(): rows_xy = lax.all_gather(local_xy, 'feat', axis=0, tiled=True)  104 us
    all_gather x1, waiting for transfers between devices, exclusive_prefix(): along_z = lax.all_gather(mine, 'z')  88.4 us
    ppermute x18, waiting for transfers between devices, stack_over(): lax.ppermute(piece, axis, [(i, (i + k) % n) for i in range(n)])  87.5 us
    all_to_all x1, blocking collectives, body(): lax.all_to_all(sorted_xy, TM, split_axis=0, concat_axis=0, tiled=True)  51.3 us
    ppermute x18, starting transfers between devices, stack_over(): lax.ppermute(piece, axis, [(i, (i + k) % n) for i in range(n)])  28 us
    gather x6, local copies, waits for them, and re-layouts, stack_over(): return jnp.take(stacked, (f - jnp.arange(n)) % n, axis=0)  13.9 us
    dot_general x1, matrix products, body(): lax.dot_general(own, rows_xy, contract, preferred_element_type=jnp.float32)  12.5 us
  transfers between devices with their start and end apart: 23, of which 18 were waited for; matrix products, arithmetic and copies ran while one was open for 0% of the time, Pallas kernels for 0%

profile of v10, /device:TPU:1, one launch (start us, length us, event | category | flops | bytes accessed | tf_op | source)
XLA Modules:
  0.0 494.2 jit_solution(9713390139657389941)
XLA Ops:
  9.0 5.8 %convolution_convert_fusion = bf16[640,2176]{1,0:T(8,128)(2,1)} fusion(bf16[640,128]{1,0:T(8,128)(2,1)} %param.8, bf16[640,2048]{1,0:T(8,128)(2,1)} %param.7, s32[640]{0:T(1024)S(1)} %convert_add_fusion), kind=kOutput, calls=%fused_computation.7 | convolution fusion | flops 1789952000 | bytes 5573120 | tf_op jit(solution)/shard_map/dot_general | solution.py:75
  14.8 3.6 reshape.126
  18.4 51.3 %all_to_all.10 = bf16[32,20,2176]{2,1,0:T(8,128)(2,1)} all-to-all(bf16[32,20,2176]{2,1,0:T(8,128)(2,1)S(1)} %reshape.126), channel_id=1, replica_groups=mesh['x'=4,'z'=4,'c'=2,'feat'=4] {'x','z','c'}, dimensions={0} | all-to-all | bytes 5570560 | tf_op jit(solution)/shard_map/all_to_all | solution.py:77
  69.7 5.3 %reshape.127 = bf16[640,2176]{1,0:T(8,128)(2,1)} reshape(bf16[32,20,2176]{2,1,0:T(8,128)(2,1)} %all_to_all.10) | data formatting | bytes 5570560 | tf_op jit(solution)/shard_map/reshape | solution.py:78
  75.1 103.8 %all-gather.4.cloned.1.call-done = bf16[2560,2176]{1,0:T(8,128)(2,1)} async-done(((bf16[640,2176]{1,0:T(8,128)(2,1)}), bf16[2560,2176]{1,0:T(8,128)(2,1)}) %all-gather.4.cloned.1.call-update) | async-done | bytes 11141136 | tf_op jit(solution)/shard_map/all_gather | solution.py:81
  178.8 12.5 %fusion.11 = f32[512,2176]{1,0:T(8,128)} fusion(bf16[2560,2176]{1,0:T(8,128)(2,1)} %all-gather.4.cloned.1.call-done, s32[]{:T(128)S(6)} %select_n.77), kind=kOutput, calls=%fused_computation.20 | convolution fusion | flops 5704253440 | bytes 18219012 | tf_op jit(solution)/shard_map/dot_general | solution.py:83
  192.2 7.5 %collective-permute-done = f32[512,2176]{1,0:T(8,128)} collective-permute-done((f32[512,2176]{1,0:T(8,128)}, f32[512,2176]{1,0:T(8,128)}, u32[]{:S(2)}, u32[]{:S(2)}) %collective-permute-start) | collective-permute-done | bytes 4456480 | tf_op jit(solution)/shard_map/ppermute | solution.py:40
  199.7 3.9 dynamic-slice_add_fusion
  203.6 88.4 %all-gather.6.cloned.1.call-done = f32[1024,2176]{1,0:T(8,128)} async-done(((f32[256,2176]{1,0:T(8,128)}), f32[1024,2176]{1,0:T(8,128)}) %all-gather.6.cloned.1.call-update) | async-done | bytes 8912912 | tf_op jit(solution)/shard_map/all_gather | solution.py:44
  292.1 5.1 %fusion.55 = (f32[256,2176]{1,0:T(8,128)S(1)}, f32[256,2176]{1,0:T(8,128)S(1)}) fusion(f32[4,256,2176]{2,1,0:T(8,128)} %bitcast.59, pred[4]{0:T(512)(128)(4,1)S(1)} %get-tuple-element.26), kind=kLoop, calls=%fused_computation.111 | loop fusion | flops 5570560 | bytes 13369348 | tf_op jit(solution)/shard_map/reduce_sum | solution.py:46
  298.4 2.4 collective-permute-start.2
  302.1 9.7 %collective-permute-done.1 = f32[64,2176]{1,0:T(8,128)S(1)} collective-permute-done((f32[64,2176]{1,0:T(8,128)S(1)}, f32[64,2176]{1,0:T(8,128)S(1)}, u32[]{:S(2)}, u32[]{:S(2)}) %collective-permute-start.1) | collective-permute-done | bytes 557088 | tf_op jit(solution)/shard_map/ppermute | solution.py:24
  311.8 12.9 %collective-permute-done.2 = f32[64,2176]{1,0:T(8,128)S(1)} collective-permute-done((f32[64,2176]{1,0:T(8,128)S(1)}, f32[64,2176]{1,0:T(8,128)S(1)}, u32[]{:S(2)}, u32[]{:S(2)}) %collective-permute-start.2) | collective-permute-done | bytes 557088 | tf_op jit(solution)/shard_map/ppermute | solution.py:24
  326.1 3.7 gather_fusion
  329.8 2.0 fusion.13
  334.4 2.0 collective-permute-start.6
  336.4 9.3 %collective-permute-done.4 = f32[64,2176]{1,0:T(8,128)S(1)} collective-permute-done((f32[64,2176]{1,0:T(8,128)S(1)}, f32[64,2176]{1,0:T(8,128)S(1)}, u32[]{:S(2)}, u32[]{:S(2)}) %collective-permute-start.4) | collective-permute-done | bytes 557088 | tf_op jit(solution)/shard_map/ppermute | solution.py:24
  345.7 11.6 %collective-permute-done.5 = f32[64,2176]{1,0:T(8,128)S(1)} collective-permute-done((f32[64,2176]{1,0:T(8,128)S(1)}, f32[64,2176]{1,0:T(8,128)S(1)}, u32[]{:S(2)}, u32[]{:S(2)}) %collective-permute-start.5) | collective-permute-done | bytes 557088 | tf_op jit(solution)/shard_map/ppermute | solution.py:24
  357.4 1.8 collective-permute-done.6
  360.6 3.7 gather_fusion.1
  364.3 1.8 broadcast_select_fusion
  369.2 4.2 collective-permute-done.7
  373.4 1.9 broadcast_select_fusion.2
  375.3 2.7 maximum_add_fusion
  378.1 2.0 copy-done
  381.4 2.4 collective-permute-start.9
  385.1 3.7 collective-permute-done.8
  388.8 5.8 %collective-permute-done.9 = f32[512,128]{1,0:T(8,128)S(1)} collective-permute-done((f32[512,128]{1,0:T(8,128)S(1)}, f32[512,128]{1,0:T(8,128)S(1)}, u32[]{:S(2)}, u32[]{:S(2)}) %collective-permute-start.9) | collective-permute-done | bytes 262176 | tf_op jit(solution)/shard_map/ppermute | solution.py:24
  395.5 4.4 fusion.19
  399.9 1.7 collective-permute-start.11
  401.6 2.0 collective-permute-start.12
  404.7 4.4 collective-permute-done.11
  409.1 6.2 %collective-permute-done.12 = f32[512,128]{1,0:T(8,128)S(1)} collective-permute-done((f32[512,128]{1,0:T(8,128)S(1)}, f32[512,128]{1,0:T(8,128)S(1)}, u32[]{:S(2)}, u32[]{:S(2)}) %collective-permute-start.12) | collective-permute-done | bytes 262176 | tf_op jit(solution)/shard_map/ppermute | solution.py:24
  416.9 1.7 multiply_reduce_fusion.3
  419.4 1.8 fusion.25
  422.5 2.7 collective-permute-start.15
  426.2 3.1 collective-permute-done.14
  429.3 7.5 %collective-permute-done.15 = f32[512,128]{1,0:T(8,128)S(1)} collective-permute-done((f32[512,128]{1,0:T(8,128)S(1)}, f32[512,128]{1,0:T(8,128)S(1)}, u32[]{:S(2)}, u32[]{:S(2)}) %collective-permute-start.15) | collective-permute-done | bytes 262176 | tf_op jit(solution)/shard_map/ppermute | solution.py:24
  438.5 1.8 multiply_reduce_fusion.1
  441.8 1.8 fusion.31
  444.9 2.7 collective-permute-start.18
  447.6 3.9 collective-permute-done.17
  451.5 7.6 %collective-permute-done.18 = f32[512,128]{1,0:T(8,128)S(1)} collective-permute-done((f32[512,128]{1,0:T(8,128)S(1)}, f32[512,128]{1,0:T(8,128)S(1)}, u32[]{:S(2)}, u32[]{:S(2)}) %collective-permute-start.18) | collective-permute-done | bytes 262176 | tf_op jit(solution)/shard_map/ppermute | solution.py:24
  460.2 2.8 gather_fusion.5
  463.0 1.9 fusion.43
  465.4 2.5 fusion.34
  468.6 8.5 %all-to-all-start.1 = ((bf16[32,20,128]{2,1,0:T(8,128)(2,1)}), bf16[32,20,128]{2,1,0:T(8,128)(2,1)S(1)}, u32[]{:S(2)}, u32[]{:S(2)}) async-start(bf16[32,20,128]{2,1,0:T(8,128)(2,1)} %reshape.131), calls=%async_computation.1 | async-start | bytes 393216 | tf_op jit(solution)/shard_map/all_to_all | solution.py:109
  477.3 8.1 %all-to-all-done.1 = bf16[32,20,128]{2,1,0:T(8,128)(2,1)S(1)} async-done(((bf16[32,20,128]{2,1,0:T(8,128)(2,1)}), bf16[32,20,128]{2,1,0:T(8,128)(2,1)S(1)}, u32[]{:S(2)}, u32[]{:S(2)}) %all-to-all-start.1) | async-done | bytes 163872 | tf_op jit(solution)/shard_map/all_to_all | solution.py:109
  (87 shorter events, 31.9 us)
Async XLA Ops:
  7.2 171.7 %all-gather.4.cloned.1.call-start = ((), (), s32[]{:S(2)}) async-start(), calls=%async_computation.2 | async-start | bytes 13926400 | tf_op jit(solution)/shard_map/all_gather | solution.py:81
  75.0 217.1 %all-gather.6.cloned.1.call-start = ((), (), s32[]{:S(2)}) async-start(), calls=%async_computation.3 | async-start | bytes 11141120 | tf_op jit(solution)/shard_map/all_gather | solution.py:44
  191.3 8.3 %collective-permute-start = (f32[512,2176]{1,0:T(8,128)}, f32[512,2176]{1,0:T(8,128)}, u32[]{:S(2)}, u32[]{:S(2)}) collective-permute-start(f32[512,2176]{1,0:T(8,128)} %fusion.11), channel_id=1, source_target_pairs={{0,4},{4,0},{1,5},{5,1},{2,6},{6,2},{3,7},{7,3},{8,12},{12,8},{9,1... | collective-permute-start | bytes 13369352 | tf_op jit(solution)/shard_map/ppermute | solution.py:40
  297.2 14.6 %collective-permute-start.1 = (f32[64,2176]{1,0:T(8,128)S(1)}, f32[64,2176]{1,0:T(8,128)S(1)}, u32[]{:S(2)}, u32[]{:S(2)}) collective-permute-start(f32[64,2176]{1,0:T(8,128)S(1)} %constant_dynamic-slice_fusion), channel_id=1, source_target_pairs={{0,32},{32,64},{64,96},{96,0},{1,33},{33,65},{65,97},{97,1},{2,34}... | collective-permute-start | bytes 1671176 | tf_op jit(solution)/shard_map/ppermute | solution.py:24
  298.4 26.2 %collective-permute-start.2 = (f32[64,2176]{1,0:T(8,128)S(1)}, f32[64,2176]{1,0:T(8,128)S(1)}, u32[]{:S(2)}, u32[]{:S(2)}) collective-permute-start(f32[64,2176]{1,0:T(8,128)S(1)} %constant_dynamic-slice_fusion), channel_id=1, source_target_pairs={{0,64},{32,96},{64,0},{96,32},{1,65},{33,97},{65,1},{97,33},{2,66}... | collective-permute-start | bytes 1671176 | tf_op jit(solution)/shard_map/ppermute | solution.py:24
  300.8 23.8 %collective-permute-start.3 = (f32[64,2176]{1,0:T(8,128)S(1)}, f32[64,2176]{1,0:T(8,128)S(1)}, u32[]{:S(2)}, u32[]{:S(2)}) collective-permute-start(f32[64,2176]{1,0:T(8,128)S(1)} %constant_dynamic-slice_fusion), channel_id=1, source_target_pairs={{0,96},{32,0},{64,32},{96,64},{1,97},{33,1},{65,33},{97,65},{2,98}... | collective-permute-start | bytes 1671176 | tf_op jit(solution)/shard_map/ppermute | solution.py:24
  331.8 13.9 %collective-permute-start.4 = (f32[64,2176]{1,0:T(8,128)S(1)}, f32[64,2176]{1,0:T(8,128)S(1)}, u32[]{:S(2)}, u32[]{:S(2)}) collective-permute-start(f32[64,2176]{1,0:T(8,128)S(1)} %fusion.13), channel_id=1, source_target_pairs={{0,8},{8,16},{16,24},{24,0},{1,9},{9,17},{17,25},{25,1},{2,10},{10... | collective-permute-start | bytes 1671176 | tf_op jit(solution)/shard_map/ppermute | solution.py:24
  333.0 24.3 %collective-permute-start.5 = (f32[64,2176]{1,0:T(8,128)S(1)}, f32[64,2176]{1,0:T(8,128)S(1)}, u32[]{:S(2)}, u32[]{:S(2)}) collective-permute-start(f32[64,2176]{1,0:T(8,128)S(1)} %fusion.13), channel_id=1, source_target_pairs={{0,16},{8,24},{16,0},{24,8},{1,17},{9,25},{17,1},{25,9},{2,18},{10... | collective-permute-start | bytes 1671176 | tf_op jit(solution)/shard_map/ppermute | solution.py:24
  334.4 24.7 %collective-permute-start.6 = (f32[64,2176]{1,0:T(8,128)S(1)}, f32[64,2176]{1,0:T(8,128)S(1)}, u32[]{:S(2)}, u32[]{:S(2)}) collective-permute-start(f32[64,2176]{1,0:T(8,128)S(1)} %fusion.13), channel_id=1, source_target_pairs={{0,24},{8,0},{16,8},{24,16},{1,25},{9,1},{17,9},{25,17},{2,26},{10... | collective-permute-start | bytes 1671176 | tf_op jit(solution)/shard_map/ppermute | solution.py:24
  367.7 5.7 %collective-permute-start.7 = (f32[256,2176]{1,0:T(8,128)}, f32[256,2176]{1,0:T(8,128)S(1)}, u32[]{:S(2)}, u32[]{:S(2)}) collective-permute-start(f32[256,2176]{1,0:T(8,128)} %bitcast_add_fusion), channel_id=1, source_target_pairs={{0,4},{4,0},{1,5},{5,1},{2,6},{6,2},{3,7},{7,3},{8,12},{12,8},{9,1... | collective-permute-start | bytes 6684680 | tf_op jit(solution)/shard_map/ppermute | solution.py:52
  378.1 2.0 copy-start
  380.2 8.6 %collective-permute-start.8 = (f32[512,128]{1,0:T(8,128)S(1)}, f32[512,128]{1,0:T(8,128)S(1)}, u32[]{:S(2)}, u32[]{:S(2)}) collective-permute-start(f32[512,128]{1,0:T(8,128)S(1)} %get-tuple-element.18), channel_id=1, source_target_pairs={{0,1},{1,2},{2,3},{3,0},{4,5},{5,6},{6,7},{7,4},{8,9},{9,10},{10,1... | collective-permute-start | bytes 786440 | tf_op jit(solution)/shard_map/ppermute | solution.py:24
  381.4 13.2 %collective-permute-start.9 = (f32[512,128]{1,0:T(8,128)S(1)}, f32[512,128]{1,0:T(8,128)S(1)}, u32[]{:S(2)}, u32[]{:S(2)}) collective-permute-start(f32[512,128]{1,0:T(8,128)S(1)} %get-tuple-element.18), channel_id=1, source_target_pairs={{0,2},{1,3},{2,0},{3,1},{4,6},{5,7},{6,4},{7,5},{8,10},{9,11},{10,... | collective-permute-start | bytes 786440 | tf_op jit(solution)/shard_map/ppermute | solution.py:24
  383.9 10.8 %collective-permute-start.10 = (f32[512,128]{1,0:T(8,128)S(1)}, f32[512,128]{1,0:T(8,128)S(1)}, u32[]{:S(2)}, u32[]{:S(2)}) collective-permute-start(f32[512,128]{1,0:T(8,128)S(1)} %get-tuple-element.18), channel_id=1, source_target_pairs={{0,3},{1,0},{2,1},{3,2},{4,7},{5,4},{6,5},{7,6},{8,11},{9,8},{10,9... | collective-permute-start | bytes 786440 | tf_op jit(solution)/shard_map/ppermute | solution.py:24
  395.5 23.6 %copy-start.1 = (f32[4,512,128]{2,1,0:T(8,128)}, f32[4,512,128]{2,1,0:T(8,128)S(1)}, u32[]{:S(2)}) copy-start(f32[4,512,128]{2,1,0:T(8,128)S(1)} %select_multiply_fusion.1) | copy-start | bytes 3145732
  399.9 9.2 %collective-permute-start.11 = (f32[512,128]{1,0:T(8,128)S(1)}, f32[512,128]{1,0:T(8,128)S(1)}, u32[]{:S(2)}, u32[]{:S(2)}) collective-permute-start(f32[512,128]{1,0:T(8,128)S(1)} %fusion.19), channel_id=1, source_target_pairs={{0,1},{1,2},{2,3},{3,0},{4,5},{5,6},{6,7},{7,4},{8,9},{9,10},{10,1... | collective-permute-start | bytes 786440 | tf_op jit(solution)/shard_map/ppermute | solution.py:24
  401.6 13.7 %collective-permute-start.12 = (f32[512,128]{1,0:T(8,128)S(1)}, f32[512,128]{1,0:T(8,128)S(1)}, u32[]{:S(2)}, u32[]{:S(2)}) collective-permute-start(f32[512,128]{1,0:T(8,128)S(1)} %fusion.19), channel_id=1, source_target_pairs={{0,2},{1,3},{2,0},{3,1},{4,6},{5,7},{6,4},{7,5},{8,10},{9,11},{10,... | collective-permute-start | bytes 786440 | tf_op jit(solution)/shard_map/ppermute | solution.py:24
  403.6 11.6 %collective-permute-start.13 = (f32[512,128]{1,0:T(8,128)S(1)}, f32[512,128]{1,0:T(8,128)S(1)}, u32[]{:S(2)}, u32[]{:S(2)}) collective-permute-start(f32[512,128]{1,0:T(8,128)S(1)} %fusion.19), channel_id=1, source_target_pairs={{0,3},{1,0},{2,1},{3,2},{4,7},{5,4},{6,5},{7,6},{8,11},{9,8},{10,9... | collective-permute-start | bytes 786440 | tf_op jit(solution)/shard_map/ppermute | solution.py:24
  415.2 4.0 slice-start
  416.9 2.5 slice-start.1
  419.4 1.8 copy-start.5
  421.3 8.1 %collective-permute-start.14 = (f32[512,128]{1,0:T(8,128)S(1)}, f32[512,128]{1,0:T(8,128)S(1)}, u32[]{:S(2)}, u32[]{:S(2)}) collective-permute-start(f32[512,128]{1,0:T(8,128)S(1)} %fusion.25), channel_id=1, source_target_pairs={{0,1},{1,2},{2,3},{3,0},{4,5},{5,6},{6,7},{7,4},{8,9},{9,10},{10,1... | collective-permute-start | bytes 786440 | tf_op jit(solution)/shard_map/ppermute | solution.py:24
  422.5 14.3 %collective-permute-start.15 = (f32[512,128]{1,0:T(8,128)S(1)}, f32[512,128]{1,0:T(8,128)S(1)}, u32[]{:S(2)}, u32[]{:S(2)}) collective-permute-start(f32[512,128]{1,0:T(8,128)S(1)} %fusion.25), channel_id=1, source_target_pairs={{0,2},{1,3},{2,0},{3,1},{4,6},{5,7},{6,4},{7,5},{8,10},{9,11},{10,... | collective-permute-start | bytes 786440 | tf_op jit(solution)/shard_map/ppermute | solution.py:24
  425.3 11.6 %collective-permute-start.16 = (f32[512,128]{1,0:T(8,128)S(1)}, f32[512,128]{1,0:T(8,128)S(1)}, u32[]{:S(2)}, u32[]{:S(2)}) collective-permute-start(f32[512,128]{1,0:T(8,128)S(1)} %fusion.25), channel_id=1, source_target_pairs={{0,3},{1,0},{2,1},{3,2},{4,7},{5,4},{6,5},{7,6},{8,11},{9,8},{10,9... | collective-permute-start | bytes 786440 | tf_op jit(solution)/shard_map/ppermute | solution.py:24
  436.8 4.9 slice-start.2
  438.5 3.3 slice-start.3
  440.3 1.2 copy-start.2
  441.8 1.8 copy-start.6
  443.6 7.9 %collective-permute-start.17 = (f32[512,128]{1,0:T(8,128)S(1)}, f32[512,128]{1,0:T(8,128)S(1)}, u32[]{:S(2)}, u32[]{:S(2)}) collective-permute-start(f32[512,128]{1,0:T(8,128)S(1)} %fusion.31), channel_id=1, source_target_pairs={{0,1},{1,2},{2,3},{3,0},{4,5},{5,6},{6,7},{7,4},{8,9},{9,10},{10,1... | collective-permute-start | bytes 786440 | tf_op jit(solution)/shard_map/ppermute | solution.py:24
  444.9 14.2 %collective-permute-start.18 = (f32[512,128]{1,0:T(8,128)S(1)}, f32[512,128]{1,0:T(8,128)S(1)}, u32[]{:S(2)}, u32[]{:S(2)}) collective-permute-start(f32[512,128]{1,0:T(8,128)S(1)} %fusion.31), channel_id=1, source_target_pairs={{0,2},{1,3},{2,0},{3,1},{4,6},{5,7},{6,4},{7,5},{8,10},{9,11},{10,... | collective-permute-start | bytes 786440 | tf_op jit(solution)/shard_map/ppermute | solution.py:24
  447.6 11.5 %collective-permute-start.19 = (f32[512,128]{1,0:T(8,128)S(1)}, f32[512,128]{1,0:T(8,128)S(1)}, u32[]{:S(2)}, u32[]{:S(2)}) collective-permute-start(f32[512,128]{1,0:T(8,128)S(1)} %fusion.31), channel_id=1, source_target_pairs={{0,3},{1,0},{2,1},{3,2},{4,7},{5,4},{6,5},{7,6},{8,11},{9,8},{10,9... | collective-permute-start | bytes 786440 | tf_op jit(solution)/shard_map/ppermute | solution.py:24
  463.0 1.9 copy-start.3
  463.0 2.4 copy-start.4
  465.4 11.7 %copy-start.7 = (bf16[640,128]{1,0:T(8,128)(2,1)S(1)}, bf16[640,128]{1,0:T(8,128)(2,1)}, u32[]{:S(2)}) copy-start(bf16[640,128]{1,0:T(8,128)(2,1)} %param.8) | copy-start | bytes 491524
  468.6 16.8 %all-to-all-start.1 = ((bf16[32,20,128]{2,1,0:T(8,128)(2,1)}), bf16[32,20,128]{2,1,0:T(8,128)(2,1)S(1)}, u32[]{:S(2)}, u32[]{:S(2)}) async-start(bf16[32,20,128]{2,1,0:T(8,128)(2,1)} %reshape.131), calls=%async_computation.1 | async-start | bytes 393216 | tf_op jit(solution)/shard_map/all_to_all | solution.py:109
Sparse Core Ops, SparseCore 0:
  75.1 103.6 all-gather.3
  203.7 88.3 all-gather.5

commit v11 on v9

--- a/solution.py
+++ b/solution.py
@@ -20,11 +20,12 @@
 
 def gather_feat(piece):
     n = lax.axis_size("feat")
-    f = lax.axis_index("feat")
     parts = [piece] + [lax.ppermute(piece, "feat", [(i, (i + k) % n) for i in range(n)]) for k in range(1, n)]
-    stacked = jnp.stack(parts)
-    full = jnp.take(stacked, (f - jnp.arange(n)) % n, axis=0)
-    return full.reshape((n * piece.shape[0],) + piece.shape[1:])
+    return jnp.concatenate(parts, axis=0)
+
+
+def own_order(f, n):
+    return (f - jnp.arange(n)) % n
 
 
 def exclusive_prefix(block):
@@ -77,7 +78,10 @@
     rows_xy = lax.all_gather(local_xy, "feat", axis=0, tiled=True)
     own = lax.dynamic_slice_in_dim(rows_xy, col_start, block_rows, 1)
     moments = exclusive_prefix(lax.dot_general(own, rows_xy, contract, preferred_element_type=jnp.float32))
-    gram_prefix = moments[:, :width]
+    fi = lax.axis_index("feat")
+    gram_prefix = jnp.take(
+        moments[:, :width].reshape(block_rows, feat_count, block_rows), own_order(fi, feat_count), axis=1
+    ).reshape(block_rows, width)
     cross_prefix = gather_feat(moments[:, width:])
     span = (lax.axis_index("x") * lax.axis_size("z") + lax.axis_index("z")) * lax.axis_size("c") + lax.axis_index("c")
     seen = (span * (tok_dev * feat_count)).astype(jnp.float32)
@@ -90,9 +94,14 @@
     solution = None
     for step in range(ITERS):
         product = jnp.dot(gram_prefix, direction, precision=lax.Precision.HIGH, preferred_element_type=jnp.float32)
-        own_dir = lax.dynamic_slice_in_dim(direction, col_start, block_rows, 0)
-        image = gather_feat(scale * product + RIDGE * own_dir)
-        alpha = norm_now / (jnp.sum(direction * image, axis=0) + TINY)
+        own_image = scale * product + RIDGE * direction[:block_rows]
+        if step + 1 < ITERS:
+            image = gather_feat(own_image)
+            curvature = jnp.sum(direction * image, axis=0)
+        else:
+            partial = jnp.sum(direction[:block_rows] * own_image, axis=0, keepdims=True)
+            curvature = jnp.sum(gather_feat(partial), axis=0)
+        alpha = norm_now / (curvature + TINY)
         update = alpha * direction
         solution = update if solution is None else solution + update
         if step + 1 < ITERS:
@@ -100,7 +109,10 @@
             norm_next = jnp.sum(residual * residual, axis=0)
             direction = residual + norm_next / (norm_now + TINY) * direction
             norm_now = norm_next
-    weights = solution.astype(jnp.bfloat16)
+    weights = jnp.take(
+        solution.astype(jnp.bfloat16).reshape(feat_count, block_rows, n_targets),
+        own_order(fi, feat_count), axis=0,
+    ).reshape(width, n_targets)
     predicted = jnp.dot(local_x, weights, preferred_element_type=jnp.float32).astype(jnp.bfloat16)
     returned = lax.all_to_all(
         predicted.reshape(spans, share, n_targets), TM, split_axis=0, concat_axis=0, tiled=True

time: 494 us -> 479 us (0.970)
  waiting for transfers between devices: 322 us -> 303 us
    ppermute x12, waiting for transfers between devices: 44.7 us -> 26.7 us  [gather_feat(): lax.ppermute(piece, 'feat', [(i, (i + k) % n) for i in range(n)])]
    gather x4 -> x3, local copies, waits for them, and re-layouts: 6.6 us -> 11.6 us  [the longest x2 10.2 us: body(): jnp.take(moments[:, :width].reshape(block_rows, feat_count, block_rows),...]
  transfers between devices with their start and end apart: 19 -> 19, of which waited for: 17 -> 14; matrix products, arithmetic and copies ran while one was open for 0% -> 3% of each run, Pallas kernels for 0% -> 0%
where the time goes in v11:
time: 479 us; the launch traced here: 478 us
  waiting for transfers between devices  303 us (63%)
  blocking collectives  51.3 us (11%)
  matrix products  31.2 us (7%)
  other arithmetic  27.6 us (6%)
  local copies, waits for them, and re-layouts  26.2 us (5%)
  starting transfers between devices  24.5 us (5%)
  between operations  14 us (3%)
    all_gather x1, waiting for transfers between devices, body(): rows_xy = lax.all_gather(local_xy, 'feat', axis=0, tiled=True)  104 us
    all_gather x1, waiting for transfers between devices, exclusive_prefix(): along_z = lax.all_gather(mine, 'z')  88.1 us
    all_to_all x1, blocking collectives, body(): lax.all_to_all(sorted_xy, TM, split_axis=0, concat_axis=0, tiled=True)  51.3 us
    all_gather x1, waiting for transfers between devices, exclusive_prefix(): along_x = lax.all_gather(piece, 'x')  32.8 us
    all_gather x1, waiting for transfers between devices, exclusive_prefix(): before_x = lax.all_gather(masked_sum(along_x, xi), 'z', axis=0, tiled=True)  32.3 us
    ppermute x12, waiting for transfers between devices, gather_feat(): lax.ppermute(piece, 'feat', [(i, (i + k) % n) for i in range(n)])  26.7 us
    ppermute x12, starting transfers between devices, gather_feat(): lax.ppermute(piece, 'feat', [(i, (i + k) % n) for i in range(n)])  14 us
    dot_general x1, matrix products, body(): lax.dot_general(own, rows_xy, contract, preferred_element_type=jnp.float32)  12.6 us
  transfers between devices with their start and end apart: 19, of which 14 were waited for; matrix products, arithmetic and copies ran while one was open for 3% of the time, Pallas kernels for 0%

profile of v11, /device:TPU:1, one launch (start us, length us, event | category | flops | bytes accessed | tf_op | source)
XLA Modules:
  0.0 478.1 jit_solution(10993216246403534223)
XLA Ops:
  7.2 1.1 fusion.19
  9.0 5.8 %convolution_convert_fusion = bf16[640,2176]{1,0:T(8,128)(2,1)} fusion(bf16[640,128]{1,0:T(8,128)(2,1)} %param.4, bf16[640,2048]{1,0:T(8,128)(2,1)} %param.3, s32[640]{0:T(1024)S(1)} %convert_add_fusion), kind=kOutput, calls=%fused_computation.3 | convolution fusion | flops 1789952000 | bytes 5573120 | tf_op jit(solution)/shard_map/dot_general | solution.py:72
  14.8 3.6 reshape.169
  18.3 51.3 %all_to_all.10 = bf16[32,20,2176]{2,1,0:T(8,128)(2,1)} all-to-all(bf16[32,20,2176]{2,1,0:T(8,128)(2,1)S(1)} %reshape.169), channel_id=1, replica_groups=mesh['x'=4,'z'=4,'c'=2,'feat'=4] {'x','z','c'}, dimensions={0} | all-to-all | bytes 5570560 | tf_op jit(solution)/shard_map/all_to_all | solution.py:74
  69.7 5.3 %reshape.170 = bf16[640,2176]{1,0:T(8,128)(2,1)} reshape(bf16[32,20,2176]{2,1,0:T(8,128)(2,1)} %all_to_all.10) | data formatting | bytes 5570560 | tf_op jit(solution)/shard_map/reshape | solution.py:75
  75.0 103.8 %all-gather.7.cloned.1.call-done = bf16[2560,2176]{1,0:T(8,128)(2,1)} async-done(((bf16[640,2176]{1,0:T(8,128)(2,1)}), bf16[2560,2176]{1,0:T(8,128)(2,1)}) %all-gather.7.cloned.1.call-update) | async-done | bytes 11141136 | tf_op jit(solution)/shard_map/all_gather | solution.py:78
  178.8 12.6 %fusion.5 = f32[512,2176]{1,0:T(8,128)} fusion(bf16[2560,2176]{1,0:T(8,128)(2,1)} %all-gather.7.cloned.1.call-done, s32[]{:T(128)S(6)} %select_n.88), kind=kOutput, calls=%fused_computation.12 | convolution fusion | flops 5704253440 | bytes 18219012 | tf_op jit(solution)/shard_map/dot_general | solution.py:80
  191.4 0.8 collective-permute-start
  192.3 7.5 %collective-permute-done = f32[512,2176]{1,0:T(8,128)} collective-permute-done((f32[512,2176]{1,0:T(8,128)}, f32[512,2176]{1,0:T(8,128)}, u32[]{:S(2)}, u32[]{:S(2)}) %collective-permute-start) | collective-permute-done | bytes 4456480 | tf_op jit(solution)/shard_map/ppermute | solution.py:37
  199.8 3.9 dynamic-slice_add_fusion
  203.8 88.1 %all-gather.11.cloned.1.call-done = f32[1024,2176]{1,0:T(8,128)} async-done(((f32[256,2176]{1,0:T(8,128)}), f32[1024,2176]{1,0:T(8,128)}) %all-gather.11.cloned.1.call-update) | async-done | bytes 8912912 | tf_op jit(solution)/shard_map/all_gather | solution.py:41
  291.8 6.5 %select_reduce_fusion = (f32[256,2176]{1,0:T(8,128)}, f32[256,2176]{1,0:T(8,128)S(1)}) fusion(f32[4,256,2176]{2,1,0:T(8,128)} %bitcast.40, pred[4]{0:T(512)(128)(4,1)S(1)} %iota_compare_fusion.13), kind=kLoop, calls=%fused_computation.2 | loop fusion | flops 5570560 | bytes 13369348 | tf_op jit(solution)/shard_map/reduce_sum | solution.py:18
  298.3 0.8 constant_dynamic-slice_fusion
  299.2 32.8 %all-gather.13.cloned.1.call-done = f32[256,2176]{1,0:T(8,128)} async-done(((f32[64,2176]{1,0:T(8,128)}), f32[256,2176]{1,0:T(8,128)}) %all-gather.13.cloned.1.call-update) | async-done | bytes 2228240 | tf_op jit(solution)/shard_map/all_gather | solution.py:46
  332.0 2.7 select_reduce_fusion.1
  334.7 32.3 %all-gather.9.cloned.1.call-done = f32[256,2176]{1,0:T(8,128)} async-done(((f32[64,2176]{1,0:T(8,128)}), f32[256,2176]{1,0:T(8,128)}) %all-gather.9.cloned.1.call-update) | async-done | bytes 2228240 | tf_op jit(solution)/shard_map/all_gather | solution.py:47
  367.0 2.5 add.133
  369.6 0.9 collective-permute-start.1
  370.7 3.9 collective-permute-done.1
  374.6 1.9 broadcast_select_fusion.1
  376.5 2.7 maximum_add_fusion
  379.8 1.3 collective-permute-start.2
  381.1 2.4 collective-permute-start.3
  383.5 1.2 collective-permute-start.4
  384.7 2.6 copy.21
  387.3 4.9 %gather_fusion = f32[4,512,512]{2,1,0:T(8,128)} fusion(f32[512,4,512]{2,0,1:T(8,128)} %bitcast.38, s32[1024]{0:T(1024)S(1)} %pad_clamp_fusion), kind=kCustom, calls=%fused_computation | custom fusion | bytes 8388624 | tf_op jit(solution)/shard_map/jit(_take)/gather | solution.py:82
  392.2 5.3 %copy.15 = f32[512,4,512]{0,2,1:T(8,128)} copy(f32[512,4,512]{2,0,1:T(8,128)} %bitcast.39) | data formatting | bytes 8388608 | tf_op jit(solution)/shard_map/jit(_take)/gather | solution.py:82
  397.5 2.5 bitcast_select_fusion
  400.0 3.5 fusion.12
  403.9 0.9 collective-permute-start.6
  404.7 1.6 collective-permute-start.7
  406.4 11.5 %collective-permute-done.5 = f32[512,128]{1,0:T(8,128)S(1)} collective-permute-done((f32[512,128]{1,0:T(8,128)S(1)}, f32[512,128]{1,0:T(8,128)S(1)}, u32[]{:S(2)}, u32[]{:S(2)}) %collective-permute-start.5) | collective-permute-done | bytes 262176 | tf_op jit(solution)/shard_map/ppermute | solution.py:23
  417.8 0.9 collective-permute-done.7
  419.6 3.5 fusion.11
  423.0 2.3 collective-permute-start.10
  425.3 1.3 collective-permute-start.9
  426.5 4.5 collective-permute-done.10
  431.0 8.3 %collective-permute-done.8 = f32[512,128]{1,0:T(8,128)S(1)} collective-permute-done((f32[512,128]{1,0:T(8,128)S(1)}, f32[512,128]{1,0:T(8,128)S(1)}, u32[]{:S(2)}, u32[]{:S(2)}) %collective-permute-start.8) | collective-permute-done | bytes 262176 | tf_op jit(solution)/shard_map/ppermute | solution.py:23
  440.1 3.5 fusion.17
  443.7 1.5 collective-permute-start.12
  445.1 1.2 collective-permute-start.13
  446.3 0.9 collective-permute-done.11
  448.4 1.4 gather_fusion.1
  449.8 1.4 bitcast_select_fusion.1
  451.2 0.9 fusion.13
  452.8 8.6 %all-to-all-start.1 = ((bf16[32,20,128]{2,1,0:T(8,128)(2,1)}), bf16[32,20,128]{2,1,0:T(8,128)(2,1)S(1)}, u32[]{:S(2)}, u32[]{:S(2)}) async-start(bf16[32,20,128]{2,1,0:T(8,128)(2,1)} %reshape.172), calls=%async_computation.1 | async-start | bytes 393216 | tf_op jit(solution)/shard_map/all_to_all | solution.py:117
  461.5 8.1 %all-to-all-done.1 = bf16[32,20,128]{2,1,0:T(8,128)(2,1)S(1)} async-done(((bf16[32,20,128]{2,1,0:T(8,128)(2,1)}), bf16[32,20,128]{2,1,0:T(8,128)(2,1)S(1)}, u32[]{:S(2)}, u32[]{:S(2)}) %all-to-all-start.1) | async-done | bytes 163872 | tf_op jit(solution)/shard_map/all_to_all | solution.py:117
  470.2 0.8 copy.17
  (50 shorter events, 6.8 us)
Async XLA Ops:
  7.2 171.7 %all-gather.7.cloned.1.call-start = ((), (), s32[]{:S(2)}) async-start(), calls=%async_computation.2 | async-start | bytes 13926400 | tf_op jit(solution)/shard_map/all_gather | solution.py:78
  75.0 216.9 %all-gather.11.cloned.1.call-start = ((), (), s32[]{:S(2)}) async-start(), calls=%async_computation.4 | async-start | bytes 11141120 | tf_op jit(solution)/shard_map/all_gather | solution.py:41
  191.4 8.3 %collective-permute-start = (f32[512,2176]{1,0:T(8,128)}, f32[512,2176]{1,0:T(8,128)}, u32[]{:S(2)}, u32[]{:S(2)}) collective-permute-start(f32[512,2176]{1,0:T(8,128)} %fusion.5), channel_id=1, source_target_pairs={{0,4},{4,0},{1,5},{5,1},{2,6},{6,2},{3,7},{7,3},{8,12},{12,8},{9,1... | collective-permute-start | bytes 13369352 | tf_op jit(solution)/shard_map/ppermute | solution.py:37
  203.7 128.3 %all-gather.13.cloned.1.call-start = ((), (), s32[]{:S(2)}) async-start(), calls=%async_computation.5 | async-start | bytes 2785280 | tf_op jit(solution)/shard_map/all_gather | solution.py:46
  299.2 67.9 %all-gather.9.cloned.1.call-start = ((), (), s32[]{:S(2)}) async-start(), calls=%async_computation.3 | async-start | bytes 2785280 | tf_op jit(solution)/shard_map/all_gather | solution.py:47
  369.6 5.0 %collective-permute-start.1 = (f32[256,2176]{1,0:T(8,128)S(1)}, f32[256,2176]{1,0:T(8,128)}, u32[]{:S(2)}, u32[]{:S(2)}) collective-permute-start(f32[256,2176]{1,0:T(8,128)S(1)} %add.133), channel_id=1, source_target_pairs={{0,4},{4,0},{1,5},{5,1},{2,6},{6,2},{3,7},{7,3},{8,12},{12,8},{9,1... | collective-permute-start | bytes 6684680 | tf_op jit(solution)/shard_map/ppermute | solution.py:49
  379.8 20.1 %collective-permute-start.2 = (f32[512,128]{1,0:T(8,128)S(1)}, f32[512,128]{1,0:T(8,128)S(1)}, u32[]{:S(2)}, u32[]{:S(2)}) collective-permute-start(f32[512,128]{1,0:T(8,128)S(1)} %slice.30), channel_id=1, source_target_pairs={{0,1},{1,2},{2,3},{3,0},{4,5},{5,6},{6,7},{7,4},{8,9},{9,10},{10,1... | collective-permute-start | bytes 786440 | tf_op jit(solution)/shard_map/ppermute | solution.py:23
  381.1 18.8 %collective-permute-start.3 = (f32[512,128]{1,0:T(8,128)S(1)}, f32[512,128]{1,0:T(8,128)S(1)}, u32[]{:S(2)}, u32[]{:S(2)}) collective-permute-start(f32[512,128]{1,0:T(8,128)S(1)} %slice.30), channel_id=1, source_target_pairs={{0,2},{1,3},{2,0},{3,1},{4,6},{5,7},{6,4},{7,5},{8,10},{9,11},{10,... | collective-permute-start | bytes 786440 | tf_op jit(solution)/shard_map/ppermute | solution.py:23
  383.5 16.4 %collective-permute-start.4 = (f32[512,128]{1,0:T(8,128)S(1)}, f32[512,128]{1,0:T(8,128)S(1)}, u32[]{:S(2)}, u32[]{:S(2)}) collective-permute-start(f32[512,128]{1,0:T(8,128)S(1)} %slice.30), channel_id=1, source_target_pairs={{0,3},{1,0},{2,1},{3,2},{4,7},{5,4},{6,5},{7,6},{8,11},{9,8},{10,9... | collective-permute-start | bytes 786440 | tf_op jit(solution)/shard_map/ppermute | solution.py:23
  403.5 14.3 %collective-permute-start.5 = (f32[512,128]{1,0:T(8,128)S(1)}, f32[512,128]{1,0:T(8,128)S(1)}, u32[]{:S(2)}, u32[]{:S(2)}) collective-permute-start(f32[512,128]{1,0:T(8,128)S(1)} %fusion.12), channel_id=1, source_target_pairs={{0,1},{1,2},{2,3},{3,0},{4,5},{5,6},{6,7},{7,4},{8,9},{9,10},{10,1... | collective-permute-start | bytes 786440 | tf_op jit(solution)/shard_map/ppermute | solution.py:23
  403.9 14.0 %collective-permute-start.6 = (f32[512,128]{1,0:T(8,128)S(1)}, f32[512,128]{1,0:T(8,128)S(1)}, u32[]{:S(2)}, u32[]{:S(2)}) collective-permute-start(f32[512,128]{1,0:T(8,128)S(1)} %fusion.12), channel_id=1, source_target_pairs={{0,2},{1,3},{2,0},{3,1},{4,6},{5,7},{6,4},{7,5},{8,10},{9,11},{10,... | collective-permute-start | bytes 786440 | tf_op jit(solution)/shard_map/ppermute | solution.py:23
  404.7 14.0 %collective-permute-start.7 = (f32[512,128]{1,0:T(8,128)S(1)}, f32[512,128]{1,0:T(8,128)S(1)}, u32[]{:S(2)}, u32[]{:S(2)}) collective-permute-start(f32[512,128]{1,0:T(8,128)S(1)} %fusion.12), channel_id=1, source_target_pairs={{0,3},{1,0},{2,1},{3,2},{4,7},{5,4},{6,5},{7,6},{8,11},{9,8},{10,9... | collective-permute-start | bytes 786440 | tf_op jit(solution)/shard_map/ppermute | solution.py:23
  423.0 8.0 %collective-permute-start.10 = (f32[512,128]{1,0:T(8,128)S(1)}, f32[512,128]{1,0:T(8,128)S(1)}, u32[]{:S(2)}, u32[]{:S(2)}) collective-permute-start(f32[512,128]{1,0:T(8,128)S(1)} %fusion.11), channel_id=1, source_target_pairs={{0,3},{1,0},{2,1},{3,2},{4,7},{5,4},{6,5},{7,6},{8,11},{9,8},{10,9... | collective-permute-start | bytes 786440 | tf_op jit(solution)/shard_map/ppermute | solution.py:23
  425.3 14.0 %collective-permute-start.8 = (f32[512,128]{1,0:T(8,128)S(1)}, f32[512,128]{1,0:T(8,128)S(1)}, u32[]{:S(2)}, u32[]{:S(2)}) collective-permute-start(f32[512,128]{1,0:T(8,128)S(1)} %fusion.11), channel_id=1, source_target_pairs={{0,1},{1,2},{2,3},{3,0},{4,5},{5,6},{6,7},{7,4},{8,9},{9,10},{10,1... | collective-permute-start | bytes 786440 | tf_op jit(solution)/shard_map/ppermute | solution.py:23
  425.3 14.0 %collective-permute-start.9 = (f32[512,128]{1,0:T(8,128)S(1)}, f32[512,128]{1,0:T(8,128)S(1)}, u32[]{:S(2)}, u32[]{:S(2)}) collective-permute-start(f32[512,128]{1,0:T(8,128)S(1)} %fusion.11), channel_id=1, source_target_pairs={{0,2},{1,3},{2,0},{3,1},{4,6},{5,7},{6,4},{7,5},{8,10},{9,11},{10,... | collective-permute-start | bytes 786440 | tf_op jit(solution)/shard_map/ppermute | solution.py:23
  443.6 7.6 %copy-start = (bf16[640,2176]{1,0:T(8,128)(2,1)S(1)}, bf16[640,2176]{1,0:T(8,128)(2,1)}, u32[]{:S(2)}) copy-start(bf16[640,2176]{1,0:T(8,128)(2,1)} %reshape.170) | copy-start | bytes 8355844
  443.6 3.7 collective-permute-start.11
  443.7 4.0 collective-permute-start.12
  445.1 2.7 collective-permute-start.13
  449.8 11.6 %copy-start.1 = (bf16[640,128]{1,0:T(8,128)(2,1)S(1)}, bf16[640,128]{1,0:T(8,128)(2,1)}, u32[]{:S(2)}) copy-start(bf16[640,128]{1,0:T(8,128)(2,1)} %param.4) | copy-start | bytes 491524
  452.8 16.9 %all-to-all-start.1 = ((bf16[32,20,128]{2,1,0:T(8,128)(2,1)}), bf16[32,20,128]{2,1,0:T(8,128)(2,1)S(1)}, u32[]{:S(2)}, u32[]{:S(2)}) async-start(bf16[32,20,128]{2,1,0:T(8,128)(2,1)} %reshape.172), calls=%async_computation.1 | async-start | bytes 393216 | tf_op jit(solution)/shard_map/all_to_all | solution.py:117
Sparse Core Ops, SparseCore 0:
  75.1 103.6 all-gather.6
  203.8 87.9 all-gather.10
  299.3 32.6 all-gather.12
  334.9 32.1 all-gather.8

commit v12 on v11

--- a/solution.py
+++ b/solution.py
@@ -20,12 +20,12 @@
 
 def gather_feat(piece):
     n = lax.axis_size("feat")
-    parts = [piece] + [lax.ppermute(piece, "feat", [(i, (i + k) % n) for i in range(n)]) for k in range(1, n)]
+    parts = [piece] + [lax.ppermute(piece, "feat", [(i, (i - k) % n) for i in range(n)]) for k in range(1, n)]
     return jnp.concatenate(parts, axis=0)
 
 
-def own_order(f, n):
-    return (f - jnp.arange(n)) % n
+def rotate(a, start, size, axis):
+    return lax.dynamic_slice_in_dim(jnp.concatenate([a, a], axis=axis), start, size, axis)
 
 
 def exclusive_prefix(block):
@@ -79,9 +79,7 @@
     own = lax.dynamic_slice_in_dim(rows_xy, col_start, block_rows, 1)
     moments = exclusive_prefix(lax.dot_general(own, rows_xy, contract, preferred_element_type=jnp.float32))
     fi = lax.axis_index("feat")
-    gram_prefix = jnp.take(
-        moments[:, :width].reshape(block_rows, feat_count, block_rows), own_order(fi, feat_count), axis=1
-    ).reshape(block_rows, width)
+    gram_prefix = rotate(moments[:, :width], fi * block_rows, width, 1)
     cross_prefix = gather_feat(moments[:, width:])
     span = (lax.axis_index("x") * lax.axis_size("z") + lax.axis_index("z")) * lax.axis_size("c") + lax.axis_index("c")
     seen = (span * (tok_dev * feat_count)).astype(jnp.float32)
@@ -109,10 +107,7 @@
             norm_next = jnp.sum(residual * residual, axis=0)
             direction = residual + norm_next / (norm_now + TINY) * direction
             norm_now = norm_next
-    weights = jnp.take(
-        solution.astype(jnp.bfloat16).reshape(feat_count, block_rows, n_targets),
-        own_order(fi, feat_count), axis=0,
-    ).reshape(width, n_targets)
+    weights = rotate(solution.astype(jnp.bfloat16), ((feat_count - fi) % feat_count) * block_rows, width, 0)
     predicted = jnp.dot(local_x, weights, preferred_element_type=jnp.float32).astype(jnp.bfloat16)
     returned = lax.all_to_all(
         predicted.reshape(spans, share, n_targets), TM, split_axis=0, concat_axis=0, tiled=True

time: 479 us -> 471 us (0.983)
  waiting for transfers between devices: 303 us -> 318 us
  local copies, waits for them, and re-layouts: 26.2 us -> 13.3 us
    ppermute x12, waiting for transfers between devices: 26.7 us -> 40.9 us  [gather_feat(): lax.ppermute(piece, 'feat', [(i, (i - k) % n) for i in range(n)])]
    gather x3 -> x0, local copies, waits for them, and re-layouts: 11.6 us -> none  [the longest x2 10.2 us: body(): jnp.take(moments[:, :width].reshape(block_rows, feat_count, block_rows),...]
    dot_general x3, matrix products: 10.4 us -> 5.47 us  [body(): jnp.dot(gram_prefix, direction, precision=lax.Precision.HIGH, preferred_e...]
  transfers between devices with their start and end apart: 19 -> 19, of which waited for: 14 -> 14; matrix products, arithmetic and copies ran while one was open for 3% -> 0% of each run, Pallas kernels for 0% -> 0%
where the time goes in v12:
time: 471 us
  waiting for transfers between devices  318 us (68%)
  blocking collectives  51.3 us (11%)
  matrix products  27.4 us (6%)
  other arithmetic  25.3 us (5%)
  starting transfers between devices  21.5 us (5%)
  between operations  14 us (3%)
  local copies, waits for them, and re-layouts  13.3 us (3%)
    all_gather x1, waiting for transfers between devices, body(): rows_xy = lax.all_gather(local_xy, 'feat', axis=0, tiled=True)  104 us
    all_gather x1, waiting for transfers between devices, exclusive_prefix(): along_z = lax.all_gather(mine, 'z')  88.2 us
    all_to_all x1, blocking collectives, body(): lax.all_to_all(sorted_xy, TM, split_axis=0, concat_axis=0, tiled=True)  51.3 us
    ppermute x12, waiting for transfers between devices, gather_feat(): lax.ppermute(piece, 'feat', [(i, (i - k) % n) for i in range(n)])  40.9 us
    all_gather x1, waiting for transfers between devices, exclusive_prefix(): along_x = lax.all_gather(piece, 'x')  32.8 us
    all_gather x1, waiting for transfers between devices, exclusive_prefix(): before_x = lax.all_gather(masked_sum(along_x, xi), 'z', axis=0, tiled=True)  32.3 us
    dot_general x1, matrix products, body(): lax.dot_general(own, rows_xy, contract, preferred_element_type=jnp.float32)  12.5 us
    ppermute x12, starting transfers between devices, gather_feat(): lax.ppermute(piece, 'feat', [(i, (i - k) % n) for i in range(n)])  11 us
  transfers between devices with their start and end apart: 19, of which 14 were waited for; matrix products, arithmetic and copies ran while one was open for 0% of the time, Pallas kernels for 0%

profile of v12, /device:TPU:1, one launch (start us, length us, event | category | flops | bytes accessed | tf_op | source)
XLA Modules:
  0.0 470.7 jit_solution(7356976778085991904)
XLA Ops:
  7.2 1.1 fusion.20
  8.3 0.7 convert_add_fusion
  9.0 5.8 %convolution_convert_fusion = bf16[640,2176]{1,0:T(8,128)(2,1)} fusion(bf16[640,128]{1,0:T(8,128)(2,1)} %param.4, bf16[640,2048]{1,0:T(8,128)(2,1)} %param.3, s32[640]{0:T(1024)S(1)} %convert_add_fusion), kind=kOutput, calls=%fused_computation.3 | convolution fusion | flops 1789952000 | bytes 5573120 | tf_op jit(solution)/shard_map/dot_general | solution.py:72
  14.8 3.6 reshape.65
  18.3 51.3 %all_to_all.10 = bf16[32,20,2176]{2,1,0:T(8,128)(2,1)} all-to-all(bf16[32,20,2176]{2,1,0:T(8,128)(2,1)S(1)} %reshape.65), channel_id=1, replica_groups=mesh['x'=4,'z'=4,'c'=2,'feat'=4] {'x','z','c'}, dimensions={0} | all-to-all | bytes 5570560 | tf_op jit(solution)/shard_map/all_to_all | solution.py:74
  69.7 5.3 %reshape.66 = bf16[640,2176]{1,0:T(8,128)(2,1)} reshape(bf16[32,20,2176]{2,1,0:T(8,128)(2,1)} %all_to_all.10) | data formatting | bytes 5570560 | tf_op jit(solution)/shard_map/reshape | solution.py:75
  75.0 103.8 %all-gather.7.cloned.1.call-done = bf16[2560,2176]{1,0:T(8,128)(2,1)} async-done(((bf16[640,2176]{1,0:T(8,128)(2,1)}), bf16[2560,2176]{1,0:T(8,128)(2,1)}) %all-gather.7.cloned.1.call-update) | async-done | bytes 11141136 | tf_op jit(solution)/shard_map/all_gather | solution.py:78
  178.8 12.5 %fusion.6 = f32[512,2176]{1,0:T(8,128)} fusion(bf16[2560,2176]{1,0:T(8,128)(2,1)} %all-gather.7.cloned.1.call-done, s32[]{:T(128)S(6)} %select_n.51), kind=kOutput, calls=%fused_computation.11 | convolution fusion | flops 5704253440 | bytes 18219012 | tf_op jit(solution)/shard_map/dot_general | solution.py:80
  191.2 0.8 collective-permute-start
  192.1 7.5 %collective-permute-done = f32[512,2176]{1,0:T(8,128)} collective-permute-done((f32[512,2176]{1,0:T(8,128)}, f32[512,2176]{1,0:T(8,128)}, u32[]{:S(2)}, u32[]{:S(2)}) %collective-permute-start) | collective-permute-done | bytes 4456480 | tf_op jit(solution)/shard_map/ppermute | solution.py:37
  199.6 3.9 dynamic-slice_add_fusion
  203.6 88.2 %all-gather.11.cloned.1.call-done = f32[1024,2176]{1,0:T(8,128)} async-done(((f32[256,2176]{1,0:T(8,128)}), f32[1024,2176]{1,0:T(8,128)}) %all-gather.11.cloned.1.call-update) | async-done | bytes 8912912 | tf_op jit(solution)/shard_map/all_gather | solution.py:41
  291.8 5.1 %select_reduce_fusion = (f32[256,2176]{1,0:T(8,128)S(1)}, f32[256,2176]{1,0:T(8,128)S(1)}) fusion(f32[4,256,2176]{2,1,0:T(8,128)} %bitcast.18, pred[4]{0:T(512)(128)(4,1)S(1)} %iota_compare_fusion.13), kind=kLoop, calls=%fused_computation | loop fusion | flops 5570560 | bytes 13369348 | tf_op jit(solution)/shard_map/reduce_sum | solution.py:18
  296.9 0.8 constant_dynamic-slice_fusion
  297.9 32.8 %all-gather.13.cloned.1.call-done = f32[256,2176]{1,0:T(8,128)} async-done(((f32[64,2176]{1,0:T(8,128)}), f32[256,2176]{1,0:T(8,128)}) %all-gather.13.cloned.1.call-update) | async-done | bytes 2228240 | tf_op jit(solution)/shard_map/all_gather | solution.py:46
  330.6 2.7 select_reduce_fusion.1
  333.4 32.3 %all-gather.9.cloned.1.call-done = f32[256,2176]{1,0:T(8,128)} async-done(((f32[64,2176]{1,0:T(8,128)}), f32[256,2176]{1,0:T(8,128)}) %all-gather.9.cloned.1.call-update) | async-done | bytes 2228240 | tf_op jit(solution)/shard_map/all_gather | solution.py:47
  365.7 3.2 add.97
  368.9 0.8 collective-permute-start.1
  369.7 4.1 collective-permute-done.1
  373.9 1.9 broadcast_select_fusion.1
  375.8 2.7 maximum_add_fusion
  378.5 0.5 slice.27
  379.1 2.5 collective-permute-start.2
  382.2 0.6 collective-permute-start.4
  382.8 1.0 fusion
  383.8 8.2 %collective-permute-done.2 = f32[512,128]{1,0:T(8,128)S(1)} collective-permute-done((f32[512,128]{1,0:T(8,128)S(1)}, f32[512,128]{1,0:T(8,128)S(1)}, u32[]{:S(2)}, u32[]{:S(2)}) %collective-permute-start.2) | collective-permute-done | bytes 262176 | tf_op jit(solution)/shard_map/ppermute | solution.py:23
  392.0 3.9 collective-permute-done.4
  395.9 1.8 fusion.13
  398.5 0.8 collective-permute-start.7
  399.3 6.0 %collective-permute-done.5 = f32[512,128]{1,0:T(8,128)S(1)} collective-permute-done((f32[512,128]{1,0:T(8,128)S(1)}, f32[512,128]{1,0:T(8,128)S(1)}, u32[]{:S(2)}, u32[]{:S(2)}) %collective-permute-start.5) | collective-permute-done | bytes 262176 | tf_op jit(solution)/shard_map/ppermute | solution.py:23
  405.3 1.7 collective-permute-done.6
  407.0 6.3 %collective-permute-done.7 = f32[512,128]{1,0:T(8,128)S(1)} collective-permute-done((f32[512,128]{1,0:T(8,128)S(1)}, f32[512,128]{1,0:T(8,128)S(1)}, u32[]{:S(2)}, u32[]{:S(2)}) %collective-permute-start.7) | collective-permute-done | bytes 262176 | tf_op jit(solution)/shard_map/ppermute | solution.py:23
  414.2 1.8 fusion.12
  416.1 2.7 collective-permute-start.8
  418.7 11.5 %collective-permute-done.10 = f32[512,128]{1,0:T(8,128)S(1)} collective-permute-done((f32[512,128]{1,0:T(8,128)S(1)}, f32[512,128]{1,0:T(8,128)S(1)}, u32[]{:S(2)}, u32[]{:S(2)}) %collective-permute-start.10) | collective-permute-done | bytes 262176 | tf_op jit(solution)/shard_map/ppermute | solution.py:23
  431.2 1.9 multiply_reduce_fusion
  433.1 0.7 copy-done.1
  433.9 1.9 fusion.18
  435.8 2.4 collective-permute-start.11
  438.1 0.7 collective-permute-start.13
  438.9 3.2 collective-permute-done.12
  442.4 2.2 fusion.14
  444.6 0.7 reshape.67
  445.3 8.7 %all-to-all-start.1 = ((bf16[32,20,128]{2,1,0:T(8,128)(2,1)}), bf16[32,20,128]{2,1,0:T(8,128)(2,1)S(1)}, u32[]{:S(2)}, u32[]{:S(2)}) async-start(bf16[32,20,128]{2,1,0:T(8,128)(2,1)} %reshape.67), calls=%async_computation.1 | async-start | bytes 393216 | tf_op jit(solution)/shard_map/all_to_all | solution.py:112
  454.1 8.1 %all-to-all-done.1 = bf16[32,20,128]{2,1,0:T(8,128)(2,1)S(1)} async-done(((bf16[32,20,128]{2,1,0:T(8,128)(2,1)}), bf16[32,20,128]{2,1,0:T(8,128)(2,1)S(1)}, u32[]{:S(2)}, u32[]{:S(2)}) %all-to-all-start.1) | async-done | bytes 163872 | tf_op jit(solution)/shard_map/all_to_all | solution.py:112
  462.8 0.8 copy.10
  463.6 0.6 broadcast_multiply_fusion
  (58 shorter events, 4.5 us)
Async XLA Ops:
  7.2 171.6 %all-gather.7.cloned.1.call-start = ((), (), s32[]{:S(2)}) async-start(), calls=%async_computation.2 | async-start | bytes 13926400 | tf_op jit(solution)/shard_map/all_gather | solution.py:78
  74.9 216.8 %all-gather.11.cloned.1.call-start = ((), (), s32[]{:S(2)}) async-start(), calls=%async_computation.4 | async-start | bytes 11141120 | tf_op jit(solution)/shard_map/all_gather | solution.py:41
  191.2 8.3 %collective-permute-start = (f32[512,2176]{1,0:T(8,128)}, f32[512,2176]{1,0:T(8,128)}, u32[]{:S(2)}, u32[]{:S(2)}) collective-permute-start(f32[512,2176]{1,0:T(8,128)} %fusion.6), channel_id=1, source_target_pairs={{0,4},{4,0},{1,5},{5,1},{2,6},{6,2},{3,7},{7,3},{8,12},{12,8},{9,1... | collective-permute-start | bytes 13369352 | tf_op jit(solution)/shard_map/ppermute | solution.py:37
  203.5 127.1 %all-gather.13.cloned.1.call-start = ((), (), s32[]{:S(2)}) async-start(), calls=%async_computation.5 | async-start | bytes 2785280 | tf_op jit(solution)/shard_map/all_gather | solution.py:46
  297.8 67.9 %all-gather.9.cloned.1.call-start = ((), (), s32[]{:S(2)}) async-start(), calls=%async_computation.3 | async-start | bytes 2785280 | tf_op jit(solution)/shard_map/all_gather | solution.py:47
  368.9 5.0 %collective-permute-start.1 = (f32[256,2176]{1,0:T(8,128)}, f32[256,2176]{1,0:T(8,128)S(1)}, u32[]{:S(2)}, u32[]{:S(2)}) collective-permute-start(f32[256,2176]{1,0:T(8,128)} %add.97), channel_id=1, source_target_pairs={{0,4},{4,0},{1,5},{5,1},{2,6},{6,2},{3,7},{7,3},{8,12},{12,8},{9,1... | collective-permute-start | bytes 6684680 | tf_op jit(solution)/shard_map/ppermute | solution.py:49
  379.1 12.9 %collective-permute-start.2 = (f32[512,128]{1,0:T(8,128)S(1)}, f32[512,128]{1,0:T(8,128)S(1)}, u32[]{:S(2)}, u32[]{:S(2)}) collective-permute-start(f32[512,128]{1,0:T(8,128)S(1)} %slice.26), channel_id=1, source_target_pairs={{0,3},{1,0},{2,1},{3,2},{4,7},{5,4},{6,5},{7,6},{8,11},{9,8},{10,9... | collective-permute-start | bytes 786440 | tf_op jit(solution)/shard_map/ppermute | solution.py:23
  381.6 10.3 %collective-permute-start.3 = (f32[512,128]{1,0:T(8,128)S(1)}, f32[512,128]{1,0:T(8,128)S(1)}, u32[]{:S(2)}, u32[]{:S(2)}) collective-permute-start(f32[512,128]{1,0:T(8,128)S(1)} %slice.26), channel_id=1, source_target_pairs={{0,2},{1,3},{2,0},{3,1},{4,6},{5,7},{6,4},{7,5},{8,10},{9,11},{10,... | collective-permute-start | bytes 786440 | tf_op jit(solution)/shard_map/ppermute | solution.py:23
  382.2 13.7 %collective-permute-start.4 = (f32[512,128]{1,0:T(8,128)S(1)}, f32[512,128]{1,0:T(8,128)S(1)}, u32[]{:S(2)}, u32[]{:S(2)}) collective-permute-start(f32[512,128]{1,0:T(8,128)S(1)} %slice.26), channel_id=1, source_target_pairs={{0,1},{1,2},{2,3},{3,0},{4,5},{5,6},{6,7},{7,4},{8,9},{9,10},{10,1... | collective-permute-start | bytes 786440 | tf_op jit(solution)/shard_map/ppermute | solution.py:23
  383.8 30.4 %copy-start = (f32[512,2048]{1,0:T(8,128)}, f32[512,2048]{1,0:T(8,128)S(1)}, u32[]{:S(2)}) copy-start(f32[512,2048]{1,0:T(8,128)S(1)} %fusion) | copy-start | bytes 12582916
  397.7 7.5 %collective-permute-start.5 = (f32[512,128]{1,0:T(8,128)S(1)}, f32[512,128]{1,0:T(8,128)S(1)}, u32[]{:S(2)}, u32[]{:S(2)}) collective-permute-start(f32[512,128]{1,0:T(8,128)S(1)} %fusion.13), channel_id=1, source_target_pairs={{0,3},{1,0},{2,1},{3,2},{4,7},{5,4},{6,5},{7,6},{8,11},{9,8},{10,9... | collective-permute-start | bytes 786440 | tf_op jit(solution)/shard_map/ppermute | solution.py:23
  397.9 9.0 %collective-permute-start.6 = (f32[512,128]{1,0:T(8,128)S(1)}, f32[512,128]{1,0:T(8,128)S(1)}, u32[]{:S(2)}, u32[]{:S(2)}) collective-permute-start(f32[512,128]{1,0:T(8,128)S(1)} %fusion.13), channel_id=1, source_target_pairs={{0,2},{1,3},{2,0},{3,1},{4,6},{5,7},{6,4},{7,5},{8,10},{9,11},{10,... | collective-permute-start | bytes 786440 | tf_op jit(solution)/shard_map/ppermute | solution.py:23
  398.5 14.8 %collective-permute-start.7 = (f32[512,128]{1,0:T(8,128)S(1)}, f32[512,128]{1,0:T(8,128)S(1)}, u32[]{:S(2)}, u32[]{:S(2)}) collective-permute-start(f32[512,128]{1,0:T(8,128)S(1)} %fusion.13), channel_id=1, source_target_pairs={{0,1},{1,2},{2,3},{3,0},{4,5},{5,6},{6,7},{7,4},{8,9},{9,10},{10,1... | collective-permute-start | bytes 786440 | tf_op jit(solution)/shard_map/ppermute | solution.py:23
  405.3 8.7 %copy-start.3 = (f32[512,128]{1,0:T(8,128)}, f32[512,128]{1,0:T(8,128)S(1)}, u32[]{:S(2)}) copy-start(f32[512,128]{1,0:T(8,128)S(1)} %collective-permute-done.5) | copy-start | bytes 786436
  407.0 7.0 %copy-start.4 = (f32[512,128]{1,0:T(8,128)}, f32[512,128]{1,0:T(8,128)S(1)}, u32[]{:S(2)}) copy-start(f32[512,128]{1,0:T(8,128)S(1)} %collective-permute-done.6) | copy-start | bytes 786436
  413.3 0.7 copy-start.5
  416.0 14.6 %copy-start.6 = (f32[512,128]{1,0:T(8,128)}, f32[512,128]{1,0:T(8,128)S(1)}, u32[]{:S(2)}) copy-start(f32[512,128]{1,0:T(8,128)S(1)} %fusion.12) | copy-start | bytes 786436
  416.0 14.3 %collective-permute-start.10 = (f32[512,128]{1,0:T(8,128)S(1)}, f32[512,128]{1,0:T(8,128)S(1)}, u32[]{:S(2)}, u32[]{:S(2)}) collective-permute-start(f32[512,128]{1,0:T(8,128)S(1)} %fusion.12), channel_id=1, source_target_pairs={{0,1},{1,2},{2,3},{3,0},{4,5},{5,6},{6,7},{7,4},{8,9},{9,10},{10,1... | collective-permute-start | bytes 786440 | tf_op jit(solution)/shard_map/ppermute | solution.py:23
  416.1 14.2 %collective-permute-start.8 = (f32[512,128]{1,0:T(8,128)S(1)}, f32[512,128]{1,0:T(8,128)S(1)}, u32[]{:S(2)}, u32[]{:S(2)}) collective-permute-start(f32[512,128]{1,0:T(8,128)S(1)} %fusion.12), channel_id=1, source_target_pairs={{0,3},{1,0},{2,1},{3,2},{4,7},{5,4},{6,5},{7,6},{8,11},{9,8},{10,9... | collective-permute-start | bytes 786440 | tf_op jit(solution)/shard_map/ppermute | solution.py:23
  418.7 11.5 %collective-permute-start.9 = (f32[512,128]{1,0:T(8,128)S(1)}, f32[512,128]{1,0:T(8,128)S(1)}, u32[]{:S(2)}, u32[]{:S(2)}) collective-permute-start(f32[512,128]{1,0:T(8,128)S(1)} %fusion.12), channel_id=1, source_target_pairs={{0,2},{1,3},{2,0},{3,1},{4,6},{5,7},{6,4},{7,5},{8,10},{9,11},{10,... | collective-permute-start | bytes 786440 | tf_op jit(solution)/shard_map/ppermute | solution.py:23
  430.3 0.7 copy-start.7
  430.3 0.8 copy-start.8
  430.3 0.9 copy-start.9
  431.1 2.7 copy-start.1
  435.8 3.1 collective-permute-start.11
  438.1 3.9 collective-permute-start.12
  438.1 3.9 collective-permute-start.13
  438.8 3.6 copy-start.2
  442.4 11.6 %copy-start.10 = (bf16[640,128]{1,0:T(8,128)(2,1)S(1)}, bf16[640,128]{1,0:T(8,128)(2,1)}, u32[]{:S(2)}) copy-start(bf16[640,128]{1,0:T(8,128)(2,1)} %param.4) | copy-start | bytes 491524
  445.3 17.0 %all-to-all-start.1 = ((bf16[32,20,128]{2,1,0:T(8,128)(2,1)}), bf16[32,20,128]{2,1,0:T(8,128)(2,1)S(1)}, u32[]{:S(2)}, u32[]{:S(2)}) async-start(bf16[32,20,128]{2,1,0:T(8,128)(2,1)} %reshape.67), calls=%async_computation.1 | async-start | bytes 393216 | tf_op jit(solution)/shard_map/all_to_all | solution.py:112
Sparse Core Ops, SparseCore 0:
  75.1 103.6 all-gather.6
  203.6 88.1 all-gather.10
  297.9 32.6 all-gather.12
  333.5 32.1 all-gather.8

commit v13 on v12

--- a/solution.py
+++ b/solution.py
@@ -34,17 +34,18 @@
     xi = lax.axis_index("x")
     rows = block.shape[0]
     half = rows // 2
-    partner = lax.ppermute(block, "c", SWAP)
-    chip = block + partner
-    below = jnp.where(ci == 1, partner, 0.0)
-    mine = lax.dynamic_slice_in_dim(chip, ci * half, half, 0)
+    wanted = lax.dynamic_slice_in_dim(block, (1 - ci) * half, half, 0)
+    partner_half = lax.ppermute(wanted, "c", SWAP)
+    mine = lax.dynamic_slice_in_dim(block, ci * half, half, 0) + partner_half
+    rest = lax.ppermute(lax.dynamic_slice_in_dim(block, 0, half, 0), "c", [(0, 1)])
+    below = jnp.where(ci == 1, jnp.concatenate([rest, partner_half], axis=0), 0.0)
     along_z = lax.all_gather(mine, "z")
     before_z = masked_sum(along_z, zi)
     total_z = jnp.sum(along_z, axis=0)
     quarter = half // lax.axis_size("z")
     piece = lax.dynamic_slice_in_dim(total_z, zi * quarter, quarter, 0)
-    along_x = lax.all_gather(piece, "x")
-    before_x = lax.all_gather(masked_sum(along_x, xi), "z", axis=0, tiled=True)
+    along_x = lax.all_gather(piece, ("x", "z")).reshape((lax.axis_size("x"), lax.axis_size("z")) + piece.shape)
+    before_x = masked_sum(along_x, xi).reshape(total_z.shape)
     mine_prefix = before_x + before_z
     other_prefix = lax.ppermute(mine_prefix, "c", SWAP)
     first = ci == 0

time: 471 us -> 479 us (1.017)
  waiting for transfers between devices: 318 us -> 325 us
    all_gather x2 -> x1, waiting for transfers between devices: 65.1 us -> 74.3 us  [exclusive_prefix(): lax.all_gather(piece, ('x', 'z'))]
    reduce_sum x0 -> x1, other arithmetic: none -> 6.45 us  [exclusive_prefix(): total_z = jnp.sum(along_z, axis=0)]
  transfers between devices with their start and end apart: 19 -> 19, of which waited for: 14 -> 17; matrix products, arithmetic and copies ran while one was open for 0% -> 1% of each run, Pallas kernels for 0% -> 0%
where the time goes in v13:
time: 479 us; the launch traced here: 478 us
  waiting for transfers between devices  325 us (68%)
  blocking collectives  51.3 us (11%)
  other arithmetic  25.3 us (5%)
  matrix products  25.2 us (5%)
  starting transfers between devices  20.4 us (4%)
  local copies, waits for them, and re-layouts  16.8 us (4%)
  between operations  14.1 us (3%)
    all_gather x1, waiting for transfers between devices, body(): rows_xy = lax.all_gather(local_xy, 'feat', axis=0, tiled=True)  104 us
    all_gather x1, waiting for transfers between devices, exclusive_prefix(): along_z = lax.all_gather(mine, 'z')  87.7 us
    all_gather x1, waiting for transfers between devices, exclusive_prefix(): lax.all_gather(piece, ('x', 'z'))  74.3 us
    all_to_all x1, blocking collectives, body(): lax.all_to_all(sorted_xy, TM, split_axis=0, concat_axis=0, tiled=True)  51.3 us
    ppermute x12, waiting for transfers between devices, gather_feat(): lax.ppermute(piece, 'feat', [(i, (i - k) % n) for i in range(n)])  42.7 us
    dot_general x1, matrix products, body(): lax.dot_general(own, rows_xy, contract, preferred_element_type=jnp.float32)  10.3 us
    ppermute x12, starting transfers between devices, gather_feat(): lax.ppermute(piece, 'feat', [(i, (i - k) % n) for i in range(n)])  10 us
  transfers between devices with their start and end apart: 19, of which 17 were waited for; matrix products, arithmetic and copies ran while one was open for 1% of the time, Pallas kernels for 0%

profile of v13, /device:TPU:1, one launch (start us, length us, event | category | flops | bytes accessed | tf_op | source)
XLA Modules:
  0.0 477.9 jit_solution(15036446819078923013)
XLA Ops:
  7.2 1.1 fusion.20
  9.0 5.8 %convolution_convert_fusion = bf16[640,2176]{1,0:T(8,128)(2,1)} fusion(bf16[640,128]{1,0:T(8,128)(2,1)} %param.4, bf16[640,2048]{1,0:T(8,128)(2,1)} %param.3, s32[640]{0:T(1024)S(1)} %convert_add_fusion), kind=kOutput, calls=%fused_computation.4 | convolution fusion | flops 1789952000 | bytes 5573120 | tf_op jit(solution)/shard_map/dot_general | solution.py:73
  14.8 3.6 reshape.71
  18.3 51.3 %all_to_all.10 = bf16[32,20,2176]{2,1,0:T(8,128)(2,1)} all-to-all(bf16[32,20,2176]{2,1,0:T(8,128)(2,1)S(1)} %reshape.71), channel_id=1, replica_groups=mesh['x'=4,'z'=4,'c'=2,'feat'=4] {'x','z','c'}, dimensions={0} | all-to-all | bytes 5570560 | tf_op jit(solution)/shard_map/all_to_all | solution.py:75
  69.7 5.3 %reshape.72 = bf16[640,2176]{1,0:T(8,128)(2,1)} reshape(bf16[32,20,2176]{2,1,0:T(8,128)(2,1)} %all_to_all.10) | data formatting | bytes 5570560 | tf_op jit(solution)/shard_map/reshape | solution.py:76
  75.0 103.8 %all-gather.6.cloned.1.call-done = bf16[2560,2176]{1,0:T(8,128)(2,1)} async-done(((bf16[640,2176]{1,0:T(8,128)(2,1)}), bf16[2560,2176]{1,0:T(8,128)(2,1)}) %all-gather.6.cloned.1.call-update) | async-done | bytes 11141136 | tf_op jit(solution)/shard_map/all_gather | solution.py:79
  178.8 10.3 %fusion.6 = f32[512,2176]{1,0:T(8,128)S(1)} fusion(bf16[2560,2176]{1,0:T(8,128)(2,1)} %all-gather.6.cloned.1.call-done, s32[]{:T(128)S(6)} %select_n.54), kind=kOutput, calls=%fused_computation.13 | convolution fusion | flops 5704253440 | bytes 18219012 | tf_op jit(solution)/shard_map/dot_general | solution.py:81
  189.1 2.6 fusion.32
  191.7 0.9 copy-done.3
  192.6 0.8 collective-permute-start
  193.4 4.2 collective-permute-done
  197.6 4.1 dynamic-slice_add_fusion
  201.8 87.7 %all-gather.8.cloned.1.call-done = f32[1024,2176]{1,0:T(8,128)} async-done(((f32[256,2176]{1,0:T(8,128)}), f32[1024,2176]{1,0:T(8,128)}) %all-gather.8.cloned.1.call-update) | async-done | bytes 8912912 | tf_op jit(solution)/shard_map/all_gather | solution.py:42
  289.5 6.5 %fusion.31 = (f32[256,2176]{1,0:T(8,128)S(1)}, f32[256,2176]{1,0:T(8,128)}) fusion(f32[4,256,2176]{2,1,0:T(8,128)} %bitcast.20, pred[4]{0:T(512)(128)(4,1)S(1)} %iota_compare_fusion.13), kind=kLoop, calls=%fused_computation.74 | loop fusion | flops 5570560 | bytes 13369348 | tf_op jit(solution)/shard_map/reduce_sum | solution.py:44
  295.9 0.8 constant_dynamic-slice_fusion
  296.8 74.3 %all-gather.10.cloned.1.call-done = f32[1024,2176]{1,0:T(8,128)} async-done(((f32[64,2176]{1,0:T(8,128)}), f32[1024,2176]{1,0:T(8,128)}) %all-gather.10.cloned.1.call-update) | async-done | bytes 8912912 | tf_op jit(solution)/shard_map/all_gather | solution.py:47
  371.2 4.7 select_reduce_fusion.1
  376.1 0.9 collective-permute-start.1
  377.0 1.3 collective-permute-start.2
  378.4 2.8 collective-permute-done.1
  381.1 1.9 broadcast_select_fusion.1
  383.0 1.1 collective-permute-done.2
  384.2 2.2 maximum_add_fusion
  386.9 2.5 collective-permute-start.3
  390.6 1.0 fusion
  391.6 8.9 %collective-permute-done.3 = f32[512,128]{1,0:T(8,128)S(1)} collective-permute-done((f32[512,128]{1,0:T(8,128)S(1)}, f32[512,128]{1,0:T(8,128)S(1)}, u32[]{:S(2)}, u32[]{:S(2)}) %collective-permute-start.3) | collective-permute-done | bytes 262176 | tf_op jit(solution)/shard_map/ppermute | solution.py:23
  400.5 4.3 collective-permute-done.5
  404.9 1.8 fusion.13
  407.4 0.8 collective-permute-start.8
  408.2 5.9 %collective-permute-done.6 = f32[512,128]{1,0:T(8,128)S(1)} collective-permute-done((f32[512,128]{1,0:T(8,128)S(1)}, f32[512,128]{1,0:T(8,128)S(1)}, u32[]{:S(2)}, u32[]{:S(2)}) %collective-permute-start.6) | collective-permute-done | bytes 262176 | tf_op jit(solution)/shard_map/ppermute | solution.py:23
  414.1 1.1 collective-permute-done.7
  415.3 6.9 %collective-permute-done.8 = f32[512,128]{1,0:T(8,128)S(1)} collective-permute-done((f32[512,128]{1,0:T(8,128)S(1)}, f32[512,128]{1,0:T(8,128)S(1)}, u32[]{:S(2)}, u32[]{:S(2)}) %collective-permute-start.8) | collective-permute-done | bytes 262176 | tf_op jit(solution)/shard_map/ppermute | solution.py:23
  423.1 1.8 fusion.12
  425.6 2.6 collective-permute-start.9
  428.2 5.7 %collective-permute-done.10 = f32[512,128]{1,0:T(8,128)S(1)} collective-permute-done((f32[512,128]{1,0:T(8,128)S(1)}, f32[512,128]{1,0:T(8,128)S(1)}, u32[]{:S(2)}, u32[]{:S(2)}) %collective-permute-start.10) | collective-permute-done | bytes 262176 | tf_op jit(solution)/shard_map/ppermute | solution.py:23
  433.9 6.4 %collective-permute-done.11 = f32[512,128]{1,0:T(8,128)S(1)} collective-permute-done((f32[512,128]{1,0:T(8,128)S(1)}, f32[512,128]{1,0:T(8,128)S(1)}, u32[]{:S(2)}, u32[]{:S(2)}) %collective-permute-start.11) | collective-permute-done | bytes 262176 | tf_op jit(solution)/shard_map/ppermute | solution.py:23
  441.2 1.9 multiply_reduce_fusion
  443.2 0.7 copy-done.1
  443.9 1.9 fusion.18
  446.5 0.8 collective-permute-start.14
  447.3 0.9 collective-permute-done.12
  448.3 1.6 collective-permute-done.13
  449.9 0.8 collective-permute-done.14
  451.0 2.2 fusion.14
  453.2 0.7 reshape.75
  453.9 7.2 %all-to-all-start.1 = ((bf16[32,20,128]{2,1,0:T(8,128)(2,1)}), bf16[32,20,128]{2,1,0:T(8,128)(2,1)S(1)}, u32[]{:S(2)}, u32[]{:S(2)}) async-start(bf16[32,20,128]{2,1,0:T(8,128)(2,1)} %reshape.75), calls=%async_computation.1 | async-start | bytes 393216 | tf_op jit(solution)/shard_map/all_to_all | solution.py:113
  461.3 8.1 %all-to-all-done.1 = bf16[32,20,128]{2,1,0:T(8,128)(2,1)S(1)} async-done(((bf16[32,20,128]{2,1,0:T(8,128)(2,1)}), bf16[32,20,128]{2,1,0:T(8,128)(2,1)S(1)}, u32[]{:S(2)}, u32[]{:S(2)}) %all-to-all-start.1) | async-done | bytes 163872 | tf_op jit(solution)/shard_map/all_to_all | solution.py:113
  469.9 0.8 copy.10
  (66 shorter events, 8.3 us)
Async XLA Ops:
  7.2 171.7 %all-gather.6.cloned.1.call-start = ((), (), s32[]{:S(2)}) async-start(), calls=%async_computation.2 | async-start | bytes 13926400 | tf_op jit(solution)/shard_map/all_gather | solution.py:79
  75.0 214.5 %all-gather.8.cloned.1.call-start = ((), (), s32[]{:S(2)}) async-start(), calls=%async_computation.3 | async-start | bytes 11141120 | tf_op jit(solution)/shard_map/all_gather | solution.py:42
  189.1 3.5 copy-start.3
  192.6 5.0 %collective-permute-start = (f32[256,2176]{1,0:T(8,128)}, f32[256,2176]{1,0:T(8,128)S(1)}, u32[]{:S(2)}, u32[]{:S(2)}) collective-permute-start(f32[256,2176]{1,0:T(8,128)} %get-tuple-element.15), channel_id=1, source_target_pairs={{0,4},{4,0},{1,5},{5,1},{2,6},{6,2},{3,7},{7,3},{8,12},{12,8},{9,1... | collective-permute-start | bytes 6684680 | tf_op jit(solution)/shard_map/ppermute | solution.py:38
  197.6 4.1 copy-start.5
  201.7 169.5 %all-gather.10.cloned.1.call-start = ((), (), s32[]{:S(2)}) async-start(), calls=%async_computation.4 | async-start | bytes 9469952 | tf_op jit(solution)/shard_map/all_gather | solution.py:47
  371.2 4.7 copy-start.4
  376.1 5.0 %collective-permute-start.1 = (f32[256,2176]{1,0:T(8,128)S(1)}, f32[256,2176]{1,0:T(8,128)}, u32[]{:S(2)}, u32[]{:S(2)}) collective-permute-start(f32[256,2176]{1,0:T(8,128)S(1)} %bitcast_add_fusion), channel_id=1, source_target_pairs={{0,4},{4,0},{1,5},{5,1},{2,6},{6,2},{3,7},{7,3},{8,12},{12,8},{9,1... | collective-permute-start | bytes 6684680 | tf_op jit(solution)/shard_map/ppermute | solution.py:50
  377.0 7.2 %collective-permute-start.2 = (f32[256,2176]{1,0:T(8,128)}, f32[256,2176]{1,0:T(8,128)}, u32[]{:S(2)}, u32[]{:S(2)}) collective-permute-start(f32[256,2176]{1,0:T(8,128)} %get-tuple-element.14), channel_id=1, source_target_pairs={{0,4},{1,5},{2,6},{3,7},{8,12},{9,13},{10,14},{11,15},{16,20},{17,... | collective-permute-start | bytes 6684680 | tf_op jit(solution)/shard_map/ppermute | solution.py:40
  378.4 5.8 %copy-start.6 = (f32[256,2176]{1,0:T(8,128)S(1)}, f32[256,2176]{1,0:T(8,128)}, u32[]{:S(2)}) copy-start(f32[256,2176]{1,0:T(8,128)} %copy-done.5) | copy-start | bytes 6684676
  386.9 13.5 %collective-permute-start.3 = (f32[512,128]{1,0:T(8,128)S(1)}, f32[512,128]{1,0:T(8,128)S(1)}, u32[]{:S(2)}, u32[]{:S(2)}) collective-permute-start(f32[512,128]{1,0:T(8,128)S(1)} %slice.26), channel_id=1, source_target_pairs={{0,3},{1,0},{2,1},{3,2},{4,7},{5,4},{6,5},{7,6},{8,11},{9,8},{10,9... | collective-permute-start | bytes 786440 | tf_op jit(solution)/shard_map/ppermute | solution.py:23
  389.5 11.0 %collective-permute-start.4 = (f32[512,128]{1,0:T(8,128)S(1)}, f32[512,128]{1,0:T(8,128)S(1)}, u32[]{:S(2)}, u32[]{:S(2)}) collective-permute-start(f32[512,128]{1,0:T(8,128)S(1)} %slice.26), channel_id=1, source_target_pairs={{0,2},{1,3},{2,0},{3,1},{4,6},{5,7},{6,4},{7,5},{8,10},{9,11},{10,... | collective-permute-start | bytes 786440 | tf_op jit(solution)/shard_map/ppermute | solution.py:23
  390.0 14.8 %collective-permute-start.5 = (f32[512,128]{1,0:T(8,128)S(1)}, f32[512,128]{1,0:T(8,128)S(1)}, u32[]{:S(2)}, u32[]{:S(2)}) collective-permute-start(f32[512,128]{1,0:T(8,128)S(1)} %slice.26), channel_id=1, source_target_pairs={{0,1},{1,2},{2,3},{3,0},{4,5},{5,6},{6,7},{7,4},{8,9},{9,10},{10,1... | collective-permute-start | bytes 786440 | tf_op jit(solution)/shard_map/ppermute | solution.py:23
  391.6 31.5 %copy-start = (f32[512,2048]{1,0:T(8,128)}, f32[512,2048]{1,0:T(8,128)S(1)}, u32[]{:S(2)}) copy-start(f32[512,2048]{1,0:T(8,128)S(1)} %fusion) | copy-start | bytes 12582916
  406.7 7.4 %collective-permute-start.6 = (f32[512,128]{1,0:T(8,128)S(1)}, f32[512,128]{1,0:T(8,128)S(1)}, u32[]{:S(2)}, u32[]{:S(2)}) collective-permute-start(f32[512,128]{1,0:T(8,128)S(1)} %fusion.13), channel_id=1, source_target_pairs={{0,3},{1,0},{2,1},{3,2},{4,7},{5,4},{6,5},{7,6},{8,11},{9,8},{10,9... | collective-permute-start | bytes 786440 | tf_op jit(solution)/shard_map/ppermute | solution.py:23
  406.8 8.5 %collective-permute-start.7 = (f32[512,128]{1,0:T(8,128)S(1)}, f32[512,128]{1,0:T(8,128)S(1)}, u32[]{:S(2)}, u32[]{:S(2)}) collective-permute-start(f32[512,128]{1,0:T(8,128)S(1)} %fusion.13), channel_id=1, source_target_pairs={{0,2},{1,3},{2,0},{3,1},{4,6},{5,7},{6,4},{7,5},{8,10},{9,11},{10,... | collective-permute-start | bytes 786440 | tf_op jit(solution)/shard_map/ppermute | solution.py:23
  407.4 14.8 %collective-permute-start.8 = (f32[512,128]{1,0:T(8,128)S(1)}, f32[512,128]{1,0:T(8,128)S(1)}, u32[]{:S(2)}, u32[]{:S(2)}) collective-permute-start(f32[512,128]{1,0:T(8,128)S(1)} %fusion.13), channel_id=1, source_target_pairs={{0,1},{1,2},{2,3},{3,0},{4,5},{5,6},{6,7},{7,4},{8,9},{9,10},{10,1... | collective-permute-start | bytes 786440 | tf_op jit(solution)/shard_map/ppermute | solution.py:23
  414.1 8.8 %copy-start.7 = (f32[512,128]{1,0:T(8,128)}, f32[512,128]{1,0:T(8,128)S(1)}, u32[]{:S(2)}) copy-start(f32[512,128]{1,0:T(8,128)S(1)} %collective-permute-done.6) | copy-start | bytes 786436
  415.3 7.6 %copy-start.8 = (f32[512,128]{1,0:T(8,128)}, f32[512,128]{1,0:T(8,128)S(1)}, u32[]{:S(2)}) copy-start(f32[512,128]{1,0:T(8,128)S(1)} %collective-permute-done.7) | copy-start | bytes 786436
  422.2 0.7 copy-start.9
  424.9 15.7 %copy-start.10 = (f32[512,128]{1,0:T(8,128)}, f32[512,128]{1,0:T(8,128)S(1)}, u32[]{:S(2)}) copy-start(f32[512,128]{1,0:T(8,128)S(1)} %fusion.12) | copy-start | bytes 786436
  424.9 9.0 %collective-permute-start.10 = (f32[512,128]{1,0:T(8,128)S(1)}, f32[512,128]{1,0:T(8,128)S(1)}, u32[]{:S(2)}, u32[]{:S(2)}) collective-permute-start(f32[512,128]{1,0:T(8,128)S(1)} %fusion.12), channel_id=1, source_target_pairs={{0,2},{1,3},{2,0},{3,1},{4,6},{5,7},{6,4},{7,5},{8,10},{9,11},{10,... | collective-permute-start | bytes 786440 | tf_op jit(solution)/shard_map/ppermute | solution.py:23
  425.6 14.8 %collective-permute-start.11 = (f32[512,128]{1,0:T(8,128)S(1)}, f32[512,128]{1,0:T(8,128)S(1)}, u32[]{:S(2)}, u32[]{:S(2)}) collective-permute-start(f32[512,128]{1,0:T(8,128)S(1)} %fusion.12), channel_id=1, source_target_pairs={{0,1},{1,2},{2,3},{3,0},{4,5},{5,6},{6,7},{7,4},{8,9},{9,10},{10,1... | collective-permute-start | bytes 786440 | tf_op jit(solution)/shard_map/ppermute | solution.py:23
  425.6 14.7 %collective-permute-start.9 = (f32[512,128]{1,0:T(8,128)S(1)}, f32[512,128]{1,0:T(8,128)S(1)}, u32[]{:S(2)}, u32[]{:S(2)}) collective-permute-start(f32[512,128]{1,0:T(8,128)S(1)} %fusion.12), channel_id=1, source_target_pairs={{0,3},{1,0},{2,1},{3,2},{4,7},{5,4},{6,5},{7,6},{8,11},{9,8},{10,9... | collective-permute-start | bytes 786440 | tf_op jit(solution)/shard_map/ppermute | solution.py:23
  433.9 6.7 %copy-start.11 = (f32[512,128]{1,0:T(8,128)}, f32[512,128]{1,0:T(8,128)S(1)}, u32[]{:S(2)}) copy-start(f32[512,128]{1,0:T(8,128)S(1)} %collective-permute-done.10) | copy-start | bytes 786436
  440.4 0.7 copy-start.12
  440.4 0.8 copy-start.13
  441.2 2.7 copy-start.1
  445.8 2.5 collective-permute-start.12
  445.9 4.0 collective-permute-start.13
  446.5 4.2 collective-permute-start.14
  447.3 3.6 copy-start.2
  451.0 10.2 %copy-start.14 = (bf16[640,128]{1,0:T(8,128)(2,1)S(1)}, bf16[640,128]{1,0:T(8,128)(2,1)}, u32[]{:S(2)}) copy-start(bf16[640,128]{1,0:T(8,128)(2,1)} %param.4) | copy-start | bytes 491524
  453.9 15.6 %all-to-all-start.1 = ((bf16[32,20,128]{2,1,0:T(8,128)(2,1)}), bf16[32,20,128]{2,1,0:T(8,128)(2,1)S(1)}, u32[]{:S(2)}, u32[]{:S(2)}) async-start(bf16[32,20,128]{2,1,0:T(8,128)(2,1)} %reshape.75), calls=%async_computation.1 | async-start | bytes 393216 | tf_op jit(solution)/shard_map/all_to_all | solution.py:113
Sparse Core Ops, SparseCore 0:
  75.1 103.6 all-gather.5
  201.8 87.6 all-gather.7
  296.9 74.1 all-gather.9

commit v14 on v12

--- a/solution.py
+++ b/solution.py
@@ -45,9 +45,12 @@
     piece = lax.dynamic_slice_in_dim(total_z, zi * quarter, quarter, 0)
     along_x = lax.all_gather(piece, "x")
     before_x = lax.all_gather(masked_sum(along_x, xi), "z", axis=0, tiled=True)
-    mine_prefix = before_x + before_z
+    return before_x + before_z, below
+
+
+def join_halves(mine_prefix, below):
     other_prefix = lax.ppermute(mine_prefix, "c", SWAP)
-    first = ci == 0
+    first = lax.axis_index("c") == 0
     top = jnp.where(first, mine_prefix, other_prefix)
     bottom = jnp.where(first, other_prefix, mine_prefix)
     return jnp.concatenate([top, bottom], axis=0) + below
@@ -77,10 +80,10 @@
     col_start = lax.axis_index("feat") * block_rows
     rows_xy = lax.all_gather(local_xy, "feat", axis=0, tiled=True)
     own = lax.dynamic_slice_in_dim(rows_xy, col_start, block_rows, 1)
-    moments = exclusive_prefix(lax.dot_general(own, rows_xy, contract, preferred_element_type=jnp.float32))
+    halves, below = exclusive_prefix(lax.dot_general(own, rows_xy, contract, preferred_element_type=jnp.float32))
     fi = lax.axis_index("feat")
-    gram_prefix = rotate(moments[:, :width], fi * block_rows, width, 1)
-    cross_prefix = gather_feat(moments[:, width:])
+    cross_prefix = gather_feat(join_halves(halves[:, width:], below[:, width:]))
+    gram_prefix = rotate(join_halves(halves[:, :width], below[:, :width]), fi * block_rows, width, 1)
     span = (lax.axis_index("x") * lax.axis_size("z") + lax.axis_index("z")) * lax.axis_size("c") + lax.axis_index("c")
     seen = (span * (tok_dev * feat_count)).astype(jnp.float32)
     scale = 1.0 / jnp.maximum(seen, 1.0)

time: 471 us -> 475 us (level)
  transfers between devices with their start and end apart: 19 -> 20, of which waited for: 14 -> 17; matrix products, arithmetic and copies ran while one was open for 0% -> 1% of each run, Pallas kernels for 0% -> 0%
where the time goes in v14:
time: 475 us; the launch traced here: 474 us
  waiting for transfers between devices  317 us (67%)
  blocking collectives  51.3 us (11%)
  other arithmetic  28.5 us (6%)
  matrix products  27.6 us (6%)
  starting transfers between devices  19.2 us (4%)
  local copies, waits for them, and re-layouts  16.3 us (3%)
  between operations  14.1 us (3%)
    all_gather x1, waiting for transfers between devices, body(): rows_xy = lax.all_gather(local_xy, 'feat', axis=0, tiled=True)  104 us
    all_gather x1, waiting for transfers between devices, exclusive_prefix(): along_z = lax.all_gather(mine, 'z')  88.1 us
    all_to_all x1, blocking collectives, body(): lax.all_to_all(sorted_xy, TM, split_axis=0, concat_axis=0, tiled=True)  51.3 us
    ppermute x12, waiting for transfers between devices, gather_feat(): lax.ppermute(piece, 'feat', [(i, (i - k) % n) for i in range(n)])  43 us
    all_gather x1, waiting for transfers between devices, exclusive_prefix(): along_x = lax.all_gather(piece, 'x')  32.8 us
    all_gather x1, waiting for transfers between devices, exclusive_prefix(): before_x = lax.all_gather(masked_sum(along_x, xi), 'z', axis=0, tiled=True)  32.3 us
    dot_general x1, matrix products, body(): lax.dot_general(own, rows_xy, contract, preferred_element_type=jnp.float32)  12.6 us
    ppermute x12, starting transfers between devices, gather_feat(): lax.ppermute(piece, 'feat', [(i, (i - k) % n) for i in range(n)])  9.55 us
  transfers between devices with their start and end apart: 20, of which 17 were waited for; matrix products, arithmetic and copies ran while one was open for 1% of the time, Pallas kernels for 0%

profile of v14, /device:TPU:1, one launch (start us, length us, event | category | flops | bytes accessed | tf_op | source)
XLA Modules:
  0.0 474.2 jit_solution(6092340199711167421)
XLA Ops:
  7.2 1.1 fusion.20
  9.0 5.8 %convolution_convert_fusion = bf16[640,2176]{1,0:T(8,128)(2,1)} fusion(bf16[640,128]{1,0:T(8,128)(2,1)} %param.4, bf16[640,2048]{1,0:T(8,128)(2,1)} %param.3, s32[640]{0:T(1024)S(1)} %convert_add_fusion), kind=kOutput, calls=%fused_computation.3 | convolution fusion | flops 1789952000 | bytes 5573120 | tf_op jit(solution)/shard_map/dot_general | solution.py:75
  14.8 3.6 reshape.65
  18.4 51.3 %all_to_all.10 = bf16[32,20,2176]{2,1,0:T(8,128)(2,1)} all-to-all(bf16[32,20,2176]{2,1,0:T(8,128)(2,1)S(1)} %reshape.65), channel_id=1, replica_groups=mesh['x'=4,'z'=4,'c'=2,'feat'=4] {'x','z','c'}, dimensions={0} | all-to-all | bytes 5570560 | tf_op jit(solution)/shard_map/all_to_all | solution.py:77
  69.7 5.3 %reshape.66 = bf16[640,2176]{1,0:T(8,128)(2,1)} reshape(bf16[32,20,2176]{2,1,0:T(8,128)(2,1)} %all_to_all.10) | data formatting | bytes 5570560 | tf_op jit(solution)/shard_map/reshape | solution.py:78
  75.1 103.8 %all-gather.7.cloned.1.call-done = bf16[2560,2176]{1,0:T(8,128)(2,1)} async-done(((bf16[640,2176]{1,0:T(8,128)(2,1)}), bf16[2560,2176]{1,0:T(8,128)(2,1)}) %all-gather.7.cloned.1.call-update) | async-done | bytes 11141136 | tf_op jit(solution)/shard_map/all_gather | solution.py:81
  178.8 12.6 %fusion.6 = f32[512,2176]{1,0:T(8,128)} fusion(bf16[2560,2176]{1,0:T(8,128)(2,1)} %all-gather.7.cloned.1.call-done, s32[]{:T(128)S(6)} %select_n.63), kind=kOutput, calls=%fused_computation.11 | convolution fusion | flops 5704253440 | bytes 18219012 | tf_op jit(solution)/shard_map/dot_general | solution.py:83
  191.5 0.8 collective-permute-start
  192.3 7.5 %collective-permute-done = f32[512,2176]{1,0:T(8,128)} collective-permute-done((f32[512,2176]{1,0:T(8,128)}, f32[512,2176]{1,0:T(8,128)}, u32[]{:S(2)}, u32[]{:S(2)}) %collective-permute-start) | collective-permute-done | bytes 4456480 | tf_op jit(solution)/shard_map/ppermute | solution.py:37
  199.8 3.9 dynamic-slice_add_fusion
  203.8 88.1 %all-gather.11.cloned.1.call-done = f32[1024,2176]{1,0:T(8,128)} async-done(((f32[256,2176]{1,0:T(8,128)}), f32[1024,2176]{1,0:T(8,128)}) %all-gather.11.cloned.1.call-update) | async-done | bytes 8912912 | tf_op jit(solution)/shard_map/all_gather | solution.py:41
  291.9 6.5 %select_reduce_fusion = (f32[256,2176]{1,0:T(8,128)}, f32[256,2176]{1,0:T(8,128)S(1)}) fusion(f32[4,256,2176]{2,1,0:T(8,128)} %bitcast.20, pred[4]{0:T(512)(128)(4,1)S(1)} %iota_compare_fusion.13), kind=kLoop, calls=%fused_computation | loop fusion | flops 5570560 | bytes 13369348 | tf_op jit(solution)/shard_map/reduce_sum | solution.py:18
  298.3 0.9 constant_dynamic-slice_fusion
  299.3 32.8 %all-gather.13.cloned.1.call-done = f32[256,2176]{1,0:T(8,128)} async-done(((f32[64,2176]{1,0:T(8,128)}), f32[256,2176]{1,0:T(8,128)}) %all-gather.13.cloned.1.call-update) | async-done | bytes 2228240 | tf_op jit(solution)/shard_map/all_gather | solution.py:46
  332.1 2.7 select_reduce_fusion.1
  334.8 32.3 %all-gather.9.cloned.1.call-done = f32[256,2176]{1,0:T(8,128)} async-done(((f32[64,2176]{1,0:T(8,128)}), f32[256,2176]{1,0:T(8,128)}) %all-gather.9.cloned.1.call-update) | async-done | bytes 2228240 | tf_op jit(solution)/shard_map/all_gather | solution.py:47
  367.1 2.5 add.100
  369.6 1.6 slice.36
  371.3 0.8 collective-permute-start.5
  372.2 2.6 broadcast_select_fusion
  374.8 1.5 collective-permute-done.1
  376.8 2.5 collective-permute-start.2
  380.6 10.1 %collective-permute-done.2 = f32[512,128]{1,0:T(8,128)S(1)} collective-permute-done((f32[512,128]{1,0:T(8,128)S(1)}, f32[512,128]{1,0:T(8,128)S(1)}, u32[]{:S(2)}, u32[]{:S(2)}) %collective-permute-start.2) | collective-permute-done | bytes 262176 | tf_op jit(solution)/shard_map/ppermute | solution.py:23
  392.0 2.8 collective-permute-done.4
  394.8 1.3 maximum_multiply_fusion
  396.2 2.5 broadcast_select_fusion.2
  398.7 0.8 slice_add_fusion
  399.5 1.0 fusion
  400.5 1.8 fusion.13
  402.3 0.8 collective-permute-start.6
  403.8 5.9 %collective-permute-done.6 = f32[512,128]{1,0:T(8,128)S(1)} collective-permute-done((f32[512,128]{1,0:T(8,128)S(1)}, f32[512,128]{1,0:T(8,128)S(1)}, u32[]{:S(2)}, u32[]{:S(2)}) %collective-permute-start.6) | collective-permute-done | bytes 262176 | tf_op jit(solution)/shard_map/ppermute | solution.py:23
  409.8 1.7 collective-permute-done.7
  411.5 7.0 %collective-permute-done.8 = f32[512,128]{1,0:T(8,128)S(1)} collective-permute-done((f32[512,128]{1,0:T(8,128)S(1)}, f32[512,128]{1,0:T(8,128)S(1)}, u32[]{:S(2)}, u32[]{:S(2)}) %collective-permute-start.8) | collective-permute-done | bytes 262176 | tf_op jit(solution)/shard_map/ppermute | solution.py:23
  419.4 1.8 fusion.12
  421.4 2.7 collective-permute-start.9
  424.0 6.2 %collective-permute-done.10 = f32[512,128]{1,0:T(8,128)S(1)} collective-permute-done((f32[512,128]{1,0:T(8,128)S(1)}, f32[512,128]{1,0:T(8,128)S(1)}, u32[]{:S(2)}, u32[]{:S(2)}) %collective-permute-start.10) | collective-permute-done | bytes 262176 | tf_op jit(solution)/shard_map/ppermute | solution.py:23
  430.2 6.0 %collective-permute-done.11 = f32[512,128]{1,0:T(8,128)S(1)} collective-permute-done((f32[512,128]{1,0:T(8,128)S(1)}, f32[512,128]{1,0:T(8,128)S(1)}, u32[]{:S(2)}, u32[]{:S(2)}) %collective-permute-start.11) | collective-permute-done | bytes 262176 | tf_op jit(solution)/shard_map/ppermute | solution.py:23
  437.0 1.9 multiply_reduce_fusion
  439.0 0.7 copy-done.1
  439.8 1.9 fusion.18
  442.2 0.9 collective-permute-start.14
  443.1 0.9 collective-permute-done.12
  444.1 1.6 collective-permute-done.13
  445.7 0.8 collective-permute-done.14
  446.8 2.2 fusion.14
  449.7 7.7 %all-to-all-start.1 = ((bf16[32,20,128]{2,1,0:T(8,128)(2,1)}), bf16[32,20,128]{2,1,0:T(8,128)(2,1)S(1)}, u32[]{:S(2)}, u32[]{:S(2)}) async-start(bf16[32,20,128]{2,1,0:T(8,128)(2,1)} %reshape.67), calls=%async_computation.1 | async-start | bytes 393216 | tf_op jit(solution)/shard_map/all_to_all | solution.py:115
  457.6 8.1 %all-to-all-done.1 = bf16[32,20,128]{2,1,0:T(8,128)(2,1)S(1)} async-done(((bf16[32,20,128]{2,1,0:T(8,128)(2,1)}), bf16[32,20,128]{2,1,0:T(8,128)(2,1)S(1)}, u32[]{:S(2)}, u32[]{:S(2)}) %all-to-all-start.1) | async-done | bytes 163872 | tf_op jit(solution)/shard_map/all_to_all | solution.py:115
  466.3 0.8 copy.10
  (74 shorter events, 9.6 us)
Async XLA Ops:
  7.2 171.7 %all-gather.7.cloned.1.call-start = ((), (), s32[]{:S(2)}) async-start(), calls=%async_computation.2 | async-start | bytes 13926400 | tf_op jit(solution)/shard_map/all_gather | solution.py:81
  75.0 216.9 %all-gather.11.cloned.1.call-start = ((), (), s32[]{:S(2)}) async-start(), calls=%async_computation.4 | async-start | bytes 11141120 | tf_op jit(solution)/shard_map/all_gather | solution.py:41
  191.5 8.3 %collective-permute-start = (f32[512,2176]{1,0:T(8,128)}, f32[512,2176]{1,0:T(8,128)}, u32[]{:S(2)}, u32[]{:S(2)}) collective-permute-start(f32[512,2176]{1,0:T(8,128)} %fusion.6), channel_id=1, source_target_pairs={{0,4},{4,0},{1,5},{5,1},{2,6},{6,2},{3,7},{7,3},{8,12},{12,8},{9,1... | collective-permute-start | bytes 13369352 | tf_op jit(solution)/shard_map/ppermute | solution.py:37
  203.7 128.3 %all-gather.13.cloned.1.call-start = ((), (), s32[]{:S(2)}) async-start(), calls=%async_computation.5 | async-start | bytes 2785280 | tf_op jit(solution)/shard_map/all_gather | solution.py:46
  299.2 67.9 %all-gather.9.cloned.1.call-start = ((), (), s32[]{:S(2)}) async-start(), calls=%async_computation.3 | async-start | bytes 2785280 | tf_op jit(solution)/shard_map/all_gather | solution.py:47
  371.3 24.9 %collective-permute-start.5 = (f32[256,2048]{1,0:T(8,128)}, f32[256,2048]{1,0:T(8,128)}, u32[]{:S(2)}, u32[]{:S(2)}) collective-permute-start(f32[256,2048]{1,0:T(8,128)} %slice.36), channel_id=1, source_target_pairs={{0,4},{4,0},{1,5},{5,1},{2,6},{6,2},{3,7},{7,3},{8,12},{12,8},{9,1... | collective-permute-start | bytes 6291464 | tf_op jit(solution)/shard_map/ppermute | solution.py:52
  372.1 4.2 collective-permute-start.1
  374.8 2.0 copy-start.2
  376.8 13.8 %collective-permute-start.2 = (f32[512,128]{1,0:T(8,128)S(1)}, f32[512,128]{1,0:T(8,128)S(1)}, u32[]{:S(2)}, u32[]{:S(2)}) collective-permute-start(f32[512,128]{1,0:T(8,128)S(1)} %slice_add_fusion.1), channel_id=1, source_target_pairs={{0,3},{1,0},{2,1},{3,2},{4,7},{5,4},{6,5},{7,6},{8,11},{9,8},{10,9... | collective-permute-start | bytes 786440 | tf_op jit(solution)/shard_map/ppermute | solution.py:23
  379.4 11.3 %collective-permute-start.3 = (f32[512,128]{1,0:T(8,128)S(1)}, f32[512,128]{1,0:T(8,128)S(1)}, u32[]{:S(2)}, u32[]{:S(2)}) collective-permute-start(f32[512,128]{1,0:T(8,128)S(1)} %slice_add_fusion.1), channel_id=1, source_target_pairs={{0,2},{1,3},{2,0},{3,1},{4,6},{5,7},{6,4},{7,5},{8,10},{9,11},{10,... | collective-permute-start | bytes 786440 | tf_op jit(solution)/shard_map/ppermute | solution.py:23
  379.9 14.9 %collective-permute-start.4 = (f32[512,128]{1,0:T(8,128)S(1)}, f32[512,128]{1,0:T(8,128)}, u32[]{:S(2)}, u32[]{:S(2)}) collective-permute-start(f32[512,128]{1,0:T(8,128)S(1)} %slice_add_fusion.1), channel_id=1, source_target_pairs={{0,1},{1,2},{2,3},{3,0},{4,5},{5,6},{6,7},{7,4},{8,9},{9,10},{10,1... | collective-permute-start | bytes 786440 | tf_op jit(solution)/shard_map/ppermute | solution.py:23
  390.6 0.7 copy-start.11
  391.3 0.7 copy-start.12
  394.8 3.8 slice-start
  396.2 2.5 slice-start.1
  400.5 18.9 %copy-start = (f32[512,2048]{1,0:T(8,128)}, f32[512,2048]{1,0:T(8,128)S(1)}, u32[]{:S(2)}) copy-start(f32[512,2048]{1,0:T(8,128)S(1)} %fusion) | copy-start | bytes 12582916
  402.3 7.5 %collective-permute-start.6 = (f32[512,128]{1,0:T(8,128)S(1)}, f32[512,128]{1,0:T(8,128)S(1)}, u32[]{:S(2)}, u32[]{:S(2)}) collective-permute-start(f32[512,128]{1,0:T(8,128)S(1)} %fusion.13), channel_id=1, source_target_pairs={{0,3},{1,0},{2,1},{3,2},{4,7},{5,4},{6,5},{7,6},{8,11},{9,8},{10,9... | collective-permute-start | bytes 786440 | tf_op jit(solution)/shard_map/ppermute | solution.py:23
  403.1 8.4 %collective-permute-start.7 = (f32[512,128]{1,0:T(8,128)S(1)}, f32[512,128]{1,0:T(8,128)S(1)}, u32[]{:S(2)}, u32[]{:S(2)}) collective-permute-start(f32[512,128]{1,0:T(8,128)S(1)} %fusion.13), channel_id=1, source_target_pairs={{0,2},{1,3},{2,0},{3,1},{4,6},{5,7},{6,4},{7,5},{8,10},{9,11},{10,... | collective-permute-start | bytes 786440 | tf_op jit(solution)/shard_map/ppermute | solution.py:23
  403.1 15.3 %collective-permute-start.8 = (f32[512,128]{1,0:T(8,128)S(1)}, f32[512,128]{1,0:T(8,128)S(1)}, u32[]{:S(2)}, u32[]{:S(2)}) collective-permute-start(f32[512,128]{1,0:T(8,128)S(1)} %fusion.13), channel_id=1, source_target_pairs={{0,1},{1,2},{2,3},{3,0},{4,5},{5,6},{6,7},{7,4},{8,9},{9,10},{10,1... | collective-permute-start | bytes 786440 | tf_op jit(solution)/shard_map/ppermute | solution.py:23
  409.8 9.4 %copy-start.4 = (f32[512,128]{1,0:T(8,128)}, f32[512,128]{1,0:T(8,128)S(1)}, u32[]{:S(2)}) copy-start(f32[512,128]{1,0:T(8,128)S(1)} %collective-permute-done.6) | copy-start | bytes 786436
  411.5 7.7 %copy-start.5 = (f32[512,128]{1,0:T(8,128)}, f32[512,128]{1,0:T(8,128)S(1)}, u32[]{:S(2)}) copy-start(f32[512,128]{1,0:T(8,128)S(1)} %collective-permute-done.7) | copy-start | bytes 786436
  418.5 0.7 copy-start.6
  421.2 15.3 %copy-start.7 = (f32[512,128]{1,0:T(8,128)}, f32[512,128]{1,0:T(8,128)S(1)}, u32[]{:S(2)}) copy-start(f32[512,128]{1,0:T(8,128)S(1)} %fusion.12) | copy-start | bytes 786436
  421.2 9.0 %collective-permute-start.10 = (f32[512,128]{1,0:T(8,128)S(1)}, f32[512,128]{1,0:T(8,128)S(1)}, u32[]{:S(2)}, u32[]{:S(2)}) collective-permute-start(f32[512,128]{1,0:T(8,128)S(1)} %fusion.12), channel_id=1, source_target_pairs={{0,2},{1,3},{2,0},{3,1},{4,6},{5,7},{6,4},{7,5},{8,10},{9,11},{10,... | collective-permute-start | bytes 786440 | tf_op jit(solution)/shard_map/ppermute | solution.py:23
  421.3 14.9 %collective-permute-start.11 = (f32[512,128]{1,0:T(8,128)S(1)}, f32[512,128]{1,0:T(8,128)S(1)}, u32[]{:S(2)}, u32[]{:S(2)}) collective-permute-start(f32[512,128]{1,0:T(8,128)S(1)} %fusion.12), channel_id=1, source_target_pairs={{0,1},{1,2},{2,3},{3,0},{4,5},{5,6},{6,7},{7,4},{8,9},{9,10},{10,1... | collective-permute-start | bytes 786440 | tf_op jit(solution)/shard_map/ppermute | solution.py:23
  421.4 14.8 %collective-permute-start.9 = (f32[512,128]{1,0:T(8,128)S(1)}, f32[512,128]{1,0:T(8,128)S(1)}, u32[]{:S(2)}, u32[]{:S(2)}) collective-permute-start(f32[512,128]{1,0:T(8,128)S(1)} %fusion.12), channel_id=1, source_target_pairs={{0,3},{1,0},{2,1},{3,2},{4,7},{5,4},{6,5},{7,6},{8,11},{9,8},{10,9... | collective-permute-start | bytes 786440 | tf_op jit(solution)/shard_map/ppermute | solution.py:23
  430.2 6.3 %copy-start.8 = (f32[512,128]{1,0:T(8,128)}, f32[512,128]{1,0:T(8,128)S(1)}, u32[]{:S(2)}) copy-start(f32[512,128]{1,0:T(8,128)S(1)} %collective-permute-done.10) | copy-start | bytes 786436
  436.2 0.7 copy-start.9
  436.2 0.8 copy-start.10
  437.0 2.7 copy-start.1
  441.6 2.5 collective-permute-start.12
  441.7 4.0 collective-permute-start.13
  442.2 4.3 collective-permute-start.14
  443.1 3.6 copy-start.3
  446.8 10.6 %copy-start.13 = (bf16[640,128]{1,0:T(8,128)(2,1)S(1)}, bf16[640,128]{1,0:T(8,128)(2,1)}, u32[]{:S(2)}) copy-start(bf16[640,128]{1,0:T(8,128)(2,1)} %param.4) | copy-start | bytes 491524
  449.7 16.1 %all-to-all-start.1 = ((bf16[32,20,128]{2,1,0:T(8,128)(2,1)}), bf16[32,20,128]{2,1,0:T(8,128)(2,1)S(1)}, u32[]{:S(2)}, u32[]{:S(2)}) async-start(bf16[32,20,128]{2,1,0:T(8,128)(2,1)} %reshape.67), calls=%async_computation.1 | async-start | bytes 393216 | tf_op jit(solution)/shard_map/all_to_all | solution.py:115
Sparse Core Ops, SparseCore 0:
  75.1 103.6 all-gather.6
  203.9 87.9 all-gather.10
  299.3 32.6 all-gather.12
  334.9 32.1 all-gather.8

commit v15 on v12

--- a/solution.py
+++ b/solution.py
@@ -2,6 +2,7 @@
 import jax.numpy as jnp
 from jax import lax
 from jax.sharding import Mesh, PartitionSpec as P
+
 
 ITERS = 3
 
@@ -28,7 +29,14 @@
     return lax.dynamic_slice_in_dim(jnp.concatenate([a, a], axis=axis), start, size, axis)
 
 
-def exclusive_prefix(block):
+def stack_over(piece, axis):
+    n = lax.axis_size(axis)
+    f = lax.axis_index(axis)
+    parts = [piece] + [lax.ppermute(piece, axis, [(i, (i + k) % n) for i in range(n)]) for k in range(1, n)]
+    return jnp.take(jnp.stack(parts), (f - jnp.arange(n)) % n, axis=0)
+
+
+def exclusive_prefix(block, stack=lax.all_gather):
     ci = lax.axis_index("c")
     zi = lax.axis_index("z")
     xi = lax.axis_index("x")
@@ -38,13 +46,14 @@
     chip = block + partner
     below = jnp.where(ci == 1, partner, 0.0)
     mine = lax.dynamic_slice_in_dim(chip, ci * half, half, 0)
-    along_z = lax.all_gather(mine, "z")
+    along_z = stack(mine, "z")
     before_z = masked_sum(along_z, zi)
     total_z = jnp.sum(along_z, axis=0)
     quarter = half // lax.axis_size("z")
     piece = lax.dynamic_slice_in_dim(total_z, zi * quarter, quarter, 0)
-    along_x = lax.all_gather(piece, "x")
-    before_x = lax.all_gather(masked_sum(along_x, xi), "z", axis=0, tiled=True)
+    along_x = stack(piece, "x")
+    summed_x = masked_sum(along_x, xi)
+    before_x = stack(summed_x, "z").reshape(total_z.shape)
     mine_prefix = before_x + before_z
     other_prefix = lax.ppermute(mine_prefix, "c", SWAP)
     first = ci == 0
@@ -77,18 +86,19 @@
     col_start = lax.axis_index("feat") * block_rows
     rows_xy = lax.all_gather(local_xy, "feat", axis=0, tiled=True)
     own = lax.dynamic_slice_in_dim(rows_xy, col_start, block_rows, 1)
-    moments = exclusive_prefix(lax.dot_general(own, rows_xy, contract, preferred_element_type=jnp.float32))
+    moments = lax.dot_general(own, rows_xy, contract, preferred_element_type=jnp.float32)
     fi = lax.axis_index("feat")
-    gram_prefix = rotate(moments[:, :width], fi * block_rows, width, 1)
-    cross_prefix = gather_feat(moments[:, width:])
+    cross_prefix = gather_feat(exclusive_prefix(moments[:, width:], stack_over))
+    gram_prefix = rotate(exclusive_prefix(moments[:, :width]), fi * block_rows, width, 1)
     span = (lax.axis_index("x") * lax.axis_size("z") + lax.axis_index("z")) * lax.axis_size("c") + lax.axis_index("c")
     seen = (span * (tok_dev * feat_count)).astype(jnp.float32)
     scale = 1.0 / jnp.maximum(seen, 1.0)
     rhs = scale * cross_prefix
+    first_norm = jnp.sum(rhs * rhs, axis=0)
 
     residual = rhs
     direction = rhs
-    norm_now = jnp.sum(residual * residual, axis=0)
+    norm_now = first_norm
     solution = None
     for step in range(ITERS):
         product = jnp.dot(gram_prefix, direction, precision=lax.Precision.HIGH, preferred_element_type=jnp.float32)

time: 471 us -> 473 us (level)
  waiting for transfers between devices: 318 us -> 291 us
  starting transfers between devices: 21.5 us -> 40.4 us
  local copies, waits for them, and re-layouts: 13.3 us -> 19.5 us
  other arithmetic: 25.3 us -> 31.2 us
    all_gather x3, waiting for transfers between devices: 153 us -> 128 us  [the longest x1 83.8 us: exclusive_prefix(): along_z = stack(mine, 'z')]
    ppermute x0 -> x9, starting transfers between devices: none -> 12.6 us  [stack_over(): lax.ppermute(piece, axis, [(i, (i + k) % n) for i in range(n)])]
    ppermute x0 -> x9, waiting for transfers between devices: none -> 7.05 us  [stack_over(): lax.ppermute(piece, axis, [(i, (i + k) % n) for i in range(n)])]
    ppermute x12, waiting for transfers between devices: 40.9 us -> 34.2 us  [gather_feat(): lax.ppermute(piece, 'feat', [(i, (i - k) % n) for i in range(n)])]
    ppermute x12, starting transfers between devices: 11 us -> 17.3 us  [gather_feat(): lax.ppermute(piece, 'feat', [(i, (i - k) % n) for i in range(n)])]
  transfers between devices with their start and end apart: 19 -> 30, of which waited for: 14 -> 21; matrix products, arithmetic and copies ran while one was open for 0% -> 2% of each run, Pallas kernels for 0% -> 0%
where the time goes in v15:
time: 473 us; the launch traced here: 472 us
  waiting for transfers between devices  291 us (62%)
  blocking collectives  51.3 us (11%)
  starting transfers between devices  40.4 us (9%)
  other arithmetic  31.2 us (7%)
  matrix products  24.8 us (5%)
  local copies, waits for them, and re-layouts  19.5 us (4%)
  between operations  14.2 us (3%)
    all_gather x1, waiting for transfers between devices, body(): rows_xy = lax.all_gather(local_xy, 'feat', axis=0, tiled=True)  104 us
    all_gather x1, waiting for transfers between devices, exclusive_prefix(): along_z = stack(mine, 'z')  83.8 us
    all_to_all x1, blocking collectives, body(): lax.all_to_all(sorted_xy, TM, split_axis=0, concat_axis=0, tiled=True)  51.3 us
    ppermute x12, waiting for transfers between devices, gather_feat(): lax.ppermute(piece, 'feat', [(i, (i - k) % n) for i in range(n)])  34.2 us
    all_gather x1, waiting for transfers between devices, exclusive_prefix(): along_x = stack(piece, 'x')  31.6 us
    ppermute x12, starting transfers between devices, gather_feat(): lax.ppermute(piece, 'feat', [(i, (i - k) % n) for i in range(n)])  17.3 us
    all_gather x1, waiting for transfers between devices, exclusive_prefix(): before_x = stack(summed_x, 'z').reshape(total_z.shape)  12.9 us
    ppermute x9, starting transfers between devices, stack_over(): lax.ppermute(piece, axis, [(i, (i + k) % n) for i in range(n)])  12.6 us
  transfers between devices with their start and end apart: 30, of which 21 were waited for; matrix products, arithmetic and copies ran while one was open for 2% of the time, Pallas kernels for 0%

profile of v15, /device:TPU:1, one launch (start us, length us, event | category | flops | bytes accessed | tf_op | source)
XLA Modules:
  0.0 472.2 jit_solution(5519632947947215163)
XLA Ops:
  9.0 5.8 %convolution_convert_fusion = bf16[640,2176]{1,0:T(8,128)(2,1)} fusion(bf16[640,128]{1,0:T(8,128)(2,1)} %param.6, bf16[640,2048]{1,0:T(8,128)(2,1)} %param.5, s32[640]{0:T(1024)S(1)} %convert_add_fusion), kind=kOutput, calls=%fused_computation.6 | convolution fusion | flops 1789952000 | bytes 5573120 | tf_op jit(solution)/shard_map/dot_general | solution.py:81
  14.8 3.6 reshape.132
  18.4 51.3 %all_to_all.10 = bf16[32,20,2176]{2,1,0:T(8,128)(2,1)} all-to-all(bf16[32,20,2176]{2,1,0:T(8,128)(2,1)S(1)} %reshape.132), channel_id=1, replica_groups=mesh['x'=4,'z'=4,'c'=2,'feat'=4] {'x','z','c'}, dimensions={0} | all-to-all | bytes 5570560 | tf_op jit(solution)/shard_map/all_to_all | solution.py:83
  69.7 5.3 %reshape.133 = bf16[640,2176]{1,0:T(8,128)(2,1)} reshape(bf16[32,20,2176]{2,1,0:T(8,128)(2,1)} %all_to_all.10) | data formatting | bytes 5570560 | tf_op jit(solution)/shard_map/reshape | solution.py:84
  75.1 103.8 %all-gather.8.cloned.1.call-done = bf16[2560,2176]{1,0:T(8,128)(2,1)} async-done(((bf16[640,2176]{1,0:T(8,128)(2,1)}), bf16[2560,2176]{1,0:T(8,128)(2,1)}) %all-gather.8.cloned.1.call-update) | async-done | bytes 11141136 | tf_op jit(solution)/shard_map/all_gather | solution.py:87
  178.8 9.8 %fusion.6 = f32[512,2176]{1,0:T(8,128)S(1)} fusion(bf16[2560,2176]{1,0:T(8,128)(2,1)} %all-gather.8.cloned.1.call-done, s32[]{:T(128)S(6)} %select_n.132), kind=kOutput, calls=%fused_computation.14 | convolution fusion | flops 5704253440 | bytes 18219012 | tf_op jit(solution)/shard_map/dot_general | solution.py:89
  188.7 2.9 slice.33
  192.8 7.1 %collective-permute-done.14 = f32[512,2048]{1,0:T(8,128)} collective-permute-done((f32[512,2048]{1,0:T(8,128)}, f32[512,2048]{1,0:T(8,128)}, u32[]{:S(2)}, u32[]{:S(2)}) %collective-permute-start.14) | collective-permute-done | bytes 4194336 | tf_op jit(solution)/shard_map/ppermute | solution.py:45
  200.0 3.9 dynamic-slice_add_fusion
  204.0 83.8 %all-gather.10.cloned.1.call-done = f32[1024,2048]{1,0:T(8,128)} async-done(((f32[256,2048]{1,0:T(8,128)}), f32[1024,2048]{1,0:T(8,128)}) %all-gather.10.cloned.1.call-update) | async-done | bytes 8388624 | tf_op jit(solution)/shard_map/all_gather | solution.py:49
  287.8 5.2 %select_reduce_fusion = (f32[256,2048]{1,0:T(8,128)S(1)}, f32[256,2048]{1,0:T(8,128)S(1)}) fusion(f32[4,256,2048]{2,1,0:T(8,128)} %bitcast.35, pred[4]{0:T(512)(128)(4,1)S(1)} %iota_compare_fusion.13), kind=kLoop, calls=%fused_computation.5 | loop fusion | flops 5242880 | bytes 12582916 | tf_op jit(solution)/shard_map/reduce_sum | solution.py:19
  294.0 31.6 %all-gather.12.cloned.1.call-done = f32[256,2048]{1,0:T(8,128)} async-done(((f32[64,2048]{1,0:T(8,128)}), f32[256,2048]{1,0:T(8,128)}) %all-gather.12.cloned.1.call-update) | async-done | bytes 2097168 | tf_op jit(solution)/shard_map/all_gather | solution.py:54
  325.6 2.7 select_reduce_fusion.1
  331.9 3.0 collective-permute-start.2
  335.3 2.3 collective-permute-start.3
  338.2 3.4 collective-permute-done.1
  342.4 1.5 collective-permute-start.5
  343.9 2.7 collective-permute-start.6
  346.6 12.9 %all-gather.14.cloned.1.call-done = f32[256,2048]{1,0:T(8,128)} async-done(((f32[64,2048]{1,0:T(8,128)}), f32[256,2048]{1,0:T(8,128)}) %all-gather.14.cloned.1.call-update) | async-done | bytes 2097168 | tf_op jit(solution)/shard_map/all_gather | solution.py:56
  359.5 3.2 add.157
  364.9 2.1 collective-permute-start.9
  368.4 3.0 collective-permute-done.8
  372.6 1.3 collective-permute-start.10
  375.8 1.3 collective-permute-start.13
  377.1 2.4 collective-permute-start.12
  379.6 1.2 collective-permute-start.11
  380.8 4.4 collective-permute-done.13
  385.2 6.6 %collective-permute-done.12 = f32[512,128]{1,0:T(8,128)S(1)} collective-permute-done((f32[512,128]{1,0:T(8,128)S(1)}, f32[512,128]{1,0:T(8,128)S(1)}, u32[]{:S(2)}, u32[]{:S(2)}) %collective-permute-start.12) | collective-permute-done | bytes 262176 | tf_op jit(solution)/shard_map/ppermute | solution.py:24
  392.5 1.2 maximum_multiply_fusion
  393.7 2.0 broadcast_select_fusion.1
  395.7 3.4 maximum_add_fusion
  400.2 1.8 fusion.13
  402.3 2.5 collective-permute-start.17
  404.8 1.1 collective-permute-start.16
  406.0 5.4 %collective-permute-done.18 = f32[512,128]{1,0:T(8,128)S(1)} collective-permute-done((f32[512,128]{1,0:T(8,128)S(1)}, f32[512,128]{1,0:T(8,128)S(1)}, u32[]{:S(2)}, u32[]{:S(2)}) %collective-permute-start.18) | collective-permute-done | bytes 262176 | tf_op jit(solution)/shard_map/ppermute | solution.py:24
  411.4 4.3 collective-permute-done.17
  417.4 1.8 fusion.12
  419.2 1.7 collective-permute-start.21
  420.8 2.2 collective-permute-start.20
  423.4 4.9 %collective-permute-done.21 = f32[512,128]{1,0:T(8,128)S(1)} collective-permute-done((f32[512,128]{1,0:T(8,128)S(1)}, f32[512,128]{1,0:T(8,128)S(1)}, u32[]{:S(2)}, u32[]{:S(2)}) %collective-permute-start.21) | collective-permute-done | bytes 262176 | tf_op jit(solution)/shard_map/ppermute | solution.py:24
  428.3 6.4 %collective-permute-done.20 = f32[512,128]{1,0:T(8,128)S(1)} collective-permute-done((f32[512,128]{1,0:T(8,128)S(1)}, f32[512,128]{1,0:T(8,128)S(1)}, u32[]{:S(2)}, u32[]{:S(2)}) %collective-permute-start.20) | collective-permute-done | bytes 262176 | tf_op jit(solution)/shard_map/ppermute | solution.py:24
  435.5 1.9 multiply_reduce_fusion
  438.2 1.9 fusion.18
  440.1 1.5 collective-permute-start.23
  441.6 1.6 collective-permute-start.24
  446.1 2.2 fusion.14
  448.9 6.5 %all-to-all-start.1 = ((bf16[32,20,128]{2,1,0:T(8,128)(2,1)}), bf16[32,20,128]{2,1,0:T(8,128)(2,1)S(1)}, u32[]{:S(2)}, u32[]{:S(2)}) async-start(bf16[32,20,128]{2,1,0:T(8,128)(2,1)} %reshape.136), calls=%async_computation.1 | async-start | bytes 393216 | tf_op jit(solution)/shard_map/all_to_all | solution.py:122
  455.6 8.1 %all-to-all-done.1 = bf16[32,20,128]{2,1,0:T(8,128)(2,1)S(1)} async-done(((bf16[32,20,128]{2,1,0:T(8,128)(2,1)}), bf16[32,20,128]{2,1,0:T(8,128)(2,1)S(1)}, u32[]{:S(2)}, u32[]{:S(2)}) %all-to-all-start.1) | async-done | bytes 163872 | tf_op jit(solution)/shard_map/all_to_all | solution.py:122
  (111 shorter events, 27.5 us)
Async XLA Ops:
  7.2 171.7 %all-gather.8.cloned.1.call-start = ((), (), s32[]{:S(2)}) async-start(), calls=%async_computation.2 | async-start | bytes 13926400 | tf_op jit(solution)/shard_map/all_gather | solution.py:87
  75.0 212.8 %all-gather.10.cloned.1.call-start = ((), (), s32[]{:S(2)}) async-start(), calls=%async_computation.3 | async-start | bytes 10485760 | tf_op jit(solution)/shard_map/all_gather | solution.py:49
  188.7 3.3 copy-start.3
  192.0 8.0 %collective-permute-start.14 = (f32[512,2048]{1,0:T(8,128)}, f32[512,2048]{1,0:T(8,128)}, u32[]{:S(2)}, u32[]{:S(2)}) collective-permute-start(f32[512,2048]{1,0:T(8,128)} %slice.33), channel_id=1, source_target_pairs={{0,4},{4,0},{1,5},{5,1},{2,6},{6,2},{3,7},{7,3},{8,12},{12,8},{9,1... | collective-permute-start | bytes 12582920 | tf_op jit(solution)/shard_map/ppermute | solution.py:45
  203.9 121.7 %all-gather.12.cloned.1.call-start = ((), (), s32[]{:S(2)}) async-start(), calls=%async_computation.4 | async-start | bytes 2621440 | tf_op jit(solution)/shard_map/all_gather | solution.py:54
  293.9 65.6 %all-gather.14.cloned.1.call-start = ((), (), s32[]{:S(2)}) async-start(), calls=%async_computation.5 | async-start | bytes 2621440 | tf_op jit(solution)/shard_map/all_gather | solution.py:56
  329.8 2.1 collective-permute-start
  331.9 9.7 %copy-start.11 = (f32[512,128]{1,0:T(8,128)}, f32[512,128]{1,0:T(8,128)S(1)}, u32[]{:S(2)}) copy-start(f32[512,128]{1,0:T(8,128)S(1)} %collective-permute-done) | copy-start | bytes 786436
  331.9 6.3 %collective-permute-start.2 = (f32[256,128]{1,0:T(8,128)S(1)}, f32[256,128]{1,0:T(8,128)S(1)}, u32[]{:S(2)}, u32[]{:S(2)}) collective-permute-start(f32[256,128]{1,0:T(8,128)S(1)} %dynamic-slice_add_fusion.1), channel_id=1, source_target_pairs={{0,16},{8,24},{16,0},{24,8},{1,17},{9,25},{17,1},{25,9},{2,18},{10... | collective-permute-start | bytes 393224 | tf_op jit(solution)/shard_map/ppermute | solution.py:35
  334.9 6.7 %collective-permute-start.1 = (f32[256,128]{1,0:T(8,128)S(1)}, f32[256,128]{1,0:T(8,128)S(1)}, u32[]{:S(2)}, u32[]{:S(2)}) collective-permute-start(f32[256,128]{1,0:T(8,128)S(1)} %dynamic-slice_add_fusion.1), channel_id=1, source_target_pairs={{0,8},{8,16},{16,24},{24,0},{1,9},{9,17},{17,25},{25,1},{2,10},{10... | collective-permute-start | bytes 393224 | tf_op jit(solution)/shard_map/ppermute | solution.py:35
  335.3 6.3 %collective-permute-start.3 = (f32[256,128]{1,0:T(8,128)S(1)}, f32[256,128]{1,0:T(8,128)S(1)}, u32[]{:S(2)}, u32[]{:S(2)}) collective-permute-start(f32[256,128]{1,0:T(8,128)S(1)} %dynamic-slice_add_fusion.1), channel_id=1, source_target_pairs={{0,24},{8,0},{16,8},{24,16},{1,25},{9,1},{17,9},{25,17},{2,26},{10... | collective-permute-start | bytes 393224 | tf_op jit(solution)/shard_map/ppermute | solution.py:35
  342.4 21.1 %collective-permute-start.5 = (f32[64,128]{1,0:T(8,128)S(1)}, f32[64,128]{1,0:T(8,128)S(1)}, u32[]{:S(2)}, u32[]{:S(2)}) collective-permute-start(f32[64,128]{1,0:T(8,128)S(1)} %constant_dynamic-slice_fusion.1), channel_id=1, source_target_pairs={{0,64},{32,96},{64,0},{96,32},{1,65},{33,97},{65,1},{97,33},{2,66}... | collective-permute-start | bytes 98312 | tf_op jit(solution)/shard_map/ppermute | solution.py:35
  343.9 19.6 %collective-permute-start.4 = (f32[64,128]{1,0:T(8,128)S(1)}, f32[64,128]{1,0:T(8,128)S(1)}, u32[]{:S(2)}, u32[]{:S(2)}) collective-permute-start(f32[64,128]{1,0:T(8,128)S(1)} %constant_dynamic-slice_fusion.1), channel_id=1, source_target_pairs={{0,32},{32,64},{64,96},{96,0},{1,33},{33,65},{65,97},{97,1},{2,34}... | collective-permute-start | bytes 98312 | tf_op jit(solution)/shard_map/ppermute | solution.py:35
  343.9 19.6 %collective-permute-start.6 = (f32[64,128]{1,0:T(8,128)S(1)}, f32[64,128]{1,0:T(8,128)S(1)}, u32[]{:S(2)}, u32[]{:S(2)}) collective-permute-start(f32[64,128]{1,0:T(8,128)S(1)} %constant_dynamic-slice_fusion.1), channel_id=1, source_target_pairs={{0,96},{32,0},{64,32},{96,64},{1,97},{33,1},{65,33},{97,65},{2,98}... | collective-permute-start | bytes 98312 | tf_op jit(solution)/shard_map/ppermute | solution.py:35
  362.7 31.0 %collective-permute-start.15 = (f32[256,2048]{1,0:T(8,128)}, f32[256,2048]{1,0:T(8,128)S(1)}, u32[]{:S(2)}, u32[]{:S(2)}) collective-permute-start(f32[256,2048]{1,0:T(8,128)} %add.157), channel_id=1, source_target_pairs={{0,4},{4,0},{1,5},{5,1},{2,6},{6,2},{3,7},{7,3},{8,12},{12,8},{9,1... | collective-permute-start | bytes 6291464 | tf_op jit(solution)/shard_map/ppermute | solution.py:58
  364.9 3.5 collective-permute-start.9
  367.0 4.4 collective-permute-start.8
  367.3 4.6 collective-permute-start.7
  372.6 2.3 collective-permute-start.10
  375.8 9.4 %collective-permute-start.13 = (f32[512,128]{1,0:T(8,128)S(1)}, f32[512,128]{1,0:T(8,128)S(1)}, u32[]{:S(2)}, u32[]{:S(2)}) collective-permute-start(f32[512,128]{1,0:T(8,128)S(1)} %maximum_add_fusion.1), channel_id=1, source_target_pairs={{0,1},{1,2},{2,3},{3,0},{4,5},{5,6},{6,7},{7,4},{8,9},{9,10},{10,1... | collective-permute-start | bytes 786440 | tf_op jit(solution)/shard_map/ppermute | solution.py:24
  377.1 14.7 %collective-permute-start.12 = (f32[512,128]{1,0:T(8,128)S(1)}, f32[512,128]{1,0:T(8,128)S(1)}, u32[]{:S(2)}, u32[]{:S(2)}) collective-permute-start(f32[512,128]{1,0:T(8,128)S(1)} %maximum_add_fusion.1), channel_id=1, source_target_pairs={{0,2},{1,3},{2,0},{3,1},{4,6},{5,7},{6,4},{7,5},{8,10},{9,11},{10,... | collective-permute-start | bytes 786440 | tf_op jit(solution)/shard_map/ppermute | solution.py:24
  379.6 12.9 %collective-permute-start.11 = (f32[512,128]{1,0:T(8,128)S(1)}, f32[512,128]{1,0:T(8,128)}, u32[]{:S(2)}, u32[]{:S(2)}) collective-permute-start(f32[512,128]{1,0:T(8,128)S(1)} %maximum_add_fusion.1), channel_id=1, source_target_pairs={{0,3},{1,0},{2,1},{3,2},{4,7},{5,4},{6,5},{7,6},{8,11},{9,8},{10,9... | collective-permute-start | bytes 786440 | tf_op jit(solution)/shard_map/ppermute | solution.py:24
  385.2 6.6 %copy-start.12 = (f32[512,128]{1,0:T(8,128)}, f32[512,128]{1,0:T(8,128)S(1)}, u32[]{:S(2)}) copy-start(f32[512,128]{1,0:T(8,128)S(1)} %collective-permute-done.13) | copy-start | bytes 786436
  391.8 0.7 copy-start.13
  400.1 17.2 %copy-start = (f32[512,2048]{1,0:T(8,128)}, f32[512,2048]{1,0:T(8,128)S(1)}, u32[]{:S(2)}) copy-start(f32[512,2048]{1,0:T(8,128)S(1)} %fusion) | copy-start | bytes 12582916
  402.0 9.4 %collective-permute-start.18 = (f32[512,128]{1,0:T(8,128)S(1)}, f32[512,128]{1,0:T(8,128)S(1)}, u32[]{:S(2)}, u32[]{:S(2)}) collective-permute-start(f32[512,128]{1,0:T(8,128)S(1)} %fusion.13), channel_id=1, source_target_pairs={{0,1},{1,2},{2,3},{3,0},{4,5},{5,6},{6,7},{7,4},{8,9},{9,10},{10,1... | collective-permute-start | bytes 786440 | tf_op jit(solution)/shard_map/ppermute | solution.py:24
  402.3 13.4 %collective-permute-start.17 = (f32[512,128]{1,0:T(8,128)S(1)}, f32[512,128]{1,0:T(8,128)S(1)}, u32[]{:S(2)}, u32[]{:S(2)}) collective-permute-start(f32[512,128]{1,0:T(8,128)S(1)} %fusion.13), channel_id=1, source_target_pairs={{0,2},{1,3},{2,0},{3,1},{4,6},{5,7},{6,4},{7,5},{8,10},{9,11},{10,... | collective-permute-start | bytes 786440 | tf_op jit(solution)/shard_map/ppermute | solution.py:24
  404.8 11.6 %collective-permute-start.16 = (f32[512,128]{1,0:T(8,128)S(1)}, f32[512,128]{1,0:T(8,128)S(1)}, u32[]{:S(2)}, u32[]{:S(2)}) collective-permute-start(f32[512,128]{1,0:T(8,128)S(1)} %fusion.13), channel_id=1, source_target_pairs={{0,3},{1,0},{2,1},{3,2},{4,7},{5,4},{6,5},{7,6},{8,11},{9,8},{10,9... | collective-permute-start | bytes 786440 | tf_op jit(solution)/shard_map/ppermute | solution.py:24
  411.4 5.8 %copy-start.4 = (f32[512,128]{1,0:T(8,128)}, f32[512,128]{1,0:T(8,128)S(1)}, u32[]{:S(2)}) copy-start(f32[512,128]{1,0:T(8,128)S(1)} %collective-permute-done.18) | copy-start | bytes 786436
  415.7 1.4 copy-start.5
  416.5 0.7 copy-start.6
  419.2 15.8 %copy-start.7 = (f32[512,128]{1,0:T(8,128)}, f32[512,128]{1,0:T(8,128)S(1)}, u32[]{:S(2)}) copy-start(f32[512,128]{1,0:T(8,128)S(1)} %fusion.12) | copy-start | bytes 786436
  419.2 9.1 %collective-permute-start.21 = (f32[512,128]{1,0:T(8,128)S(1)}, f32[512,128]{1,0:T(8,128)S(1)}, u32[]{:S(2)}, u32[]{:S(2)}) collective-permute-start(f32[512,128]{1,0:T(8,128)S(1)} %fusion.12), channel_id=1, source_target_pairs={{0,1},{1,2},{2,3},{3,0},{4,5},{5,6},{6,7},{7,4},{8,9},{9,10},{10,1... | collective-permute-start | bytes 786440 | tf_op jit(solution)/shard_map/ppermute | solution.py:24
  420.8 13.8 %collective-permute-start.20 = (f32[512,128]{1,0:T(8,128)S(1)}, f32[512,128]{1,0:T(8,128)S(1)}, u32[]{:S(2)}, u32[]{:S(2)}) collective-permute-start(f32[512,128]{1,0:T(8,128)S(1)} %fusion.12), channel_id=1, source_target_pairs={{0,2},{1,3},{2,0},{3,1},{4,6},{5,7},{6,4},{7,5},{8,10},{9,11},{10,... | collective-permute-start | bytes 786440 | tf_op jit(solution)/shard_map/ppermute | solution.py:24
  423.0 11.6 %collective-permute-start.19 = (f32[512,128]{1,0:T(8,128)S(1)}, f32[512,128]{1,0:T(8,128)S(1)}, u32[]{:S(2)}, u32[]{:S(2)}) collective-permute-start(f32[512,128]{1,0:T(8,128)S(1)} %fusion.12), channel_id=1, source_target_pairs={{0,3},{1,0},{2,1},{3,2},{4,7},{5,4},{6,5},{7,6},{8,11},{9,8},{10,9... | collective-permute-start | bytes 786440 | tf_op jit(solution)/shard_map/ppermute | solution.py:24
  428.3 6.7 %copy-start.8 = (f32[512,128]{1,0:T(8,128)}, f32[512,128]{1,0:T(8,128)S(1)}, u32[]{:S(2)}) copy-start(f32[512,128]{1,0:T(8,128)S(1)} %collective-permute-done.21) | copy-start | bytes 786436
  434.6 0.7 copy-start.9
  434.7 0.8 copy-start.10
  435.5 2.7 copy-start.1
  440.1 4.2 collective-permute-start.23
  441.6 3.6 collective-permute-start.24
  443.3 2.4 collective-permute-start.22
  444.3 1.8 copy-start.2
  446.1 9.4 %copy-start.14 = (bf16[640,128]{1,0:T(8,128)(2,1)S(1)}, bf16[640,128]{1,0:T(8,128)(2,1)}, u32[]{:S(2)}) copy-start(bf16[640,128]{1,0:T(8,128)(2,1)} %param.6) | copy-start | bytes 491524
  448.9 14.8 %all-to-all-start.1 = ((bf16[32,20,128]{2,1,0:T(8,128)(2,1)}), bf16[32,20,128]{2,1,0:T(8,128)(2,1)S(1)}, u32[]{:S(2)}, u32[]{:S(2)}) async-start(bf16[32,20,128]{2,1,0:T(8,128)(2,1)} %reshape.136), calls=%async_computation.1 | async-start | bytes 393216 | tf_op jit(solution)/shard_map/all_to_all | solution.py:122
Sparse Core Ops, SparseCore 0:
  75.1 103.6 all-gather.7
  204.0 83.7 all-gather.9
  294.0 31.5 all-gather.11
  328.4 31.0 all-gather.13

commit v16 on v15

--- a/solution.py
+++ b/solution.py
@@ -86,10 +86,11 @@
     col_start = lax.axis_index("feat") * block_rows
     rows_xy = lax.all_gather(local_xy, "feat", axis=0, tiled=True)
     own = lax.dynamic_slice_in_dim(rows_xy, col_start, block_rows, 1)
-    moments = lax.dot_general(own, rows_xy, contract, preferred_element_type=jnp.float32)
+    gram_part = lax.dot_general(own, rows_xy[:, :width], contract, preferred_element_type=jnp.float32)
+    cross_part = lax.dot_general(own, rows_xy[:, width:], contract, preferred_element_type=jnp.float32)
     fi = lax.axis_index("feat")
-    cross_prefix = gather_feat(exclusive_prefix(moments[:, width:], stack_over))
-    gram_prefix = rotate(exclusive_prefix(moments[:, :width]), fi * block_rows, width, 1)
+    cross_prefix = gather_feat(exclusive_prefix(cross_part, stack_over))
+    gram_prefix = rotate(exclusive_prefix(gram_part), fi * block_rows, width, 1)
     span = (lax.axis_index("x") * lax.axis_size("z") + lax.axis_index("z")) * lax.axis_size("c") + lax.axis_index("c")
     seen = (span * (tok_dev * feat_count)).astype(jnp.float32)
     scale = 1.0 / jnp.maximum(seen, 1.0)

time: 473 us -> 472 us (level)
    dot_general x1 -> x2, matrix products: 9.83 us -> 13.3 us  [the longest x1 10.5 us: body(): lax.dot_general(own, rows_xy[:, :width], contract, preferred_element_type...]
  transfers between devices with their start and end apart: 30 -> 30, of which waited for: 21 -> 22; matrix products, arithmetic and copies ran while one was open for 2% -> 3% of each run, Pallas kernels for 0% -> 0%
where the time goes in v16:
time: 472 us; the launch traced here: 471 us
  waiting for transfers between devices  292 us (62%)
  blocking collectives  51.3 us (11%)
  starting transfers between devices  39.4 us (8%)
  other arithmetic  31.1 us (7%)
  matrix products  28.2 us (6%)
  local copies, waits for them, and re-layouts  15.3 us (3%)
  between operations  14.1 us (3%)
    all_gather x1, waiting for transfers between devices, body(): rows_xy = lax.all_gather(local_xy, 'feat', axis=0, tiled=True)  104 us
    all_gather x1, waiting for transfers between devices, exclusive_prefix(): along_z = stack(mine, 'z')  83.9 us
    all_to_all x1, blocking collectives, body(): lax.all_to_all(sorted_xy, TM, split_axis=0, concat_axis=0, tiled=True)  51.3 us
    ppermute x12, waiting for transfers between devices, gather_feat(): lax.ppermute(piece, 'feat', [(i, (i - k) % n) for i in range(n)])  34.2 us
    all_gather x1, waiting for transfers between devices, exclusive_prefix(): along_x = stack(piece, 'x')  31.6 us
    ppermute x12, starting transfers between devices, gather_feat(): lax.ppermute(piece, 'feat', [(i, (i - k) % n) for i in range(n)])  17.2 us
    ppermute x9, starting transfers between devices, stack_over(): lax.ppermute(piece, axis, [(i, (i + k) % n) for i in range(n)])  11.8 us
    all_gather x1, waiting for transfers between devices, exclusive_prefix(): before_x = stack(summed_x, 'z').reshape(total_z.shape)  11.7 us
  transfers between devices with their start and end apart: 30, of which 22 were waited for; matrix products, arithmetic and copies ran while one was open for 3% of the time, Pallas kernels for 0%

profile of v16, /device:TPU:1, one launch (start us, length us, event | category | flops | bytes accessed | tf_op | source)
XLA Modules:
  0.0 471.4 jit_solution(17305843906863882076)
XLA Ops:
  9.0 5.8 %convolution_convert_fusion = bf16[640,2176]{1,0:T(8,128)(2,1)} fusion(bf16[640,128]{1,0:T(8,128)(2,1)} %param.6, bf16[640,2048]{1,0:T(8,128)(2,1)} %param.5, s32[640]{0:T(1024)S(1)} %convert_add_fusion), kind=kOutput, calls=%fused_computation.8 | convolution fusion | flops 1789952000 | bytes 5573120 | tf_op jit(solution)/shard_map/dot_general | solution.py:81
  14.8 3.6 reshape.132
  18.3 51.3 %all_to_all.10 = bf16[32,20,2176]{2,1,0:T(8,128)(2,1)} all-to-all(bf16[32,20,2176]{2,1,0:T(8,128)(2,1)S(1)} %reshape.132), channel_id=1, replica_groups=mesh['x'=4,'z'=4,'c'=2,'feat'=4] {'x','z','c'}, dimensions={0} | all-to-all | bytes 5570560 | tf_op jit(solution)/shard_map/all_to_all | solution.py:83
  69.7 5.3 %reshape.133 = bf16[640,2176]{1,0:T(8,128)(2,1)} reshape(bf16[32,20,2176]{2,1,0:T(8,128)(2,1)} %all_to_all.10) | data formatting | bytes 5570560 | tf_op jit(solution)/shard_map/reshape | solution.py:84
  75.1 103.8 %all-gather.8.cloned.1.call-done = bf16[2560,2176]{1,0:T(8,128)(2,1)} async-done(((bf16[640,2176]{1,0:T(8,128)(2,1)}), bf16[2560,2176]{1,0:T(8,128)(2,1)}) %all-gather.8.cloned.1.call-update) | async-done | bytes 11141136 | tf_op jit(solution)/shard_map/all_gather | solution.py:87
  178.9 10.5 %fusion = f32[512,2048]{1,0:T(8,128)} fusion(bf16[2560,2176]{1,0:T(8,128)(2,1)} %all-gather.8.cloned.1.call-done, s32[]{:T(128)S(6)} %select_n.132), kind=kOutput, calls=%fused_computation.3 | convolution fusion | flops 5368709120 | bytes 17301508 | tf_op jit(solution)/shard_map/dot_general | solution.py:89
  190.3 7.1 %collective-permute-done.14 = f32[512,2048]{1,0:T(8,128)} collective-permute-done((f32[512,2048]{1,0:T(8,128)}, f32[512,2048]{1,0:T(8,128)}, u32[]{:S(2)}, u32[]{:S(2)}) %collective-permute-start.14) | collective-permute-done | bytes 4194336 | tf_op jit(solution)/shard_map/ppermute | solution.py:45
  197.4 3.9 dynamic-slice_add_fusion
  201.4 83.9 %all-gather.10.cloned.1.call-done = f32[1024,2048]{1,0:T(8,128)} async-done(((f32[256,2048]{1,0:T(8,128)}), f32[1024,2048]{1,0:T(8,128)}) %all-gather.10.cloned.1.call-update) | async-done | bytes 8388624 | tf_op jit(solution)/shard_map/all_gather | solution.py:49
  285.2 5.2 %select_reduce_fusion = (f32[256,2048]{1,0:T(8,128)S(1)}, f32[256,2048]{1,0:T(8,128)S(1)}) fusion(f32[4,256,2048]{2,1,0:T(8,128)} %bitcast.34, pred[4]{0:T(512)(128)(4,1)S(1)} %iota_compare_fusion.13), kind=kLoop, calls=%fused_computation.7 | loop fusion | flops 5242880 | bytes 12582916 | tf_op jit(solution)/shard_map/reduce_sum | solution.py:19
  291.4 31.6 %all-gather.12.cloned.1.call-done = f32[256,2048]{1,0:T(8,128)} async-done(((f32[64,2048]{1,0:T(8,128)}), f32[256,2048]{1,0:T(8,128)}) %all-gather.12.cloned.1.call-update) | async-done | bytes 2097168 | tf_op jit(solution)/shard_map/all_gather | solution.py:54
  323.0 2.7 select_reduce_fusion.1
  326.3 2.8 fusion.9
  330.0 1.1 collective-permute-done
  331.1 3.0 collective-permute-start.2
  334.5 2.3 collective-permute-start.3
  337.4 4.8 %collective-permute-done.1 = f32[256,128]{1,0:T(8,128)S(1)} collective-permute-done((f32[256,128]{1,0:T(8,128)S(1)}, f32[256,128]{1,0:T(8,128)S(1)}, u32[]{:S(2)}, u32[]{:S(2)}) %collective-permute-start.1) | collective-permute-done | bytes 131104 | tf_op jit(solution)/shard_map/ppermute | solution.py:35
  344.1 2.7 collective-permute-start.6
  346.8 11.7 %all-gather.14.cloned.1.call-done = f32[256,2048]{1,0:T(8,128)} async-done(((f32[64,2048]{1,0:T(8,128)}), f32[256,2048]{1,0:T(8,128)}) %all-gather.14.cloned.1.call-update) | async-done | bytes 2097168 | tf_op jit(solution)/shard_map/all_gather | solution.py:56
  358.4 3.2 add.157
  363.5 2.5 collective-permute-start.9
  367.3 3.0 collective-permute-done.8
  371.6 1.3 collective-permute-start.10
  374.9 1.3 collective-permute-start.13
  376.2 2.4 collective-permute-start.12
  378.7 1.2 collective-permute-start.11
  379.9 4.4 collective-permute-done.13
  384.3 6.6 %collective-permute-done.12 = f32[512,128]{1,0:T(8,128)S(1)} collective-permute-done((f32[512,128]{1,0:T(8,128)S(1)}, f32[512,128]{1,0:T(8,128)S(1)}, u32[]{:S(2)}, u32[]{:S(2)}) %collective-permute-start.12) | collective-permute-done | bytes 262176 | tf_op jit(solution)/shard_map/ppermute | solution.py:24
  391.6 1.2 maximum_multiply_fusion
  392.8 2.0 broadcast_select_fusion.1
  394.8 3.4 maximum_add_fusion
  399.3 1.8 fusion.16
  401.4 2.5 collective-permute-start.17
  403.9 1.1 collective-permute-start.16
  405.1 5.4 %collective-permute-done.18 = f32[512,128]{1,0:T(8,128)S(1)} collective-permute-done((f32[512,128]{1,0:T(8,128)S(1)}, f32[512,128]{1,0:T(8,128)S(1)}, u32[]{:S(2)}, u32[]{:S(2)}) %collective-permute-start.18) | collective-permute-done | bytes 262176 | tf_op jit(solution)/shard_map/ppermute | solution.py:24
  410.5 4.3 collective-permute-done.17
  416.5 1.8 fusion.15
  418.3 1.7 collective-permute-start.21
  420.0 2.2 collective-permute-start.20
  422.5 4.9 %collective-permute-done.21 = f32[512,128]{1,0:T(8,128)S(1)} collective-permute-done((f32[512,128]{1,0:T(8,128)S(1)}, f32[512,128]{1,0:T(8,128)S(1)}, u32[]{:S(2)}, u32[]{:S(2)}) %collective-permute-start.21) | collective-permute-done | bytes 262176 | tf_op jit(solution)/shard_map/ppermute | solution.py:24
  427.4 6.3 %collective-permute-done.20 = f32[512,128]{1,0:T(8,128)S(1)} collective-permute-done((f32[512,128]{1,0:T(8,128)S(1)}, f32[512,128]{1,0:T(8,128)S(1)}, u32[]{:S(2)}, u32[]{:S(2)}) %collective-permute-start.20) | collective-permute-done | bytes 262176 | tf_op jit(solution)/shard_map/ppermute | solution.py:24
  434.6 1.9 multiply_reduce_fusion
  437.3 1.9 fusion.21
  439.2 1.5 collective-permute-start.23
  440.7 1.6 collective-permute-start.24
  445.2 2.1 fusion.17
  448.1 6.6 %all-to-all-start.1 = ((bf16[32,20,128]{2,1,0:T(8,128)(2,1)}), bf16[32,20,128]{2,1,0:T(8,128)(2,1)S(1)}, u32[]{:S(2)}, u32[]{:S(2)}) async-start(bf16[32,20,128]{2,1,0:T(8,128)(2,1)} %reshape.136), calls=%async_computation.1 | async-start | bytes 393216 | tf_op jit(solution)/shard_map/all_to_all | solution.py:123
  454.8 8.1 %all-to-all-done.1 = bf16[32,20,128]{2,1,0:T(8,128)(2,1)S(1)} async-done(((bf16[32,20,128]{2,1,0:T(8,128)(2,1)}), bf16[32,20,128]{2,1,0:T(8,128)(2,1)S(1)}, u32[]{:S(2)}, u32[]{:S(2)}) %all-to-all-start.1) | async-done | bytes 163872 | tf_op jit(solution)/shard_map/all_to_all | solution.py:123
  (108 shorter events, 25.8 us)
Async XLA Ops:
  7.2 171.7 %all-gather.8.cloned.1.call-start = ((), (), s32[]{:S(2)}) async-start(), calls=%async_computation.2 | async-start | bytes 13926400 | tf_op jit(solution)/shard_map/all_gather | solution.py:87
  75.1 210.2 %all-gather.10.cloned.1.call-start = ((), (), s32[]{:S(2)}) async-start(), calls=%async_computation.3 | async-start | bytes 10485760 | tf_op jit(solution)/shard_map/all_gather | solution.py:49
  189.4 8.0 %collective-permute-start.14 = (f32[512,2048]{1,0:T(8,128)}, f32[512,2048]{1,0:T(8,128)}, u32[]{:S(2)}, u32[]{:S(2)}) collective-permute-start(f32[512,2048]{1,0:T(8,128)} %fusion), channel_id=1, source_target_pairs={{0,4},{4,0},{1,5},{5,1},{2,6},{6,2},{3,7},{7,3},{8,12},{12,8},{9,1... | collective-permute-start | bytes 12582920 | tf_op jit(solution)/shard_map/ppermute | solution.py:45
  201.3 121.7 %all-gather.12.cloned.1.call-start = ((), (), s32[]{:S(2)}) async-start(), calls=%async_computation.4 | async-start | bytes 2621440 | tf_op jit(solution)/shard_map/all_gather | solution.py:54
  291.3 67.1 %all-gather.14.cloned.1.call-start = ((), (), s32[]{:S(2)}) async-start(), calls=%async_computation.5 | async-start | bytes 2621440 | tf_op jit(solution)/shard_map/all_gather | solution.py:56
  329.0 2.1 collective-permute-start
  331.1 11.9 %copy-start.10 = (f32[512,128]{1,0:T(8,128)}, f32[512,128]{1,0:T(8,128)S(1)}, u32[]{:S(2)}) copy-start(f32[512,128]{1,0:T(8,128)S(1)} %collective-permute-done) | copy-start | bytes 786436
  331.1 6.3 %collective-permute-start.2 = (f32[256,128]{1,0:T(8,128)S(1)}, f32[256,128]{1,0:T(8,128)S(1)}, u32[]{:S(2)}, u32[]{:S(2)}) collective-permute-start(f32[256,128]{1,0:T(8,128)S(1)} %dynamic-slice_add_fusion.1), channel_id=1, source_target_pairs={{0,16},{8,24},{16,0},{24,8},{1,17},{9,25},{17,1},{25,9},{2,18},{10... | collective-permute-start | bytes 393224 | tf_op jit(solution)/shard_map/ppermute | solution.py:35
  334.1 8.1 %collective-permute-start.1 = (f32[256,128]{1,0:T(8,128)S(1)}, f32[256,128]{1,0:T(8,128)S(1)}, u32[]{:S(2)}, u32[]{:S(2)}) collective-permute-start(f32[256,128]{1,0:T(8,128)S(1)} %dynamic-slice_add_fusion.1), channel_id=1, source_target_pairs={{0,8},{8,16},{16,24},{24,0},{1,9},{9,17},{17,25},{25,1},{2,10},{10... | collective-permute-start | bytes 393224 | tf_op jit(solution)/shard_map/ppermute | solution.py:35
  334.5 8.5 %collective-permute-start.3 = (f32[256,128]{1,0:T(8,128)S(1)}, f32[256,128]{1,0:T(8,128)S(1)}, u32[]{:S(2)}, u32[]{:S(2)}) collective-permute-start(f32[256,128]{1,0:T(8,128)S(1)} %dynamic-slice_add_fusion.1), channel_id=1, source_target_pairs={{0,24},{8,0},{16,8},{24,16},{1,25},{9,1},{17,9},{25,17},{2,26},{10... | collective-permute-start | bytes 393224 | tf_op jit(solution)/shard_map/ppermute | solution.py:35
  343.8 18.4 %collective-permute-start.5 = (f32[64,128]{1,0:T(8,128)S(1)}, f32[64,128]{1,0:T(8,128)S(1)}, u32[]{:S(2)}, u32[]{:S(2)}) collective-permute-start(f32[64,128]{1,0:T(8,128)S(1)} %constant_dynamic-slice_fusion.1), channel_id=1, source_target_pairs={{0,64},{32,96},{64,0},{96,32},{1,65},{33,97},{65,1},{97,33},{2,66}... | collective-permute-start | bytes 98312 | tf_op jit(solution)/shard_map/ppermute | solution.py:35
  344.1 18.1 %collective-permute-start.4 = (f32[64,128]{1,0:T(8,128)S(1)}, f32[64,128]{1,0:T(8,128)S(1)}, u32[]{:S(2)}, u32[]{:S(2)}) collective-permute-start(f32[64,128]{1,0:T(8,128)S(1)} %constant_dynamic-slice_fusion.1), channel_id=1, source_target_pairs={{0,32},{32,64},{64,96},{96,0},{1,33},{33,65},{65,97},{97,1},{2,34}... | collective-permute-start | bytes 98312 | tf_op jit(solution)/shard_map/ppermute | solution.py:35
  344.1 18.1 %collective-permute-start.6 = (f32[64,128]{1,0:T(8,128)S(1)}, f32[64,128]{1,0:T(8,128)S(1)}, u32[]{:S(2)}, u32[]{:S(2)}) collective-permute-start(f32[64,128]{1,0:T(8,128)S(1)} %constant_dynamic-slice_fusion.1), channel_id=1, source_target_pairs={{0,96},{32,0},{64,32},{96,64},{1,97},{33,1},{65,33},{97,65},{2,98}... | collective-permute-start | bytes 98312 | tf_op jit(solution)/shard_map/ppermute | solution.py:35
  361.6 31.2 %collective-permute-start.15 = (f32[256,2048]{1,0:T(8,128)}, f32[256,2048]{1,0:T(8,128)S(1)}, u32[]{:S(2)}, u32[]{:S(2)}) collective-permute-start(f32[256,2048]{1,0:T(8,128)} %add.157), channel_id=1, source_target_pairs={{0,4},{4,0},{1,5},{5,1},{2,6},{6,2},{3,7},{7,3},{8,12},{12,8},{9,1... | collective-permute-start | bytes 6291464 | tf_op jit(solution)/shard_map/ppermute | solution.py:58
  363.5 3.8 collective-permute-start.9
  366.0 4.3 collective-permute-start.8
  366.5 4.4 collective-permute-start.7
  371.6 2.3 collective-permute-start.10
  374.9 9.4 %collective-permute-start.13 = (f32[512,128]{1,0:T(8,128)S(1)}, f32[512,128]{1,0:T(8,128)S(1)}, u32[]{:S(2)}, u32[]{:S(2)}) collective-permute-start(f32[512,128]{1,0:T(8,128)S(1)} %maximum_add_fusion.1), channel_id=1, source_target_pairs={{0,1},{1,2},{2,3},{3,0},{4,5},{5,6},{6,7},{7,4},{8,9},{9,10},{10,1... | collective-permute-start | bytes 786440 | tf_op jit(solution)/shard_map/ppermute | solution.py:24
  376.2 14.7 %collective-permute-start.12 = (f32[512,128]{1,0:T(8,128)S(1)}, f32[512,128]{1,0:T(8,128)S(1)}, u32[]{:S(2)}, u32[]{:S(2)}) collective-permute-start(f32[512,128]{1,0:T(8,128)S(1)} %maximum_add_fusion.1), channel_id=1, source_target_pairs={{0,2},{1,3},{2,0},{3,1},{4,6},{5,7},{6,4},{7,5},{8,10},{9,11},{10,... | collective-permute-start | bytes 786440 | tf_op jit(solution)/shard_map/ppermute | solution.py:24
  378.7 13.0 %collective-permute-start.11 = (f32[512,128]{1,0:T(8,128)S(1)}, f32[512,128]{1,0:T(8,128)}, u32[]{:S(2)}, u32[]{:S(2)}) collective-permute-start(f32[512,128]{1,0:T(8,128)S(1)} %maximum_add_fusion.1), channel_id=1, source_target_pairs={{0,3},{1,0},{2,1},{3,2},{4,7},{5,4},{6,5},{7,6},{8,11},{9,8},{10,9... | collective-permute-start | bytes 786440 | tf_op jit(solution)/shard_map/ppermute | solution.py:24
  384.3 6.6 %copy-start.11 = (f32[512,128]{1,0:T(8,128)}, f32[512,128]{1,0:T(8,128)S(1)}, u32[]{:S(2)}) copy-start(f32[512,128]{1,0:T(8,128)S(1)} %collective-permute-done.13) | copy-start | bytes 786436
  390.9 0.7 copy-start.12
  399.2 17.2 %copy-start = (f32[512,2048]{1,0:T(8,128)}, f32[512,2048]{1,0:T(8,128)S(1)}, u32[]{:S(2)}) copy-start(f32[512,2048]{1,0:T(8,128)S(1)} %fusion.2) | copy-start | bytes 12582916
  401.1 9.4 %collective-permute-start.18 = (f32[512,128]{1,0:T(8,128)S(1)}, f32[512,128]{1,0:T(8,128)S(1)}, u32[]{:S(2)}, u32[]{:S(2)}) collective-permute-start(f32[512,128]{1,0:T(8,128)S(1)} %fusion.16), channel_id=1, source_target_pairs={{0,1},{1,2},{2,3},{3,0},{4,5},{5,6},{6,7},{7,4},{8,9},{9,10},{10,1... | collective-permute-start | bytes 786440 | tf_op jit(solution)/shard_map/ppermute | solution.py:24
  401.4 13.4 %collective-permute-start.17 = (f32[512,128]{1,0:T(8,128)S(1)}, f32[512,128]{1,0:T(8,128)S(1)}, u32[]{:S(2)}, u32[]{:S(2)}) collective-permute-start(f32[512,128]{1,0:T(8,128)S(1)} %fusion.16), channel_id=1, source_target_pairs={{0,2},{1,3},{2,0},{3,1},{4,6},{5,7},{6,4},{7,5},{8,10},{9,11},{10,... | collective-permute-start | bytes 786440 | tf_op jit(solution)/shard_map/ppermute | solution.py:24
  403.9 11.7 %collective-permute-start.16 = (f32[512,128]{1,0:T(8,128)S(1)}, f32[512,128]{1,0:T(8,128)S(1)}, u32[]{:S(2)}, u32[]{:S(2)}) collective-permute-start(f32[512,128]{1,0:T(8,128)S(1)} %fusion.16), channel_id=1, source_target_pairs={{0,3},{1,0},{2,1},{3,2},{4,7},{5,4},{6,5},{7,6},{8,11},{9,8},{10,9... | collective-permute-start | bytes 786440 | tf_op jit(solution)/shard_map/ppermute | solution.py:24
  410.5 5.8 %copy-start.3 = (f32[512,128]{1,0:T(8,128)}, f32[512,128]{1,0:T(8,128)S(1)}, u32[]{:S(2)}) copy-start(f32[512,128]{1,0:T(8,128)S(1)} %collective-permute-done.18) | copy-start | bytes 786436
  414.8 1.4 copy-start.4
  415.6 0.7 copy-start.5
  418.3 15.8 %copy-start.6 = (f32[512,128]{1,0:T(8,128)}, f32[512,128]{1,0:T(8,128)S(1)}, u32[]{:S(2)}) copy-start(f32[512,128]{1,0:T(8,128)S(1)} %fusion.15) | copy-start | bytes 786436
  418.3 9.1 %collective-permute-start.21 = (f32[512,128]{1,0:T(8,128)S(1)}, f32[512,128]{1,0:T(8,128)S(1)}, u32[]{:S(2)}, u32[]{:S(2)}) collective-permute-start(f32[512,128]{1,0:T(8,128)S(1)} %fusion.15), channel_id=1, source_target_pairs={{0,1},{1,2},{2,3},{3,0},{4,5},{5,6},{6,7},{7,4},{8,9},{9,10},{10,1... | collective-permute-start | bytes 786440 | tf_op jit(solution)/shard_map/ppermute | solution.py:24
  420.0 13.8 %collective-permute-start.20 = (f32[512,128]{1,0:T(8,128)S(1)}, f32[512,128]{1,0:T(8,128)S(1)}, u32[]{:S(2)}, u32[]{:S(2)}) collective-permute-start(f32[512,128]{1,0:T(8,128)S(1)} %fusion.15), channel_id=1, source_target_pairs={{0,2},{1,3},{2,0},{3,1},{4,6},{5,7},{6,4},{7,5},{8,10},{9,11},{10,... | collective-permute-start | bytes 786440 | tf_op jit(solution)/shard_map/ppermute | solution.py:24
  422.1 11.6 %collective-permute-start.19 = (f32[512,128]{1,0:T(8,128)S(1)}, f32[512,128]{1,0:T(8,128)S(1)}, u32[]{:S(2)}, u32[]{:S(2)}) collective-permute-start(f32[512,128]{1,0:T(8,128)S(1)} %fusion.15), channel_id=1, source_target_pairs={{0,3},{1,0},{2,1},{3,2},{4,7},{5,4},{6,5},{7,6},{8,11},{9,8},{10,9... | collective-permute-start | bytes 786440 | tf_op jit(solution)/shard_map/ppermute | solution.py:24
  427.4 6.7 %copy-start.7 = (f32[512,128]{1,0:T(8,128)}, f32[512,128]{1,0:T(8,128)S(1)}, u32[]{:S(2)}) copy-start(f32[512,128]{1,0:T(8,128)S(1)} %collective-permute-done.21) | copy-start | bytes 786436
  433.8 0.7 copy-start.8
  433.8 0.8 copy-start.9
  434.6 2.7 copy-start.1
  439.2 4.2 collective-permute-start.23
  440.7 3.6 collective-permute-start.24
  442.4 2.4 collective-permute-start.22
  443.4 1.8 copy-start.2
  445.2 9.5 %copy-start.13 = (bf16[640,128]{1,0:T(8,128)(2,1)S(1)}, bf16[640,128]{1,0:T(8,128)(2,1)}, u32[]{:S(2)}) copy-start(bf16[640,128]{1,0:T(8,128)(2,1)} %param.6) | copy-start | bytes 491524
  448.1 14.9 %all-to-all-start.1 = ((bf16[32,20,128]{2,1,0:T(8,128)(2,1)}), bf16[32,20,128]{2,1,0:T(8,128)(2,1)S(1)}, u32[]{:S(2)}, u32[]{:S(2)}) async-start(bf16[32,20,128]{2,1,0:T(8,128)(2,1)} %reshape.136), calls=%async_computation.1 | async-start | bytes 393216 | tf_op jit(solution)/shard_map/all_to_all | solution.py:123
Sparse Core Ops, SparseCore 0:
  75.2 103.6 all-gather.7
  201.4 83.7 all-gather.9
  291.4 31.5 all-gather.11
  325.8 32.5 all-gather.13

commit v17 on v16

--- a/solution.py
+++ b/solution.py
@@ -36,16 +36,38 @@
     return jnp.take(jnp.stack(parts), (f - jnp.arange(n)) % n, axis=0)
 
 
-def exclusive_prefix(block, stack=lax.all_gather):
+def core_level(block):
+    ci = lax.axis_index("c")
+    half = block.shape[0] // 2
+    partner = lax.ppermute(block, "c", SWAP)
+    chip = block + partner
+    below = jnp.where(ci == 1, partner, 0.0)
+    return lax.dynamic_slice_in_dim(chip, ci * half, half, 0), below
+
+
+def core_level_by_halves(left, right):
+    ci = lax.axis_index("c")
+    half = left.shape[1] // 2
+    contract = (((0,), (0,)), ((), ()))
+    wanted = lax.dot_general(
+        lax.dynamic_slice_in_dim(left, (1 - ci) * half, half, 1), right, contract, preferred_element_type=jnp.float32
+    )
+    partner_half = lax.ppermute(wanted, "c", SWAP)
+    kept = lax.dot_general(
+        lax.dynamic_slice_in_dim(left, ci * half, half, 1), right, contract, preferred_element_type=jnp.float32
+    )
+    mine = kept + partner_half
+    rest = lax.ppermute(kept, "c", [(0, 1)])
+    below = jnp.where(ci == 1, jnp.concatenate([rest, partner_half], axis=0), 0.0)
+    return mine, below
+
+
+def exclusive_prefix(block, stack=lax.all_gather, first=None):
     ci = lax.axis_index("c")
     zi = lax.axis_index("z")
     xi = lax.axis_index("x")
-    rows = block.shape[0]
-    half = rows // 2
-    partner = lax.ppermute(block, "c", SWAP)
-    chip = block + partner
-    below = jnp.where(ci == 1, partner, 0.0)
-    mine = lax.dynamic_slice_in_dim(chip, ci * half, half, 0)
+    mine, below = core_level(block) if first is None else first
+    half = mine.shape[0]
     along_z = stack(mine, "z")
     before_z = masked_sum(along_z, zi)
     total_z = jnp.sum(along_z, axis=0)
@@ -70,10 +92,9 @@
     block_rows = width // feat_count
     share = tok_dev // spans
     contract = (((0,), (0,)), ((), ()))
-    highest = lax.Precision.HIGHEST
     hot = (span_of[:, None] == jnp.arange(spans)[None, :]).astype(jnp.float32)
     earlier = (jnp.arange(tok_dev)[:, None] > jnp.arange(tok_dev)[None, :]).astype(jnp.float32)
-    before = jnp.dot(earlier, hot, precision=highest, preferred_element_type=jnp.float32)
+    before = jnp.dot(earlier.astype(jnp.bfloat16), hot.astype(jnp.bfloat16), preferred_element_type=jnp.float32)
     rank = jnp.sum(before * hot, axis=1).astype(jnp.int32)
     dest = span_of * share + rank
     permute = (dest[None, :] == jnp.arange(tok_dev)[:, None]).astype(jnp.bfloat16)
@@ -86,11 +107,11 @@
     col_start = lax.axis_index("feat") * block_rows
     rows_xy = lax.all_gather(local_xy, "feat", axis=0, tiled=True)
     own = lax.dynamic_slice_in_dim(rows_xy, col_start, block_rows, 1)
-    gram_part = lax.dot_general(own, rows_xy[:, :width], contract, preferred_element_type=jnp.float32)
     cross_part = lax.dot_general(own, rows_xy[:, width:], contract, preferred_element_type=jnp.float32)
     fi = lax.axis_index("feat")
     cross_prefix = gather_feat(exclusive_prefix(cross_part, stack_over))
-    gram_prefix = rotate(exclusive_prefix(gram_part), fi * block_rows, width, 1)
+    first = core_level_by_halves(own, rows_xy[:, :width])
+    gram_prefix = rotate(exclusive_prefix(None, first=first), fi * block_rows, width, 1)
     span = (lax.axis_index("x") * lax.axis_size("z") + lax.axis_index("z")) * lax.axis_size("c") + lax.axis_index("c")
     seen = (span * (tok_dev * feat_count)).astype(jnp.float32)
     scale = 1.0 / jnp.maximum(seen, 1.0)

time: 472 us -> 476 us (level)
  matrix products: 28.2 us -> 37.4 us
  other arithmetic: 31.1 us -> 23.2 us
    dot_general x2 -> x3, matrix products: 11.6 us -> 20.6 us  [the longest x1 10.3 us: core_level_by_halves(): lax.dot_general(lax.dynamic_slice_in_dim(left, ci * half, half, 1), right...]
  transfers between devices with their start and end apart: 30 -> 31, of which waited for: 22 -> 22; matrix products, arithmetic and copies ran while one was open for 3% -> 3% of each run, Pallas kernels for 0% -> 0%
where the time goes in v17:
time: 476 us; the launch traced here: 475 us
  waiting for transfers between devices  292 us (61%)
  blocking collectives  51.3 us (11%)
  starting transfers between devices  41.3 us (9%)
  matrix products  37.4 us (8%)
  other arithmetic  23.2 us (5%)
  local copies, waits for them, and re-layouts  15.4 us (3%)
  between operations  14.2 us (3%)
    all_gather x1, waiting for transfers between devices, body(): rows_xy = lax.all_gather(local_xy, 'feat', axis=0, tiled=True)  104 us
    all_gather x1, waiting for transfers between devices, exclusive_prefix(): along_z = stack(mine, 'z')  83.8 us
    all_to_all x1, blocking collectives, body(): lax.all_to_all(sorted_xy, TM, split_axis=0, concat_axis=0, tiled=True)  51.3 us
    ppermute x12, waiting for transfers between devices, gather_feat(): lax.ppermute(piece, 'feat', [(i, (i - k) % n) for i in range(n)])  34.1 us
    all_gather x1, waiting for transfers between devices, exclusive_prefix(): along_x = stack(piece, 'x')  31.4 us
    ppermute x12, starting transfers between devices, gather_feat(): lax.ppermute(piece, 'feat', [(i, (i - k) % n) for i in range(n)])  17.8 us
    ppermute x9, starting transfers between devices, stack_over(): lax.ppermute(piece, axis, [(i, (i + k) % n) for i in range(n)])  11.8 us
    all_gather x1, waiting for transfers between devices, exclusive_prefix(): before_x = stack(summed_x, 'z').reshape(total_z.shape)  11.7 us
  transfers between devices with their start and end apart: 31, of which 22 were waited for; matrix products, arithmetic and copies ran while one was open for 3% of the time, Pallas kernels for 0%

profile of v17, /device:TPU:1, one launch (start us, length us, event | category | flops | bytes accessed | tf_op | source)
XLA Modules:
  0.0 475.2 jit_solution(6733824666473482370)
XLA Ops:
  9.0 5.8 %convolution_convert_fusion = bf16[640,2176]{1,0:T(8,128)(2,1)} fusion(bf16[640,128]{1,0:T(8,128)(2,1)} %param.6, bf16[640,2048]{1,0:T(8,128)(2,1)} %param.5, s32[640]{0:T(1024)S(1)} %convert_add_fusion), kind=kOutput, calls=%fused_computation.10 | convolution fusion | flops 1789952000 | bytes 5573120 | tf_op jit(solution)/shard_map/dot_general | solution.py:102
  14.8 3.6 reshape.132
  18.3 51.3 %all_to_all.10 = bf16[32,20,2176]{2,1,0:T(8,128)(2,1)} all-to-all(bf16[32,20,2176]{2,1,0:T(8,128)(2,1)S(1)} %reshape.132), channel_id=1, replica_groups=mesh['x'=4,'z'=4,'c'=2,'feat'=4] {'x','z','c'}, dimensions={0} | all-to-all | bytes 5570560 | tf_op jit(solution)/shard_map/all_to_all | solution.py:104
  69.7 5.3 %reshape.133 = bf16[640,2176]{1,0:T(8,128)(2,1)} reshape(bf16[32,20,2176]{2,1,0:T(8,128)(2,1)} %all_to_all.10) | data formatting | bytes 5570560 | tf_op jit(solution)/shard_map/reshape | solution.py:105
  75.1 103.8 %all-gather.8.cloned.1.call-done = bf16[2560,2176]{1,0:T(8,128)(2,1)} async-done(((bf16[640,2176]{1,0:T(8,128)(2,1)}), bf16[2560,2176]{1,0:T(8,128)(2,1)}) %all-gather.8.cloned.1.call-update) | async-done | bytes 11141136 | tf_op jit(solution)/shard_map/all_gather | solution.py:108
  178.8 9.2 %fusion = f32[256,2048]{1,0:T(8,128)} fusion(bf16[2560,2176]{1,0:T(8,128)(2,1)} %all-gather.8.cloned.1.call-done, s32[]{:T(128)S(6)} %dynamic_slice.35), kind=kOutput, calls=%fused_computation.3 | convolution fusion | flops 2684354560 | bytes 13893636 | tf_op jit(solution)/shard_map/dot_general | solution.py:52
  188.7 4.0 collective-permute-done.14
  192.7 10.3 %fusion.43 = (f32[256,2048]{1,0:T(8,128)}, f32[256,2048]{1,0:T(8,128)}) fusion(f32[256,2048]{1,0:T(8,128)S(1)} %collective-permute-done.14, bf16[2560,2176]{1,0:T(8,128)(2,1)} %all-gather.8.cloned.1.call-done, s32[]{:T(128)S(6)} %dynamic_slice.33), kind=kOutput, calls=%fused_computation.119 | convolution fusion | flops 2684878848 | bytes 18087940 | tf_op jit(solution)/shard_map/dot_general | solution.py:56
  203.1 83.8 %all-gather.10.cloned.1.call-done = f32[1024,2048]{1,0:T(8,128)} async-done(((f32[256,2048]{1,0:T(8,128)}), f32[1024,2048]{1,0:T(8,128)}) %all-gather.10.cloned.1.call-update) | async-done | bytes 8388624 | tf_op jit(solution)/shard_map/all_gather | solution.py:71
  287.0 5.2 %select_reduce_fusion = (f32[256,2048]{1,0:T(8,128)S(1)}, f32[256,2048]{1,0:T(8,128)S(1)}) fusion(f32[4,256,2048]{2,1,0:T(8,128)} %bitcast.34, pred[4]{0:T(512)(128)(4,1)S(1)} %iota_compare_fusion.7), kind=kLoop, calls=%fused_computation.9 | loop fusion | flops 5242880 | bytes 12582916 | tf_op jit(solution)/shard_map/reduce_sum | solution.py:19
  293.3 31.4 %all-gather.12.cloned.1.call-done = f32[256,2048]{1,0:T(8,128)} async-done(((f32[64,2048]{1,0:T(8,128)}), f32[256,2048]{1,0:T(8,128)}) %all-gather.12.cloned.1.call-update) | async-done | bytes 2097168 | tf_op jit(solution)/shard_map/all_gather | solution.py:76
  324.7 2.7 select_reduce_fusion.1
  327.5 2.9 fusion.10
  332.4 3.0 collective-permute-start.2
  335.8 2.3 collective-permute-start.3
  338.7 4.4 collective-permute-done.1
  343.1 1.2 collective-permute-done.3
  345.3 2.7 collective-permute-start.6
  348.0 11.7 %all-gather.14.cloned.1.call-done = f32[256,2048]{1,0:T(8,128)} async-done(((f32[64,2048]{1,0:T(8,128)}), f32[256,2048]{1,0:T(8,128)}) %all-gather.14.cloned.1.call-update) | async-done | bytes 2097168 | tf_op jit(solution)/shard_map/all_gather | solution.py:78
  359.7 3.2 add.165
  364.1 2.7 collective-permute-start.9
  367.9 3.3 collective-permute-done.8
  372.3 1.3 collective-permute-start.16
  373.7 1.4 collective-permute-start.10
  375.1 3.7 collective-permute-done.10
  379.8 1.3 collective-permute-start.13
  381.1 2.3 collective-permute-start.12
  383.5 1.2 collective-permute-start.11
  384.7 4.1 collective-permute-done.13
  388.8 6.5 %collective-permute-done.12 = f32[512,128]{1,0:T(8,128)S(1)} collective-permute-done((f32[512,128]{1,0:T(8,128)S(1)}, f32[512,128]{1,0:T(8,128)S(1)}, u32[]{:S(2)}, u32[]{:S(2)}) %collective-permute-start.12) | collective-permute-done | bytes 262176 | tf_op jit(solution)/shard_map/ppermute | solution.py:24
  396.0 1.2 maximum_multiply_fusion
  397.2 2.7 broadcast_select_fusion.1
  402.2 1.8 fusion.18
  405.0 2.2 collective-permute-start.18
  408.4 4.4 collective-permute-done.19
  412.8 6.0 %collective-permute-done.18 = f32[512,128]{1,0:T(8,128)S(1)} collective-permute-done((f32[512,128]{1,0:T(8,128)S(1)}, f32[512,128]{1,0:T(8,128)S(1)}, u32[]{:S(2)}, u32[]{:S(2)}) %collective-permute-start.18) | collective-permute-done | bytes 262176 | tf_op jit(solution)/shard_map/ppermute | solution.py:24
  419.8 1.8 fusion.17
  421.6 2.1 collective-permute-start.22
  423.7 2.3 collective-permute-start.21
  426.2 4.2 collective-permute-done.22
  430.4 7.1 %collective-permute-done.21 = f32[512,128]{1,0:T(8,128)S(1)} collective-permute-done((f32[512,128]{1,0:T(8,128)S(1)}, f32[512,128]{1,0:T(8,128)S(1)}, u32[]{:S(2)}, u32[]{:S(2)}) %collective-permute-start.21) | collective-permute-done | bytes 262176 | tf_op jit(solution)/shard_map/ppermute | solution.py:24
  438.4 1.9 multiply_reduce_fusion
  441.1 1.9 fusion.23
  443.0 1.2 collective-permute-start.24
  444.2 2.1 collective-permute-start.25
  449.0 2.2 fusion.19
  451.9 6.5 %all-to-all-start.1 = ((bf16[32,20,128]{2,1,0:T(8,128)(2,1)}), bf16[32,20,128]{2,1,0:T(8,128)(2,1)S(1)}, u32[]{:S(2)}, u32[]{:S(2)}) async-start(bf16[32,20,128]{2,1,0:T(8,128)(2,1)} %reshape.136), calls=%async_computation.1 | async-start | bytes 393216 | tf_op jit(solution)/shard_map/all_to_all | solution.py:144
  458.6 8.1 %all-to-all-done.1 = bf16[32,20,128]{2,1,0:T(8,128)(2,1)S(1)} async-done(((bf16[32,20,128]{2,1,0:T(8,128)(2,1)}), bf16[32,20,128]{2,1,0:T(8,128)(2,1)S(1)}, u32[]{:S(2)}, u32[]{:S(2)}) %all-to-all-start.1) | async-done | bytes 163872 | tf_op jit(solution)/shard_map/all_to_all | solution.py:144
  (114 shorter events, 25.6 us)
Async XLA Ops:
  7.2 171.7 %all-gather.8.cloned.1.call-start = ((), (), s32[]{:S(2)}) async-start(), calls=%async_computation.2 | async-start | bytes 13926400 | tf_op jit(solution)/shard_map/all_gather | solution.py:108
  75.0 212.0 %all-gather.10.cloned.1.call-start = ((), (), s32[]{:S(2)}) async-start(), calls=%async_computation.3 | async-start | bytes 10485760 | tf_op jit(solution)/shard_map/all_gather | solution.py:71
  188.1 4.6 collective-permute-start.14
  192.7 10.3 %copy-start.7 = (f32[256,2048]{1,0:T(8,128)}, f32[256,2048]{1,0:T(8,128)S(1)}, u32[]{:S(2)}) copy-start(f32[256,2048]{1,0:T(8,128)S(1)} %collective-permute-done.14) | copy-start | bytes 6291460
  203.1 121.7 %all-gather.12.cloned.1.call-start = ((), (), s32[]{:S(2)}) async-start(), calls=%async_computation.4 | async-start | bytes 2621440 | tf_op jit(solution)/shard_map/all_gather | solution.py:76
  293.0 66.6 %all-gather.14.cloned.1.call-start = ((), (), s32[]{:S(2)}) async-start(), calls=%async_computation.5 | async-start | bytes 2621440 | tf_op jit(solution)/shard_map/all_gather | solution.py:78
  330.3 2.1 collective-permute-start
  332.4 11.9 %copy-start.12 = (f32[512,128]{1,0:T(8,128)}, f32[512,128]{1,0:T(8,128)S(1)}, u32[]{:S(2)}) copy-start(f32[512,128]{1,0:T(8,128)S(1)} %collective-permute-done) | copy-start | bytes 786436
  332.4 6.3 %collective-permute-start.2 = (f32[256,128]{1,0:T(8,128)S(1)}, f32[256,128]{1,0:T(8,128)S(1)}, u32[]{:S(2)}, u32[]{:S(2)}) collective-permute-start(f32[256,128]{1,0:T(8,128)S(1)} %dynamic-slice_add_fusion), channel_id=1, source_target_pairs={{0,16},{8,24},{16,0},{24,8},{1,17},{9,25},{17,1},{25,9},{2,18},{10... | collective-permute-start | bytes 393224 | tf_op jit(solution)/shard_map/ppermute | solution.py:35
  335.4 7.7 %collective-permute-start.1 = (f32[256,128]{1,0:T(8,128)S(1)}, f32[256,128]{1,0:T(8,128)S(1)}, u32[]{:S(2)}, u32[]{:S(2)}) collective-permute-start(f32[256,128]{1,0:T(8,128)S(1)} %dynamic-slice_add_fusion), channel_id=1, source_target_pairs={{0,8},{8,16},{16,24},{24,0},{1,9},{9,17},{17,25},{25,1},{2,10},{10... | collective-permute-start | bytes 393224 | tf_op jit(solution)/shard_map/ppermute | solution.py:35
  335.8 8.6 %collective-permute-start.3 = (f32[256,128]{1,0:T(8,128)S(1)}, f32[256,128]{1,0:T(8,128)S(1)}, u32[]{:S(2)}, u32[]{:S(2)}) collective-permute-start(f32[256,128]{1,0:T(8,128)S(1)} %dynamic-slice_add_fusion), channel_id=1, source_target_pairs={{0,24},{8,0},{16,8},{24,16},{1,25},{9,1},{17,9},{25,17},{2,26},{10... | collective-permute-start | bytes 393224 | tf_op jit(solution)/shard_map/ppermute | solution.py:35
  345.1 18.3 %collective-permute-start.5 = (f32[64,128]{1,0:T(8,128)S(1)}, f32[64,128]{1,0:T(8,128)S(1)}, u32[]{:S(2)}, u32[]{:S(2)}) collective-permute-start(f32[64,128]{1,0:T(8,128)S(1)} %constant_dynamic-slice_fusion.1), channel_id=1, source_target_pairs={{0,64},{32,96},{64,0},{96,32},{1,65},{33,97},{65,1},{97,33},{2,66}... | collective-permute-start | bytes 98312 | tf_op jit(solution)/shard_map/ppermute | solution.py:35
  345.2 18.2 %collective-permute-start.4 = (f32[64,128]{1,0:T(8,128)S(1)}, f32[64,128]{1,0:T(8,128)S(1)}, u32[]{:S(2)}, u32[]{:S(2)}) collective-permute-start(f32[64,128]{1,0:T(8,128)S(1)} %constant_dynamic-slice_fusion.1), channel_id=1, source_target_pairs={{0,32},{32,64},{64,96},{96,0},{1,33},{33,65},{65,97},{97,1},{2,34}... | collective-permute-start | bytes 98312 | tf_op jit(solution)/shard_map/ppermute | solution.py:35
  345.3 18.1 %collective-permute-start.6 = (f32[64,128]{1,0:T(8,128)S(1)}, f32[64,128]{1,0:T(8,128)S(1)}, u32[]{:S(2)}, u32[]{:S(2)}) collective-permute-start(f32[64,128]{1,0:T(8,128)S(1)} %constant_dynamic-slice_fusion.1), channel_id=1, source_target_pairs={{0,96},{32,0},{64,32},{96,64},{1,97},{33,1},{65,33},{97,65},{2,98}... | collective-permute-start | bytes 98312 | tf_op jit(solution)/shard_map/ppermute | solution.py:35
  362.9 34.4 %collective-permute-start.15 = (f32[256,2048]{1,0:T(8,128)}, f32[256,2048]{1,0:T(8,128)}, u32[]{:S(2)}, u32[]{:S(2)}) collective-permute-start(f32[256,2048]{1,0:T(8,128)} %add.165), channel_id=1, source_target_pairs={{0,4},{4,0},{1,5},{5,1},{2,6},{6,2},{3,7},{7,3},{8,12},{12,8},{9,1... | collective-permute-start | bytes 6291464 | tf_op jit(solution)/shard_map/ppermute | solution.py:80
  364.1 3.7 collective-permute-start.9
  366.8 4.4 collective-permute-start.8
  367.1 4.6 collective-permute-start.7
  372.3 27.6 %collective-permute-start.16 = (f32[256,2048]{1,0:T(8,128)}, f32[256,2048]{1,0:T(8,128)S(1)}, u32[]{:S(2)}, u32[]{:S(2)}) collective-permute-start(f32[256,2048]{1,0:T(8,128)} %get-tuple-element.22), channel_id=1, source_target_pairs={{0,4},{1,5},{2,6},{3,7},{8,12},{9,13},{10,14},{11,15},{16,20},{17,... | collective-permute-start | bytes 6291464 | tf_op jit(solution)/shard_map/ppermute | solution.py:60
  373.7 5.1 %collective-permute-start.10 = (f32[256,128]{1,0:T(8,128)S(1)}, f32[256,128]{1,0:T(8,128)S(1)}, u32[]{:S(2)}, u32[]{:S(2)}) collective-permute-start(f32[256,128]{1,0:T(8,128)S(1)} %bitcast_add_fusion), channel_id=1, source_target_pairs={{0,4},{4,0},{1,5},{5,1},{2,6},{6,2},{3,7},{7,3},{8,12},{12,8},{9,1... | collective-permute-start | bytes 393224 | tf_op jit(solution)/shard_map/ppermute | solution.py:80
  379.8 9.0 %collective-permute-start.13 = (f32[512,128]{1,0:T(8,128)S(1)}, f32[512,128]{1,0:T(8,128)S(1)}, u32[]{:S(2)}, u32[]{:S(2)}) collective-permute-start(f32[512,128]{1,0:T(8,128)S(1)} %maximum_add_fusion.1), channel_id=1, source_target_pairs={{0,1},{1,2},{2,3},{3,0},{4,5},{5,6},{6,7},{7,4},{8,9},{9,10},{10,1... | collective-permute-start | bytes 786440 | tf_op jit(solution)/shard_map/ppermute | solution.py:24
  381.1 14.2 %collective-permute-start.12 = (f32[512,128]{1,0:T(8,128)S(1)}, f32[512,128]{1,0:T(8,128)S(1)}, u32[]{:S(2)}, u32[]{:S(2)}) collective-permute-start(f32[512,128]{1,0:T(8,128)S(1)} %maximum_add_fusion.1), channel_id=1, source_target_pairs={{0,2},{1,3},{2,0},{3,1},{4,6},{5,7},{6,4},{7,5},{8,10},{9,11},{10,... | collective-permute-start | bytes 786440 | tf_op jit(solution)/shard_map/ppermute | solution.py:24
  383.5 12.6 %collective-permute-start.11 = (f32[512,128]{1,0:T(8,128)S(1)}, f32[512,128]{1,0:T(8,128)}, u32[]{:S(2)}, u32[]{:S(2)}) collective-permute-start(f32[512,128]{1,0:T(8,128)S(1)} %maximum_add_fusion.1), channel_id=1, source_target_pairs={{0,3},{1,0},{2,1},{3,2},{4,7},{5,4},{6,5},{7,6},{8,11},{9,8},{10,9... | collective-permute-start | bytes 786440 | tf_op jit(solution)/shard_map/ppermute | solution.py:24
  388.8 6.5 %copy-start.13 = (f32[512,128]{1,0:T(8,128)}, f32[512,128]{1,0:T(8,128)S(1)}, u32[]{:S(2)}) copy-start(f32[512,128]{1,0:T(8,128)S(1)} %collective-permute-done.13) | copy-start | bytes 786436
  395.3 0.7 copy-start.14
  397.2 2.9 copy-start.8
  402.2 17.7 %copy-start = (f32[512,2048]{1,0:T(8,128)}, f32[512,2048]{1,0:T(8,128)S(1)}, u32[]{:S(2)}) copy-start(f32[512,2048]{1,0:T(8,128)S(1)} %fusion.4) | copy-start | bytes 12582916
  404.0 8.8 %collective-permute-start.19 = (f32[512,128]{1,0:T(8,128)S(1)}, f32[512,128]{1,0:T(8,128)S(1)}, u32[]{:S(2)}, u32[]{:S(2)}) collective-permute-start(f32[512,128]{1,0:T(8,128)S(1)} %fusion.18), channel_id=1, source_target_pairs={{0,1},{1,2},{2,3},{3,0},{4,5},{5,6},{6,7},{7,4},{8,9},{9,10},{10,1... | collective-permute-start | bytes 786440 | tf_op jit(solution)/shard_map/ppermute | solution.py:24
  405.0 13.8 %collective-permute-start.18 = (f32[512,128]{1,0:T(8,128)S(1)}, f32[512,128]{1,0:T(8,128)S(1)}, u32[]{:S(2)}, u32[]{:S(2)}) collective-permute-start(f32[512,128]{1,0:T(8,128)S(1)} %fusion.18), channel_id=1, source_target_pairs={{0,2},{1,3},{2,0},{3,1},{4,6},{5,7},{6,4},{7,5},{8,10},{9,11},{10,... | collective-permute-start | bytes 786440 | tf_op jit(solution)/shard_map/ppermute | solution.py:24
  407.2 11.6 %collective-permute-start.17 = (f32[512,128]{1,0:T(8,128)S(1)}, f32[512,128]{1,0:T(8,128)S(1)}, u32[]{:S(2)}, u32[]{:S(2)}) collective-permute-start(f32[512,128]{1,0:T(8,128)S(1)} %fusion.18), channel_id=1, source_target_pairs={{0,3},{1,0},{2,1},{3,2},{4,7},{5,4},{6,5},{7,6},{8,11},{9,8},{10,9... | collective-permute-start | bytes 786440 | tf_op jit(solution)/shard_map/ppermute | solution.py:24
  412.8 6.7 %copy-start.3 = (f32[512,128]{1,0:T(8,128)}, f32[512,128]{1,0:T(8,128)S(1)}, u32[]{:S(2)}) copy-start(f32[512,128]{1,0:T(8,128)S(1)} %collective-permute-done.19) | copy-start | bytes 786436
  418.8 0.7 copy-start.4
  418.8 0.8 copy-start.5
  421.6 16.2 %copy-start.6 = (f32[512,128]{1,0:T(8,128)}, f32[512,128]{1,0:T(8,128)S(1)}, u32[]{:S(2)}) copy-start(f32[512,128]{1,0:T(8,128)S(1)} %fusion.17) | copy-start | bytes 786436
  421.6 8.8 %collective-permute-start.22 = (f32[512,128]{1,0:T(8,128)S(1)}, f32[512,128]{1,0:T(8,128)S(1)}, u32[]{:S(2)}, u32[]{:S(2)}) collective-permute-start(f32[512,128]{1,0:T(8,128)S(1)} %fusion.17), channel_id=1, source_target_pairs={{0,1},{1,2},{2,3},{3,0},{4,5},{5,6},{6,7},{7,4},{8,9},{9,10},{10,1... | collective-permute-start | bytes 786440 | tf_op jit(solution)/shard_map/ppermute | solution.py:24
  423.7 13.8 %collective-permute-start.21 = (f32[512,128]{1,0:T(8,128)S(1)}, f32[512,128]{1,0:T(8,128)S(1)}, u32[]{:S(2)}, u32[]{:S(2)}) collective-permute-start(f32[512,128]{1,0:T(8,128)S(1)} %fusion.17), channel_id=1, source_target_pairs={{0,2},{1,3},{2,0},{3,1},{4,6},{5,7},{6,4},{7,5},{8,10},{9,11},{10,... | collective-permute-start | bytes 786440 | tf_op jit(solution)/shard_map/ppermute | solution.py:24
  426.0 11.5 %collective-permute-start.20 = (f32[512,128]{1,0:T(8,128)S(1)}, f32[512,128]{1,0:T(8,128)S(1)}, u32[]{:S(2)}, u32[]{:S(2)}) collective-permute-start(f32[512,128]{1,0:T(8,128)S(1)} %fusion.17), channel_id=1, source_target_pairs={{0,3},{1,0},{2,1},{3,2},{4,7},{5,4},{6,5},{7,6},{8,11},{9,8},{10,9... | collective-permute-start | bytes 786440 | tf_op jit(solution)/shard_map/ppermute | solution.py:24
  430.4 7.4 %copy-start.9 = (f32[512,128]{1,0:T(8,128)}, f32[512,128]{1,0:T(8,128)S(1)}, u32[]{:S(2)}) copy-start(f32[512,128]{1,0:T(8,128)S(1)} %collective-permute-done.22) | copy-start | bytes 786436
  437.6 0.7 copy-start.10
  437.6 0.8 copy-start.11
  438.4 2.7 copy-start.1
  443.0 4.0 collective-permute-start.24
  444.2 3.8 collective-permute-start.25
  446.3 2.4 collective-permute-start.23
  447.0 2.0 copy-start.2
  449.0 9.4 %copy-start.15 = (bf16[640,128]{1,0:T(8,128)(2,1)S(1)}, bf16[640,128]{1,0:T(8,128)(2,1)}, u32[]{:S(2)}) copy-start(bf16[640,128]{1,0:T(8,128)(2,1)} %param.6) | copy-start | bytes 491524
  451.9 14.8 %all-to-all-start.1 = ((bf16[32,20,128]{2,1,0:T(8,128)(2,1)}), bf16[32,20,128]{2,1,0:T(8,128)(2,1)S(1)}, u32[]{:S(2)}, u32[]{:S(2)}) async-start(bf16[32,20,128]{2,1,0:T(8,128)(2,1)} %reshape.136), calls=%async_computation.1 | async-start | bytes 393216 | tf_op jit(solution)/shard_map/all_to_all | solution.py:144
Sparse Core Ops, SparseCore 0:
  75.1 103.6 all-gather.7
  203.2 83.7 all-gather.9
  293.2 31.5 all-gather.11
  327.6 32.0 all-gather.13
